TPU v7x, 128 devices: a whole 4x4x4 slice. The times are simulated.
128 devices in a mesh: vessel: 8 (over x, core), blk: 16 (over z, y).
Axes of the slice: x: 4, y: 4, z: 4, core: 2. Of those that a mesh axis runs over, the one named last changes fastest.
Arguments:
- populations: float32 [19, 64, 512, 128], P(None, 'vessel', 'blk'), may hold values from 0.5 to 1.5
- voxel_mask: int32 [64, 512, 128], P('vessel', 'blk'), may hold values from 0 to 2
- tracer: float32 [64, 32, 256], P('blk', 'vessel'), may hold values from -6 to 6
Outputs:
- final_populations: float32 [19, 64, 512, 128], P(None, 'vessel', 'blk')
- final_tracer: float32 [64, 32, 256], P('blk', 'vessel')
All inputs are finite; a program needn't handle non-finite values.
Results may differ from a plain program's by a relative error of at most 0.0001.
Values sent between devices are 32-bit elements; how exact they have to be, the bound alone decides.
No kernel may reach another device: no remote copies, remote signals or barrier semaphores. Data moves between devices by JAX's collectives and lax.ppermute only.
A program may use at most 128 MiB of HBM per device.

v0:
```python
import functools

import jax
import jax.numpy as jnp
import numpy as np
from jax import lax
from jax.experimental import pallas as pl
from jax.experimental.pallas import tpu as pltpu
from jax.sharding import PartitionSpec as P

STEPS = 4
TRACER_STEPS = 2


VELOCITY = np.array(
    [
        [0, 0, 0],
        [1, 0, 0],
        [-1, 0, 0],
        [0, 1, 0],
        [0, -1, 0],
        [0, 0, 1],
        [0, 0, -1],
        [1, 1, 0],
        [-1, -1, 0],
        [1, -1, 0],
        [-1, 1, 0],
        [1, 0, 1],
        [-1, 0, -1],
        [1, 0, -1],
        [-1, 0, 1],
        [0, 1, 1],
        [0, -1, -1],
        [0, 1, -1],
        [0, -1, 1],
    ]
)
WEIGHTS = np.array([1.0 / 3.0] + [1.0 / 18.0] * 6 + [1.0 / 36.0] * 12)
OPPOSITE = [0, 2, 1, 4, 3, 6, 5, 8, 7, 10, 9, 12, 11, 14, 13, 16, 15, 18, 17]
relax_rate = 1.25
pore_damping = 0.5
advect_gain = 8.0
diffusion = 0.1

NPOP = 19
CX = [int(v) for v in VELOCITY[:, 0]]
CY = [int(v) for v in VELOCITY[:, 1]]
CZ = [int(v) for v in VELOCITY[:, 2]]
CXP = [i for i in range(NPOP) if CX[i] == 1]
CXM = [i for i in range(NPOP) if CX[i] == -1]
CYP = [i for i in range(NPOP) if CY[i] == 1]
CYM = [i for i in range(NPOP) if CY[i] == -1]
SHIFTED = [i for i in range(NPOP) if CX[i] != 0 or CY[i] != 0]
ROWS = 8
YOFF = 8


def moments_chunk(g):
    w0 = jnp.float32(WEIGHTS[0])
    w1 = jnp.float32(WEIGHTS[1])
    w2 = jnp.float32(WEIGHTS[7])
    s1 = ((g[1] + g[2]) + (g[3] + g[4])) + (g[5] + g[6])
    s2 = (((g[7] + g[8]) + (g[9] + g[10])) + ((g[11] + g[12]) + (g[13] + g[14]))) + (
        (g[15] + g[16]) + (g[17] + g[18])
    )
    density = w0 * g[0] + w1 * s1 + w2 * s2
    mx = w1 * (g[1] - g[2]) + w2 * (((g[7] - g[8]) + (g[9] - g[10])) + ((g[11] - g[12]) + (g[13] - g[14])))
    my = w1 * (g[3] - g[4]) + w2 * (((g[7] - g[8]) + (g[10] - g[9])) + ((g[15] - g[16]) + (g[17] - g[18])))
    mz = w1 * (g[5] - g[6]) + w2 * (((g[11] - g[12]) + (g[14] - g[13])) + ((g[15] - g[16]) + (g[18] - g[17])))
    return density, (mx, my, mz)


def collide_chunk(g, mask):
    density, (mx, my, mz) = moments_chunk(g)
    ux = mx / density
    uy = my / density
    uz = mz / density
    porous = mask == 1
    ux = jnp.where(porous, pore_damping * ux, ux)
    uy = jnp.where(porous, pore_damping * uy, uy)
    uz = jnp.where(porous, pore_damping * uz, uz)
    speed_sq = ux * ux + uy * uy + uz * uz
    solid = mask == 2
    comps = (ux, uy, uz)
    out = [None] * NPOP
    for i in range(NPOP):
        proj = None
        for d in range(3):
            c = int(VELOCITY[i, d])
            if c == 0:
                continue
            term = comps[d] if c > 0 else -comps[d]
            proj = term if proj is None else proj + term
        if proj is None:
            balance = density * (1.0 - 1.5 * speed_sq)
        else:
            balance = density * (1.0 + 3.0 * proj + 4.5 * proj * proj - 1.5 * speed_sq)
        relaxed = g[i] + relax_rate * (balance - g[i])
        out[i] = jnp.where(solid, g[OPPOSITE[i]], relaxed)
    return out


def lb_kernel(mode, nx, ny, *refs):
    if mode == "first":
        src_ref, mask_ref = refs[:2]
        rest = refs[2:]
    else:
        src_ref, mask_ref, xlo, xhi, ylo, yhi, k7, k8, k9, k10 = refs[:10]
        rest = refs[10:]
    if mode == "last":
        out_ref, coarse_ref, ext, flow_s = rest
    else:
        out_ref, fxh, fxl, fyh, fyl, o7, o8, o9, o10 = rest[:9]
        ext = rest[9] if mode == "mid" else None

    if mode != "first":
        for i in SHIFTED:
            ext[i, 1 : nx + 1, YOFF : YOFF + ny, :] = src_ref[i]
        for k, i in enumerate(CXP):
            ext[i, 0, YOFF : YOFF + ny, :] = xlo[k]
        for k, i in enumerate(CXM):
            ext[i, nx + 1, YOFF : YOFF + ny, :] = xhi[k]
        for k, i in enumerate(CYP):
            for x in range(nx):
                ext[i, x + 1, YOFF - 1 : YOFF, :] = ylo[k, x : x + 1, :]
        for k, i in enumerate(CYM):
            for x in range(nx):
                ext[i, x + 1, YOFF + ny : YOFF + ny + 1, :] = yhi[k, x : x + 1, :]
        ext[7, 0, YOFF - 1 : YOFF, :] = k7[...]
        ext[8, nx + 1, YOFF + ny : YOFF + ny + 1, :] = k8[...]
        ext[9, 0, YOFF + ny : YOFF + ny + 1, :] = k9[...]
        ext[10, nx + 1, YOFF - 1 : YOFF, :] = k10[...]

    def body(x, carry):
        for y0 in range(0, ny, ROWS):
            g = []
            for i in range(NPOP):
                if mode == "first":
                    v = src_ref[i, x, pl.ds(y0, ROWS), :]
                elif i in SHIFTED:
                    v = ext[i, x + 1 - CX[i], pl.ds(YOFF + y0 - CY[i], ROWS), :]
                else:
                    v = src_ref[i, x, pl.ds(y0, ROWS), :]
                if mode != "first" and CZ[i] != 0:
                    v = pltpu.roll(v, CZ[i] % v.shape[1], 1)
                g.append(v)
            mask = mask_ref[x, pl.ds(y0, ROWS), :]
            if mode == "last":
                for i in range(NPOP):
                    out_ref[i, x, pl.ds(y0, ROWS), :] = g[i]
                density, mom = moments_chunk(g)
                solid = mask == 2
                for d in range(3):
                    flow_s[d, x, pl.ds(y0, ROWS), :] = jnp.where(solid, jnp.float32(0.0), mom[d] / density)
            else:
                post = collide_chunk(g, mask)
                for i in range(NPOP):
                    out_ref[i, x, pl.ds(y0, ROWS), :] = post[i]
        return carry

    lax.fori_loop(0, nx, body, 0)

    if mode == "last":
        nz = flow_s.shape[3]
        pz = (
            lax.broadcasted_iota(jnp.int32, (nz // 2, nz), 1) // 2 == lax.broadcasted_iota(jnp.int32, (nz // 2, nz), 0)
        ).astype(jnp.float32)
        py = (
            lax.broadcasted_iota(jnp.int32, (ny, ny // 2), 0) // 2 == lax.broadcasted_iota(jnp.int32, (ny, ny // 2), 1)
        ).astype(jnp.float32)
        for d in range(3):
            for xp in range(nx // 2):
                plane = flow_s[d, 2 * xp] + flow_s[d, 2 * xp + 1]
                zy = lax.dot_general(
                    pz,
                    plane,
                    (((1,), (1,)), ((), ())),
                    precision=lax.Precision.HIGHEST,
                    preferred_element_type=jnp.float32,
                )
                zc = jnp.dot(zy, py, precision=lax.Precision.HIGHEST, preferred_element_type=jnp.float32)
                coarse_ref[d, xp] = zc * jnp.float32(0.125)
    else:
        for k, i in enumerate(CXP):
            fxh[k] = out_ref[i, nx - 1]
        for k, i in enumerate(CXM):
            fxl[k] = out_ref[i, 0]
        for k, i in enumerate(CYP):
            for x in range(nx):
                fyh[k, x : x + 1, :] = out_ref[i, x, ny - 1 : ny, :]
        for k, i in enumerate(CYM):
            for x in range(nx):
                fyl[k, x : x + 1, :] = out_ref[i, x, 0:1, :]
        o7[...] = out_ref[7, nx - 1, ny - 1 : ny, :]
        o8[...] = out_ref[8, 0, 0:1, :]
        o9[...] = out_ref[9, nx - 1, 0:1, :]
        o10[...] = out_ref[10, 0, ny - 1 : ny, :]


def lb_call(mode, src, mask, halos=()):
    _, nx, ny, nz = src.shape
    f32 = jnp.float32
    vmem = pl.BlockSpec(memory_space=pltpu.VMEM)
    n_in = 2 + len(halos)
    scratch = []
    if mode == "last":
        out_shape = (
            jax.ShapeDtypeStruct(src.shape, f32),
            jax.ShapeDtypeStruct((3, nx // 2, nz // 2, ny // 2), f32),
        )
        scratch = [pltpu.VMEM((NPOP, nx + 2, ny + 2 * YOFF, nz), f32), pltpu.VMEM((3, nx, ny, nz), f32)]
    else:
        out_shape = (
            jax.ShapeDtypeStruct(src.shape, f32),
            jax.ShapeDtypeStruct((len(CXP), ny, nz), f32),
            jax.ShapeDtypeStruct((len(CXM), ny, nz), f32),
            jax.ShapeDtypeStruct((len(CYP), nx, nz), f32),
            jax.ShapeDtypeStruct((len(CYM), nx, nz), f32),
        ) + tuple(jax.ShapeDtypeStruct((1, nz), f32) for _ in range(4))
        if mode == "mid":
            scratch = [pltpu.VMEM((NPOP, nx + 2, ny + 2 * YOFF, nz), f32)]
    cells = nx * ny * nz
    cost = pl.CostEstimate(flops=320 * cells, transcendentals=0, bytes_accessed=2 * NPOP * 4 * cells + 4 * cells)
    return pl.pallas_call(
        functools.partial(lb_kernel, mode, nx, ny),
        out_shape=out_shape,
        in_specs=[vmem] * n_in,
        out_specs=tuple(vmem for _ in out_shape),
        scratch_shapes=scratch,
        cost_estimate=cost,
        compiler_params=pltpu.CompilerParams(vmem_limit_bytes=48 * 1024 * 1024),
    )(src, mask, *halos)


def send(x, dv, db):
    nv = lax.axis_size("vessel")
    nb = lax.axis_size("blk")
    if db == 0:
        return lax.ppermute(x, "vessel", [(i, (i + dv) % nv) for i in range(nv)])
    if dv == 0:
        return lax.ppermute(x, "blk", [(i, (i + db) % nb) for i in range(nb)])
    pairs = []
    for v in range(nv):
        for b in range(nb):
            pairs.append((v * nb + b, ((v + dv) % nv) * nb + (b + db) % nb))
    return lax.ppermute(x, ("vessel", "blk"), pairs)


def exchange(faces):
    fxh, fxl, fyh, fyl, o7, o8, o9, o10 = faces
    return (
        send(fxh, 1, 0),
        send(fxl, -1, 0),
        send(fyh, 0, 1),
        send(fyl, 0, -1),
        send(o7, 1, 1),
        send(o8, -1, -1),
        send(o9, 1, -1),
        send(o10, -1, 1),
    )


def tracer_update(c, fx, fy, fz):
    flux_x = fx * c
    flux_y = fy[1:-1, 1:-1] * c[1:-1, 1:-1]
    flux_z = fz * c
    center = c[1:-1, 1:-1]
    div_x = (flux_x[1:-1, 2:] - flux_x[1:-1, :-2]) * 0.5
    div_y = (jnp.roll(flux_y, -1, 2) - jnp.roll(flux_y, 1, 2)) * 0.5
    div_z = (flux_z[2:, 1:-1] - flux_z[:-2, 1:-1]) * 0.5
    divergence = div_x + div_y + div_z
    beside_all = (
        (c[1:-1, 2:] + c[1:-1, :-2])
        + (jnp.roll(center, -1, 2) + jnp.roll(center, 1, 2))
        + (c[2:, 1:-1] + c[:-2, 1:-1])
    )
    laplace = beside_all - 6.0 * center
    return center - advect_gain * divergence + diffusion * laplace


def local(populations, voxel_mask, tracer):
    post, *faces = lb_call("first", populations, voxel_mask)
    for step in range(1, STEPS):
        halos = exchange(faces)
        post, *faces = lb_call("mid", post, voxel_mask, halos)
    halos = exchange(faces)
    state, coarse = lb_call("last", post, voxel_mask, halos)
    moved = lax.all_to_all(coarse, "blk", split_axis=2, concat_axis=3, tiled=True)
    flow = jnp.transpose(moved, (0, 2, 1, 3))
    w = TRACER_STEPS
    q = jnp.concatenate([tracer[None], flow], axis=0)
    nzb, nxb = q.shape[1], q.shape[2]
    zlo = send(q[:, nzb - w :], 0, 1)
    zhi = send(q[:, :w], 0, -1)
    xlo = send(q[:, :, nxb - w :], 1, 0)
    xhi = send(q[:, :, :w], -1, 0)
    c_mm = send(q[:, nzb - w :, nxb - w :], 1, 1)
    c_pp = send(q[:, :w, :w], -1, -1)
    c_mp = send(q[:, nzb - w :, :w], -1, 1)
    c_pm = send(q[:, :w, nxb - w :], 1, -1)
    ext = jnp.concatenate(
        [
            jnp.concatenate([c_mm, zlo, c_mp], axis=2),
            jnp.concatenate([xlo, q, xhi], axis=2),
            jnp.concatenate([c_pm, zhi, c_pp], axis=2),
        ],
        axis=1,
    )
    conc, fx, fy, fz = ext[0], ext[1], ext[2], ext[3]
    for step in range(TRACER_STEPS):
        conc = tracer_update(conc, fx, fy, fz)
        fx, fy, fz = fx[1:-1, 1:-1], fy[1:-1, 1:-1], fz[1:-1, 1:-1]
    return (state, conc)


def solution(mesh):
    placed = (P(None, "vessel", "blk", None), P("vessel", "blk", None), P("blk", "vessel", None))
    return jax.shard_map(
        local,
        mesh=mesh,
        in_specs=placed,
        out_specs=(P(None, "vessel", "blk", None), P("blk", "vessel", None)),
        check_vma=False,
    )
```

profile of v0, /device:TPU:0, one launch (start us, length us, event | category | flops | bytes accessed | tf_op | source)
XLA Modules:
  0.0 174.3 jit_solution(9141534733256965125)
XLA Ops:
  0.6 0.9 copy-done
  1.5 1.7 copy-done.2
  3.2 1.4 shard_map.50
  4.7 2.9 %collective-permute-start.1 = (f32[5,32,128]{2,1,0:T(8,128)S(1)}, f32[5,32,128]{2,1,0:T(8,128)S(1)}, u32[]{:S(2)}, u32[]{:S(2)}) collective-permute-start(f32[5,32,128]{2,1,0:T(8,128)S(1)} %get-tuple-element.42), channel_id=1, source_target_pairs={{0,112},{16,0},{32,16},{48,32},{64,48},{80,64},{96,80},{112,96},{1... | collective-permute-start | bytes 245768 | tf_op jit(solution)/shard_map/ppermute | solution.py:239
  7.6 1.7 collective-permute-start.2
  9.3 4.9 %collective-permute-start.3 = (f32[5,8,128]{2,1,0:T(8,128)S(1)}, f32[5,8,128]{2,1,0:T(8,128)S(1)}, u32[]{:S(2)}, u32[]{:S(2)}) collective-permute-start(f32[5,8,128]{2,1,0:T(8,128)S(1)} %get-tuple-element.44), channel_id=1, source_target_pairs={{0,15},{1,0},{2,1},{3,2},{4,3},{5,4},{6,5},{7,6},{8,7},{9,8},{10,9... | collective-permute-start | bytes 61448 | tf_op jit(solution)/shard_map/ppermute | solution.py:241
  14.2 8.4 %collective-permute-done.4.refs_6_ = f32[1,128]{1,0:T(1,128)S(1)} collective-permute-done((f32[1,128]{1,0:T(1,128)S(1)}, f32[1,128]{1,0:T(1,128)S(1)}, u32[]{:S(2)}, u32[]{:S(2)}) %collective-permute-start.4) | collective-permute-done | bytes 544 | tf_op jit(solution)/shard_map/ppermute | solution.py:246
  22.6 3.0 %collective-permute-done.5.refs_7_ = f32[1,128]{1,0:T(1,128)S(1)} collective-permute-done((f32[1,128]{1,0:T(1,128)S(1)}, f32[1,128]{1,0:T(1,128)S(1)}, u32[]{:S(2)}, u32[]{:S(2)}) %collective-permute-start.5) | collective-permute-done | bytes 544 | tf_op jit(solution)/shard_map/ppermute | solution.py:246
  25.5 1.8 %collective-permute-start.6 = (f32[1,128]{1,0:T(1,128)S(1)}, f32[1,128]{1,0:T(1,128)S(1)}, u32[]{:S(2)}, u32[]{:S(2)}) collective-permute-start(f32[1,128]{1,0:T(1,128)S(1)} %get-tuple-element.47), channel_id=1, source_target_pairs={{0,31},{1,16},{2,17},{3,18},{4,19},{5,20},{6,21},{7,22},{8,23},{9,... | collective-permute-start | bytes 1544 | tf_op jit(solution)/shard_map/ppermute | solution.py:246
  27.4 3.2 %collective-permute-done.6.refs_8_ = f32[1,128]{1,0:T(1,128)S(1)} collective-permute-done((f32[1,128]{1,0:T(1,128)S(1)}, f32[1,128]{1,0:T(1,128)S(1)}, u32[]{:S(2)}, u32[]{:S(2)}) %collective-permute-start.6) | collective-permute-done | bytes 544 | tf_op jit(solution)/shard_map/ppermute | solution.py:246
  30.6 6.3 %collective-permute-done.7.refs_9_ = f32[1,128]{1,0:T(1,128)S(1)} collective-permute-done((f32[1,128]{1,0:T(1,128)S(1)}, f32[1,128]{1,0:T(1,128)S(1)}, u32[]{:S(2)}, u32[]{:S(2)}) %collective-permute-start.7) | collective-permute-done | bytes 544 | tf_op jit(solution)/shard_map/ppermute | solution.py:246
  36.9 2.2 %shard_map.51 = (f32[19,8,32,128]{3,2,1,0:T(8,128)S(1)}, f32[5,32,128]{2,1,0:T(8,128)S(1)}, f32[5,32,128]{2,1,0:T(8,128)S(1)}, f32[5,8,128]{2,1,0:T(8,128)S(1)},...) custom-call(f32[19,8,32,128]{3,2,1,0:T(8,128)S(1)} %get-tuple-elemen, ...), custom_call_target="tpu_custom_call" | custom-call | flops 10485760 | bytes 5111808 | tf_op jit(solution)/shard_map/pallas_call | solution.py:224
  39.1 2.9 %collective-permute-start.9 = (f32[5,32,128]{2,1,0:T(8,128)S(1)}, f32[5,32,128]{2,1,0:T(8,128)S(1)}, u32[]{:S(2)}, u32[]{:S(2)}) collective-permute-start(f32[5,32,128]{2,1,0:T(8,128)S(1)} %get-tuple-element.51), channel_id=1, source_target_pairs={{0,112},{16,0},{32,16},{48,32},{64,48},{80,64},{96,80},{112,96},{1... | collective-permute-start | bytes 245768 | tf_op jit(solution)/shard_map/ppermute | solution.py:239
  42.1 5.3 %collective-permute-start.11 = (f32[5,8,128]{2,1,0:T(8,128)S(1)}, f32[5,8,128]{2,1,0:T(8,128)S(1)}, u32[]{:S(2)}, u32[]{:S(2)}) collective-permute-start(f32[5,8,128]{2,1,0:T(8,128)S(1)} %get-tuple-element.53), channel_id=1, source_target_pairs={{0,15},{1,0},{2,1},{3,2},{4,3},{5,4},{6,5},{7,6},{8,7},{9,8},{10,9... | collective-permute-start | bytes 61448 | tf_op jit(solution)/shard_map/ppermute | solution.py:241
  47.4 8.4 %collective-permute-done.12.refs_6_ = f32[1,128]{1,0:T(1,128)S(1)} collective-permute-done((f32[1,128]{1,0:T(1,128)S(1)}, f32[1,128]{1,0:T(1,128)S(1)}, u32[]{:S(2)}, u32[]{:S(2)}) %collective-permute-start.12) | collective-permute-done | bytes 544 | tf_op jit(solution)/shard_map/ppermute | solution.py:246
  55.8 3.0 %collective-permute-done.13.refs_7_ = f32[1,128]{1,0:T(1,128)S(1)} collective-permute-done((f32[1,128]{1,0:T(1,128)S(1)}, f32[1,128]{1,0:T(1,128)S(1)}, u32[]{:S(2)}, u32[]{:S(2)}) %collective-permute-start.13) | collective-permute-done | bytes 544 | tf_op jit(solution)/shard_map/ppermute | solution.py:246
  58.8 5.1 %collective-permute-done.14.refs_8_ = f32[1,128]{1,0:T(1,128)S(1)} collective-permute-done((f32[1,128]{1,0:T(1,128)S(1)}, f32[1,128]{1,0:T(1,128)S(1)}, u32[]{:S(2)}, u32[]{:S(2)}) %collective-permute-start.14) | collective-permute-done | bytes 544 | tf_op jit(solution)/shard_map/ppermute | solution.py:246
  63.9 6.3 %collective-permute-done.15.refs_9_ = f32[1,128]{1,0:T(1,128)S(1)} collective-permute-done((f32[1,128]{1,0:T(1,128)S(1)}, f32[1,128]{1,0:T(1,128)S(1)}, u32[]{:S(2)}, u32[]{:S(2)}) %collective-permute-start.15) | collective-permute-done | bytes 544 | tf_op jit(solution)/shard_map/ppermute | solution.py:246
  70.2 2.2 %shard_map.52 = (f32[19,8,32,128]{3,2,1,0:T(8,128)S(1)}, f32[5,32,128]{2,1,0:T(8,128)S(1)}, f32[5,32,128]{2,1,0:T(8,128)S(1)}, f32[5,8,128]{2,1,0:T(8,128)S(1)},...) custom-call(f32[19,8,32,128]{3,2,1,0:T(8,128)S(1)} %get-tuple-elemen, ...), custom_call_target="tpu_custom_call" | custom-call | flops 10485760 | bytes 5111808 | tf_op jit(solution)/shard_map/pallas_call | solution.py:224
  72.4 2.9 %collective-permute-start.17 = (f32[5,32,128]{2,1,0:T(8,128)S(1)}, f32[5,32,128]{2,1,0:T(8,128)S(1)}, u32[]{:S(2)}, u32[]{:S(2)}) collective-permute-start(f32[5,32,128]{2,1,0:T(8,128)S(1)} %get-tuple-element.60), channel_id=1, source_target_pairs={{0,112},{16,0},{32,16},{48,32},{64,48},{80,64},{96,80},{112,96},{1... | collective-permute-start | bytes 245768 | tf_op jit(solution)/shard_map/ppermute | solution.py:239
  75.4 5.3 %collective-permute-start.19 = (f32[5,8,128]{2,1,0:T(8,128)S(1)}, f32[5,8,128]{2,1,0:T(8,128)S(1)}, u32[]{:S(2)}, u32[]{:S(2)}) collective-permute-start(f32[5,8,128]{2,1,0:T(8,128)S(1)} %get-tuple-element.62), channel_id=1, source_target_pairs={{0,15},{1,0},{2,1},{3,2},{4,3},{5,4},{6,5},{7,6},{8,7},{9,8},{10,9... | collective-permute-start | bytes 61448 | tf_op jit(solution)/shard_map/ppermute | solution.py:241
  80.7 8.4 %collective-permute-done.20.refs_6_ = f32[1,128]{1,0:T(1,128)S(1)} collective-permute-done((f32[1,128]{1,0:T(1,128)S(1)}, f32[1,128]{1,0:T(1,128)S(1)}, u32[]{:S(2)}, u32[]{:S(2)}) %collective-permute-start.20) | collective-permute-done | bytes 544 | tf_op jit(solution)/shard_map/ppermute | solution.py:246
  89.1 3.0 %collective-permute-done.21.refs_7_ = f32[1,128]{1,0:T(1,128)S(1)} collective-permute-done((f32[1,128]{1,0:T(1,128)S(1)}, f32[1,128]{1,0:T(1,128)S(1)}, u32[]{:S(2)}, u32[]{:S(2)}) %collective-permute-start.21) | collective-permute-done | bytes 544 | tf_op jit(solution)/shard_map/ppermute | solution.py:246
  92.1 5.1 %collective-permute-done.22.refs_8_ = f32[1,128]{1,0:T(1,128)S(1)} collective-permute-done((f32[1,128]{1,0:T(1,128)S(1)}, f32[1,128]{1,0:T(1,128)S(1)}, u32[]{:S(2)}, u32[]{:S(2)}) %collective-permute-start.22) | collective-permute-done | bytes 544 | tf_op jit(solution)/shard_map/ppermute | solution.py:246
  97.1 6.3 %collective-permute-done.23.refs_9_ = f32[1,128]{1,0:T(1,128)S(1)} collective-permute-done((f32[1,128]{1,0:T(1,128)S(1)}, f32[1,128]{1,0:T(1,128)S(1)}, u32[]{:S(2)}, u32[]{:S(2)}) %collective-permute-start.23) | collective-permute-done | bytes 544 | tf_op jit(solution)/shard_map/ppermute | solution.py:246
  103.4 2.2 %shard_map.53 = (f32[19,8,32,128]{3,2,1,0:T(8,128)S(1)}, f32[5,32,128]{2,1,0:T(8,128)S(1)}, f32[5,32,128]{2,1,0:T(8,128)S(1)}, f32[5,8,128]{2,1,0:T(8,128)S(1)},...) custom-call(f32[19,8,32,128]{3,2,1,0:T(8,128)S(1)} %get-tuple-elemen, ...), custom_call_target="tpu_custom_call" | custom-call | flops 10485760 | bytes 5111808 | tf_op jit(solution)/shard_map/pallas_call | solution.py:224
  105.7 2.9 %collective-permute-start.25 = (f32[5,32,128]{2,1,0:T(8,128)S(1)}, f32[5,32,128]{2,1,0:T(8,128)S(1)}, u32[]{:S(2)}, u32[]{:S(2)}) collective-permute-start(f32[5,32,128]{2,1,0:T(8,128)S(1)} %get-tuple-element.69), channel_id=1, source_target_pairs={{0,112},{16,0},{32,16},{48,32},{64,48},{80,64},{96,80},{112,96},{1... | collective-permute-start | bytes 245768 | tf_op jit(solution)/shard_map/ppermute | solution.py:239
  108.6 5.3 %collective-permute-start.27 = (f32[5,8,128]{2,1,0:T(8,128)S(1)}, f32[5,8,128]{2,1,0:T(8,128)S(1)}, u32[]{:S(2)}, u32[]{:S(2)}) collective-permute-start(f32[5,8,128]{2,1,0:T(8,128)S(1)} %get-tuple-element.71), channel_id=1, source_target_pairs={{0,15},{1,0},{2,1},{3,2},{4,3},{5,4},{6,5},{7,6},{8,7},{9,8},{10,9... | collective-permute-start | bytes 61448 | tf_op jit(solution)/shard_map/ppermute | solution.py:241
  114.0 8.4 %collective-permute-done.28.refs_6_ = f32[1,128]{1,0:T(1,128)S(1)} collective-permute-done((f32[1,128]{1,0:T(1,128)S(1)}, f32[1,128]{1,0:T(1,128)S(1)}, u32[]{:S(2)}, u32[]{:S(2)}) %collective-permute-start.28) | collective-permute-done | bytes 544 | tf_op jit(solution)/shard_map/ppermute | solution.py:246
  122.3 3.0 %collective-permute-done.29.refs_7_ = f32[1,128]{1,0:T(1,128)S(1)} collective-permute-done((f32[1,128]{1,0:T(1,128)S(1)}, f32[1,128]{1,0:T(1,128)S(1)}, u32[]{:S(2)}, u32[]{:S(2)}) %collective-permute-start.29) | collective-permute-done | bytes 544 | tf_op jit(solution)/shard_map/ppermute | solution.py:246
  125.3 5.1 %collective-permute-done.30.refs_8_ = f32[1,128]{1,0:T(1,128)S(1)} collective-permute-done((f32[1,128]{1,0:T(1,128)S(1)}, f32[1,128]{1,0:T(1,128)S(1)}, u32[]{:S(2)}, u32[]{:S(2)}) %collective-permute-start.30) | collective-permute-done | bytes 544 | tf_op jit(solution)/shard_map/ppermute | solution.py:246
  130.4 6.3 %collective-permute-done.31.refs_9_ = f32[1,128]{1,0:T(1,128)S(1)} collective-permute-done((f32[1,128]{1,0:T(1,128)S(1)}, f32[1,128]{1,0:T(1,128)S(1)}, u32[]{:S(2)}, u32[]{:S(2)}) %collective-permute-start.31) | collective-permute-done | bytes 544 | tf_op jit(solution)/shard_map/ppermute | solution.py:246
  136.7 2.6 %shard_map.54 = (f32[19,8,32,128]{3,2,1,0:T(8,128)}, f32[3,4,64,16]{3,2,1,0:T(8,128)S(1)}) custom-call(f32[19,8,32,128]{3,2,1,0:T(8,128)S(1)} %get-tuple-element.67.refs_0_, s32[8,32,128]{2,1,0:T(8,128)S(1)} %copy-done.1, f32[5,32,128]{2,1,0:T(8,128)S(1)} %collective-permute-done.24.refs_2_, f32[5,32,128]{2,1,0:T(8,128)S(1)} %collective-permute-done.25.refs_3_, ...), custom_call_target="tpu_custom_call" | custom-call | flops 10485760 | bytes 5111808 | tf_op jit(solution)/shard_map/pallas_call | solution.py:224
  139.3 0.3 copy.9
  139.6 0.3 reshape.4
  139.9 11.9 %all_to_all.18 = f32[16,1,768]{2,1,0:T(1,128)S(1)} all-to-all(f32[16,1,768]{2,1,0:T(1,128)S(1)} %reshape.4), channel_id=1, replica_groups=mesh['vessel'=8,'blk'=16] {'blk'}, dimensions={0} | all-to-all | bytes 98304 | tf_op jit(solution)/shard_map/all_to_all | solution.py:288
  151.8 0.5 broadcast.4
  152.3 0.8 reduce
  153.1 0.3 reshape.5
  153.9 3.1 %collective-permute-start.34 = (f32[4,2,2,256]{3,2,1,0:T(2,128)S(1)}, f32[4,2,2,256]{3,2,1,0:T(2,128)S(1)}, u32[]{:S(2)}, u32[]{:S(2)}) collective-permute-start(f32[4,2,2,256]{3,2,1,0:T(2,128)S(1)} %get-tuple-element.91), channel_id=1, source_target_pairs={{0,113},{1,114},{2,115},{3,116},{4,117},{5,118},{6,119},{7,120},{8... | collective-permute-start | bytes 49160 | tf_op jit(solution)/shard_map/ppermute | solution.py:246
  157.0 1.4 collective-permute-start.33
  158.4 1.0 collective-permute-start.37
  159.4 3.1 %collective-permute-done.32 = f32[4,2,2,256]{3,2,1,0:T(2,128)S(1)} collective-permute-done((f32[4,2,2,256]{3,2,1,0:T(2,128)S(1)}, f32[4,2,2,256]{3,2,1,0:T(2,128)S(1)}, u32[]{:S(2)}, u32[]{:S(2)}) %collective-permute-start.32) | collective-permute-done | bytes 16416 | tf_op jit(solution)/shard_map/ppermute | solution.py:246
  162.5 2.3 %collective-permute-start.36 = (f32[4,4,2,256]{3,2,1,0:T(2,128)S(1)}, f32[4,4,2,256]{3,2,1,0:T(2,128)S(1)}, u32[]{:S(2)}, u32[]{:S(2)}) collective-permute-start(f32[4,4,2,256]{3,2,1,0:T(2,128)S(1)} %get-tuple-element.97), channel_id=1, source_target_pairs={{0,112},{16,0},{32,16},{48,32},{64,48},{80,64},{96,80},{112,96},{1... | collective-permute-start | bytes 98312 | tf_op jit(solution)/shard_map/ppermute | solution.py:239
  164.8 1.3 collective-permute-start.38
  166.1 5.1 %collective-permute-start.39 = (f32[4,2,2,256]{3,2,1,0:T(2,128)S(1)}, f32[4,2,2,256]{3,2,1,0:T(2,128)S(1)}, u32[]{:S(2)}, u32[]{:S(2)}) collective-permute-start(f32[4,2,2,256]{3,2,1,0:T(2,128)S(1)} %get-tuple-element.93), channel_id=1, source_target_pairs={{0,127},{1,112},{2,113},{3,114},{4,115},{5,116},{6,117},{7,118},{8... | collective-permute-start | bytes 49160 | tf_op jit(solution)/shard_map/ppermute | solution.py:246
  171.3 1.4 collective-permute-done.39
  173.6 0.7 fusion.19
  (70 shorter events, 1.4 us)
Async XLA Ops:
  0.6 0.9 copy-start
  1.5 1.7 copy-start.2
  3.2 33.7 %copy-start.1 = (s32[8,32,128]{2,1,0:T(8,128)S(1)}, s32[8,32,128]{2,1,0:T(8,128)}, u32[]{:S(2)}) copy-start(s32[8,32,128]{2,1,0:T(8,128)} %refs_1_.9) | copy-start | bytes 393220
  4.6 32.3 %collective-permute-start = (f32[5,32,128]{2,1,0:T(8,128)S(1)}, f32[5,32,128]{2,1,0:T(8,128)S(1)}, u32[]{:S(2)}, u32[]{:S(2)}) collective-permute-start(f32[5,32,128]{2,1,0:T(8,128)S(1)} %get-tuple-element.41), channel_id=1, source_target_pairs={{0,16},{16,32},{32,48},{48,64},{64,80},{80,96},{96,112},{112,0},{1... | collective-permute-start | bytes 245768 | tf_op jit(solution)/shard_map/ppermute | solution.py:239
  4.7 32.3 %collective-permute-start.1 = (f32[5,32,128]{2,1,0:T(8,128)S(1)}, f32[5,32,128]{2,1,0:T(8,128)S(1)}, u32[]{:S(2)}, u32[]{:S(2)}) collective-permute-start(f32[5,32,128]{2,1,0:T(8,128)S(1)} %get-tuple-element.42), channel_id=1, source_target_pairs={{0,112},{16,0},{32,16},{48,32},{64,48},{80,64},{96,80},{112,96},{1... | collective-permute-start | bytes 245768 | tf_op jit(solution)/shard_map/ppermute | solution.py:239
  7.6 29.3 %collective-permute-start.2 = (f32[5,8,128]{2,1,0:T(8,128)S(1)}, f32[5,8,128]{2,1,0:T(8,128)S(1)}, u32[]{:S(2)}, u32[]{:S(2)}) collective-permute-start(f32[5,8,128]{2,1,0:T(8,128)S(1)} %get-tuple-element.43), channel_id=1, source_target_pairs={{0,1},{1,2},{2,3},{3,4},{4,5},{5,6},{6,7},{7,8},{8,9},{9,10},{10,1... | collective-permute-start | bytes 61448 | tf_op jit(solution)/shard_map/ppermute | solution.py:241
  9.3 27.6 %collective-permute-start.3 = (f32[5,8,128]{2,1,0:T(8,128)S(1)}, f32[5,8,128]{2,1,0:T(8,128)S(1)}, u32[]{:S(2)}, u32[]{:S(2)}) collective-permute-start(f32[5,8,128]{2,1,0:T(8,128)S(1)} %get-tuple-element.44), channel_id=1, source_target_pairs={{0,15},{1,0},{2,1},{3,2},{4,3},{5,4},{6,5},{7,6},{8,7},{9,8},{10,9... | collective-permute-start | bytes 61448 | tf_op jit(solution)/shard_map/ppermute | solution.py:241
  14.2 8.4 %collective-permute-start.4 = (f32[1,128]{1,0:T(1,128)S(1)}, f32[1,128]{1,0:T(1,128)S(1)}, u32[]{:S(2)}, u32[]{:S(2)}) collective-permute-start(f32[1,128]{1,0:T(1,128)S(1)} %get-tuple-element.45), channel_id=1, source_target_pairs={{0,17},{1,18},{2,19},{3,20},{4,21},{5,22},{6,23},{7,24},{8,25},{9,... | collective-permute-start | bytes 1544 | tf_op jit(solution)/shard_map/ppermute | solution.py:246
  22.6 3.0 %collective-permute-start.5 = (f32[1,128]{1,0:T(1,128)S(1)}, f32[1,128]{1,0:T(1,128)S(1)}, u32[]{:S(2)}, u32[]{:S(2)}) collective-permute-start(f32[1,128]{1,0:T(1,128)S(1)} %get-tuple-element.46), channel_id=1, source_target_pairs={{0,127},{1,112},{2,113},{3,114},{4,115},{5,116},{6,117},{7,118},{8... | collective-permute-start | bytes 1544 | tf_op jit(solution)/shard_map/ppermute | solution.py:246
  25.5 5.1 %collective-permute-start.6 = (f32[1,128]{1,0:T(1,128)S(1)}, f32[1,128]{1,0:T(1,128)S(1)}, u32[]{:S(2)}, u32[]{:S(2)}) collective-permute-start(f32[1,128]{1,0:T(1,128)S(1)} %get-tuple-element.47), channel_id=1, source_target_pairs={{0,31},{1,16},{2,17},{3,18},{4,19},{5,20},{6,21},{7,22},{8,23},{9,... | collective-permute-start | bytes 1544 | tf_op jit(solution)/shard_map/ppermute | solution.py:246
  30.6 6.3 %collective-permute-start.7 = (f32[1,128]{1,0:T(1,128)S(1)}, f32[1,128]{1,0:T(1,128)S(1)}, u32[]{:S(2)}, u32[]{:S(2)}) collective-permute-start(f32[1,128]{1,0:T(1,128)S(1)} %get-tuple-element.48), channel_id=1, source_target_pairs={{0,113},{1,114},{2,115},{3,116},{4,117},{5,118},{6,119},{7,120},{8... | collective-permute-start | bytes 1544 | tf_op jit(solution)/shard_map/ppermute | solution.py:246
  39.1 31.0 %collective-permute-start.8 = (f32[5,32,128]{2,1,0:T(8,128)S(1)}, f32[5,32,128]{2,1,0:T(8,128)S(1)}, u32[]{:S(2)}, u32[]{:S(2)}) collective-permute-start(f32[5,32,128]{2,1,0:T(8,128)S(1)} %get-tuple-element.50), channel_id=1, source_target_pairs={{0,16},{16,32},{32,48},{48,64},{64,80},{80,96},{96,112},{112,0},{1... | collective-permute-start | bytes 245768 | tf_op jit(solution)/shard_map/ppermute | solution.py:239
  39.1 31.0 %collective-permute-start.9 = (f32[5,32,128]{2,1,0:T(8,128)S(1)}, f32[5,32,128]{2,1,0:T(8,128)S(1)}, u32[]{:S(2)}, u32[]{:S(2)}) collective-permute-start(f32[5,32,128]{2,1,0:T(8,128)S(1)} %get-tuple-element.51), channel_id=1, source_target_pairs={{0,112},{16,0},{32,16},{48,32},{64,48},{80,64},{96,80},{112,96},{1... | collective-permute-start | bytes 245768 | tf_op jit(solution)/shard_map/ppermute | solution.py:239
  42.1 28.1 %collective-permute-start.10 = (f32[5,8,128]{2,1,0:T(8,128)S(1)}, f32[5,8,128]{2,1,0:T(8,128)S(1)}, u32[]{:S(2)}, u32[]{:S(2)}) collective-permute-start(f32[5,8,128]{2,1,0:T(8,128)S(1)} %get-tuple-element.52), channel_id=1, source_target_pairs={{0,1},{1,2},{2,3},{3,4},{4,5},{5,6},{6,7},{7,8},{8,9},{9,10},{10,1... | collective-permute-start | bytes 61448 | tf_op jit(solution)/shard_map/ppermute | solution.py:241
  42.1 28.1 %collective-permute-start.11 = (f32[5,8,128]{2,1,0:T(8,128)S(1)}, f32[5,8,128]{2,1,0:T(8,128)S(1)}, u32[]{:S(2)}, u32[]{:S(2)}) collective-permute-start(f32[5,8,128]{2,1,0:T(8,128)S(1)} %get-tuple-element.53), channel_id=1, source_target_pairs={{0,15},{1,0},{2,1},{3,2},{4,3},{5,4},{6,5},{7,6},{8,7},{9,8},{10,9... | collective-permute-start | bytes 61448 | tf_op jit(solution)/shard_map/ppermute | solution.py:241
  47.4 8.4 %collective-permute-start.12 = (f32[1,128]{1,0:T(1,128)S(1)}, f32[1,128]{1,0:T(1,128)S(1)}, u32[]{:S(2)}, u32[]{:S(2)}) collective-permute-start(f32[1,128]{1,0:T(1,128)S(1)} %get-tuple-element.54), channel_id=1, source_target_pairs={{0,17},{1,18},{2,19},{3,20},{4,21},{5,22},{6,23},{7,24},{8,25},{9,... | collective-permute-start | bytes 1544 | tf_op jit(solution)/shard_map/ppermute | solution.py:246
  55.8 3.0 %collective-permute-start.13 = (f32[1,128]{1,0:T(1,128)S(1)}, f32[1,128]{1,0:T(1,128)S(1)}, u32[]{:S(2)}, u32[]{:S(2)}) collective-permute-start(f32[1,128]{1,0:T(1,128)S(1)} %get-tuple-element.55), channel_id=1, source_target_pairs={{0,127},{1,112},{2,113},{3,114},{4,115},{5,116},{6,117},{7,118},{8... | collective-permute-start | bytes 1544 | tf_op jit(solution)/shard_map/ppermute | solution.py:246
  58.8 5.1 %collective-permute-start.14 = (f32[1,128]{1,0:T(1,128)S(1)}, f32[1,128]{1,0:T(1,128)S(1)}, u32[]{:S(2)}, u32[]{:S(2)}) collective-permute-start(f32[1,128]{1,0:T(1,128)S(1)} %get-tuple-element.56), channel_id=1, source_target_pairs={{0,31},{1,16},{2,17},{3,18},{4,19},{5,20},{6,21},{7,22},{8,23},{9,... | collective-permute-start | bytes 1544 | tf_op jit(solution)/shard_map/ppermute | solution.py:246
  63.9 6.3 %collective-permute-start.15 = (f32[1,128]{1,0:T(1,128)S(1)}, f32[1,128]{1,0:T(1,128)S(1)}, u32[]{:S(2)}, u32[]{:S(2)}) collective-permute-start(f32[1,128]{1,0:T(1,128)S(1)} %get-tuple-element.57), channel_id=1, source_target_pairs={{0,113},{1,114},{2,115},{3,116},{4,117},{5,118},{6,119},{7,120},{8... | collective-permute-start | bytes 1544 | tf_op jit(solution)/shard_map/ppermute | solution.py:246
  72.4 31.0 %collective-permute-start.16 = (f32[5,32,128]{2,1,0:T(8,128)S(1)}, f32[5,32,128]{2,1,0:T(8,128)S(1)}, u32[]{:S(2)}, u32[]{:S(2)}) collective-permute-start(f32[5,32,128]{2,1,0:T(8,128)S(1)} %get-tuple-element.59), channel_id=1, source_target_pairs={{0,16},{16,32},{32,48},{48,64},{64,80},{80,96},{96,112},{112,0},{1... | collective-permute-start | bytes 245768 | tf_op jit(solution)/shard_map/ppermute | solution.py:239
  72.4 31.0 %collective-permute-start.17 = (f32[5,32,128]{2,1,0:T(8,128)S(1)}, f32[5,32,128]{2,1,0:T(8,128)S(1)}, u32[]{:S(2)}, u32[]{:S(2)}) collective-permute-start(f32[5,32,128]{2,1,0:T(8,128)S(1)} %get-tuple-element.60), channel_id=1, source_target_pairs={{0,112},{16,0},{32,16},{48,32},{64,48},{80,64},{96,80},{112,96},{1... | collective-permute-start | bytes 245768 | tf_op jit(solution)/shard_map/ppermute | solution.py:239
  75.3 28.1 %collective-permute-start.18 = (f32[5,8,128]{2,1,0:T(8,128)S(1)}, f32[5,8,128]{2,1,0:T(8,128)S(1)}, u32[]{:S(2)}, u32[]{:S(2)}) collective-permute-start(f32[5,8,128]{2,1,0:T(8,128)S(1)} %get-tuple-element.61), channel_id=1, source_target_pairs={{0,1},{1,2},{2,3},{3,4},{4,5},{5,6},{6,7},{7,8},{8,9},{9,10},{10,1... | collective-permute-start | bytes 61448 | tf_op jit(solution)/shard_map/ppermute | solution.py:241
  75.4 28.1 %collective-permute-start.19 = (f32[5,8,128]{2,1,0:T(8,128)S(1)}, f32[5,8,128]{2,1,0:T(8,128)S(1)}, u32[]{:S(2)}, u32[]{:S(2)}) collective-permute-start(f32[5,8,128]{2,1,0:T(8,128)S(1)} %get-tuple-element.62), channel_id=1, source_target_pairs={{0,15},{1,0},{2,1},{3,2},{4,3},{5,4},{6,5},{7,6},{8,7},{9,8},{10,9... | collective-permute-start | bytes 61448 | tf_op jit(solution)/shard_map/ppermute | solution.py:241
  80.7 8.4 %collective-permute-start.20 = (f32[1,128]{1,0:T(1,128)S(1)}, f32[1,128]{1,0:T(1,128)S(1)}, u32[]{:S(2)}, u32[]{:S(2)}) collective-permute-start(f32[1,128]{1,0:T(1,128)S(1)} %get-tuple-element.63), channel_id=1, source_target_pairs={{0,17},{1,18},{2,19},{3,20},{4,21},{5,22},{6,23},{7,24},{8,25},{9,... | collective-permute-start | bytes 1544 | tf_op jit(solution)/shard_map/ppermute | solution.py:246
  89.1 3.0 %collective-permute-start.21 = (f32[1,128]{1,0:T(1,128)S(1)}, f32[1,128]{1,0:T(1,128)S(1)}, u32[]{:S(2)}, u32[]{:S(2)}) collective-permute-start(f32[1,128]{1,0:T(1,128)S(1)} %get-tuple-element.64), channel_id=1, source_target_pairs={{0,127},{1,112},{2,113},{3,114},{4,115},{5,116},{6,117},{7,118},{8... | collective-permute-start | bytes 1544 | tf_op jit(solution)/shard_map/ppermute | solution.py:246
  92.1 5.1 %collective-permute-start.22 = (f32[1,128]{1,0:T(1,128)S(1)}, f32[1,128]{1,0:T(1,128)S(1)}, u32[]{:S(2)}, u32[]{:S(2)}) collective-permute-start(f32[1,128]{1,0:T(1,128)S(1)} %get-tuple-element.65), channel_id=1, source_target_pairs={{0,31},{1,16},{2,17},{3,18},{4,19},{5,20},{6,21},{7,22},{8,23},{9,... | collective-permute-start | bytes 1544 | tf_op jit(solution)/shard_map/ppermute | solution.py:246
  97.1 6.3 %collective-permute-start.23 = (f32[1,128]{1,0:T(1,128)S(1)}, f32[1,128]{1,0:T(1,128)S(1)}, u32[]{:S(2)}, u32[]{:S(2)}) collective-permute-start(f32[1,128]{1,0:T(1,128)S(1)} %get-tuple-element.66), channel_id=1, source_target_pairs={{0,113},{1,114},{2,115},{3,116},{4,117},{5,118},{6,119},{7,120},{8... | collective-permute-start | bytes 1544 | tf_op jit(solution)/shard_map/ppermute | solution.py:246
  105.6 31.0 %collective-permute-start.24 = (f32[5,32,128]{2,1,0:T(8,128)S(1)}, f32[5,32,128]{2,1,0:T(8,128)S(1)}, u32[]{:S(2)}, u32[]{:S(2)}) collective-permute-start(f32[5,32,128]{2,1,0:T(8,128)S(1)} %get-tuple-element.68), channel_id=1, source_target_pairs={{0,16},{16,32},{32,48},{48,64},{64,80},{80,96},{96,112},{112,0},{1... | collective-permute-start | bytes 245768 | tf_op jit(solution)/shard_map/ppermute | solution.py:239
  105.7 31.0 %collective-permute-start.25 = (f32[5,32,128]{2,1,0:T(8,128)S(1)}, f32[5,32,128]{2,1,0:T(8,128)S(1)}, u32[]{:S(2)}, u32[]{:S(2)}) collective-permute-start(f32[5,32,128]{2,1,0:T(8,128)S(1)} %get-tuple-element.69), channel_id=1, source_target_pairs={{0,112},{16,0},{32,16},{48,32},{64,48},{80,64},{96,80},{112,96},{1... | collective-permute-start | bytes 245768 | tf_op jit(solution)/shard_map/ppermute | solution.py:239
  108.6 28.1 %collective-permute-start.26 = (f32[5,8,128]{2,1,0:T(8,128)S(1)}, f32[5,8,128]{2,1,0:T(8,128)S(1)}, u32[]{:S(2)}, u32[]{:S(2)}) collective-permute-start(f32[5,8,128]{2,1,0:T(8,128)S(1)} %get-tuple-element.70), channel_id=1, source_target_pairs={{0,1},{1,2},{2,3},{3,4},{4,5},{5,6},{6,7},{7,8},{8,9},{9,10},{10,1... | collective-permute-start | bytes 61448 | tf_op jit(solution)/shard_map/ppermute | solution.py:241
  108.6 28.1 %collective-permute-start.27 = (f32[5,8,128]{2,1,0:T(8,128)S(1)}, f32[5,8,128]{2,1,0:T(8,128)S(1)}, u32[]{:S(2)}, u32[]{:S(2)}) collective-permute-start(f32[5,8,128]{2,1,0:T(8,128)S(1)} %get-tuple-element.71), channel_id=1, source_target_pairs={{0,15},{1,0},{2,1},{3,2},{4,3},{5,4},{6,5},{7,6},{8,7},{9,8},{10,9... | collective-permute-start | bytes 61448 | tf_op jit(solution)/shard_map/ppermute | solution.py:241
  113.9 8.4 %collective-permute-start.28 = (f32[1,128]{1,0:T(1,128)S(1)}, f32[1,128]{1,0:T(1,128)S(1)}, u32[]{:S(2)}, u32[]{:S(2)}) collective-permute-start(f32[1,128]{1,0:T(1,128)S(1)} %get-tuple-element.72), channel_id=1, source_target_pairs={{0,17},{1,18},{2,19},{3,20},{4,21},{5,22},{6,23},{7,24},{8,25},{9,... | collective-permute-start | bytes 1544 | tf_op jit(solution)/shard_map/ppermute | solution.py:246
  122.3 3.0 %collective-permute-start.29 = (f32[1,128]{1,0:T(1,128)S(1)}, f32[1,128]{1,0:T(1,128)S(1)}, u32[]{:S(2)}, u32[]{:S(2)}) collective-permute-start(f32[1,128]{1,0:T(1,128)S(1)} %get-tuple-element.73), channel_id=1, source_target_pairs={{0,127},{1,112},{2,113},{3,114},{4,115},{5,116},{6,117},{7,118},{8... | collective-permute-start | bytes 1544 | tf_op jit(solution)/shard_map/ppermute | solution.py:246
  125.3 5.1 %collective-permute-start.30 = (f32[1,128]{1,0:T(1,128)S(1)}, f32[1,128]{1,0:T(1,128)S(1)}, u32[]{:S(2)}, u32[]{:S(2)}) collective-permute-start(f32[1,128]{1,0:T(1,128)S(1)} %get-tuple-element.74), channel_id=1, source_target_pairs={{0,31},{1,16},{2,17},{3,18},{4,19},{5,20},{6,21},{7,22},{8,23},{9,... | collective-permute-start | bytes 1544 | tf_op jit(solution)/shard_map/ppermute | solution.py:246
  130.4 6.3 %collective-permute-start.31 = (f32[1,128]{1,0:T(1,128)S(1)}, f32[1,128]{1,0:T(1,128)S(1)}, u32[]{:S(2)}, u32[]{:S(2)}) collective-permute-start(f32[1,128]{1,0:T(1,128)S(1)} %get-tuple-element.75), channel_id=1, source_target_pairs={{0,113},{1,114},{2,115},{3,116},{4,117},{5,118},{6,119},{7,120},{8... | collective-permute-start | bytes 1544 | tf_op jit(solution)/shard_map/ppermute | solution.py:246
  136.7 17.0 %copy-start.3 = (f32[4,4,256]{2,1,0:T(4,128)S(1)}, f32[4,4,256]{2,1,0:T(4,128)}, u32[]{:S(2)}) copy-start(f32[4,4,256]{2,1,0:T(4,128)} %param.5) | copy-start | bytes 49156
  153.8 8.7 %collective-permute-start.32 = (f32[4,2,2,256]{3,2,1,0:T(2,128)S(1)}, f32[4,2,2,256]{3,2,1,0:T(2,128)S(1)}, u32[]{:S(2)}, u32[]{:S(2)}) collective-permute-start(f32[4,2,2,256]{3,2,1,0:T(2,128)S(1)} %get-tuple-element.90), channel_id=1, source_target_pairs={{0,17},{1,18},{2,19},{3,20},{4,21},{5,22},{6,23},{7,24},{8,25},{9,... | collective-permute-start | bytes 49160 | tf_op jit(solution)/shard_map/ppermute | solution.py:246
  153.9 10.9 %collective-permute-start.34 = (f32[4,2,2,256]{3,2,1,0:T(2,128)S(1)}, f32[4,2,2,256]{3,2,1,0:T(2,128)S(1)}, u32[]{:S(2)}, u32[]{:S(2)}) collective-permute-start(f32[4,2,2,256]{3,2,1,0:T(2,128)S(1)} %get-tuple-element.91), channel_id=1, source_target_pairs={{0,113},{1,114},{2,115},{3,116},{4,117},{5,118},{6,119},{7,120},{8... | collective-permute-start | bytes 49160 | tf_op jit(solution)/shard_map/ppermute | solution.py:246
  157.0 15.7 %collective-permute-start.33 = (f32[4,2,4,256]{3,2,1,0:T(4,128)S(1)}, f32[4,2,4,256]{3,2,1,0:T(4,128)S(1)}, u32[]{:S(2)}, u32[]{:S(2)}) collective-permute-start(f32[4,2,4,256]{3,2,1,0:T(4,128)S(1)} %get-tuple-element.94), channel_id=1, source_target_pairs={{0,1},{1,2},{2,3},{3,4},{4,5},{5,6},{6,7},{7,8},{8,9},{9,10},{10,1... | collective-permute-start | bytes 98312 | tf_op jit(solution)/shard_map/ppermute | solution.py:241
  158.4 14.3 %collective-permute-start.35 = (f32[4,4,2,256]{3,2,1,0:T(2,128)S(1)}, f32[4,4,2,256]{3,2,1,0:T(2,128)S(1)}, u32[]{:S(2)}, u32[]{:S(2)}) collective-permute-start(f32[4,4,2,256]{3,2,1,0:T(2,128)S(1)} %get-tuple-element.96), channel_id=1, source_target_pairs={{0,16},{16,32},{32,48},{48,64},{64,80},{80,96},{96,112},{112,0},{1... | collective-permute-start | bytes 98312 | tf_op jit(solution)/shard_map/ppermute | solution.py:239
  158.4 7.7 %collective-permute-start.37 = (f32[4,2,2,256]{3,2,1,0:T(2,128)S(1)}, f32[4,2,2,256]{3,2,1,0:T(2,128)S(1)}, u32[]{:S(2)}, u32[]{:S(2)}) collective-permute-start(f32[4,2,2,256]{3,2,1,0:T(2,128)S(1)} %get-tuple-element.92), channel_id=1, source_target_pairs={{0,31},{1,16},{2,17},{3,18},{4,19},{5,20},{6,21},{7,22},{8,23},{9,... | collective-permute-start | bytes 49160 | tf_op jit(solution)/shard_map/ppermute | solution.py:246
  162.5 10.3 %collective-permute-start.36 = (f32[4,4,2,256]{3,2,1,0:T(2,128)S(1)}, f32[4,4,2,256]{3,2,1,0:T(2,128)S(1)}, u32[]{:S(2)}, u32[]{:S(2)}) collective-permute-start(f32[4,4,2,256]{3,2,1,0:T(2,128)S(1)} %get-tuple-element.97), channel_id=1, source_target_pairs={{0,112},{16,0},{32,16},{48,32},{64,48},{80,64},{96,80},{112,96},{1... | collective-permute-start | bytes 98312 | tf_op jit(solution)/shard_map/ppermute | solution.py:239
  164.8 7.9 %collective-permute-start.38 = (f32[4,2,4,256]{3,2,1,0:T(4,128)S(1)}, f32[4,2,4,256]{3,2,1,0:T(4,128)S(1)}, u32[]{:S(2)}, u32[]{:S(2)}) collective-permute-start(f32[4,2,4,256]{3,2,1,0:T(4,128)S(1)} %get-tuple-element.95), channel_id=1, source_target_pairs={{0,15},{1,0},{2,1},{3,2},{4,3},{5,4},{6,5},{7,6},{8,7},{9,8},{10,9... | collective-permute-start | bytes 98312 | tf_op jit(solution)/shard_map/ppermute | solution.py:241
  166.1 6.6 %collective-permute-start.39 = (f32[4,2,2,256]{3,2,1,0:T(2,128)S(1)}, f32[4,2,2,256]{3,2,1,0:T(2,128)S(1)}, u32[]{:S(2)}, u32[]{:S(2)}) collective-permute-start(f32[4,2,2,256]{3,2,1,0:T(2,128)S(1)} %get-tuple-element.93), channel_id=1, source_target_pairs={{0,127},{1,112},{2,113},{3,114},{4,115},{5,116},{6,117},{7,118},{8... | collective-permute-start | bytes 49160 | tf_op jit(solution)/shard_map/ppermute | solution.py:246
where the time goes:
time: 175 us; the launch traced here: 174 us
  waiting for transfers between devices  93.6 us (53%)
  starting transfers between devices  50.7 us (29%)
  blocking collectives  11.9 us (7%)
  Pallas kernels  10.6 us (6%)
  local copies, waits for them, and re-layouts  4.82 us (3%)
  other arithmetic  1.8 us (1%)
    ppermute x20, waiting for transfers between devices, send(): return lax.ppermute(x, ('vessel', 'blk'), pairs)  93.5 us
    ppermute x10, starting transfers between devices, send(): return lax.ppermute(x, 'blk', [(i, (i + db) % nb) for i in range(nb)])  25.4 us
    ppermute x10, starting transfers between devices, send(): return lax.ppermute(x, 'vessel', [(i, (i + dv) % nv) for i in range(nv)])  14.2 us
    all_to_all x1, blocking collectives, local(): lax.all_to_all(coarse, 'blk', split_axis=2, concat_axis=3, tiled=True)  11.9 us
    ppermute x20, starting transfers between devices, send(): return lax.ppermute(x, ('vessel', 'blk'), pairs)  11.1 us
    pallas_call x5, Pallas kernels, lb_call(): pl.pallas_call(functools.partial(lb_kernel, mode, nx, ny), out_shape=out_...  10.6 us
  transfers between devices with their start and end apart: 40, of which 18 were waited for; matrix products, arithmetic and copies ran while one was open for 0% of the time, Pallas kernels for 0%

commit v1 on v0

v1 whole, which is shorter than its diff:
```python
import functools

import jax
import jax.numpy as jnp
import numpy as np
from jax import lax
from jax.experimental import pallas as pl
from jax.experimental.pallas import tpu as pltpu
from jax.sharding import PartitionSpec as P

STEPS = 4
TRACER_STEPS = 2


VELOCITY = np.array(
    [
        [0, 0, 0],
        [1, 0, 0],
        [-1, 0, 0],
        [0, 1, 0],
        [0, -1, 0],
        [0, 0, 1],
        [0, 0, -1],
        [1, 1, 0],
        [-1, -1, 0],
        [1, -1, 0],
        [-1, 1, 0],
        [1, 0, 1],
        [-1, 0, -1],
        [1, 0, -1],
        [-1, 0, 1],
        [0, 1, 1],
        [0, -1, -1],
        [0, 1, -1],
        [0, -1, 1],
    ]
)
WEIGHTS = np.array([1.0 / 3.0] + [1.0 / 18.0] * 6 + [1.0 / 36.0] * 12)
OPPOSITE = [0, 2, 1, 4, 3, 6, 5, 8, 7, 10, 9, 12, 11, 14, 13, 16, 15, 18, 17]
relax_rate = 1.25
pore_damping = 0.5
advect_gain = 8.0
diffusion = 0.1

NPOP = 19
CX = [int(v) for v in VELOCITY[:, 0]]
CY = [int(v) for v in VELOCITY[:, 1]]
CZ = [int(v) for v in VELOCITY[:, 2]]
CXP = [i for i in range(NPOP) if CX[i] == 1]
CXM = [i for i in range(NPOP) if CX[i] == -1]
CYP = [i for i in range(NPOP) if CY[i] == 1]
CYM = [i for i in range(NPOP) if CY[i] == -1]
SHIFTED = [i for i in range(NPOP) if CX[i] != 0 or CY[i] != 0]
ROWS = 8
YOFF = 8


def moments_chunk(g):
    w0 = jnp.float32(WEIGHTS[0])
    w1 = jnp.float32(WEIGHTS[1])
    w2 = jnp.float32(WEIGHTS[7])
    s1 = ((g[1] + g[2]) + (g[3] + g[4])) + (g[5] + g[6])
    s2 = (((g[7] + g[8]) + (g[9] + g[10])) + ((g[11] + g[12]) + (g[13] + g[14]))) + (
        (g[15] + g[16]) + (g[17] + g[18])
    )
    density = w0 * g[0] + w1 * s1 + w2 * s2
    mx = w1 * (g[1] - g[2]) + w2 * (((g[7] - g[8]) + (g[9] - g[10])) + ((g[11] - g[12]) + (g[13] - g[14])))
    my = w1 * (g[3] - g[4]) + w2 * (((g[7] - g[8]) + (g[10] - g[9])) + ((g[15] - g[16]) + (g[17] - g[18])))
    mz = w1 * (g[5] - g[6]) + w2 * (((g[11] - g[12]) + (g[14] - g[13])) + ((g[15] - g[16]) + (g[18] - g[17])))
    return density, (mx, my, mz)


def collide_chunk(g, mask):
    density, (mx, my, mz) = moments_chunk(g)
    ux = mx / density
    uy = my / density
    uz = mz / density
    porous = mask == 1
    ux = jnp.where(porous, pore_damping * ux, ux)
    uy = jnp.where(porous, pore_damping * uy, uy)
    uz = jnp.where(porous, pore_damping * uz, uz)
    speed_sq = ux * ux + uy * uy + uz * uz
    solid = mask == 2
    comps = (ux, uy, uz)
    out = [None] * NPOP
    for i in range(NPOP):
        proj = None
        for d in range(3):
            c = int(VELOCITY[i, d])
            if c == 0:
                continue
            term = comps[d] if c > 0 else -comps[d]
            proj = term if proj is None else proj + term
        if proj is None:
            balance = density * (1.0 - 1.5 * speed_sq)
        else:
            balance = density * (1.0 + 3.0 * proj + 4.5 * proj * proj - 1.5 * speed_sq)
        relaxed = g[i] + relax_rate * (balance - g[i])
        out[i] = jnp.where(solid, g[OPPOSITE[i]], relaxed)
    return out


def lb_kernel(halo, nx, ny, *refs):
    g0, mask_ref, xlo, xhi, ylo, yhi, c_mm, c_mp, c_pm, c_pp = refs[:10]
    out_ref, coarse_ref, abuf, bbuf, flow_s = refs[10:]
    h = halo
    top = YOFF
    abuf[0:NPOP, h : h + nx, top : top + ny, :] = g0[...]
    abuf[NPOP, h : h + nx, top : top + ny, :] = mask_ref[...].astype(jnp.float32)
    abuf[:, 0:h, top : top + ny, :] = xlo[...]
    abuf[:, h + nx : 2 * h + nx, top : top + ny, :] = xhi[...]
    abuf[:, h : h + nx, top - h : top, :] = ylo[...]
    abuf[:, h : h + nx, top + ny : top + ny + h, :] = yhi[...]
    abuf[:, 0:h, top - h : top, :] = c_mm[...]
    abuf[:, h + nx : 2 * h + nx, top - h : top, :] = c_mp[...]
    abuf[:, 0:h, top + ny : top + ny + h, :] = c_pm[...]
    abuf[:, h + nx : 2 * h + nx, top + ny : top + ny + h, :] = c_pp[...]

    bufs = [bbuf, abuf]
    offs = [top] + [h - s for s in range(1, h + 1)]

    def run_step(s):
        src = abuf if s == 0 else bufs[(s - 1) % 2]
        dst = bufs[s % 2]
        if s == 0:
            rows = list(range(0, top + ny + h, ROWS))
        else:
            rows = list(range(0, ny + 2 * (h - s), ROWS))
        shift = offs[s - 1] - offs[s] if s > 0 else 0

        def body(x, carry):
            for r in rows:
                g = []
                for i in range(NPOP):
                    if s == 0:
                        v = src[i, x, pl.ds(r, ROWS), :]
                    else:
                        v = src[i, x - CX[i], pl.ds(r + shift - CY[i], ROWS), :]
                        if CZ[i] != 0:
                            v = pltpu.roll(v, CZ[i] % v.shape[1], 1)
                    g.append(v)
                mask = abuf[NPOP, x, pl.ds(r - offs[s] + top, ROWS), :]
                post = collide_chunk(g, mask)
                for i in range(NPOP):
                    dst[i, x, pl.ds(r, ROWS), :] = post[i]
            return carry

        lax.fori_loop(s, nx + 2 * h - s, body, 0)

    for s in range(h):
        run_step(s)

    src = bufs[(h - 1) % 2]
    shift = offs[h - 1] - 0

    def last_body(x, carry):
        for r in range(0, ny, ROWS):
            g = []
            for i in range(NPOP):
                v = src[i, x + h - CX[i], pl.ds(r + shift - CY[i], ROWS), :]
                if CZ[i] != 0:
                    v = pltpu.roll(v, CZ[i] % v.shape[1], 1)
                g.append(v)
                out_ref[i, x, pl.ds(r, ROWS), :] = v
            mask = abuf[NPOP, x + h, pl.ds(r + top, ROWS), :]
            density, mom = moments_chunk(g)
            solid = mask == 2
            for d in range(3):
                flow_s[d, x, pl.ds(r, ROWS), :] = jnp.where(solid, jnp.float32(0.0), mom[d] / density)
        return carry

    lax.fori_loop(0, nx, last_body, 0)

    nz = flow_s.shape[3]
    pz = (
        lax.broadcasted_iota(jnp.int32, (nz // 2, nz), 1) // 2 == lax.broadcasted_iota(jnp.int32, (nz // 2, nz), 0)
    ).astype(jnp.float32)
    py = (
        lax.broadcasted_iota(jnp.int32, (ny, ny // 2), 0) // 2 == lax.broadcasted_iota(jnp.int32, (ny, ny // 2), 1)
    ).astype(jnp.float32)
    for d in range(3):
        for xp in range(nx // 2):
            plane = flow_s[d, 2 * xp] + flow_s[d, 2 * xp + 1]
            zy = lax.dot_general(
                pz,
                plane,
                (((1,), (1,)), ((), ())),
                precision=lax.Precision.HIGHEST,
                preferred_element_type=jnp.float32,
            )
            zc = jnp.dot(zy, py, precision=lax.Precision.HIGHEST, preferred_element_type=jnp.float32)
            coarse_ref[d, xp] = zc * jnp.float32(0.125)


def lb_call(g0, mask, halos, halo):
    _, nx, ny, nz = g0.shape
    f32 = jnp.float32
    vmem = pl.BlockSpec(memory_space=pltpu.VMEM)
    rows = YOFF + ny + 2 * halo
    rows = -(-rows // ROWS) * ROWS
    out_shape = (
        jax.ShapeDtypeStruct(g0.shape, f32),
        jax.ShapeDtypeStruct((3, nx // 2, nz // 2, ny // 2), f32),
    )
    scratch = [
        pltpu.VMEM((NPOP + 1, nx + 2 * halo, rows, nz), f32),
        pltpu.VMEM((NPOP, nx + 2 * halo, rows, nz), f32),
        pltpu.VMEM((3, nx, ny, nz), f32),
    ]
    cells = (nx + halo) * (ny + 2 * halo) * nz * halo
    cost = pl.CostEstimate(flops=320 * cells, transcendentals=0, bytes_accessed=2 * NPOP * 4 * nx * ny * nz * 2)
    return pl.pallas_call(
        functools.partial(lb_kernel, halo, nx, ny),
        out_shape=out_shape,
        in_specs=[vmem] * (2 + len(halos)),
        out_specs=(vmem, vmem),
        scratch_shapes=scratch,
        cost_estimate=cost,
        compiler_params=pltpu.CompilerParams(vmem_limit_bytes=60 * 1024 * 1024),
    )(g0, mask, *halos)


def send(x, dv, db):
    nv = lax.axis_size("vessel")
    nb = lax.axis_size("blk")
    if db == 0:
        return lax.ppermute(x, "vessel", [(i, (i + dv) % nv) for i in range(nv)])
    if dv == 0:
        return lax.ppermute(x, "blk", [(i, (i + db) % nb) for i in range(nb)])
    pairs = []
    for v in range(nv):
        for b in range(nb):
            pairs.append((v * nb + b, ((v + dv) % nv) * nb + (b + db) % nb))
    return lax.ppermute(x, ("vessel", "blk"), pairs)


def lattice_halos(g0, mask, h):
    _, nx, ny, _ = g0.shape
    maskf = mask.astype(jnp.float32)[None]

    def piece(xs, ys):
        return jnp.concatenate([g0[:, xs, ys], maskf[:, xs, ys]], axis=0)

    lo_x, hi_x = slice(nx - h, nx), slice(0, h)
    lo_y, hi_y = slice(ny - h, ny), slice(0, h)
    whole_x, whole_y = slice(0, nx), slice(0, ny)
    return (
        send(piece(lo_x, whole_y), 1, 0),
        send(piece(hi_x, whole_y), -1, 0),
        send(piece(whole_x, lo_y), 0, 1),
        send(piece(whole_x, hi_y), 0, -1),
        send(piece(lo_x, lo_y), 1, 1),
        send(piece(hi_x, lo_y), -1, 1),
        send(piece(lo_x, hi_y), 1, -1),
        send(piece(hi_x, hi_y), -1, -1),
    )


def tracer_update(c, fx, fy, fz):
    flux_x = fx * c
    flux_y = fy[1:-1, 1:-1] * c[1:-1, 1:-1]
    flux_z = fz * c
    center = c[1:-1, 1:-1]
    div_x = (flux_x[1:-1, 2:] - flux_x[1:-1, :-2]) * 0.5
    div_y = (jnp.roll(flux_y, -1, 2) - jnp.roll(flux_y, 1, 2)) * 0.5
    div_z = (flux_z[2:, 1:-1] - flux_z[:-2, 1:-1]) * 0.5
    divergence = div_x + div_y + div_z
    beside_all = (
        (c[1:-1, 2:] + c[1:-1, :-2])
        + (jnp.roll(center, -1, 2) + jnp.roll(center, 1, 2))
        + (c[2:, 1:-1] + c[:-2, 1:-1])
    )
    laplace = beside_all - 6.0 * center
    return center - advect_gain * divergence + diffusion * laplace


def local(populations, voxel_mask, tracer):
    halos = lattice_halos(populations, voxel_mask, STEPS)
    state, coarse = lb_call(populations, voxel_mask, halos, STEPS)
    moved = lax.all_to_all(coarse, "blk", split_axis=2, concat_axis=3, tiled=True)
    flow = jnp.transpose(moved, (0, 2, 1, 3))
    w = TRACER_STEPS
    q = jnp.concatenate([tracer[None], flow], axis=0)
    nzb, nxb = q.shape[1], q.shape[2]
    zlo = send(q[:, nzb - w :], 0, 1)
    zhi = send(q[:, :w], 0, -1)
    xlo = send(q[:, :, nxb - w :], 1, 0)
    xhi = send(q[:, :, :w], -1, 0)
    c_mm = send(q[:, nzb - w :, nxb - w :], 1, 1)
    c_pp = send(q[:, :w, :w], -1, -1)
    c_mp = send(q[:, nzb - w :, :w], -1, 1)
    c_pm = send(q[:, :w, nxb - w :], 1, -1)
    ext = jnp.concatenate(
        [
            jnp.concatenate([c_mm, zlo, c_mp], axis=2),
            jnp.concatenate([xlo, q, xhi], axis=2),
            jnp.concatenate([c_pm, zhi, c_pp], axis=2),
        ],
        axis=1,
    )
    conc, fx, fy, fz = ext[0], ext[1], ext[2], ext[3]
    for step in range(TRACER_STEPS):
        conc = tracer_update(conc, fx, fy, fz)
        fx, fy, fz = fx[1:-1, 1:-1], fy[1:-1, 1:-1], fz[1:-1, 1:-1]
    return (state, conc)


def solution(mesh):
    placed = (P(None, "vessel", "blk", None), P("vessel", "blk", None), P("blk", "vessel", None))
    return jax.shard_map(
        local,
        mesh=mesh,
        in_specs=placed,
        out_specs=(P(None, "vessel", "blk", None), P("blk", "vessel", None)),
        check_vma=False,
    )
```

time: 175 us -> 105 us (0.60)
  waiting for transfers between devices: 93.6 us -> 33.5 us
  starting transfers between devices: 50.7 us -> 26.4 us
  Pallas kernels: 10.6 us -> 20.5 us
  local copies, waits for them, and re-layouts: 4.82 us -> 6.7 us
    ppermute x20 -> x8, waiting for transfers between devices: 93.5 us -> 33.5 us  [send(): return lax.ppermute(x, ('vessel', 'blk'), pairs)]
    ppermute x10 -> x4, starting transfers between devices: 25.4 us -> 7.36 us  [send(): return lax.ppermute(x, 'blk', [(i, (i + db) % nb) for i in range(nb)])]
    pallas_call x5 -> x1, Pallas kernels: 10.6 us -> 20.5 us  [lb_call(): pl.pallas_call(functools.partial(lb_kernel, halo, nx, ny), out_shape=out_...]
    ppermute x10 -> x4, starting transfers between devices: 14.2 us -> 5.91 us  [send(): return lax.ppermute(x, 'vessel', [(i, (i + dv) % nv) for i in range(nv)])]
    slice x0 -> x6, local copies, waits for them, and re-layouts: none -> 2.21 us  [piece(): return jnp.concatenate([g0[:, xs, ys], maskf[:, xs, ys]], axis=0)]
    ppermute x20 -> x8, starting transfers between devices: 11.1 us -> 13.1 us  [send(): return lax.ppermute(x, ('vessel', 'blk'), pairs)]
  transfers between devices with their start and end apart: 40 -> 16, of which waited for: 18 -> 3; matrix products, arithmetic and copies ran while one was open for 0% -> 1% of each run, Pallas kernels for 0% -> 0%
where the time goes in v1:
time: 105 us; the launch traced here: 104 us
  waiting for transfers between devices  33.5 us (32%)
  starting transfers between devices  26.4 us (25%)
  Pallas kernels  20.5 us (20%)
  blocking collectives  12.9 us (12%)
  local copies, waits for them, and re-layouts  6.7 us (6%)
  other arithmetic  3.23 us (3%)
    ppermute x8, waiting for transfers between devices, send(): return lax.ppermute(x, ('vessel', 'blk'), pairs)  33.5 us
    pallas_call x1, Pallas kernels, lb_call(): pl.pallas_call(functools.partial(lb_kernel, halo, nx, ny), out_shape=out_...  20.5 us
    ppermute x8, starting transfers between devices, send(): return lax.ppermute(x, ('vessel', 'blk'), pairs)  13.1 us
    all_to_all x1, blocking collectives, local(): lax.all_to_all(coarse, 'blk', split_axis=2, concat_axis=3, tiled=True)  12.9 us
    ppermute x4, starting transfers between devices, send(): return lax.ppermute(x, 'blk', [(i, (i + db) % nb) for i in range(nb)])  7.36 us
    ppermute x4, starting transfers between devices, send(): return lax.ppermute(x, 'vessel', [(i, (i + dv) % nv) for i in range(nv)])  5.91 us
    slice x6, local copies, waits for them, and re-layouts, piece(): return jnp.concatenate([g0[:, xs, ys], maskf[:, xs, ys]], axis=0)  2.21 us
  transfers between devices with their start and end apart: 16, of which 3 were waited for; matrix products, arithmetic and copies ran while one was open for 1% of the time, Pallas kernels for 0%

profile of v1, /device:TPU:0, one launch (start us, length us, event | category | flops | bytes accessed | tf_op | source)
XLA Modules:
  0.0 104.3 jit_solution(10726673114840920131)
XLA Ops:
  0.6 0.9 convert_bitcast_fusion
  1.6 1.9 %fusion.30 = (f32[19,4,32,128]{3,2,1,0:T(8,128)S(1)}, f32[19,4,32,128]{3,2,1,0:T(8,128)S(1)}) fusion(f32[19,8,32,128]{3,2,1,0:T(8,128)} %refs_0_.1), kind=kLoop, calls=%fused_computation.74 | loop fusion | bytes 4980736 | tf_op jit(solution)/shard_map/slice | solution.py:242
  3.5 0.1 pad_maximum_fusion
  3.6 0.0 collective-permute-start
  3.6 0.0 copy-start
  3.6 0.1 pad_maximum_fusion.1
  3.7 2.9 %collective-permute-start.1 = (f32[20,4,32,128]{3,2,1,0:T(8,128)S(1)}, f32[20,4,32,128]{3,2,1,0:T(8,128)}, u32[]{:S(2)}, u32[]{:S(2)}) collective-permute-start(f32[20,4,32,128]{3,2,1,0:T(8,128)S(1)} %pad_maximum_fusion.1), channel_id=1, source_target_pairs={{0,112},{16,0},{32,16},{48,32},{64,48},{80,64},{96,80},{112,96},{1... | collective-permute-start | bytes 3932168 | tf_op jit(solution)/shard_map/ppermute | solution.py:227
  6.7 0.1 fusion.28
  6.8 1.6 %collective-permute-start.4 = (f32[20,4,4,128]{3,2,1,0:T(4,128)S(1)}, f32[20,4,4,128]{3,2,1,0:T(4,128)S(1)}, u32[]{:S(2)}, u32[]{:S(2)}) collective-permute-start(f32[20,4,4,128]{3,2,1,0:T(4,128)S(1)} %pad_maximum_fusion.4), channel_id=1, source_target_pairs={{0,17},{1,18},{2,19},{3,20},{4,21},{5,22},{6,23},{7,24},{8,25},{9,... | collective-permute-start | bytes 491528 | tf_op jit(solution)/shard_map/ppermute | solution.py:234
  8.4 3.7 %collective-permute-start.5 = (f32[20,4,4,128]{3,2,1,0:T(4,128)S(1)}, f32[20,4,4,128]{3,2,1,0:T(4,128)S(1)}, u32[]{:S(2)}, u32[]{:S(2)}) collective-permute-start(f32[20,4,4,128]{3,2,1,0:T(4,128)S(1)} %pad_maximum_fusion.5), channel_id=1, source_target_pairs={{0,113},{1,114},{2,115},{3,116},{4,117},{5,118},{6,119},{7,120},{8... | collective-permute-start | bytes 491528 | tf_op jit(solution)/shard_map/ppermute | solution.py:234
  12.1 1.6 %collective-permute-start.6 = (f32[20,4,4,128]{3,2,1,0:T(4,128)S(1)}, f32[20,4,4,128]{3,2,1,0:T(4,128)S(1)}, u32[]{:S(2)}, u32[]{:S(2)}) collective-permute-start(f32[20,4,4,128]{3,2,1,0:T(4,128)S(1)} %pad_maximum_fusion.6), channel_id=1, source_target_pairs={{0,31},{1,16},{2,17},{3,18},{4,19},{5,20},{6,21},{7,22},{8,23},{9,... | collective-permute-start | bytes 491528 | tf_op jit(solution)/shard_map/ppermute | solution.py:234
  13.7 0.2 fusion.29
  13.9 0.1 pad_maximum_fusion.2
  14.0 0.1 pad_maximum_fusion.3
  14.0 16.7 %collective-permute-done.4.refs_6_ = f32[20,4,4,128]{3,2,1,0:T(4,128)S(1)} collective-permute-done((f32[20,4,4,128]{3,2,1,0:T(4,128)S(1)}, f32[20,4,4,128]{3,2,1,0:T(4,128)S(1)}, u32[]{:S(2)}, u32[]{:S(2)}) %collective-permute-start.4) | collective-permute-done | bytes 163872 | tf_op jit(solution)/shard_map/ppermute | solution.py:234
  30.7 5.3 %collective-permute-start.3 = (f32[20,8,4,128]{3,2,1,0:T(4,128)S(1)}, f32[20,8,4,128]{3,2,1,0:T(4,128)S(1)}, u32[]{:S(2)}, u32[]{:S(2)}) collective-permute-start(f32[20,8,4,128]{3,2,1,0:T(4,128)S(1)} %pad_maximum_fusion.3), channel_id=1, source_target_pairs={{0,15},{1,0},{2,1},{3,2},{4,3},{5,4},{6,5},{7,6},{8,7},{9,8},{10,9... | collective-permute-start | bytes 983048 | tf_op jit(solution)/shard_map/ppermute | solution.py:229
  36.1 0.0 collective-permute-done.6.refs_8_
  36.1 0.1 collective-permute-start.7
  36.2 8.2 %collective-permute-done.7.refs_9_ = f32[20,4,4,128]{3,2,1,0:T(4,128)S(1)} collective-permute-done((f32[20,4,4,128]{3,2,1,0:T(4,128)S(1)}, f32[20,4,4,128]{3,2,1,0:T(4,128)S(1)}, u32[]{:S(2)}, u32[]{:S(2)}) %collective-permute-start.7) | collective-permute-done | bytes 163872 | tf_op jit(solution)/shard_map/ppermute | solution.py:234
  44.5 0.6 copy-done.8
  45.1 0.1 copy-done.2
  45.2 0.1 copy-done.3
  45.3 0.4 copy-done.1
  45.7 20.5 %shard_map.50 = (f32[19,8,32,128]{3,2,1,0:T(8,128)}, f32[3,4,64,16]{3,2,1,0:T(8,128)}) custom-call(f32[19,8,32,128]{3,2,1,0:T(8,128)} %refs_0_.1, s32[8,32,128]{2,1,0:T(8,128)} %refs_1_.1, f32[20,4,32,128]{3,2,1,0:T(8,128)} %copy-done.1, f32[20,4,32,128]{3,2,1,0:T(8,128)} %collective-permute-done.1.refs_3_, f32[20,8,4,128]{3,2,1,0:T(4,128)} %copy-done.2, ...), custom_call_target="tpu_custom_call" | custom-call | flops 78643200 | bytes 9961472 | tf_op jit(solution)/shard_map/pallas_call | solution.py:212
  66.3 1.3 %copy.9 = f32[3,4,64,16]{3,1,0,2:T(4,128)S(1)} copy(f32[3,4,64,16]{3,2,1,0:T(8,128)} %get-tuple-element.5) | data formatting | bytes 98304 | tf_op jit(solution)/shard_map/pallas_call | solution.py:212
  67.5 0.0 copy-start.4
  67.5 0.3 reshape.4
  67.9 12.9 %all_to_all.18 = f32[16,1,768]{2,1,0:T(1,128)S(1)} all-to-all(f32[16,1,768]{2,1,0:T(1,128)S(1)} %reshape.4), channel_id=1, replica_groups=mesh['vessel'=8,'blk'=16] {'blk'}, dimensions={0} | all-to-all | bytes 98304 | tf_op jit(solution)/shard_map/all_to_all | solution.py:280
  80.8 0.5 broadcast.4
  81.3 0.8 reduce
  82.1 0.3 reshape.5
  82.4 0.1 copy.7
  82.5 0.2 all_to_all.16
  82.8 0.1 collective-permute-start.10
  82.9 5.1 %collective-permute-start.13 = (f32[4,2,2,256]{3,2,1,0:T(2,128)S(1)}, f32[4,2,2,256]{3,2,1,0:T(2,128)S(1)}, u32[]{:S(2)}, u32[]{:S(2)}) collective-permute-start(f32[4,2,2,256]{3,2,1,0:T(2,128)S(1)} %get-tuple-element.36), channel_id=1, source_target_pairs={{0,31},{1,16},{2,17},{3,18},{4,19},{5,20},{6,21},{7,22},{8,23},{9,... | collective-permute-start | bytes 49160 | tf_op jit(solution)/shard_map/ppermute | solution.py:234
  88.0 1.1 %collective-permute-start.15 = (f32[4,2,2,256]{3,2,1,0:T(2,128)S(1)}, f32[4,2,2,256]{3,2,1,0:T(2,128)S(1)}, u32[]{:S(2)}, u32[]{:S(2)}) collective-permute-start(f32[4,2,2,256]{3,2,1,0:T(2,128)S(1)} %get-tuple-element.37), channel_id=1, source_target_pairs={{0,127},{1,112},{2,113},{3,114},{4,115},{5,116},{6,117},{7,118},{8... | collective-permute-start | bytes 49160 | tf_op jit(solution)/shard_map/ppermute | solution.py:234
  89.1 3.0 %collective-permute-start.12 = (f32[4,4,2,256]{3,2,1,0:T(2,128)S(1)}, f32[4,4,2,256]{3,2,1,0:T(2,128)S(1)}, u32[]{:S(2)}, u32[]{:S(2)}) collective-permute-start(f32[4,4,2,256]{3,2,1,0:T(2,128)S(1)} %get-tuple-element.41), channel_id=1, source_target_pairs={{0,112},{16,0},{32,16},{48,32},{64,48},{80,64},{96,80},{112,96},{1... | collective-permute-start | bytes 98312 | tf_op jit(solution)/shard_map/ppermute | solution.py:227
  92.1 2.0 %collective-permute-start.9 = (f32[4,2,4,256]{3,2,1,0:T(4,128)S(1)}, f32[4,2,4,256]{3,2,1,0:T(4,128)S(1)}, u32[]{:S(2)}, u32[]{:S(2)}) collective-permute-start(f32[4,2,4,256]{3,2,1,0:T(4,128)S(1)} %get-tuple-element.38), channel_id=1, source_target_pairs={{0,1},{1,2},{2,3},{3,4},{4,5},{5,6},{6,7},{7,8},{8,9},{9,10},{10,1... | collective-permute-start | bytes 98312 | tf_op jit(solution)/shard_map/ppermute | solution.py:229
  94.1 8.6 %collective-permute-done.8 = f32[4,2,2,256]{3,2,1,0:T(2,128)S(1)} collective-permute-done((f32[4,2,2,256]{3,2,1,0:T(2,128)S(1)}, f32[4,2,2,256]{3,2,1,0:T(2,128)S(1)}, u32[]{:S(2)}, u32[]{:S(2)}) %collective-permute-start.8) | collective-permute-done | bytes 16416 | tf_op jit(solution)/shard_map/ppermute | solution.py:234
  102.7 0.1 maximum_maximum_fusion
  102.9 0.1 fusion.35
  103.0 0.1 fusion.34
  103.1 0.1 slice_multiply_fusion.1
  103.2 0.1 fusion.41
  103.3 0.1 fusion.40
  103.4 0.1 fusion.37
  103.5 0.1 fusion.36
  103.6 0.7 fusion.19
  (43 shorter events, 0.4 us)
Async XLA Ops:
  3.6 40.8 %collective-permute-start = (f32[20,4,32,128]{3,2,1,0:T(8,128)S(1)}, f32[20,4,32,128]{3,2,1,0:T(8,128)S(1)}, u32[]{:S(2)}, u32[]{:S(2)}) collective-permute-start(f32[20,4,32,128]{3,2,1,0:T(8,128)S(1)} %pad_maximum_fusion), channel_id=1, source_target_pairs={{0,16},{16,32},{32,48},{48,64},{64,80},{80,96},{96,112},{112,0},{1... | collective-permute-start | bytes 3932168 | tf_op jit(solution)/shard_map/ppermute | solution.py:227
  3.6 3.1 %copy-start = (f32[19,8,32,128]{3,2,1,0:T(8,128)S(1)}, f32[19,8,32,128]{3,2,1,0:T(8,128)}, u32[]{:S(2)}) copy-start(f32[19,8,32,128]{3,2,1,0:T(8,128)} %refs_0_.1) | copy-start | bytes 7471108
  3.7 40.7 %collective-permute-start.1 = (f32[20,4,32,128]{3,2,1,0:T(8,128)S(1)}, f32[20,4,32,128]{3,2,1,0:T(8,128)}, u32[]{:S(2)}, u32[]{:S(2)}) collective-permute-start(f32[20,4,32,128]{3,2,1,0:T(8,128)S(1)} %pad_maximum_fusion.1), channel_id=1, source_target_pairs={{0,112},{16,0},{32,16},{48,32},{64,48},{80,64},{96,80},{112,96},{1... | collective-permute-start | bytes 3932168 | tf_op jit(solution)/shard_map/ppermute | solution.py:227
  6.8 23.9 %collective-permute-start.4 = (f32[20,4,4,128]{3,2,1,0:T(4,128)S(1)}, f32[20,4,4,128]{3,2,1,0:T(4,128)S(1)}, u32[]{:S(2)}, u32[]{:S(2)}) collective-permute-start(f32[20,4,4,128]{3,2,1,0:T(4,128)S(1)} %pad_maximum_fusion.4), channel_id=1, source_target_pairs={{0,17},{1,18},{2,19},{3,20},{4,21},{5,22},{6,23},{7,24},{8,25},{9,... | collective-permute-start | bytes 491528 | tf_op jit(solution)/shard_map/ppermute | solution.py:234
  8.4 22.3 %collective-permute-start.5 = (f32[20,4,4,128]{3,2,1,0:T(4,128)S(1)}, f32[20,4,4,128]{3,2,1,0:T(4,128)S(1)}, u32[]{:S(2)}, u32[]{:S(2)}) collective-permute-start(f32[20,4,4,128]{3,2,1,0:T(4,128)S(1)} %pad_maximum_fusion.5), channel_id=1, source_target_pairs={{0,113},{1,114},{2,115},{3,116},{4,117},{5,118},{6,119},{7,120},{8... | collective-permute-start | bytes 491528 | tf_op jit(solution)/shard_map/ppermute | solution.py:234
  12.1 24.0 %collective-permute-start.6 = (f32[20,4,4,128]{3,2,1,0:T(4,128)S(1)}, f32[20,4,4,128]{3,2,1,0:T(4,128)S(1)}, u32[]{:S(2)}, u32[]{:S(2)}) collective-permute-start(f32[20,4,4,128]{3,2,1,0:T(4,128)S(1)} %pad_maximum_fusion.6), channel_id=1, source_target_pairs={{0,31},{1,16},{2,17},{3,18},{4,19},{5,20},{6,21},{7,22},{8,23},{9,... | collective-permute-start | bytes 491528 | tf_op jit(solution)/shard_map/ppermute | solution.py:234
  30.7 13.7 %copy-start.5 = (f32[20,4,4,128]{3,2,1,0:T(4,128)}, f32[20,4,4,128]{3,2,1,0:T(4,128)S(1)}, u32[]{:S(2)}) copy-start(f32[20,4,4,128]{3,2,1,0:T(4,128)S(1)} %collective-permute-done.4.refs_6_) | copy-start | bytes 491524
  30.7 13.7 %collective-permute-start.2 = (f32[20,8,4,128]{3,2,1,0:T(4,128)S(1)}, f32[20,8,4,128]{3,2,1,0:T(4,128)S(1)}, u32[]{:S(2)}, u32[]{:S(2)}) collective-permute-start(f32[20,8,4,128]{3,2,1,0:T(4,128)S(1)} %pad_maximum_fusion.2), channel_id=1, source_target_pairs={{0,1},{1,2},{2,3},{3,4},{4,5},{5,6},{6,7},{7,8},{8,9},{9,10},{10,1... | collective-permute-start | bytes 983048 | tf_op jit(solution)/shard_map/ppermute | solution.py:229
  30.7 13.7 %copy-start.6 = (f32[20,4,4,128]{3,2,1,0:T(4,128)}, f32[20,4,4,128]{3,2,1,0:T(4,128)S(1)}, u32[]{:S(2)}) copy-start(f32[20,4,4,128]{3,2,1,0:T(4,128)S(1)} %collective-permute-done.5.refs_7_) | copy-start | bytes 491524
  30.7 13.7 %collective-permute-start.3 = (f32[20,8,4,128]{3,2,1,0:T(4,128)S(1)}, f32[20,8,4,128]{3,2,1,0:T(4,128)S(1)}, u32[]{:S(2)}, u32[]{:S(2)}) collective-permute-start(f32[20,8,4,128]{3,2,1,0:T(4,128)S(1)} %pad_maximum_fusion.3), channel_id=1, source_target_pairs={{0,15},{1,0},{2,1},{3,2},{4,3},{5,4},{6,5},{7,6},{8,7},{9,8},{10,9... | collective-permute-start | bytes 983048 | tf_op jit(solution)/shard_map/ppermute | solution.py:229
  36.1 8.3 %copy-start.7 = (f32[20,4,4,128]{3,2,1,0:T(4,128)}, f32[20,4,4,128]{3,2,1,0:T(4,128)S(1)}, u32[]{:S(2)}) copy-start(f32[20,4,4,128]{3,2,1,0:T(4,128)S(1)} %collective-permute-done.6.refs_8_) | copy-start | bytes 491524
  36.1 8.3 %collective-permute-start.7 = (f32[20,4,4,128]{3,2,1,0:T(4,128)S(1)}, f32[20,4,4,128]{3,2,1,0:T(4,128)S(1)}, u32[]{:S(2)}, u32[]{:S(2)}) collective-permute-start(f32[20,4,4,128]{3,2,1,0:T(4,128)S(1)} %pad_maximum_fusion.7), channel_id=1, source_target_pairs={{0,127},{1,112},{2,113},{3,114},{4,115},{5,116},{6,117},{7,118},{8... | collective-permute-start | bytes 491528 | tf_op jit(solution)/shard_map/ppermute | solution.py:234
  44.4 0.7 copy-start.8
  44.4 0.8 copy-start.2
  44.4 0.9 copy-start.3
  44.4 1.3 %copy-start.1 = (f32[20,4,32,128]{3,2,1,0:T(8,128)}, f32[20,4,32,128]{3,2,1,0:T(8,128)S(1)}, u32[]{:S(2)}) copy-start(f32[20,4,32,128]{3,2,1,0:T(8,128)S(1)} %collective-permute-done.refs_2_) | copy-start | bytes 3932164
  67.5 15.2 %copy-start.4 = (f32[4,4,256]{2,1,0:T(4,128)S(1)}, f32[4,4,256]{2,1,0:T(4,128)}, u32[]{:S(2)}) copy-start(f32[4,4,256]{2,1,0:T(4,128)} %param.5) | copy-start | bytes 49156
  82.8 9.3 %collective-permute-start.10 = (f32[4,2,2,256]{3,2,1,0:T(2,128)S(1)}, f32[4,2,2,256]{3,2,1,0:T(2,128)S(1)}, u32[]{:S(2)}, u32[]{:S(2)}) collective-permute-start(f32[4,2,2,256]{3,2,1,0:T(2,128)S(1)} %get-tuple-element.35), channel_id=1, source_target_pairs={{0,113},{1,114},{2,115},{3,116},{4,117},{5,118},{6,119},{7,120},{8... | collective-permute-start | bytes 49160 | tf_op jit(solution)/shard_map/ppermute | solution.py:234
  82.9 9.2 %collective-permute-start.13 = (f32[4,2,2,256]{3,2,1,0:T(2,128)S(1)}, f32[4,2,2,256]{3,2,1,0:T(2,128)S(1)}, u32[]{:S(2)}, u32[]{:S(2)}) collective-permute-start(f32[4,2,2,256]{3,2,1,0:T(2,128)S(1)} %get-tuple-element.36), channel_id=1, source_target_pairs={{0,31},{1,16},{2,17},{3,18},{4,19},{5,20},{6,21},{7,22},{8,23},{9,... | collective-permute-start | bytes 49160 | tf_op jit(solution)/shard_map/ppermute | solution.py:234
  88.0 6.1 %collective-permute-start.15 = (f32[4,2,2,256]{3,2,1,0:T(2,128)S(1)}, f32[4,2,2,256]{3,2,1,0:T(2,128)S(1)}, u32[]{:S(2)}, u32[]{:S(2)}) collective-permute-start(f32[4,2,2,256]{3,2,1,0:T(2,128)S(1)} %get-tuple-element.37), channel_id=1, source_target_pairs={{0,127},{1,112},{2,113},{3,114},{4,115},{5,116},{6,117},{7,118},{8... | collective-permute-start | bytes 49160 | tf_op jit(solution)/shard_map/ppermute | solution.py:234
  89.1 13.6 %collective-permute-start.11 = (f32[4,4,2,256]{3,2,1,0:T(2,128)S(1)}, f32[4,4,2,256]{3,2,1,0:T(2,128)S(1)}, u32[]{:S(2)}, u32[]{:S(2)}) collective-permute-start(f32[4,4,2,256]{3,2,1,0:T(2,128)S(1)} %get-tuple-element.40), channel_id=1, source_target_pairs={{0,16},{16,32},{32,48},{48,64},{64,80},{80,96},{96,112},{112,0},{1... | collective-permute-start | bytes 98312 | tf_op jit(solution)/shard_map/ppermute | solution.py:227
  89.1 13.6 %collective-permute-start.12 = (f32[4,4,2,256]{3,2,1,0:T(2,128)S(1)}, f32[4,4,2,256]{3,2,1,0:T(2,128)S(1)}, u32[]{:S(2)}, u32[]{:S(2)}) collective-permute-start(f32[4,4,2,256]{3,2,1,0:T(2,128)S(1)} %get-tuple-element.41), channel_id=1, source_target_pairs={{0,112},{16,0},{32,16},{48,32},{64,48},{80,64},{96,80},{112,96},{1... | collective-permute-start | bytes 98312 | tf_op jit(solution)/shard_map/ppermute | solution.py:227
  92.1 10.6 %collective-permute-start.14 = (f32[4,2,4,256]{3,2,1,0:T(4,128)S(1)}, f32[4,2,4,256]{3,2,1,0:T(4,128)S(1)}, u32[]{:S(2)}, u32[]{:S(2)}) collective-permute-start(f32[4,2,4,256]{3,2,1,0:T(4,128)S(1)} %get-tuple-element.39), channel_id=1, source_target_pairs={{0,15},{1,0},{2,1},{3,2},{4,3},{5,4},{6,5},{7,6},{8,7},{9,8},{10,9... | collective-permute-start | bytes 98312 | tf_op jit(solution)/shard_map/ppermute | solution.py:229
  92.1 10.6 %collective-permute-start.9 = (f32[4,2,4,256]{3,2,1,0:T(4,128)S(1)}, f32[4,2,4,256]{3,2,1,0:T(4,128)S(1)}, u32[]{:S(2)}, u32[]{:S(2)}) collective-permute-start(f32[4,2,4,256]{3,2,1,0:T(4,128)S(1)} %get-tuple-element.38), channel_id=1, source_target_pairs={{0,1},{1,2},{2,3},{3,4},{4,5},{5,6},{6,7},{7,8},{8,9},{9,10},{10,1... | collective-permute-start | bytes 98312 | tf_op jit(solution)/shard_map/ppermute | solution.py:229
  94.1 8.6 %collective-permute-start.8 = (f32[4,2,2,256]{3,2,1,0:T(2,128)S(1)}, f32[4,2,2,256]{3,2,1,0:T(2,128)S(1)}, u32[]{:S(2)}, u32[]{:S(2)}) collective-permute-start(f32[4,2,2,256]{3,2,1,0:T(2,128)S(1)} %get-tuple-element.34), channel_id=1, source_target_pairs={{0,17},{1,18},{2,19},{3,20},{4,21},{5,22},{6,23},{7,24},{8,25},{9,... | collective-permute-start | bytes 49160 | tf_op jit(solution)/shard_map/ppermute | solution.py:234

commit v2 on v1

--- a/solution.py
+++ b/solution.py
@@ -107,14 +107,15 @@
     top = YOFF
     abuf[0:NPOP, h : h + nx, top : top + ny, :] = g0[...]
     abuf[NPOP, h : h + nx, top : top + ny, :] = mask_ref[...].astype(jnp.float32)
-    abuf[:, 0:h, top : top + ny, :] = xlo[...]
-    abuf[:, h + nx : 2 * h + nx, top : top + ny, :] = xhi[...]
-    abuf[:, h : h + nx, top - h : top, :] = ylo[...]
-    abuf[:, h : h + nx, top + ny : top + ny + h, :] = yhi[...]
-    abuf[:, 0:h, top - h : top, :] = c_mm[...]
-    abuf[:, h + nx : 2 * h + nx, top - h : top, :] = c_mp[...]
-    abuf[:, 0:h, top + ny : top + ny + h, :] = c_pm[...]
-    abuf[:, h + nx : 2 * h + nx, top + ny : top + ny + h, :] = c_pp[...]
+    planes = NPOP + 1
+    abuf[:, 0:h, top : top + ny, :] = xlo[0:planes]
+    abuf[:, h + nx : 2 * h + nx, top : top + ny, :] = xhi[0:planes]
+    abuf[:, h : h + nx, top - h : top, :] = ylo[0:planes]
+    abuf[:, h : h + nx, top + ny : top + ny + h, :] = yhi[0:planes]
+    abuf[:, 0:h, top - h : top, :] = c_mm[0:planes]
+    abuf[:, h + nx : 2 * h + nx, top - h : top, :] = c_mp[0:planes]
+    abuf[:, 0:h, top + ny : top + ny + h, :] = c_pm[0:planes]
+    abuf[:, h + nx : 2 * h + nx, top + ny : top + ny + h, :] = c_pp[0:planes]
 
     bufs = [bbuf, abuf]
     offs = [top] + [h - s for s in range(1, h + 1)]
@@ -234,26 +235,27 @@
     return lax.ppermute(x, ("vessel", "blk"), pairs)
 
 
-def lattice_halos(g0, mask, h):
-    _, nx, ny, _ = g0.shape
+def lattice_halos(g0, mask, conc, h, w):
+    _, nx, ny, nz = g0.shape
+    nzc, nxc, nyc = conc.shape
     maskf = mask.astype(jnp.float32)[None]
-
-    def piece(xs, ys):
-        return jnp.concatenate([g0[:, xs, ys], maskf[:, xs, ys]], axis=0)
-
-    lo_x, hi_x = slice(nx - h, nx), slice(0, h)
-    lo_y, hi_y = slice(ny - h, ny), slice(0, h)
-    whole_x, whole_y = slice(0, nx), slice(0, ny)
-    return (
-        send(piece(lo_x, whole_y), 1, 0),
-        send(piece(hi_x, whole_y), -1, 0),
-        send(piece(whole_x, lo_y), 0, 1),
-        send(piece(whole_x, hi_y), 0, -1),
-        send(piece(lo_x, lo_y), 1, 1),
-        send(piece(hi_x, lo_y), -1, 1),
-        send(piece(lo_x, hi_y), 1, -1),
-        send(piece(hi_x, hi_y), -1, -1),
-    )
+    lat = {1: slice(nx - h, nx), -1: slice(0, h), 0: slice(0, nx)}
+    lat_y = {1: slice(ny - h, ny), -1: slice(0, h), 0: slice(0, ny)}
+    trc_x = {1: slice(nxc - w, nxc), -1: slice(0, w), 0: slice(0, nxc)}
+    trc_z = {1: slice(nzc - w, nzc), -1: slice(0, w), 0: slice(0, nzc)}
+    order = ((1, 0), (-1, 0), (0, 1), (0, -1), (1, 1), (-1, 1), (1, -1), (-1, -1))
+    pieces, tracer_pieces = [], []
+    for dv, db in order:
+        xs, ys = lat[dv], lat_y[db]
+        lb = jnp.concatenate([g0[:, xs, ys], maskf[:, xs, ys]], axis=0)
+        tp = conc[trc_z[db], trc_x[dv]]
+        plane = lb.shape[1] * lb.shape[2] * nz
+        flat = jnp.pad(tp.reshape(-1), (0, plane - tp.size))
+        msg = jnp.concatenate([lb, flat.reshape(1, lb.shape[1], lb.shape[2], nz)], axis=0)
+        got = send(msg, dv, db)
+        pieces.append(got)
+        tracer_pieces.append(got[NPOP + 1].reshape(-1)[: tp.size].reshape(tp.shape))
+    return pieces, tracer_pieces
 
 
 def tracer_update(c, fx, fy, fz):
@@ -275,30 +277,31 @@
 
 
 def local(populations, voxel_mask, tracer):
-    halos = lattice_halos(populations, voxel_mask, STEPS)
+    w = TRACER_STEPS
+    halos, tp = lattice_halos(populations, voxel_mask, tracer, STEPS, w)
     state, coarse = lb_call(populations, voxel_mask, halos, STEPS)
-    moved = lax.all_to_all(coarse, "blk", split_axis=2, concat_axis=3, tiled=True)
-    flow = jnp.transpose(moved, (0, 2, 1, 3))
-    w = TRACER_STEPS
-    q = jnp.concatenate([tracer[None], flow], axis=0)
-    nzb, nxb = q.shape[1], q.shape[2]
-    zlo = send(q[:, nzb - w :], 0, 1)
-    zhi = send(q[:, :w], 0, -1)
-    xlo = send(q[:, :, nxb - w :], 1, 0)
-    xhi = send(q[:, :, :w], -1, 0)
-    c_mm = send(q[:, nzb - w :, nxb - w :], 1, 1)
-    c_pp = send(q[:, :w, :w], -1, -1)
-    c_mp = send(q[:, nzb - w :, :w], -1, 1)
-    c_pm = send(q[:, :w, nxb - w :], 1, -1)
-    ext = jnp.concatenate(
+    nzt = coarse.shape[2]
+    nb = lax.axis_size("blk")
+    zb = nzt // nb
+    ring = jnp.concatenate([coarse[:, :, nzt - w :], coarse, coarse[:, :, :zb]], axis=2)
+    head = ring[:, :, : nb * zb].reshape(3, coarse.shape[1], nb, zb, coarse.shape[3])
+    tail = ring[:, :, zb : zb + nb * zb].reshape(3, coarse.shape[1], nb, zb, coarse.shape[3])
+    windows = jnp.concatenate([head, tail], axis=3)[:, :, :, : zb + 2 * w]
+    moved = lax.all_to_all(windows, "blk", split_axis=2, concat_axis=4, tiled=True)
+    flow = moved[:, :, 0]
+    nxb = flow.shape[1]
+    flow = jnp.concatenate([send(flow[:, nxb - w :], 1, 0), flow, send(flow[:, :w], -1, 0)], axis=1)
+    flow = jnp.transpose(flow, (0, 2, 1, 3))
+    xlo, xhi, zlo, zhi, c_mm, c_mp, c_pm, c_pp = tp
+    conc = jnp.concatenate(
         [
-            jnp.concatenate([c_mm, zlo, c_mp], axis=2),
-            jnp.concatenate([xlo, q, xhi], axis=2),
-            jnp.concatenate([c_pm, zhi, c_pp], axis=2),
+            jnp.concatenate([c_mm, zlo, c_mp], axis=1),
+            jnp.concatenate([xlo, tracer, xhi], axis=1),
+            jnp.concatenate([c_pm, zhi, c_pp], axis=1),
         ],
-        axis=1,
-    )
-    conc, fx, fy, fz = ext[0], ext[1], ext[2], ext[3]
+        axis=0,
+    )
+    fx, fy, fz = flow[0], flow[1], flow[2]
     for step in range(TRACER_STEPS):
         conc = tracer_update(conc, fx, fy, fz)
         fx, fy, fz = fx[1:-1, 1:-1], fy[1:-1, 1:-1], fz[1:-1, 1:-1]

time: 105 us -> 86.6 us (0.82)
  waiting for transfers between devices: 33.5 us -> 16.1 us
  blocking collectives: 12.9 us -> 0 us
  local copies, waits for them, and re-layouts: 6.7 us -> 11 us
  starting transfers between devices: 26.4 us -> 30.3 us
  other arithmetic: 3.23 us -> 6.24 us
    ppermute x8 -> x4, waiting for transfers between devices: 33.5 us -> 7.47 us  [send(): return lax.ppermute(x, ('vessel', 'blk'), pairs)]
    all_to_all x1 -> x0, blocking collectives: 12.9 us -> none  [local(): lax.all_to_all(coarse, 'blk', split_axis=2, concat_axis=3, tiled=True)]
    all_to_all x0 -> x1, waiting for transfers between devices: none -> 6.89 us  [local(): lax.all_to_all(windows, 'blk', split_axis=2, concat_axis=4, tiled=True)]
    all_to_all x0 -> x1, starting transfers between devices: none -> 6.12 us  [local(): lax.all_to_all(windows, 'blk', split_axis=2, concat_axis=4, tiled=True)]
    concatenate x12 -> x9, other arithmetic: 0.67 us -> 3.93 us  [the longest x8 2.71 us: lattice_halos(): jnp.concatenate([lb, flat.reshape(1, lb.shape[1], lb.shape[2], nz)], axis=0)]
    slice x6 -> x21, local copies, waits for them, and re-layouts: 2.21 us -> 5.39 us  [the longest x6 1.97 us: lattice_halos(): lb = jnp.concatenate([g0[:, xs, ys], maskf[:, xs, ys]], axis=0)]
    ppermute x8 -> x4, starting transfers between devices: 13.1 us -> 10.7 us  [send(): return lax.ppermute(x, ('vessel', 'blk'), pairs)]
    ppermute x4, starting transfers between devices: 5.91 us -> 8.03 us  [send(): return lax.ppermute(x, 'vessel', [(i, (i + dv) % nv) for i in range(nv)])]
  transfers between devices with their start and end apart: 16 -> 11, of which waited for: 3 -> 3; matrix products, arithmetic and copies ran while one was open for 1% -> 5% of each run, Pallas kernels for 0% -> 0%
where the time goes in v2:
time: 86.6 us; the launch traced here: 85.5 us
  starting transfers between devices  30.3 us (35%)
  Pallas kernels  20.6 us (24%)
  waiting for transfers between devices  16.1 us (19%)
  local copies, waits for them, and re-layouts  11 us (13%)
  other arithmetic  6.24 us (7%)
  between operations  1.18 us (1%)
    pallas_call x1, Pallas kernels, lb_call(): pl.pallas_call(functools.partial(lb_kernel, halo, nx, ny), out_shape=out_...  20.6 us
    ppermute x4, starting transfers between devices, send(): return lax.ppermute(x, ('vessel', 'blk'), pairs)  10.7 us
    ppermute x4, starting transfers between devices, send(): return lax.ppermute(x, 'vessel', [(i, (i + dv) % nv) for i in range(nv)])  8.03 us
    ppermute x4, waiting for transfers between devices, send(): return lax.ppermute(x, ('vessel', 'blk'), pairs)  7.47 us
    all_to_all x1, waiting for transfers between devices, local(): lax.all_to_all(windows, 'blk', split_axis=2, concat_axis=4, tiled=True)  6.89 us
    all_to_all x1, starting transfers between devices, local(): lax.all_to_all(windows, 'blk', split_axis=2, concat_axis=4, tiled=True)  6.12 us
    ppermute x2, starting transfers between devices, send(): return lax.ppermute(x, 'blk', [(i, (i + db) % nb) for i in range(nb)])  5.45 us
    unnamed x36, local copies, waits for them, and re-layouts  3.45 us
  transfers between devices with their start and end apart: 11, of which 3 were waited for; matrix products, arithmetic and copies ran while one was open for 5% of the time, Pallas kernels for 0%

profile of v2, /device:TPU:0, one launch (start us, length us, event | category | flops | bytes accessed | tf_op | source)
XLA Modules:
  0.0 85.5 jit_solution(3856350017760762351)
XLA Ops:
  0.6 0.8 slice_bitcast_fusion.7
  1.5 0.9 %convert_bitcast_fusion = f32[1,8,32,128]{3,2,1,0:T(8,128)S(1)} fusion(s32[8,32,128]{2,1,0:T(8,128)} %refs_1_.1), kind=kLoop, calls=%fused_computation.12 | loop fusion | flops 32768 | bytes 262144 | tf_op jit(solution)/shard_map/broadcast_in_dim | solution.py:241
  2.4 1.6 %fusion.22 = (f32[19,4,4,128]{3,2,1,0:T(4,128)S(1)}, f32[19,4,4,128]{3,2,1,0:T(4,128)S(1)}, f32[19,4,4,128]{3,2,1,0:T(4,128)S(1)}, f32[19,4,4,128]{3,2,1,0:T(4,128)S(1)}) fusion(f32[19,8,32,128]{3,2,1,0:T(8,128)} %refs_0_.1), kind=kLoop, calls=%fused_computation.72 | loop fusion | bytes 1245184 | tf_op jit(solution)/shard_map/slice | solution.py:250
  4.0 1.2 %collective-permute-start.4 = (f32[21,4,4,128]{3,2,1,0:T(4,128)S(1)}, f32[21,4,4,128]{3,2,1,0:T(4,128)S(1)}, u32[]{:S(2)}, u32[]{:S(2)}) collective-permute-start(f32[21,4,4,128]{3,2,1,0:T(4,128)S(1)} %pad_maximum_fusion.7), channel_id=1, source_target_pairs={{0,17},{1,18},{2,19},{3,20},{4,21},{5,22},{6,23},{7,24},{8,25},{9,... | collective-permute-start | bytes 516104 | tf_op jit(solution)/shard_map/ppermute | solution.py:235
  5.3 4.0 %collective-permute-start.5 = (f32[21,4,4,128]{3,2,1,0:T(4,128)S(1)}, f32[21,4,4,128]{3,2,1,0:T(4,128)S(1)}, u32[]{:S(2)}, u32[]{:S(2)}) collective-permute-start(f32[21,4,4,128]{3,2,1,0:T(4,128)S(1)} %pad_maximum_fusion.8), channel_id=1, source_target_pairs={{0,113},{1,114},{2,115},{3,116},{4,117},{5,118},{6,119},{7,120},{8... | collective-permute-start | bytes 516104 | tf_op jit(solution)/shard_map/ppermute | solution.py:235
  9.3 1.2 %collective-permute-start.6 = (f32[21,4,4,128]{3,2,1,0:T(4,128)S(1)}, f32[21,4,4,128]{3,2,1,0:T(4,128)S(1)}, u32[]{:S(2)}, u32[]{:S(2)}) collective-permute-start(f32[21,4,4,128]{3,2,1,0:T(4,128)S(1)} %pad_maximum_fusion.9), channel_id=1, source_target_pairs={{0,31},{1,16},{2,17},{3,18},{4,19},{5,20},{6,21},{7,22},{8,23},{9,... | collective-permute-start | bytes 516104 | tf_op jit(solution)/shard_map/ppermute | solution.py:235
  10.6 0.2 fusion.24
  10.8 1.2 %pad_maximum_fusion = f32[21,4,32,128]{3,2,1,0:T(8,128)} fusion(f32[1,4,32,128]{3,2,1,0:T(8,128)S(1)} %bitcast.67, f32[1,4,32,128]{3,2,1,0:T(8,128)S(1)} %get-tuple-element.34, f32[19,4,32,128]{3,2,1,0:T(8,128)S(1)} %get-tuple-element.19), kind=kLoop, calls=%fused_computation | loop fusion | flops 688128 | bytes 2752512 | tf_op jit(solution)/shard_map/concatenate | solution.py:254
  12.0 2.5 %collective-permute-start = (f32[21,4,32,128]{3,2,1,0:T(8,128)}, f32[21,4,32,128]{3,2,1,0:T(8,128)}, u32[]{:S(2)}, u32[]{:S(2)}) collective-permute-start(f32[21,4,32,128]{3,2,1,0:T(8,128)} %pad_maximum_fusion), channel_id=1, source_target_pairs={{0,16},{16,32},{32,48},{48,64},{64,80},{80,96},{96,112},{112,0},{1... | collective-permute-start | bytes 4128776 | tf_op jit(solution)/shard_map/ppermute | solution.py:228
  14.5 1.2 %pad_maximum_fusion.1 = f32[21,4,32,128]{3,2,1,0:T(8,128)} fusion(f32[1,4,32,128]{3,2,1,0:T(8,128)S(1)} %bitcast.66, f32[1,4,32,128]{3,2,1,0:T(8,128)S(1)} %get-tuple-element.33, f32[19,4,32,128]{3,2,1,0:T(8,128)S(1)} %get-tuple-element.18), kind=kLoop, calls=%fused_computation.1 | loop fusion | flops 688128 | bytes 2752512 | tf_op jit(solution)/shard_map/concatenate | solution.py:254
  15.7 2.6 %collective-permute-start.1 = (f32[21,4,32,128]{3,2,1,0:T(8,128)}, f32[21,4,32,128]{3,2,1,0:T(8,128)}, u32[]{:S(2)}, u32[]{:S(2)}) collective-permute-start(f32[21,4,32,128]{3,2,1,0:T(8,128)} %pad_maximum_fusion.1), channel_id=1, source_target_pairs={{0,112},{16,0},{32,16},{48,32},{64,48},{80,64},{96,80},{112,96},{1... | collective-permute-start | bytes 4128776 | tf_op jit(solution)/shard_map/ppermute | solution.py:228
  18.3 0.2 fusion.23
  18.6 4.3 %collective-permute-start.7 = (f32[21,4,4,128]{3,2,1,0:T(4,128)S(1)}, f32[21,4,4,128]{3,2,1,0:T(4,128)S(1)}, u32[]{:S(2)}, u32[]{:S(2)}) collective-permute-start(f32[21,4,4,128]{3,2,1,0:T(4,128)S(1)} %pad_maximum_fusion.10), channel_id=1, source_target_pairs={{0,127},{1,112},{2,113},{3,114},{4,115},{5,116},{6,117},{7,118},{8... | collective-permute-start | bytes 516104 | tf_op jit(solution)/shard_map/ppermute | solution.py:235
  22.9 0.1 pad_maximum_fusion.6
  23.1 0.1 pad_maximum_fusion.5
  23.2 0.1 collective-permute-start.2
  23.3 5.4 %collective-permute-start.3 = (f32[21,8,4,128]{3,2,1,0:T(4,128)S(1)}, f32[21,8,4,128]{3,2,1,0:T(4,128)S(1)}, u32[]{:S(2)}, u32[]{:S(2)}) collective-permute-start(f32[21,8,4,128]{3,2,1,0:T(4,128)S(1)} %pad_maximum_fusion.6), channel_id=1, source_target_pairs={{0,15},{1,0},{2,1},{3,2},{4,3},{5,4},{6,5},{7,6},{8,7},{9,8},{10,9... | collective-permute-start | bytes 1032200 | tf_op jit(solution)/shard_map/ppermute | solution.py:230
  28.7 7.5 %collective-permute-done.7.refs_9_ = f32[21,4,4,128]{3,2,1,0:T(4,128)S(1)} collective-permute-done((f32[21,4,4,128]{3,2,1,0:T(4,128)S(1)}, f32[21,4,4,128]{3,2,1,0:T(4,128)S(1)}, u32[]{:S(2)}, u32[]{:S(2)}) %collective-permute-start.7) | collective-permute-done | bytes 172064 | tf_op jit(solution)/shard_map/ppermute | solution.py:235
  36.4 0.5 copy-done.7
  36.9 0.1 copy-done.1
  37.0 0.1 copy-done.2
  37.1 20.6 %shard_map.50 = (f32[19,8,32,128]{3,2,1,0:T(8,128)}, f32[3,4,64,16]{3,2,1,0:T(8,128)}) custom-call(f32[19,8,32,128]{3,2,1,0:T(8,128)} %refs_0_.1, s32[8,32,128]{2,1,0:T(8,128)} %refs_1_.1, f32[21,4,32,128]{3,2,1,0:T(8,128)} %collective-permute-done.refs_2_, f32[21,4,32,128]{3,2,1,0:T(8,128)} %collective-permute-done.1.refs_3_, f32[21,8,4,128]{3,2,1,0:T(4,128)} %copy-done.1, ...), custom_call_target="tpu_custom_call" | custom-call | flops 78643200 | bytes 9961472 | tf_op jit(solution)/shard_map/pallas_call | solution.py:213
  57.7 0.8 slice.328
  58.5 0.8 slice.330
  59.3 0.8 slice.385
  60.2 1.2 %pad_maximum_fusion.4 = (f32[3,4,64,16]{3,2,1,0:T(8,128)S(1)}, f32[3,4,64,16]{3,2,1,0:T(8,128)S(1)}) fusion(f32[3,4,64,16]{3,2,1,0:T(8,128)} %get-tuple-element.5, f32[3,4,2,16]{3,2,1,0:T(2,128)S(1)} %slice.328, f32[3,4,4,16]{3,2,1,0:T(4,128)S(1)} %slice.330), kind=kLoop, calls=%fused_computation.4 | loop fusion | flops 24576 | bytes 152064 | tf_op jit(solution)/shard_map/concatenate | solution.py:286
  61.5 0.2 copy_bitcast_fusion
  61.7 0.9 %reshape.119 = f32[16,1,1536]{2,1,0:T(1,128)} reshape(f32[16,3,4,8,16]{4,3,2,1,0:T(8,128)S(1)} %copy_bitcast_fusion) | data formatting | bytes 196608
  62.6 6.1 %all-to-all-start = ((f32[16,1,1536]{2,1,0:T(1,128)}), f32[16,1,1536]{2,1,0:T(1,128)S(1)}, u32[]{:S(2)}, u32[]{:S(2)}) async-start(f32[16,1,1536]{2,1,0:T(1,128)} %reshape.119), calls=%async_computation | async-start | bytes 196608 | tf_op jit(solution)/shard_map/all_to_all | solution.py:290
  68.8 0.8 slice.387
  69.7 6.9 %all-to-all-done = f32[16,1,1536]{2,1,0:T(1,128)S(1)} async-done(((f32[16,1,1536]{2,1,0:T(1,128)}), f32[16,1,1536]{2,1,0:T(1,128)S(1)}, u32[]{:S(2)}, u32[]{:S(2)}) %all-to-all-start) | async-done | bytes 98336 | tf_op jit(solution)/shard_map/all_to_all | solution.py:290
  76.6 0.5 broadcast.20
  77.1 0.9 %reduce = f32[16,1536]{1,0:T(8,128)S(1)} reduce(f32[16,1,1536]{2,1,0:T(1,128)S(1)} %all-to-all-done, f32[]{:T(128)} %broadcast.20), dimensions={1}, to_apply=%all_to_all.11.reduce_sub_computation | reduce | bytes 196612 | tf_op jit(solution)/shard_map/all_to_all | solution.py:290
  78.0 0.3 reshape.120
  78.3 0.5 copy.39
  78.8 0.3 squeeze.12
  79.1 2.9 %collective-permute-start.9 = (f32[3,2,8,256]{3,2,1,0:T(8,128)S(1)}, f32[3,2,8,256]{3,2,1,0:T(8,128)S(1)}, u32[]{:S(2)}, u32[]{:S(2)}) collective-permute-start(f32[3,2,8,256]{3,2,1,0:T(8,128)S(1)} %get-tuple-element.36), channel_id=1, source_target_pairs={{0,112},{16,0},{32,16},{48,32},{64,48},{80,64},{96,80},{112,96},{1... | collective-permute-start | bytes 147464 | tf_op jit(solution)/shard_map/ppermute | solution.py:228
  82.1 1.8 %collective-permute-done.8 = f32[3,2,8,256]{3,2,1,0:T(8,128)S(1)} collective-permute-done((f32[3,2,8,256]{3,2,1,0:T(8,128)S(1)}, f32[3,2,8,256]{3,2,1,0:T(8,128)S(1)}, u32[]{:S(2)}, u32[]{:S(2)}) %collective-permute-start.8) | collective-permute-done | bytes 49184 | tf_op jit(solution)/shard_map/ppermute | solution.py:228
  84.0 0.1 fusion.34
  84.0 0.1 fusion.33
  84.1 0.1 fusion.30
  84.2 0.1 fusion.29
  84.3 0.1 slice_multiply_fusion.1
  84.5 0.1 fusion.36
  84.6 0.1 fusion.31
  84.6 0.1 fusion.32
  84.7 0.1 fusion.13
  84.8 0.6 copy.40
  (80 shorter events, 0.8 us)
Async XLA Ops:
  0.6 9.9 %copy-start.3 = (f32[4,4,256]{2,1,0:T(4,128)S(1)}, f32[4,4,256]{2,1,0:T(4,128)}, u32[]{:S(2)}) copy-start(f32[4,4,256]{2,1,0:T(4,128)} %param.5) | copy-start | bytes 49156
  2.4 8.2 %copy-start = (f32[19,8,32,128]{3,2,1,0:T(8,128)S(1)}, f32[19,8,32,128]{3,2,1,0:T(8,128)}, u32[]{:S(2)}) copy-start(f32[19,8,32,128]{3,2,1,0:T(8,128)} %refs_0_.1) | copy-start | bytes 7471108
  4.0 14.5 %collective-permute-start.4 = (f32[21,4,4,128]{3,2,1,0:T(4,128)S(1)}, f32[21,4,4,128]{3,2,1,0:T(4,128)S(1)}, u32[]{:S(2)}, u32[]{:S(2)}) collective-permute-start(f32[21,4,4,128]{3,2,1,0:T(4,128)S(1)} %pad_maximum_fusion.7), channel_id=1, source_target_pairs={{0,17},{1,18},{2,19},{3,20},{4,21},{5,22},{6,23},{7,24},{8,25},{9,... | collective-permute-start | bytes 516104 | tf_op jit(solution)/shard_map/ppermute | solution.py:235
  5.3 17.9 %collective-permute-start.5 = (f32[21,4,4,128]{3,2,1,0:T(4,128)S(1)}, f32[21,4,4,128]{3,2,1,0:T(4,128)S(1)}, u32[]{:S(2)}, u32[]{:S(2)}) collective-permute-start(f32[21,4,4,128]{3,2,1,0:T(4,128)S(1)} %pad_maximum_fusion.8), channel_id=1, source_target_pairs={{0,113},{1,114},{2,115},{3,116},{4,117},{5,118},{6,119},{7,120},{8... | collective-permute-start | bytes 516104 | tf_op jit(solution)/shard_map/ppermute | solution.py:235
  9.3 14.0 %collective-permute-start.6 = (f32[21,4,4,128]{3,2,1,0:T(4,128)S(1)}, f32[21,4,4,128]{3,2,1,0:T(4,128)S(1)}, u32[]{:S(2)}, u32[]{:S(2)}) collective-permute-start(f32[21,4,4,128]{3,2,1,0:T(4,128)S(1)} %pad_maximum_fusion.9), channel_id=1, source_target_pairs={{0,31},{1,16},{2,17},{3,18},{4,19},{5,20},{6,21},{7,22},{8,23},{9,... | collective-permute-start | bytes 516104 | tf_op jit(solution)/shard_map/ppermute | solution.py:235
  12.0 24.4 %collective-permute-start = (f32[21,4,32,128]{3,2,1,0:T(8,128)}, f32[21,4,32,128]{3,2,1,0:T(8,128)}, u32[]{:S(2)}, u32[]{:S(2)}) collective-permute-start(f32[21,4,32,128]{3,2,1,0:T(8,128)} %pad_maximum_fusion), channel_id=1, source_target_pairs={{0,16},{16,32},{32,48},{48,64},{64,80},{80,96},{96,112},{112,0},{1... | collective-permute-start | bytes 4128776 | tf_op jit(solution)/shard_map/ppermute | solution.py:228
  15.7 20.6 %collective-permute-start.1 = (f32[21,4,32,128]{3,2,1,0:T(8,128)}, f32[21,4,32,128]{3,2,1,0:T(8,128)}, u32[]{:S(2)}, u32[]{:S(2)}) collective-permute-start(f32[21,4,32,128]{3,2,1,0:T(8,128)} %pad_maximum_fusion.1), channel_id=1, source_target_pairs={{0,112},{16,0},{32,16},{48,32},{64,48},{80,64},{96,80},{112,96},{1... | collective-permute-start | bytes 4128776 | tf_op jit(solution)/shard_map/ppermute | solution.py:228
  18.6 17.8 %copy-start.4 = (f32[21,4,4,128]{3,2,1,0:T(4,128)}, f32[21,4,4,128]{3,2,1,0:T(4,128)S(1)}, u32[]{:S(2)}) copy-start(f32[21,4,4,128]{3,2,1,0:T(4,128)S(1)} %collective-permute-done.4.refs_6_) | copy-start | bytes 516100
  18.6 17.6 %collective-permute-start.7 = (f32[21,4,4,128]{3,2,1,0:T(4,128)S(1)}, f32[21,4,4,128]{3,2,1,0:T(4,128)S(1)}, u32[]{:S(2)}, u32[]{:S(2)}) collective-permute-start(f32[21,4,4,128]{3,2,1,0:T(4,128)S(1)} %pad_maximum_fusion.10), channel_id=1, source_target_pairs={{0,127},{1,112},{2,113},{3,114},{4,115},{5,116},{6,117},{7,118},{8... | collective-permute-start | bytes 516104 | tf_op jit(solution)/shard_map/ppermute | solution.py:235
  23.2 13.2 %copy-start.5 = (f32[21,4,4,128]{3,2,1,0:T(4,128)}, f32[21,4,4,128]{3,2,1,0:T(4,128)S(1)}, u32[]{:S(2)}) copy-start(f32[21,4,4,128]{3,2,1,0:T(4,128)S(1)} %collective-permute-done.5.refs_7_) | copy-start | bytes 516100
  23.2 13.0 %collective-permute-start.2 = (f32[21,8,4,128]{3,2,1,0:T(4,128)S(1)}, f32[21,8,4,128]{3,2,1,0:T(4,128)S(1)}, u32[]{:S(2)}, u32[]{:S(2)}) collective-permute-start(f32[21,8,4,128]{3,2,1,0:T(4,128)S(1)} %pad_maximum_fusion.5), channel_id=1, source_target_pairs={{0,1},{1,2},{2,3},{3,4},{4,5},{5,6},{6,7},{7,8},{8,9},{9,10},{10,1... | collective-permute-start | bytes 1032200 | tf_op jit(solution)/shard_map/ppermute | solution.py:230
  23.3 13.1 %copy-start.6 = (f32[21,4,4,128]{3,2,1,0:T(4,128)}, f32[21,4,4,128]{3,2,1,0:T(4,128)S(1)}, u32[]{:S(2)}) copy-start(f32[21,4,4,128]{3,2,1,0:T(4,128)S(1)} %collective-permute-done.6.refs_8_) | copy-start | bytes 516100
  23.3 12.9 %collective-permute-start.3 = (f32[21,8,4,128]{3,2,1,0:T(4,128)S(1)}, f32[21,8,4,128]{3,2,1,0:T(4,128)S(1)}, u32[]{:S(2)}, u32[]{:S(2)}) collective-permute-start(f32[21,8,4,128]{3,2,1,0:T(4,128)S(1)} %pad_maximum_fusion.6), channel_id=1, source_target_pairs={{0,15},{1,0},{2,1},{3,2},{4,3},{5,4},{6,5},{7,6},{8,7},{9,8},{10,9... | collective-permute-start | bytes 1032200 | tf_op jit(solution)/shard_map/ppermute | solution.py:230
  36.2 0.7 copy-start.7
  36.2 0.8 copy-start.1
  36.3 0.8 copy-start.2
  62.6 13.9 %all-to-all-start = ((f32[16,1,1536]{2,1,0:T(1,128)}), f32[16,1,1536]{2,1,0:T(1,128)S(1)}, u32[]{:S(2)}, u32[]{:S(2)}) async-start(f32[16,1,1536]{2,1,0:T(1,128)} %reshape.119), calls=%async_computation | async-start | bytes 196608 | tf_op jit(solution)/shard_map/all_to_all | solution.py:290
  79.1 4.7 %collective-permute-start.8 = (f32[3,2,8,256]{3,2,1,0:T(8,128)S(1)}, f32[3,2,8,256]{3,2,1,0:T(8,128)S(1)}, u32[]{:S(2)}, u32[]{:S(2)}) collective-permute-start(f32[3,2,8,256]{3,2,1,0:T(8,128)S(1)} %get-tuple-element.35), channel_id=1, source_target_pairs={{0,16},{16,32},{32,48},{48,64},{64,80},{80,96},{96,112},{112,0},{1... | collective-permute-start | bytes 147464 | tf_op jit(solution)/shard_map/ppermute | solution.py:228
  79.1 4.7 %collective-permute-start.9 = (f32[3,2,8,256]{3,2,1,0:T(8,128)S(1)}, f32[3,2,8,256]{3,2,1,0:T(8,128)S(1)}, u32[]{:S(2)}, u32[]{:S(2)}) collective-permute-start(f32[3,2,8,256]{3,2,1,0:T(8,128)S(1)} %get-tuple-element.36), channel_id=1, source_target_pairs={{0,112},{16,0},{32,16},{48,32},{64,48},{80,64},{96,80},{112,96},{1... | collective-permute-start | bytes 147464 | tf_op jit(solution)/shard_map/ppermute | solution.py:228

commit v3 on v2

--- a/solution.py
+++ b/solution.py
@@ -64,39 +64,50 @@
         (g[15] + g[16]) + (g[17] + g[18])
     )
     density = w0 * g[0] + w1 * s1 + w2 * s2
-    mx = w1 * (g[1] - g[2]) + w2 * (((g[7] - g[8]) + (g[9] - g[10])) + ((g[11] - g[12]) + (g[13] - g[14])))
-    my = w1 * (g[3] - g[4]) + w2 * (((g[7] - g[8]) + (g[10] - g[9])) + ((g[15] - g[16]) + (g[17] - g[18])))
-    mz = w1 * (g[5] - g[6]) + w2 * (((g[11] - g[12]) + (g[14] - g[13])) + ((g[15] - g[16]) + (g[18] - g[17])))
+    d1, d3, d5 = g[1] - g[2], g[3] - g[4], g[5] - g[6]
+    d7, d9, d11, d13 = g[7] - g[8], g[9] - g[10], g[11] - g[12], g[13] - g[14]
+    d15, d17 = g[15] - g[16], g[17] - g[18]
+    mx = w1 * d1 + w2 * ((d7 + d9) + (d11 + d13))
+    my = w1 * d3 + w2 * ((d7 - d9) + (d15 + d17))
+    mz = w1 * d5 + w2 * ((d11 - d13) + (d15 - d17))
     return density, (mx, my, mz)
+
+
+PAIRS = [(1, 2), (3, 4), (5, 6), (7, 8), (9, 10), (11, 12), (13, 14), (15, 16), (17, 18)]
 
 
 def collide_chunk(g, mask):
     density, (mx, my, mz) = moments_chunk(g)
-    ux = mx / density
-    uy = my / density
-    uz = mz / density
-    porous = mask == 1
-    ux = jnp.where(porous, pore_damping * ux, ux)
-    uy = jnp.where(porous, pore_damping * uy, uy)
-    uz = jnp.where(porous, pore_damping * uz, uz)
-    speed_sq = ux * ux + uy * uy + uz * uz
+    scale = jnp.where(mask == 1, jnp.float32(pore_damping), jnp.float32(1.0))
+    k = (1.0 / density) * scale
+    ux = mx * k
+    uy = my * k
+    uz = mz * k
+    base = 1.0 - 1.5 * (ux * ux + uy * uy + uz * uz)
+    dens = relax_rate * density
+    keep = 1.0 - relax_rate
     solid = mask == 2
-    comps = (ux, uy, uz)
+    proj = {
+        1: ux,
+        3: uy,
+        5: uz,
+        7: ux + uy,
+        9: ux - uy,
+        11: ux + uz,
+        13: ux - uz,
+        15: uy + uz,
+        17: uy - uz,
+    }
     out = [None] * NPOP
-    for i in range(NPOP):
-        proj = None
-        for d in range(3):
-            c = int(VELOCITY[i, d])
-            if c == 0:
-                continue
-            term = comps[d] if c > 0 else -comps[d]
-            proj = term if proj is None else proj + term
-        if proj is None:
-            balance = density * (1.0 - 1.5 * speed_sq)
-        else:
-            balance = density * (1.0 + 3.0 * proj + 4.5 * proj * proj - 1.5 * speed_sq)
-        relaxed = g[i] + relax_rate * (balance - g[i])
-        out[i] = jnp.where(solid, g[OPPOSITE[i]], relaxed)
+    out[0] = jnp.where(solid, g[0], dens * base + keep * g[0])
+    for i, j in PAIRS:
+        p = proj[i]
+        q = base + 4.5 * (p * p)
+        t = 3.0 * p
+        relaxed_i = dens * (q + t) + keep * g[i]
+        relaxed_j = dens * (q - t) + keep * g[j]
+        out[i] = jnp.where(solid, g[j], relaxed_i)
+        out[j] = jnp.where(solid, g[i], relaxed_j)
     return out
 
 
@@ -165,9 +176,10 @@
                 out_ref[i, x, pl.ds(r, ROWS), :] = v
             mask = abuf[NPOP, x + h, pl.ds(r + top, ROWS), :]
             density, mom = moments_chunk(g)
+            inv = 1.0 / density
             solid = mask == 2
             for d in range(3):
-                flow_s[d, x, pl.ds(r, ROWS), :] = jnp.where(solid, jnp.float32(0.0), mom[d] / density)
+                flow_s[d, x, pl.ds(r, ROWS), :] = jnp.where(solid, jnp.float32(0.0), mom[d] * inv)
         return carry
 
     lax.fori_loop(0, nx, last_body, 0)

time: 86.6 us -> 84.3 us (0.973)
  Pallas kernels: 20.6 us -> 18.2 us
    pallas_call x1, Pallas kernels: 20.6 us -> 18.2 us  [lb_call(): pl.pallas_call(functools.partial(lb_kernel, halo, nx, ny), out_shape=out_...]
where the time goes in v3:
time: 84.3 us; the launch traced here: 83.1 us
  starting transfers between devices  30.3 us (36%)
  Pallas kernels  18.2 us (22%)
  waiting for transfers between devices  16.1 us (19%)
  local copies, waits for them, and re-layouts  11 us (13%)
  other arithmetic  6.24 us (7%)
  between operations  1.18 us (1%)
    pallas_call x1, Pallas kernels, lb_call(): pl.pallas_call(functools.partial(lb_kernel, halo, nx, ny), out_shape=out_...  18.2 us
    ppermute x4, starting transfers between devices, send(): return lax.ppermute(x, ('vessel', 'blk'), pairs)  10.7 us
    ppermute x4, starting transfers between devices, send(): return lax.ppermute(x, 'vessel', [(i, (i + dv) % nv) for i in range(nv)])  8.03 us
    ppermute x4, waiting for transfers between devices, send(): return lax.ppermute(x, ('vessel', 'blk'), pairs)  7.47 us
    all_to_all x1, waiting for transfers between devices, local(): lax.all_to_all(windows, 'blk', split_axis=2, concat_axis=4, tiled=True)  6.89 us
    all_to_all x1, starting transfers between devices, local(): lax.all_to_all(windows, 'blk', split_axis=2, concat_axis=4, tiled=True)  6.12 us
    ppermute x2, starting transfers between devices, send(): return lax.ppermute(x, 'blk', [(i, (i + db) % nb) for i in range(nb)])  5.45 us
    unnamed x36, local copies, waits for them, and re-layouts  3.45 us
  transfers between devices with their start and end apart: 11, of which 3 were waited for; matrix products, arithmetic and copies ran while one was open for 5% of the time, Pallas kernels for 0%

profile of v3, /device:TPU:0, one launch (start us, length us, event | category | flops | bytes accessed | tf_op | source)
XLA Modules:
  0.0 83.1 jit_solution(8463331043121528098)
XLA Ops:
  0.6 0.8 slice_bitcast_fusion.7
  1.5 0.9 %convert_bitcast_fusion = f32[1,8,32,128]{3,2,1,0:T(8,128)S(1)} fusion(s32[8,32,128]{2,1,0:T(8,128)} %refs_1_.1), kind=kLoop, calls=%fused_computation.12 | loop fusion | flops 32768 | bytes 262144 | tf_op jit(solution)/shard_map/broadcast_in_dim | solution.py:253
  2.4 1.6 %fusion.22 = (f32[19,4,4,128]{3,2,1,0:T(4,128)S(1)}, f32[19,4,4,128]{3,2,1,0:T(4,128)S(1)}, f32[19,4,4,128]{3,2,1,0:T(4,128)S(1)}, f32[19,4,4,128]{3,2,1,0:T(4,128)S(1)}) fusion(f32[19,8,32,128]{3,2,1,0:T(8,128)} %refs_0_.1), kind=kLoop, calls=%fused_computation.72 | loop fusion | bytes 1245184 | tf_op jit(solution)/shard_map/slice | solution.py:262
  4.0 1.2 %collective-permute-start.4 = (f32[21,4,4,128]{3,2,1,0:T(4,128)S(1)}, f32[21,4,4,128]{3,2,1,0:T(4,128)S(1)}, u32[]{:S(2)}, u32[]{:S(2)}) collective-permute-start(f32[21,4,4,128]{3,2,1,0:T(4,128)S(1)} %pad_maximum_fusion.7), channel_id=1, source_target_pairs={{0,17},{1,18},{2,19},{3,20},{4,21},{5,22},{6,23},{7,24},{8,25},{9,... | collective-permute-start | bytes 516104 | tf_op jit(solution)/shard_map/ppermute | solution.py:247
  5.3 4.0 %collective-permute-start.5 = (f32[21,4,4,128]{3,2,1,0:T(4,128)S(1)}, f32[21,4,4,128]{3,2,1,0:T(4,128)S(1)}, u32[]{:S(2)}, u32[]{:S(2)}) collective-permute-start(f32[21,4,4,128]{3,2,1,0:T(4,128)S(1)} %pad_maximum_fusion.8), channel_id=1, source_target_pairs={{0,113},{1,114},{2,115},{3,116},{4,117},{5,118},{6,119},{7,120},{8... | collective-permute-start | bytes 516104 | tf_op jit(solution)/shard_map/ppermute | solution.py:247
  9.3 1.2 %collective-permute-start.6 = (f32[21,4,4,128]{3,2,1,0:T(4,128)S(1)}, f32[21,4,4,128]{3,2,1,0:T(4,128)S(1)}, u32[]{:S(2)}, u32[]{:S(2)}) collective-permute-start(f32[21,4,4,128]{3,2,1,0:T(4,128)S(1)} %pad_maximum_fusion.9), channel_id=1, source_target_pairs={{0,31},{1,16},{2,17},{3,18},{4,19},{5,20},{6,21},{7,22},{8,23},{9,... | collective-permute-start | bytes 516104 | tf_op jit(solution)/shard_map/ppermute | solution.py:247
  10.6 0.2 fusion.24
  10.8 1.2 %pad_maximum_fusion = f32[21,4,32,128]{3,2,1,0:T(8,128)} fusion(f32[1,4,32,128]{3,2,1,0:T(8,128)S(1)} %bitcast.67, f32[1,4,32,128]{3,2,1,0:T(8,128)S(1)} %get-tuple-element.34, f32[19,4,32,128]{3,2,1,0:T(8,128)S(1)} %get-tuple-element.19), kind=kLoop, calls=%fused_computation | loop fusion | flops 688128 | bytes 2752512 | tf_op jit(solution)/shard_map/concatenate | solution.py:266
  12.0 2.5 %collective-permute-start = (f32[21,4,32,128]{3,2,1,0:T(8,128)}, f32[21,4,32,128]{3,2,1,0:T(8,128)}, u32[]{:S(2)}, u32[]{:S(2)}) collective-permute-start(f32[21,4,32,128]{3,2,1,0:T(8,128)} %pad_maximum_fusion), channel_id=1, source_target_pairs={{0,16},{16,32},{32,48},{48,64},{64,80},{80,96},{96,112},{112,0},{1... | collective-permute-start | bytes 4128776 | tf_op jit(solution)/shard_map/ppermute | solution.py:240
  14.5 1.2 %pad_maximum_fusion.1 = f32[21,4,32,128]{3,2,1,0:T(8,128)} fusion(f32[1,4,32,128]{3,2,1,0:T(8,128)S(1)} %bitcast.66, f32[1,4,32,128]{3,2,1,0:T(8,128)S(1)} %get-tuple-element.33, f32[19,4,32,128]{3,2,1,0:T(8,128)S(1)} %get-tuple-element.18), kind=kLoop, calls=%fused_computation.1 | loop fusion | flops 688128 | bytes 2752512 | tf_op jit(solution)/shard_map/concatenate | solution.py:266
  15.7 2.6 %collective-permute-start.1 = (f32[21,4,32,128]{3,2,1,0:T(8,128)}, f32[21,4,32,128]{3,2,1,0:T(8,128)}, u32[]{:S(2)}, u32[]{:S(2)}) collective-permute-start(f32[21,4,32,128]{3,2,1,0:T(8,128)} %pad_maximum_fusion.1), channel_id=1, source_target_pairs={{0,112},{16,0},{32,16},{48,32},{64,48},{80,64},{96,80},{112,96},{1... | collective-permute-start | bytes 4128776 | tf_op jit(solution)/shard_map/ppermute | solution.py:240
  18.3 0.2 fusion.23
  18.6 4.3 %collective-permute-start.7 = (f32[21,4,4,128]{3,2,1,0:T(4,128)S(1)}, f32[21,4,4,128]{3,2,1,0:T(4,128)S(1)}, u32[]{:S(2)}, u32[]{:S(2)}) collective-permute-start(f32[21,4,4,128]{3,2,1,0:T(4,128)S(1)} %pad_maximum_fusion.10), channel_id=1, source_target_pairs={{0,127},{1,112},{2,113},{3,114},{4,115},{5,116},{6,117},{7,118},{8... | collective-permute-start | bytes 516104 | tf_op jit(solution)/shard_map/ppermute | solution.py:247
  22.9 0.1 pad_maximum_fusion.6
  23.1 0.1 pad_maximum_fusion.5
  23.2 0.1 collective-permute-start.2
  23.3 5.4 %collective-permute-start.3 = (f32[21,8,4,128]{3,2,1,0:T(4,128)S(1)}, f32[21,8,4,128]{3,2,1,0:T(4,128)S(1)}, u32[]{:S(2)}, u32[]{:S(2)}) collective-permute-start(f32[21,8,4,128]{3,2,1,0:T(4,128)S(1)} %pad_maximum_fusion.6), channel_id=1, source_target_pairs={{0,15},{1,0},{2,1},{3,2},{4,3},{5,4},{6,5},{7,6},{8,7},{9,8},{10,9... | collective-permute-start | bytes 1032200 | tf_op jit(solution)/shard_map/ppermute | solution.py:242
  28.7 7.5 %collective-permute-done.7.refs_9_ = f32[21,4,4,128]{3,2,1,0:T(4,128)S(1)} collective-permute-done((f32[21,4,4,128]{3,2,1,0:T(4,128)S(1)}, f32[21,4,4,128]{3,2,1,0:T(4,128)S(1)}, u32[]{:S(2)}, u32[]{:S(2)}) %collective-permute-start.7) | collective-permute-done | bytes 172064 | tf_op jit(solution)/shard_map/ppermute | solution.py:247
  36.4 0.5 copy-done.7
  36.9 0.1 copy-done.1
  37.0 0.1 copy-done.2
  37.1 18.2 %shard_map.50 = (f32[19,8,32,128]{3,2,1,0:T(8,128)}, f32[3,4,64,16]{3,2,1,0:T(8,128)}) custom-call(f32[19,8,32,128]{3,2,1,0:T(8,128)} %refs_0_.1, s32[8,32,128]{2,1,0:T(8,128)} %refs_1_.1, f32[21,4,32,128]{3,2,1,0:T(8,128)} %collective-permute-done.refs_2_, f32[21,4,32,128]{3,2,1,0:T(8,128)} %collective-permute-done.1.refs_3_, f32[21,8,4,128]{3,2,1,0:T(4,128)} %copy-done.1, ...), custom_call_target="tpu_custom_call" | custom-call | flops 78643200 | bytes 9961472 | tf_op jit(solution)/shard_map/pallas_call | solution.py:225
  55.3 0.8 slice.328
  56.1 0.8 slice.330
  57.0 0.8 %slice.385 = f32[1,4,32,128]{3,2,1,0:T(8,128)S(1)} slice(f32[21,4,32,128]{3,2,1,0:T(8,128)} %collective-permute-done.refs_2_), slice={[20:21], [0:4], [0:32], [0:128]} | slice | bytes 131072 | tf_op jit(solution)/shard_map/slice | solution.py:269
  57.9 1.2 %pad_maximum_fusion.4 = (f32[3,4,64,16]{3,2,1,0:T(8,128)S(1)}, f32[3,4,64,16]{3,2,1,0:T(8,128)S(1)}) fusion(f32[3,4,64,16]{3,2,1,0:T(8,128)} %get-tuple-element.5, f32[3,4,2,16]{3,2,1,0:T(2,128)S(1)} %slice.328, f32[3,4,4,16]{3,2,1,0:T(4,128)S(1)} %slice.330), kind=kLoop, calls=%fused_computation.4 | loop fusion | flops 24576 | bytes 152064 | tf_op jit(solution)/shard_map/concatenate | solution.py:298
  59.1 0.2 copy_bitcast_fusion
  59.3 0.9 %reshape.119 = f32[16,1,1536]{2,1,0:T(1,128)} reshape(f32[16,3,4,8,16]{4,3,2,1,0:T(8,128)S(1)} %copy_bitcast_fusion) | data formatting | bytes 196608
  60.3 6.1 %all-to-all-start = ((f32[16,1,1536]{2,1,0:T(1,128)}), f32[16,1,1536]{2,1,0:T(1,128)S(1)}, u32[]{:S(2)}, u32[]{:S(2)}) async-start(f32[16,1,1536]{2,1,0:T(1,128)} %reshape.119), calls=%async_computation | async-start | bytes 196608 | tf_op jit(solution)/shard_map/all_to_all | solution.py:302
  66.4 0.8 %slice.387 = f32[1,4,32,128]{3,2,1,0:T(8,128)S(1)} slice(f32[21,4,32,128]{3,2,1,0:T(8,128)} %collective-permute-done.1.refs_3_), slice={[20:21], [0:4], [0:32], [0:128]} | slice | bytes 131072 | tf_op jit(solution)/shard_map/slice | solution.py:269
  67.3 6.9 %all-to-all-done = f32[16,1,1536]{2,1,0:T(1,128)S(1)} async-done(((f32[16,1,1536]{2,1,0:T(1,128)}), f32[16,1,1536]{2,1,0:T(1,128)S(1)}, u32[]{:S(2)}, u32[]{:S(2)}) %all-to-all-start) | async-done | bytes 98336 | tf_op jit(solution)/shard_map/all_to_all | solution.py:302
  74.2 0.5 broadcast.20
  74.7 0.9 %reduce = f32[16,1536]{1,0:T(8,128)S(1)} reduce(f32[16,1,1536]{2,1,0:T(1,128)S(1)} %all-to-all-done, f32[]{:T(128)} %broadcast.20), dimensions={1}, to_apply=%all_to_all.11.reduce_sub_computation | reduce | bytes 196612 | tf_op jit(solution)/shard_map/all_to_all | solution.py:302
  75.6 0.3 reshape.120
  75.9 0.5 copy.39
  76.4 0.3 squeeze.12
  76.8 2.9 %collective-permute-start.9 = (f32[3,2,8,256]{3,2,1,0:T(8,128)S(1)}, f32[3,2,8,256]{3,2,1,0:T(8,128)S(1)}, u32[]{:S(2)}, u32[]{:S(2)}) collective-permute-start(f32[3,2,8,256]{3,2,1,0:T(8,128)S(1)} %get-tuple-element.36), channel_id=1, source_target_pairs={{0,112},{16,0},{32,16},{48,32},{64,48},{80,64},{96,80},{112,96},{1... | collective-permute-start | bytes 147464 | tf_op jit(solution)/shard_map/ppermute | solution.py:240
  79.7 1.8 %collective-permute-done.8 = f32[3,2,8,256]{3,2,1,0:T(8,128)S(1)} collective-permute-done((f32[3,2,8,256]{3,2,1,0:T(8,128)S(1)}, f32[3,2,8,256]{3,2,1,0:T(8,128)S(1)}, u32[]{:S(2)}, u32[]{:S(2)}) %collective-permute-start.8) | collective-permute-done | bytes 49184 | tf_op jit(solution)/shard_map/ppermute | solution.py:240
  81.6 0.1 fusion.34
  81.7 0.1 fusion.33
  81.7 0.1 fusion.30
  81.8 0.1 fusion.29
  81.9 0.1 slice_multiply_fusion.1
  82.1 0.1 fusion.36
  82.2 0.1 fusion.31
  82.3 0.1 fusion.32
  82.4 0.1 fusion.13
  82.5 0.6 copy.40
  (80 shorter events, 0.8 us)
Async XLA Ops:
  0.6 9.9 %copy-start.3 = (f32[4,4,256]{2,1,0:T(4,128)S(1)}, f32[4,4,256]{2,1,0:T(4,128)}, u32[]{:S(2)}) copy-start(f32[4,4,256]{2,1,0:T(4,128)} %param.5) | copy-start | bytes 49156
  2.4 8.2 %copy-start = (f32[19,8,32,128]{3,2,1,0:T(8,128)S(1)}, f32[19,8,32,128]{3,2,1,0:T(8,128)}, u32[]{:S(2)}) copy-start(f32[19,8,32,128]{3,2,1,0:T(8,128)} %refs_0_.1) | copy-start | bytes 7471108
  4.0 14.5 %collective-permute-start.4 = (f32[21,4,4,128]{3,2,1,0:T(4,128)S(1)}, f32[21,4,4,128]{3,2,1,0:T(4,128)S(1)}, u32[]{:S(2)}, u32[]{:S(2)}) collective-permute-start(f32[21,4,4,128]{3,2,1,0:T(4,128)S(1)} %pad_maximum_fusion.7), channel_id=1, source_target_pairs={{0,17},{1,18},{2,19},{3,20},{4,21},{5,22},{6,23},{7,24},{8,25},{9,... | collective-permute-start | bytes 516104 | tf_op jit(solution)/shard_map/ppermute | solution.py:247
  5.3 17.9 %collective-permute-start.5 = (f32[21,4,4,128]{3,2,1,0:T(4,128)S(1)}, f32[21,4,4,128]{3,2,1,0:T(4,128)S(1)}, u32[]{:S(2)}, u32[]{:S(2)}) collective-permute-start(f32[21,4,4,128]{3,2,1,0:T(4,128)S(1)} %pad_maximum_fusion.8), channel_id=1, source_target_pairs={{0,113},{1,114},{2,115},{3,116},{4,117},{5,118},{6,119},{7,120},{8... | collective-permute-start | bytes 516104 | tf_op jit(solution)/shard_map/ppermute | solution.py:247
  9.3 14.0 %collective-permute-start.6 = (f32[21,4,4,128]{3,2,1,0:T(4,128)S(1)}, f32[21,4,4,128]{3,2,1,0:T(4,128)S(1)}, u32[]{:S(2)}, u32[]{:S(2)}) collective-permute-start(f32[21,4,4,128]{3,2,1,0:T(4,128)S(1)} %pad_maximum_fusion.9), channel_id=1, source_target_pairs={{0,31},{1,16},{2,17},{3,18},{4,19},{5,20},{6,21},{7,22},{8,23},{9,... | collective-permute-start | bytes 516104 | tf_op jit(solution)/shard_map/ppermute | solution.py:247
  12.0 24.4 %collective-permute-start = (f32[21,4,32,128]{3,2,1,0:T(8,128)}, f32[21,4,32,128]{3,2,1,0:T(8,128)}, u32[]{:S(2)}, u32[]{:S(2)}) collective-permute-start(f32[21,4,32,128]{3,2,1,0:T(8,128)} %pad_maximum_fusion), channel_id=1, source_target_pairs={{0,16},{16,32},{32,48},{48,64},{64,80},{80,96},{96,112},{112,0},{1... | collective-permute-start | bytes 4128776 | tf_op jit(solution)/shard_map/ppermute | solution.py:240
  15.7 20.6 %collective-permute-start.1 = (f32[21,4,32,128]{3,2,1,0:T(8,128)}, f32[21,4,32,128]{3,2,1,0:T(8,128)}, u32[]{:S(2)}, u32[]{:S(2)}) collective-permute-start(f32[21,4,32,128]{3,2,1,0:T(8,128)} %pad_maximum_fusion.1), channel_id=1, source_target_pairs={{0,112},{16,0},{32,16},{48,32},{64,48},{80,64},{96,80},{112,96},{1... | collective-permute-start | bytes 4128776 | tf_op jit(solution)/shard_map/ppermute | solution.py:240
  18.6 17.8 %copy-start.4 = (f32[21,4,4,128]{3,2,1,0:T(4,128)}, f32[21,4,4,128]{3,2,1,0:T(4,128)S(1)}, u32[]{:S(2)}) copy-start(f32[21,4,4,128]{3,2,1,0:T(4,128)S(1)} %collective-permute-done.4.refs_6_) | copy-start | bytes 516100
  18.6 17.6 %collective-permute-start.7 = (f32[21,4,4,128]{3,2,1,0:T(4,128)S(1)}, f32[21,4,4,128]{3,2,1,0:T(4,128)S(1)}, u32[]{:S(2)}, u32[]{:S(2)}) collective-permute-start(f32[21,4,4,128]{3,2,1,0:T(4,128)S(1)} %pad_maximum_fusion.10), channel_id=1, source_target_pairs={{0,127},{1,112},{2,113},{3,114},{4,115},{5,116},{6,117},{7,118},{8... | collective-permute-start | bytes 516104 | tf_op jit(solution)/shard_map/ppermute | solution.py:247
  23.2 13.2 %copy-start.5 = (f32[21,4,4,128]{3,2,1,0:T(4,128)}, f32[21,4,4,128]{3,2,1,0:T(4,128)S(1)}, u32[]{:S(2)}) copy-start(f32[21,4,4,128]{3,2,1,0:T(4,128)S(1)} %collective-permute-done.5.refs_7_) | copy-start | bytes 516100
  23.2 13.0 %collective-permute-start.2 = (f32[21,8,4,128]{3,2,1,0:T(4,128)S(1)}, f32[21,8,4,128]{3,2,1,0:T(4,128)S(1)}, u32[]{:S(2)}, u32[]{:S(2)}) collective-permute-start(f32[21,8,4,128]{3,2,1,0:T(4,128)S(1)} %pad_maximum_fusion.5), channel_id=1, source_target_pairs={{0,1},{1,2},{2,3},{3,4},{4,5},{5,6},{6,7},{7,8},{8,9},{9,10},{10,1... | collective-permute-start | bytes 1032200 | tf_op jit(solution)/shard_map/ppermute | solution.py:242
  23.3 13.1 %copy-start.6 = (f32[21,4,4,128]{3,2,1,0:T(4,128)}, f32[21,4,4,128]{3,2,1,0:T(4,128)S(1)}, u32[]{:S(2)}) copy-start(f32[21,4,4,128]{3,2,1,0:T(4,128)S(1)} %collective-permute-done.6.refs_8_) | copy-start | bytes 516100
  23.3 12.9 %collective-permute-start.3 = (f32[21,8,4,128]{3,2,1,0:T(4,128)S(1)}, f32[21,8,4,128]{3,2,1,0:T(4,128)S(1)}, u32[]{:S(2)}, u32[]{:S(2)}) collective-permute-start(f32[21,8,4,128]{3,2,1,0:T(4,128)S(1)} %pad_maximum_fusion.6), channel_id=1, source_target_pairs={{0,15},{1,0},{2,1},{3,2},{4,3},{5,4},{6,5},{7,6},{8,7},{9,8},{10,9... | collective-permute-start | bytes 1032200 | tf_op jit(solution)/shard_map/ppermute | solution.py:242
  36.2 0.7 copy-start.7
  36.2 0.8 copy-start.1
  36.3 0.8 %copy-start.2 = (f32[21,8,4,128]{3,2,1,0:T(4,128)}, f32[21,8,4,128]{3,2,1,0:T(4,128)S(1)}, u32[]{:S(2)}) copy-start(f32[21,8,4,128]{3,2,1,0:T(4,128)S(1)} %collective-permute-done.3.refs_5_) | copy-start | bytes 1032196
  60.3 13.9 %all-to-all-start = ((f32[16,1,1536]{2,1,0:T(1,128)}), f32[16,1,1536]{2,1,0:T(1,128)S(1)}, u32[]{:S(2)}, u32[]{:S(2)}) async-start(f32[16,1,1536]{2,1,0:T(1,128)} %reshape.119), calls=%async_computation | async-start | bytes 196608 | tf_op jit(solution)/shard_map/all_to_all | solution.py:302
  76.7 4.7 %collective-permute-start.8 = (f32[3,2,8,256]{3,2,1,0:T(8,128)S(1)}, f32[3,2,8,256]{3,2,1,0:T(8,128)S(1)}, u32[]{:S(2)}, u32[]{:S(2)}) collective-permute-start(f32[3,2,8,256]{3,2,1,0:T(8,128)S(1)} %get-tuple-element.35), channel_id=1, source_target_pairs={{0,16},{16,32},{32,48},{48,64},{64,80},{80,96},{96,112},{112,0},{1... | collective-permute-start | bytes 147464 | tf_op jit(solution)/shard_map/ppermute | solution.py:240
  76.8 4.7 %collective-permute-start.9 = (f32[3,2,8,256]{3,2,1,0:T(8,128)S(1)}, f32[3,2,8,256]{3,2,1,0:T(8,128)S(1)}, u32[]{:S(2)}, u32[]{:S(2)}) collective-permute-start(f32[3,2,8,256]{3,2,1,0:T(8,128)S(1)} %get-tuple-element.36), channel_id=1, source_target_pairs={{0,112},{16,0},{32,16},{48,32},{64,48},{80,64},{96,80},{112,96},{1... | collective-permute-start | bytes 147464 | tf_op jit(solution)/shard_map/ppermute | solution.py:240

commit v4 on v3

--- a/solution.py
+++ b/solution.py
@@ -112,8 +112,8 @@
 
 
 def lb_kernel(halo, nx, ny, *refs):
-    g0, mask_ref, xlo, xhi, ylo, yhi, c_mm, c_mp, c_pm, c_pp = refs[:10]
-    out_ref, coarse_ref, abuf, bbuf, flow_s = refs[10:]
+    g0, mask_ref, pw_ref, py_ref, xlo, xhi, ylo, yhi, c_mm, c_mp, c_pm, c_pp = refs[:12]
+    out_ref, coarse_ref, abuf, bbuf, flow_s = refs[12:]
     h = halo
     top = YOFF
     abuf[0:NPOP, h : h + nx, top : top + ny, :] = g0[...]
@@ -184,36 +184,40 @@
 
     lax.fori_loop(0, nx, last_body, 0)
 
-    nz = flow_s.shape[3]
-    pz = (
-        lax.broadcasted_iota(jnp.int32, (nz // 2, nz), 1) // 2 == lax.broadcasted_iota(jnp.int32, (nz // 2, nz), 0)
-    ).astype(jnp.float32)
-    py = (
-        lax.broadcasted_iota(jnp.int32, (ny, ny // 2), 0) // 2 == lax.broadcasted_iota(jnp.int32, (ny, ny // 2), 1)
-    ).astype(jnp.float32)
+    nwin, win = coarse_ref.shape[0], coarse_ref.shape[3]
+    pw = pw_ref[...]
+    py = py_ref[...]
     for d in range(3):
         for xp in range(nx // 2):
             plane = flow_s[d, 2 * xp] + flow_s[d, 2 * xp + 1]
             zy = lax.dot_general(
-                pz,
+                pw,
                 plane,
                 (((1,), (1,)), ((), ())),
                 precision=lax.Precision.HIGHEST,
                 preferred_element_type=jnp.float32,
             )
             zc = jnp.dot(zy, py, precision=lax.Precision.HIGHEST, preferred_element_type=jnp.float32)
-            coarse_ref[d, xp] = zc * jnp.float32(0.125)
-
-
-def lb_call(g0, mask, halos, halo):
+            zc = zc * jnp.float32(0.125)
+            for j in range(nwin):
+                coarse_ref[j, d, xp] = zc[j * win : (j + 1) * win]
+
+
+def lb_call(g0, mask, halos, halo, nwin, w):
     _, nx, ny, nz = g0.shape
+    zb = nz // 2 // nwin
+    win = zb + 2 * w
+    rows = np.arange(nwin * win)
+    coarse_z = (rows // win * zb - w + rows % win) % (nz // 2)
+    pw = jnp.asarray((np.arange(nz)[None, :] // 2 == coarse_z[:, None]).astype(np.float32))
+    py = jnp.asarray((np.arange(ny)[:, None] // 2 == np.arange(ny // 2)[None, :]).astype(np.float32))
     f32 = jnp.float32
     vmem = pl.BlockSpec(memory_space=pltpu.VMEM)
     rows = YOFF + ny + 2 * halo
     rows = -(-rows // ROWS) * ROWS
     out_shape = (
         jax.ShapeDtypeStruct(g0.shape, f32),
-        jax.ShapeDtypeStruct((3, nx // 2, nz // 2, ny // 2), f32),
+        jax.ShapeDtypeStruct((nwin, 3, nx // 2, win, ny // 2), f32),
     )
     scratch = [
         pltpu.VMEM((NPOP + 1, nx + 2 * halo, rows, nz), f32),
@@ -225,12 +229,12 @@
     return pl.pallas_call(
         functools.partial(lb_kernel, halo, nx, ny),
         out_shape=out_shape,
-        in_specs=[vmem] * (2 + len(halos)),
+        in_specs=[vmem] * (4 + len(halos)),
         out_specs=(vmem, vmem),
         scratch_shapes=scratch,
         cost_estimate=cost,
         compiler_params=pltpu.CompilerParams(vmem_limit_bytes=60 * 1024 * 1024),
-    )(g0, mask, *halos)
+    )(g0, mask, pw, py, *halos)
 
 
 def send(x, dv, db):
@@ -291,19 +295,12 @@
 def local(populations, voxel_mask, tracer):
     w = TRACER_STEPS
     halos, tp = lattice_halos(populations, voxel_mask, tracer, STEPS, w)
-    state, coarse = lb_call(populations, voxel_mask, halos, STEPS)
-    nzt = coarse.shape[2]
     nb = lax.axis_size("blk")
-    zb = nzt // nb
-    ring = jnp.concatenate([coarse[:, :, nzt - w :], coarse, coarse[:, :, :zb]], axis=2)
-    head = ring[:, :, : nb * zb].reshape(3, coarse.shape[1], nb, zb, coarse.shape[3])
-    tail = ring[:, :, zb : zb + nb * zb].reshape(3, coarse.shape[1], nb, zb, coarse.shape[3])
-    windows = jnp.concatenate([head, tail], axis=3)[:, :, :, : zb + 2 * w]
-    moved = lax.all_to_all(windows, "blk", split_axis=2, concat_axis=4, tiled=True)
-    flow = moved[:, :, 0]
-    nxb = flow.shape[1]
-    flow = jnp.concatenate([send(flow[:, nxb - w :], 1, 0), flow, send(flow[:, :w], -1, 0)], axis=1)
-    flow = jnp.transpose(flow, (0, 2, 1, 3))
+    state, windows = lb_call(populations, voxel_mask, halos, STEPS, nb, w)
+    moved = lax.all_to_all(windows, "blk", split_axis=0, concat_axis=0, tiled=True)
+    _, _, nxb, nzw, nys = moved.shape
+    flow = jnp.transpose(moved, (1, 3, 2, 0, 4)).reshape(3, nzw, nxb, nb * nys)
+    flow = jnp.concatenate([send(flow[:, :, nxb - w :], 1, 0), flow, send(flow[:, :, :w], -1, 0)], axis=2)
     xlo, xhi, zlo, zhi, c_mm, c_mp, c_pm, c_pp = tp
     conc = jnp.concatenate(
         [

time: 84.3 us -> 84.6 us (level)
  local copies, waits for them, and re-layouts: 11 us -> 13.6 us
  starting transfers between devices: 30.3 us -> 27.9 us
  Pallas kernels: 18.2 us -> 19.1 us
    ppermute x4, waiting for transfers between devices: 7.47 us -> 0.01 us  [send(): return lax.ppermute(x, ('vessel', 'blk'), pairs)]
    ppermute x2, waiting for transfers between devices: 0.01 us -> 4.21 us  [send(): return lax.ppermute(x, 'blk', [(i, (i + db) % nb) for i in range(nb)])]
    ppermute x4, waiting for transfers between devices: 1.77 us -> 4.74 us  [send(): return lax.ppermute(x, 'vessel', [(i, (i + dv) % nv) for i in range(nv)])]
    slice x12, local copies, waits for them, and re-layouts: 1.8 us -> 4.47 us  [lattice_halos(): tracer_pieces.append(got[NPOP + 1].reshape(-1)[:tp.size].reshape(tp.shape))]
    ppermute x4, starting transfers between devices: 8.03 us -> 5.92 us  [send(): return lax.ppermute(x, 'vessel', [(i, (i + dv) % nv) for i in range(nv)])]
    all_to_all x1, starting transfers between devices: 6.12 us -> 4.24 us  [local(): lax.all_to_all(windows, 'blk', split_axis=0, concat_axis=0, tiled=True)]
    slice x3 -> x1, local copies, waits for them, and re-layouts: 1.61 us -> 0.01 us  [local(): flow[:, :, :w]]
    ppermute x4, starting transfers between devices: 10.7 us -> 12.3 us  [send(): return lax.ppermute(x, ('vessel', 'blk'), pairs)]
  transfers between devices with their start and end apart: 11 -> 11, of which waited for: 3 -> 4; matrix products, arithmetic and copies ran while one was open for 5% -> 11% of each run, Pallas kernels for 0% -> 0%
where the time goes in v4:
time: 84.6 us; the launch traced here: 83.4 us
  starting transfers between devices  27.9 us (33%)
  Pallas kernels  19.1 us (23%)
  waiting for transfers between devices  15.9 us (19%)
  local copies, waits for them, and re-layouts  13.6 us (16%)
  other arithmetic  5.88 us (7%)
  between operations  1.01 us (1%)
    pallas_call x1, Pallas kernels, lb_call(): pl.pallas_call(functools.partial(lb_kernel, halo, nx, ny), out_shape=out_...  19.1 us
    ppermute x4, starting transfers between devices, send(): return lax.ppermute(x, ('vessel', 'blk'), pairs)  12.3 us
    all_to_all x1, waiting for transfers between devices, local(): lax.all_to_all(windows, 'blk', split_axis=0, concat_axis=0, tiled=True)  6.89 us
    ppermute x4, starting transfers between devices, send(): return lax.ppermute(x, 'vessel', [(i, (i + dv) % nv) for i in range(nv)])  5.92 us
    ppermute x2, starting transfers between devices, send(): return lax.ppermute(x, 'blk', [(i, (i + db) % nb) for i in range(nb)])  5.48 us
    unnamed x36, local copies, waits for them, and re-layouts  4.94 us
    ppermute x4, waiting for transfers between devices, send(): return lax.ppermute(x, 'vessel', [(i, (i + dv) % nv) for i in range(nv)])  4.74 us
    slice x12, local copies, waits for them, and re-layouts, lattice_halos(): tracer_pieces.append(got[NPOP + 1].reshape(-1)[:tp.size].reshape(tp.shape))  4.47 us
  transfers between devices with their start and end apart: 11, of which 4 were waited for; matrix products, arithmetic and copies ran while one was open for 11% of the time, Pallas kernels for 0%

profile of v4, /device:TPU:0, one launch (start us, length us, event | category | flops | bytes accessed | tf_op | source)
XLA Modules:
  0.0 83.4 jit_solution(1526238052944531035)
XLA Ops:
  0.6 0.8 slice_bitcast_fusion.7
  1.4 0.9 %convert_bitcast_fusion = f32[1,8,32,128]{3,2,1,0:T(8,128)S(1)} fusion(s32[8,32,128]{2,1,0:T(8,128)} %refs_1_.1), kind=kLoop, calls=%fused_computation.8 | loop fusion | flops 32768 | bytes 262144 | tf_op jit(solution)/shard_map/broadcast_in_dim | solution.py:257
  2.4 1.6 %fusion.22 = (f32[19,4,4,128]{3,2,1,0:T(4,128)S(1)}, f32[19,4,4,128]{3,2,1,0:T(4,128)S(1)}, f32[19,4,4,128]{3,2,1,0:T(4,128)S(1)}, f32[19,4,4,128]{3,2,1,0:T(4,128)S(1)}) fusion(f32[19,8,32,128]{3,2,1,0:T(8,128)} %refs_0_.1), kind=kLoop, calls=%fused_computation.71 | loop fusion | bytes 1245184 | tf_op jit(solution)/shard_map/slice | solution.py:266
  4.0 1.2 %collective-permute-start.4 = (f32[21,4,4,128]{3,2,1,0:T(4,128)S(1)}, f32[21,4,4,128]{3,2,1,0:T(4,128)S(1)}, u32[]{:S(2)}, u32[]{:S(2)}) collective-permute-start(f32[21,4,4,128]{3,2,1,0:T(4,128)S(1)} %pad_maximum_fusion.4), channel_id=1, source_target_pairs={{0,17},{1,18},{2,19},{3,20},{4,21},{5,22},{6,23},{7,24},{8,25},{9,... | collective-permute-start | bytes 516104 | tf_op jit(solution)/shard_map/ppermute | solution.py:251
  5.2 4.0 %collective-permute-start.5 = (f32[21,4,4,128]{3,2,1,0:T(4,128)S(1)}, f32[21,4,4,128]{3,2,1,0:T(4,128)S(1)}, u32[]{:S(2)}, u32[]{:S(2)}) collective-permute-start(f32[21,4,4,128]{3,2,1,0:T(4,128)S(1)} %pad_maximum_fusion.5), channel_id=1, source_target_pairs={{0,113},{1,114},{2,115},{3,116},{4,117},{5,118},{6,119},{7,120},{8... | collective-permute-start | bytes 516104 | tf_op jit(solution)/shard_map/ppermute | solution.py:251
  9.3 1.2 %collective-permute-start.6 = (f32[21,4,4,128]{3,2,1,0:T(4,128)S(1)}, f32[21,4,4,128]{3,2,1,0:T(4,128)}, u32[]{:S(2)}, u32[]{:S(2)}) collective-permute-start(f32[21,4,4,128]{3,2,1,0:T(4,128)S(1)} %pad_maximum_fusion.6), channel_id=1, source_target_pairs={{0,31},{1,16},{2,17},{3,18},{4,19},{5,20},{6,21},{7,22},{8,23},{9,... | collective-permute-start | bytes 516104 | tf_op jit(solution)/shard_map/ppermute | solution.py:251
  10.5 0.7 pad_maximum_fusion.7
  11.2 5.9 %collective-permute-start.7 = (f32[21,4,4,128]{3,2,1,0:T(4,128)}, f32[21,4,4,128]{3,2,1,0:T(4,128)}, u32[]{:S(2)}, u32[]{:S(2)}) collective-permute-start(f32[21,4,4,128]{3,2,1,0:T(4,128)} %pad_maximum_fusion.7), channel_id=1, source_target_pairs={{0,127},{1,112},{2,113},{3,114},{4,115},{5,116},{6,117},{7,118},{8... | collective-permute-start | bytes 516104 | tf_op jit(solution)/shard_map/ppermute | solution.py:251
  17.2 0.4 fusion.24
  17.6 1.2 %pad_maximum_fusion = f32[21,4,32,128]{3,2,1,0:T(8,128)} fusion(f32[1,4,32,128]{3,2,1,0:T(8,128)S(1)} %bitcast.55, f32[1,4,32,128]{3,2,1,0:T(8,128)S(1)} %get-tuple-element.30, f32[19,4,32,128]{3,2,1,0:T(8,128)S(1)} %get-tuple-element.17), kind=kLoop, calls=%fused_computation | loop fusion | flops 688128 | bytes 2752512 | tf_op jit(solution)/shard_map/concatenate | solution.py:270
  18.8 0.2 fusion.23
  19.0 0.1 pad_maximum_fusion.1
  19.1 0.9 %pad_maximum_fusion.3 = f32[21,8,4,128]{3,2,1,0:T(4,128)} fusion(f32[1,8,4,128]{3,2,1,0:T(4,128)S(1)} %bitcast.57, f32[1,8,4,128]{3,2,1,0:T(4,128)S(1)} %get-tuple-element.27, f32[19,8,4,128]{3,2,1,0:T(4,128)S(1)} %get-tuple-element.14), kind=kLoop, calls=%fused_computation.3 | loop fusion | flops 172032 | bytes 688128 | tf_op jit(solution)/shard_map/concatenate | solution.py:270
  20.0 3.0 %collective-permute-start.1 = (f32[21,4,32,128]{3,2,1,0:T(8,128)S(1)}, f32[21,4,32,128]{3,2,1,0:T(8,128)S(1)}, u32[]{:S(2)}, u32[]{:S(2)}) collective-permute-start(f32[21,4,32,128]{3,2,1,0:T(8,128)S(1)} %pad_maximum_fusion.1), channel_id=1, source_target_pairs={{0,112},{16,0},{32,16},{48,32},{64,48},{80,64},{96,80},{112,96},{1... | collective-permute-start | bytes 4128776 | tf_op jit(solution)/shard_map/ppermute | solution.py:244
  23.0 0.8 pad_maximum_fusion.2
  23.8 0.7 collective-permute-start.2
  24.5 4.8 %collective-permute-start.3 = (f32[21,8,4,128]{3,2,1,0:T(4,128)}, f32[21,8,4,128]{3,2,1,0:T(4,128)S(1)}, u32[]{:S(2)}, u32[]{:S(2)}) collective-permute-start(f32[21,8,4,128]{3,2,1,0:T(4,128)} %pad_maximum_fusion.3), channel_id=1, source_target_pairs={{0,15},{1,0},{2,1},{3,2},{4,3},{5,4},{6,5},{7,6},{8,7},{9,8},{10,9... | collective-permute-start | bytes 1032200 | tf_op jit(solution)/shard_map/ppermute | solution.py:246
  29.3 0.7 slice.371
  30.0 0.7 slice.373
  30.7 4.2 %collective-permute-done.2.refs_6_ = f32[21,8,4,128]{3,2,1,0:T(4,128)S(1)} collective-permute-done((f32[21,8,4,128]{3,2,1,0:T(4,128)}, f32[21,8,4,128]{3,2,1,0:T(4,128)S(1)}, u32[]{:S(2)}, u32[]{:S(2)}) %collective-permute-start.2) | collective-permute-done | bytes 344096 | tf_op jit(solution)/shard_map/ppermute | solution.py:246
  35.1 3.0 %collective-permute-done.refs_4_ = f32[21,4,32,128]{3,2,1,0:T(8,128)} collective-permute-done((f32[21,4,32,128]{3,2,1,0:T(8,128)}, f32[21,4,32,128]{3,2,1,0:T(8,128)}, u32[]{:S(2)}, u32[]{:S(2)}) %collective-permute-start) | collective-permute-done | bytes 1376288 | tf_op jit(solution)/shard_map/ppermute | solution.py:244
  38.0 0.8 %slice.367 = f32[1,4,32,128]{3,2,1,0:T(8,128)S(1)} slice(f32[21,4,32,128]{3,2,1,0:T(8,128)} %collective-permute-done.refs_4_), slice={[20:21], [0:4], [0:32], [0:128]} | slice | bytes 131072 | tf_op jit(solution)/shard_map/slice | solution.py:273
  38.9 0.7 slice.305
  39.5 0.7 slice.368
  40.3 1.1 %copy-done.1 = f32[21,4,32,128]{3,2,1,0:T(8,128)} copy-done((f32[21,4,32,128]{3,2,1,0:T(8,128)}, f32[21,4,32,128]{3,2,1,0:T(8,128)S(1)}, u32[]{:S(2)}) %copy-start.1) | copy-done | bytes 1376280
  41.3 19.1 %shard_map.68 = (f32[19,8,32,128]{3,2,1,0:T(8,128)}, f32[16,3,4,8,16]{4,3,2,1,0:T(8,128)}) custom-call(f32[19,8,32,128]{3,2,1,0:T(8,128)} %refs_0_.1, s32[8,32,128]{2,1,0:T(8,128)} %refs_1_.1, f32[128,128]{1,0:T(8,128)} %constant.10.clone.refs_2_, f32[32,16]{1,0:T(8,128)} %constant.5.clone.refs_3_, f32[21,4,32,128]{3,2,1,0:T(8,128)} %collective-permute-done.refs_4_, ...), custom_call_target="tpu_custom_call" | custom-call | flops 78643200 | bytes 9961472 | tf_op jit(solution)/shard_map/pallas_call | solution.py:229
  60.5 2.1 %reshape.114 = f32[16,1,1536]{2,1,0:T(1,128)} reshape(f32[16,3,4,8,16]{4,3,2,1,0:T(8,128)} %get-tuple-element.5) | data formatting | bytes 196608
  62.5 4.2 %all-to-all-start = ((f32[16,1,1536]{2,1,0:T(1,128)}), f32[16,1,1536]{2,1,0:T(1,128)S(1)}, u32[]{:S(2)}, u32[]{:S(2)}) async-start(f32[16,1,1536]{2,1,0:T(1,128)} %reshape.114), calls=%async_computation | async-start | bytes 196608 | tf_op jit(solution)/shard_map/all_to_all | solution.py:300
  66.8 0.8 %slice.369 = f32[1,4,32,128]{3,2,1,0:T(8,128)S(1)} slice(f32[21,4,32,128]{3,2,1,0:T(8,128)} %copy-done.1), slice={[20:21], [0:4], [0:32], [0:128]} | slice | bytes 131072 | tf_op jit(solution)/shard_map/slice | solution.py:273
  67.7 6.9 %all-to-all-done = f32[16,1,1536]{2,1,0:T(1,128)S(1)} async-done(((f32[16,1,1536]{2,1,0:T(1,128)}), f32[16,1,1536]{2,1,0:T(1,128)S(1)}, u32[]{:S(2)}, u32[]{:S(2)}) %all-to-all-start) | async-done | bytes 98336 | tf_op jit(solution)/shard_map/all_to_all | solution.py:300
  74.6 0.5 broadcast.20
  75.1 0.9 %reduce = f32[16,1536]{1,0:T(8,128)S(1)} reduce(f32[16,1,1536]{2,1,0:T(1,128)S(1)} %all-to-all-done, f32[]{:T(128)} %broadcast.20), dimensions={1}, to_apply=%all_to_all.3.reduce_sub_computation | reduce | bytes 196612 | tf_op jit(solution)/shard_map/all_to_all | solution.py:300
  76.0 0.3 reshape.115
  76.3 0.5 copy.16
  76.7 0.3 reshape.113
  77.1 2.9 %collective-permute-start.9 = (f32[3,8,2,256]{3,1,2,0:T(8,128)S(1)}, f32[3,8,2,256]{3,1,2,0:T(8,128)S(1)}, u32[]{:S(2)}, u32[]{:S(2)}) collective-permute-start(f32[3,8,2,256]{3,1,2,0:T(8,128)S(1)} %get-tuple-element.31), channel_id=1, source_target_pairs={{0,112},{16,0},{32,16},{48,32},{64,48},{80,64},{96,80},{112,96},{1... | collective-permute-start | bytes 147464 | tf_op jit(solution)/shard_map/ppermute | solution.py:244
  80.1 1.8 %collective-permute-done.8 = f32[3,8,2,256]{3,1,2,0:T(8,128)S(1)} collective-permute-done((f32[3,8,2,256]{3,1,2,0:T(8,128)S(1)}, f32[3,8,2,256]{3,1,2,0:T(8,128)S(1)}, u32[]{:S(2)}, u32[]{:S(2)}) %collective-permute-start.8) | collective-permute-done | bytes 49184 | tf_op jit(solution)/shard_map/ppermute | solution.py:244
  81.9 0.1 fusion.34
  82.0 0.1 fusion.33
  82.1 0.1 fusion.30
  82.2 0.1 fusion.29
  82.3 0.1 slice_multiply_fusion.1
  82.4 0.1 fusion.35
  82.5 0.1 fusion.36
  82.6 0.1 fusion.31
  82.6 0.1 fusion.32
  82.7 0.1 fusion.13
  82.8 0.6 copy.17
  (75 shorter events, 0.6 us)
Async XLA Ops:
  2.4 14.8 %copy-start.4 = (f32[4,4,256]{2,1,0:T(4,128)S(1)}, f32[4,4,256]{2,1,0:T(4,128)}, u32[]{:S(2)}) copy-start(f32[4,4,256]{2,1,0:T(4,128)} %param.7) | copy-start | bytes 49156
  2.4 14.8 %copy-start = (f32[19,8,32,128]{3,2,1,0:T(8,128)S(1)}, f32[19,8,32,128]{3,2,1,0:T(8,128)}, u32[]{:S(2)}) copy-start(f32[19,8,32,128]{3,2,1,0:T(8,128)} %refs_0_.1) | copy-start | bytes 7471108
  4.0 16.0 %collective-permute-start.4 = (f32[21,4,4,128]{3,2,1,0:T(4,128)S(1)}, f32[21,4,4,128]{3,2,1,0:T(4,128)S(1)}, u32[]{:S(2)}, u32[]{:S(2)}) collective-permute-start(f32[21,4,4,128]{3,2,1,0:T(4,128)S(1)} %pad_maximum_fusion.4), channel_id=1, source_target_pairs={{0,17},{1,18},{2,19},{3,20},{4,21},{5,22},{6,23},{7,24},{8,25},{9,... | collective-permute-start | bytes 516104 | tf_op jit(solution)/shard_map/ppermute | solution.py:251
  5.2 18.6 %collective-permute-start.5 = (f32[21,4,4,128]{3,2,1,0:T(4,128)S(1)}, f32[21,4,4,128]{3,2,1,0:T(4,128)S(1)}, u32[]{:S(2)}, u32[]{:S(2)}) collective-permute-start(f32[21,4,4,128]{3,2,1,0:T(4,128)S(1)} %pad_maximum_fusion.5), channel_id=1, source_target_pairs={{0,113},{1,114},{2,115},{3,116},{4,117},{5,118},{6,119},{7,120},{8... | collective-permute-start | bytes 516104 | tf_op jit(solution)/shard_map/ppermute | solution.py:251
  9.3 15.2 %collective-permute-start.6 = (f32[21,4,4,128]{3,2,1,0:T(4,128)S(1)}, f32[21,4,4,128]{3,2,1,0:T(4,128)}, u32[]{:S(2)}, u32[]{:S(2)}) collective-permute-start(f32[21,4,4,128]{3,2,1,0:T(4,128)S(1)} %pad_maximum_fusion.6), channel_id=1, source_target_pairs={{0,31},{1,16},{2,17},{3,18},{4,19},{5,20},{6,21},{7,22},{8,23},{9,... | collective-permute-start | bytes 516104 | tf_op jit(solution)/shard_map/ppermute | solution.py:251
  11.2 18.8 %collective-permute-start.7 = (f32[21,4,4,128]{3,2,1,0:T(4,128)}, f32[21,4,4,128]{3,2,1,0:T(4,128)}, u32[]{:S(2)}, u32[]{:S(2)}) collective-permute-start(f32[21,4,4,128]{3,2,1,0:T(4,128)} %pad_maximum_fusion.7), channel_id=1, source_target_pairs={{0,127},{1,112},{2,113},{3,114},{4,115},{5,116},{6,117},{7,118},{8... | collective-permute-start | bytes 516104 | tf_op jit(solution)/shard_map/ppermute | solution.py:251
  18.8 19.3 %collective-permute-start = (f32[21,4,32,128]{3,2,1,0:T(8,128)}, f32[21,4,32,128]{3,2,1,0:T(8,128)}, u32[]{:S(2)}, u32[]{:S(2)}) collective-permute-start(f32[21,4,32,128]{3,2,1,0:T(8,128)} %pad_maximum_fusion), channel_id=1, source_target_pairs={{0,16},{16,32},{32,48},{48,64},{64,80},{80,96},{96,112},{112,0},{1... | collective-permute-start | bytes 4128776 | tf_op jit(solution)/shard_map/ppermute | solution.py:244
  20.0 3.8 %copy-start.5 = (f32[21,4,4,128]{3,2,1,0:T(4,128)}, f32[21,4,4,128]{3,2,1,0:T(4,128)S(1)}, u32[]{:S(2)}) copy-start(f32[21,4,4,128]{3,2,1,0:T(4,128)S(1)} %collective-permute-done.4.refs_8_) | copy-start | bytes 516100
  20.0 20.3 %collective-permute-start.1 = (f32[21,4,32,128]{3,2,1,0:T(8,128)S(1)}, f32[21,4,32,128]{3,2,1,0:T(8,128)S(1)}, u32[]{:S(2)}, u32[]{:S(2)}) collective-permute-start(f32[21,4,32,128]{3,2,1,0:T(8,128)S(1)} %pad_maximum_fusion.1), channel_id=1, source_target_pairs={{0,112},{16,0},{32,16},{48,32},{64,48},{80,64},{96,80},{112,96},{1... | collective-permute-start | bytes 4128776 | tf_op jit(solution)/shard_map/ppermute | solution.py:244
  23.8 0.7 copy-start.6
  23.8 11.1 %collective-permute-start.2 = (f32[21,8,4,128]{3,2,1,0:T(4,128)}, f32[21,8,4,128]{3,2,1,0:T(4,128)S(1)}, u32[]{:S(2)}, u32[]{:S(2)}) collective-permute-start(f32[21,8,4,128]{3,2,1,0:T(4,128)} %pad_maximum_fusion.2), channel_id=1, source_target_pairs={{0,1},{1,2},{2,3},{3,4},{4,5},{5,6},{6,7},{7,8},{8,9},{9,10},{10,1... | collective-permute-start | bytes 1032200 | tf_op jit(solution)/shard_map/ppermute | solution.py:246
  24.5 10.5 %collective-permute-start.3 = (f32[21,8,4,128]{3,2,1,0:T(4,128)}, f32[21,8,4,128]{3,2,1,0:T(4,128)S(1)}, u32[]{:S(2)}, u32[]{:S(2)}) collective-permute-start(f32[21,8,4,128]{3,2,1,0:T(4,128)} %pad_maximum_fusion.3), channel_id=1, source_target_pairs={{0,15},{1,0},{2,1},{3,2},{4,3},{5,4},{6,5},{7,6},{8,7},{9,8},{10,9... | collective-permute-start | bytes 1032200 | tf_op jit(solution)/shard_map/ppermute | solution.py:246
  34.9 5.3 %copy-start.2 = (f32[21,8,4,128]{3,2,1,0:T(4,128)}, f32[21,8,4,128]{3,2,1,0:T(4,128)S(1)}, u32[]{:S(2)}) copy-start(f32[21,8,4,128]{3,2,1,0:T(4,128)S(1)} %collective-permute-done.2.refs_6_) | copy-start | bytes 1032196
  35.0 5.3 %copy-start.3 = (f32[21,8,4,128]{3,2,1,0:T(4,128)}, f32[21,8,4,128]{3,2,1,0:T(4,128)S(1)}, u32[]{:S(2)}) copy-start(f32[21,8,4,128]{3,2,1,0:T(4,128)S(1)} %collective-permute-done.3.refs_7_) | copy-start | bytes 1032196
  40.3 1.1 %copy-start.1 = (f32[21,4,32,128]{3,2,1,0:T(8,128)}, f32[21,4,32,128]{3,2,1,0:T(8,128)S(1)}, u32[]{:S(2)}) copy-start(f32[21,4,32,128]{3,2,1,0:T(8,128)S(1)} %collective-permute-done.1.refs_5_) | copy-start | bytes 4128772
  62.5 12.1 %all-to-all-start = ((f32[16,1,1536]{2,1,0:T(1,128)}), f32[16,1,1536]{2,1,0:T(1,128)S(1)}, u32[]{:S(2)}, u32[]{:S(2)}) async-start(f32[16,1,1536]{2,1,0:T(1,128)} %reshape.114), calls=%async_computation | async-start | bytes 196608 | tf_op jit(solution)/shard_map/all_to_all | solution.py:300
  77.1 4.7 %collective-permute-start.8 = (f32[3,8,2,256]{3,1,2,0:T(8,128)S(1)}, f32[3,8,2,256]{3,1,2,0:T(8,128)S(1)}, u32[]{:S(2)}, u32[]{:S(2)}) collective-permute-start(f32[3,8,2,256]{3,1,2,0:T(8,128)S(1)} %get-tuple-element.32), channel_id=1, source_target_pairs={{0,16},{16,32},{32,48},{48,64},{64,80},{80,96},{96,112},{112,0},{1... | collective-permute-start | bytes 147464 | tf_op jit(solution)/shard_map/ppermute | solution.py:244
  77.1 4.7 %collective-permute-start.9 = (f32[3,8,2,256]{3,1,2,0:T(8,128)S(1)}, f32[3,8,2,256]{3,1,2,0:T(8,128)S(1)}, u32[]{:S(2)}, u32[]{:S(2)}) collective-permute-start(f32[3,8,2,256]{3,1,2,0:T(8,128)S(1)} %get-tuple-element.31), channel_id=1, source_target_pairs={{0,112},{16,0},{32,16},{48,32},{64,48},{80,64},{96,80},{112,96},{1... | collective-permute-start | bytes 147464 | tf_op jit(solution)/shard_map/ppermute | solution.py:244

commit v5 on v3

--- a/solution.py
+++ b/solution.py
@@ -128,28 +128,22 @@
     abuf[:, 0:h, top + ny : top + ny + h, :] = c_pm[0:planes]
     abuf[:, h + nx : 2 * h + nx, top + ny : top + ny + h, :] = c_pp[0:planes]
 
-    bufs = [bbuf, abuf]
+    bufs = [abuf, bbuf]
     offs = [top] + [h - s for s in range(1, h + 1)]
 
     def run_step(s):
-        src = abuf if s == 0 else bufs[(s - 1) % 2]
+        src = bufs[(s - 1) % 2]
         dst = bufs[s % 2]
-        if s == 0:
-            rows = list(range(0, top + ny + h, ROWS))
-        else:
-            rows = list(range(0, ny + 2 * (h - s), ROWS))
-        shift = offs[s - 1] - offs[s] if s > 0 else 0
+        rows = list(range(0, ny + 2 * (h - s), ROWS))
+        shift = offs[s - 1] - offs[s]
 
         def body(x, carry):
             for r in rows:
                 g = []
                 for i in range(NPOP):
-                    if s == 0:
-                        v = src[i, x, pl.ds(r, ROWS), :]
-                    else:
-                        v = src[i, x - CX[i], pl.ds(r + shift - CY[i], ROWS), :]
-                        if CZ[i] != 0:
-                            v = pltpu.roll(v, CZ[i] % v.shape[1], 1)
+                    v = src[i, x - CX[i], pl.ds(r + shift - CY[i], ROWS), :]
+                    if CZ[i] != 0:
+                        v = pltpu.roll(v, CZ[i] % v.shape[1], 1)
                     g.append(v)
                 mask = abuf[NPOP, x, pl.ds(r - offs[s] + top, ROWS), :]
                 post = collide_chunk(g, mask)
@@ -159,7 +153,7 @@
 
         lax.fori_loop(s, nx + 2 * h - s, body, 0)
 
-    for s in range(h):
+    for s in range(1, h):
         run_step(s)
 
     src = bufs[(h - 1) % 2]
@@ -247,27 +241,66 @@
     return lax.ppermute(x, ("vessel", "blk"), pairs)
 
 
+ORDER = ((1, 0), (-1, 0), (0, 1), (0, -1), (1, 1), (-1, 1), (1, -1), (-1, -1))
+
+
+def edge(n, h, d):
+    return {1: slice(n - h, n), -1: slice(0, h), 0: slice(0, n)}[d]
+
+
+def first_kernel(h, nx, ny, *refs):
+    g0, mask_ref = refs[:2]
+    tplanes = refs[2:10]
+    post_ref = refs[10]
+    msgs = refs[11:19]
+
+    def body(x, carry):
+        for r in range(0, ny, ROWS):
+            g = [g0[i, x, pl.ds(r, ROWS), :] for i in range(NPOP)]
+            post = collide_chunk(g, mask_ref[x, pl.ds(r, ROWS), :])
+            for i in range(NPOP):
+                post_ref[i, x, pl.ds(r, ROWS), :] = post[i]
+        return carry
+
+    lax.fori_loop(0, nx, body, 0)
+    for k, (dv, db) in enumerate(ORDER):
+        xs, ys = edge(nx, h, dv), edge(ny, h, db)
+        msgs[k][0:NPOP] = post_ref[:, xs, ys, :]
+        msgs[k][NPOP] = mask_ref[xs, ys, :].astype(jnp.float32)
+        msgs[k][NPOP + 1] = tplanes[k][...]
+
+
 def lattice_halos(g0, mask, conc, h, w):
     _, nx, ny, nz = g0.shape
-    nzc, nxc, nyc = conc.shape
-    maskf = mask.astype(jnp.float32)[None]
-    lat = {1: slice(nx - h, nx), -1: slice(0, h), 0: slice(0, nx)}
-    lat_y = {1: slice(ny - h, ny), -1: slice(0, h), 0: slice(0, ny)}
-    trc_x = {1: slice(nxc - w, nxc), -1: slice(0, w), 0: slice(0, nxc)}
-    trc_z = {1: slice(nzc - w, nzc), -1: slice(0, w), 0: slice(0, nzc)}
-    order = ((1, 0), (-1, 0), (0, 1), (0, -1), (1, 1), (-1, 1), (1, -1), (-1, -1))
+    nzc, nxc, _ = conc.shape
+    f32 = jnp.float32
+    tplanes, tshapes = [], []
+    for dv, db in ORDER:
+        a, b = (h if dv else nx), (h if db else ny)
+        tp = conc[edge(nzc, w, db), edge(nxc, w, dv)]
+        tshapes.append(tp.shape)
+        tplanes.append(jnp.pad(tp.reshape(-1), (0, a * b * nz - tp.size)).reshape(a, b, nz))
+    vmem = pl.BlockSpec(memory_space=pltpu.VMEM)
+    out_shape = (jax.ShapeDtypeStruct(g0.shape, f32),) + tuple(
+        jax.ShapeDtypeStruct((NPOP + 2,) + t.shape, f32) for t in tplanes
+    )
+    cells = nx * ny * nz
+    outs = pl.pallas_call(
+        functools.partial(first_kernel, h, nx, ny),
+        out_shape=out_shape,
+        in_specs=[vmem] * 10,
+        out_specs=tuple(vmem for _ in out_shape),
+        cost_estimate=pl.CostEstimate(flops=200 * cells, transcendentals=0, bytes_accessed=NPOP * 4 * cells * 3),
+        compiler_params=pltpu.CompilerParams(vmem_limit_bytes=48 * 1024 * 1024),
+    )(g0, mask, *tplanes)
+    post0, msgs = outs[0], outs[1:]
     pieces, tracer_pieces = [], []
-    for dv, db in order:
-        xs, ys = lat[dv], lat_y[db]
-        lb = jnp.concatenate([g0[:, xs, ys], maskf[:, xs, ys]], axis=0)
-        tp = conc[trc_z[db], trc_x[dv]]
-        plane = lb.shape[1] * lb.shape[2] * nz
-        flat = jnp.pad(tp.reshape(-1), (0, plane - tp.size))
-        msg = jnp.concatenate([lb, flat.reshape(1, lb.shape[1], lb.shape[2], nz)], axis=0)
+    for (dv, db), msg, shape in zip(ORDER, msgs, tshapes):
         got = send(msg, dv, db)
         pieces.append(got)
-        tracer_pieces.append(got[NPOP + 1].reshape(-1)[: tp.size].reshape(tp.shape))
-    return pieces, tracer_pieces
+        size = int(np.prod(shape))
+        tracer_pieces.append(got[NPOP + 1].reshape(-1)[:size].reshape(shape))
+    return post0, pieces, tracer_pieces
 
 
 def tracer_update(c, fx, fy, fz):
@@ -290,8 +323,8 @@
 
 def local(populations, voxel_mask, tracer):
     w = TRACER_STEPS
-    halos, tp = lattice_halos(populations, voxel_mask, tracer, STEPS, w)
-    state, coarse = lb_call(populations, voxel_mask, halos, STEPS)
+    post0, halos, tp = lattice_halos(populations, voxel_mask, tracer, STEPS, w)
+    state, coarse = lb_call(post0, voxel_mask, halos, STEPS)
     nzt = coarse.shape[2]
     nb = lax.axis_size("blk")
     zb = nzt // nb

time: 84.3 us -> 91.8 us (1.089)
  waiting for transfers between devices: 16.1 us -> 24.7 us
  other arithmetic: 6.24 us -> 2.6 us
  local copies, waits for them, and re-layouts: 11 us -> 14.1 us
  starting transfers between devices: 30.3 us -> 28.3 us
  Pallas kernels: 18.2 us -> 19.6 us
    ppermute x4, waiting for transfers between devices: 7.47 us -> 13.8 us  [send(): return lax.ppermute(x, ('vessel', 'blk'), pairs)]
    pallas_call x0 -> x1, Pallas kernels: none -> 4.81 us  [lattice_halos(): pl.pallas_call(functools.partial(first_kernel, h, nx, ny), out_shape=out_...]
    pallas_call x1, Pallas kernels: 18.2 us -> 14.8 us  [lb_call(): pl.pallas_call(functools.partial(lb_kernel, halo, nx, ny), out_shape=out_...]
    ppermute x2, waiting for transfers between devices: 0.01 us -> 3.16 us  [send(): return lax.ppermute(x, 'blk', [(i, (i + db) % nb) for i in range(nb)])]
    concatenate x8 -> x0, other arithmetic: 2.71 us -> none  [lattice_halos(): jnp.concatenate([lb, flat.reshape(1, lb.shape[1], lb.shape[2], nz)], axis=0)]
    ppermute x4, starting transfers between devices: 8.03 us -> 5.92 us  [send(): return lax.ppermute(x, 'vessel', [(i, (i + dv) % nv) for i in range(nv)])]
    all_to_all x1, starting transfers between devices: 6.12 us -> 7.82 us  [local(): lax.all_to_all(windows, 'blk', split_axis=2, concat_axis=4, tiled=True)]
    unnamed x36 -> x26, local copies, waits for them, and re-layouts: 3.45 us -> 5.12 us
  transfers between devices with their start and end apart: 11 -> 11, of which waited for: 3 -> 5; matrix products, arithmetic and copies ran while one was open for 5% -> 6% of each run, Pallas kernels for 0% -> 0%
where the time goes in v5:
time: 91.8 us; the launch traced here: 90.4 us
  starting transfers between devices  28.3 us (31%)
  waiting for transfers between devices  24.7 us (27%)
  Pallas kernels  19.6 us (21%)
  local copies, waits for them, and re-layouts  14.1 us (15%)
  other arithmetic  2.6 us (3%)
  between operations  0.97 us (1%)
    pallas_call x1, Pallas kernels, lb_call(): pl.pallas_call(functools.partial(lb_kernel, halo, nx, ny), out_shape=out_...  14.8 us
    ppermute x4, waiting for transfers between devices, send(): return lax.ppermute(x, ('vessel', 'blk'), pairs)  13.8 us
    ppermute x4, starting transfers between devices, send(): return lax.ppermute(x, ('vessel', 'blk'), pairs)  9.2 us
    all_to_all x1, starting transfers between devices, local(): lax.all_to_all(windows, 'blk', split_axis=2, concat_axis=4, tiled=True)  7.82 us
    all_to_all x1, waiting for transfers between devices, local(): lax.all_to_all(windows, 'blk', split_axis=2, concat_axis=4, tiled=True)  5.97 us
    ppermute x4, starting transfers between devices, send(): return lax.ppermute(x, 'vessel', [(i, (i + dv) % nv) for i in range(nv)])  5.92 us
    ppermute x2, starting transfers between devices, send(): return lax.ppermute(x, 'blk', [(i, (i + db) % nb) for i in range(nb)])  5.4 us
    slice x12, local copies, waits for them, and re-layouts, lattice_halos(): tracer_pieces.append(got[NPOP + 1].reshape(-1)[:size].reshape(shape))  5.22 us
  transfers between devices with their start and end apart: 11, of which 5 were waited for; matrix products, arithmetic and copies ran while one was open for 6% of the time, Pallas kernels for 0%

profile of v5, /device:TPU:0, one launch (start us, length us, event | category | flops | bytes accessed | tf_op | source)
XLA Modules:
  0.0 90.4 jit_solution(2025966065776402415)
XLA Ops:
  0.6 0.8 slice_bitcast_fusion.7
  1.4 0.8 slice_bitcast_fusion.5
  2.2 0.7 slice_bitcast_fusion.3
  3.1 0.9 copy-done
  4.0 4.8 %shard_map.50 = (f32[19,8,32,128]{3,2,1,0:T(8,128)}, f32[21,4,32,128]{3,2,1,0:T(8,128)S(1)}, f32[21,4,32,128]{3,2,1,0:T(8,128)S(1)}, f32[21,8,4,128]{3,2,1,0:T(4...) custom-call(f32[19,8,32,128]{3,2,1,0:T(8,128)} %refs_0_.1, ...), custom_call_target="tpu_custom_call" | custom-call | flops 6553600 | bytes 7471104 | tf_op jit(solution)/shard_map/pallas_call | solution.py:288
  8.8 1.1 %collective-permute-start.4 = (f32[21,4,4,128]{3,2,1,0:T(4,128)S(1)}, f32[21,4,4,128]{3,2,1,0:T(4,128)S(1)}, u32[]{:S(2)}, u32[]{:S(2)}) collective-permute-start(f32[21,4,4,128]{3,2,1,0:T(4,128)S(1)} %get-tuple-element.18), channel_id=1, source_target_pairs={{0,17},{1,18},{2,19},{3,20},{4,21},{5,22},{6,23},{7,24},{8,25},{9,... | collective-permute-start | bytes 516104 | tf_op jit(solution)/shard_map/ppermute | solution.py:241
  9.9 1.6 %collective-permute-start = (f32[21,4,32,128]{3,2,1,0:T(8,128)S(1)}, f32[21,4,32,128]{3,2,1,0:T(8,128)}, u32[]{:S(2)}, u32[]{:S(2)}) collective-permute-start(f32[21,4,32,128]{3,2,1,0:T(8,128)S(1)} %get-tuple-element.14), channel_id=1, source_target_pairs={{0,16},{16,32},{32,48},{48,64},{64,80},{80,96},{96,112},{112,0},{1... | collective-permute-start | bytes 4128776 | tf_op jit(solution)/shard_map/ppermute | solution.py:234
  11.5 1.4 %collective-permute-start.1 = (f32[21,4,32,128]{3,2,1,0:T(8,128)S(1)}, f32[21,4,32,128]{3,2,1,0:T(8,128)}, u32[]{:S(2)}, u32[]{:S(2)}) collective-permute-start(f32[21,4,32,128]{3,2,1,0:T(8,128)S(1)} %get-tuple-element.15), channel_id=1, source_target_pairs={{0,112},{16,0},{32,16},{48,32},{64,48},{80,64},{96,80},{112,96},{1... | collective-permute-start | bytes 4128776 | tf_op jit(solution)/shard_map/ppermute | solution.py:234
  12.9 3.7 %collective-permute-start.6 = (f32[21,4,4,128]{3,2,1,0:T(4,128)}, f32[21,4,4,128]{3,2,1,0:T(4,128)}, u32[]{:S(2)}, u32[]{:S(2)}) collective-permute-start(f32[21,4,4,128]{3,2,1,0:T(4,128)} %get-tuple-element.20), channel_id=1, source_target_pairs={{0,31},{1,16},{2,17},{3,18},{4,19},{5,20},{6,21},{7,22},{8,23},{9,... | collective-permute-start | bytes 516104 | tf_op jit(solution)/shard_map/ppermute | solution.py:241
  16.6 0.1 collective-permute-start.5
  16.8 3.5 %collective-permute-done.4.refs_6_ = f32[21,4,4,128]{3,2,1,0:T(4,128)S(1)} collective-permute-done((f32[21,4,4,128]{3,2,1,0:T(4,128)S(1)}, f32[21,4,4,128]{3,2,1,0:T(4,128)S(1)}, u32[]{:S(2)}, u32[]{:S(2)}) %collective-permute-start.4) | collective-permute-done | bytes 172064 | tf_op jit(solution)/shard_map/ppermute | solution.py:241
  20.2 4.2 %collective-permute-start.7 = (f32[21,4,4,128]{3,2,1,0:T(4,128)}, f32[21,4,4,128]{3,2,1,0:T(4,128)}, u32[]{:S(2)}, u32[]{:S(2)}) collective-permute-start(f32[21,4,4,128]{3,2,1,0:T(4,128)} %get-tuple-element.21), channel_id=1, source_target_pairs={{0,127},{1,112},{2,113},{3,114},{4,115},{5,116},{6,117},{7,118},{8... | collective-permute-start | bytes 516104 | tf_op jit(solution)/shard_map/ppermute | solution.py:241
  24.5 10.3 %collective-permute-done.6.refs_8_ = f32[21,4,4,128]{3,2,1,0:T(4,128)} collective-permute-done((f32[21,4,4,128]{3,2,1,0:T(4,128)}, f32[21,4,4,128]{3,2,1,0:T(4,128)}, u32[]{:S(2)}, u32[]{:S(2)}) %collective-permute-start.6) | collective-permute-done | bytes 172064 | tf_op jit(solution)/shard_map/ppermute | solution.py:241
  34.8 1.3 %collective-permute-start.2 = (f32[21,8,4,128]{3,2,1,0:T(4,128)S(1)}, f32[21,8,4,128]{3,2,1,0:T(4,128)}, u32[]{:S(2)}, u32[]{:S(2)}) collective-permute-start(f32[21,8,4,128]{3,2,1,0:T(4,128)S(1)} %get-tuple-element.16), channel_id=1, source_target_pairs={{0,1},{1,2},{2,3},{3,4},{4,5},{5,6},{6,7},{7,8},{8,9},{9,10},{10,1... | collective-permute-start | bytes 1032200 | tf_op jit(solution)/shard_map/ppermute | solution.py:236
  36.1 0.7 slice.317
  36.8 4.1 %collective-permute-start.3 = (f32[21,8,4,128]{3,2,1,0:T(4,128)S(1)}, f32[21,8,4,128]{3,2,1,0:T(4,128)}, u32[]{:S(2)}, u32[]{:S(2)}) collective-permute-start(f32[21,8,4,128]{3,2,1,0:T(4,128)S(1)} %get-tuple-element.17), channel_id=1, source_target_pairs={{0,15},{1,0},{2,1},{3,2},{4,3},{5,4},{6,5},{7,6},{8,7},{9,8},{10,9... | collective-permute-start | bytes 1032200 | tf_op jit(solution)/shard_map/ppermute | solution.py:236
  40.9 0.7 slice.312
  41.6 0.7 slice.319
  42.3 3.2 %collective-permute-done.2.refs_4_ = f32[21,8,4,128]{3,2,1,0:T(4,128)} collective-permute-done((f32[21,8,4,128]{3,2,1,0:T(4,128)S(1)}, f32[21,8,4,128]{3,2,1,0:T(4,128)}, u32[]{:S(2)}, u32[]{:S(2)}) %collective-permute-start.2) | collective-permute-done | bytes 344096 | tf_op jit(solution)/shard_map/ppermute | solution.py:236
  45.5 0.7 slice.311
  46.2 0.7 slice.318
  47.0 14.8 %shard_map.51 = (f32[19,8,32,128]{3,2,1,0:T(8,128)}, f32[3,4,64,16]{3,2,1,0:T(8,128)}) custom-call(f32[19,8,32,128]{3,2,1,0:T(8,128)} %get-tuple-element.13.refs_0_, s32[8,32,128]{2,1,0:T(8,128)} %refs_1_.3, f32[21,4,32,128]{3,2,1,0:T(8,128)} %collective-permute-done.refs_2_, f32[21,4,32,128]{3,2,1,0:T(8,128)} %collective-permute-done.1.refs_3_, ...), custom_call_target="tpu_custom_call" | custom-call | flops 78643200 | bytes 9961472 | tf_op jit(solution)/shard_map/pallas_call | solution.py:219
  61.8 0.8 slice.266
  62.6 0.8 slice.264
  63.4 1.2 %pad_maximum_fusion.2 = (f32[3,4,64,16]{3,2,1,0:T(8,128)S(1)}, f32[3,4,64,16]{3,2,1,0:T(8,128)S(1)}) fusion(f32[3,4,64,16]{3,2,1,0:T(8,128)} %get-tuple-element.23, f32[3,4,2,16]{3,2,1,0:T(2,128)S(1)} %slice.264, f32[3,4,4,16]{3,2,1,0:T(4,128)S(1)} %slice.266), kind=kLoop, calls=%fused_computation.2 | loop fusion | flops 24576 | bytes 152064 | tf_op jit(solution)/shard_map/concatenate | solution.py:331
  64.7 0.2 copy_bitcast_fusion
  64.9 0.9 %reshape.119 = f32[16,1,1536]{2,1,0:T(1,128)} reshape(f32[16,3,4,8,16]{4,3,2,1,0:T(8,128)S(1)} %copy_bitcast_fusion) | data formatting | bytes 196608
  65.8 7.8 %all-to-all-start = ((f32[16,1,1536]{2,1,0:T(1,128)}), f32[16,1,1536]{2,1,0:T(1,128)S(1)}, u32[]{:S(2)}, u32[]{:S(2)}) async-start(f32[16,1,1536]{2,1,0:T(1,128)} %reshape.119), calls=%async_computation | async-start | bytes 196608 | tf_op jit(solution)/shard_map/all_to_all | solution.py:335
  73.7 0.8 slice.313
  74.6 0.8 slice.315
  75.5 6.0 %all-to-all-done = f32[16,1,1536]{2,1,0:T(1,128)S(1)} async-done(((f32[16,1,1536]{2,1,0:T(1,128)}), f32[16,1,1536]{2,1,0:T(1,128)S(1)}, u32[]{:S(2)}, u32[]{:S(2)}) %all-to-all-start) | async-done | bytes 98336 | tf_op jit(solution)/shard_map/all_to_all | solution.py:335
  81.5 0.5 broadcast.20
  82.0 0.9 reduce
  82.9 0.3 reshape.120
  83.2 0.5 copy.39
  83.7 0.3 squeeze.12
  84.1 2.9 %collective-permute-start.9 = (f32[3,2,8,256]{3,2,1,0:T(8,128)S(1)}, f32[3,2,8,256]{3,2,1,0:T(8,128)S(1)}, u32[]{:S(2)}, u32[]{:S(2)}) collective-permute-start(f32[3,2,8,256]{3,2,1,0:T(8,128)S(1)} %get-tuple-element.38), channel_id=1, source_target_pairs={{0,112},{16,0},{32,16},{48,32},{64,48},{80,64},{96,80},{112,96},{1... | collective-permute-start | bytes 147464 | tf_op jit(solution)/shard_map/ppermute | solution.py:234
  87.0 1.8 %collective-permute-done.8 = f32[3,2,8,256]{3,2,1,0:T(8,128)S(1)} collective-permute-done((f32[3,2,8,256]{3,2,1,0:T(8,128)S(1)}, f32[3,2,8,256]{3,2,1,0:T(8,128)S(1)}, u32[]{:S(2)}, u32[]{:S(2)}) %collective-permute-start.8) | collective-permute-done | bytes 49184 | tf_op jit(solution)/shard_map/ppermute | solution.py:234
  88.9 0.1 fusion.27
  89.0 0.1 fusion.28
  89.0 0.1 fusion.23
  89.1 0.1 fusion.24
  89.2 0.1 slice_multiply_fusion.1
  89.3 0.1 fusion.30
  89.5 0.1 fusion.26
  89.6 0.1 fusion.25
  89.7 0.1 fusion.13
  89.8 0.6 copy.40
  (56 shorter events, 0.6 us)
Async XLA Ops:
  3.1 0.9 %copy-start = (s32[8,32,128]{2,1,0:T(8,128)S(1)}, s32[8,32,128]{2,1,0:T(8,128)}, u32[]{:S(2)}) copy-start(s32[8,32,128]{2,1,0:T(8,128)} %refs_1_.3) | copy-start | bytes 393220
  8.8 11.4 %collective-permute-start.4 = (f32[21,4,4,128]{3,2,1,0:T(4,128)S(1)}, f32[21,4,4,128]{3,2,1,0:T(4,128)S(1)}, u32[]{:S(2)}, u32[]{:S(2)}) collective-permute-start(f32[21,4,4,128]{3,2,1,0:T(4,128)S(1)} %get-tuple-element.18), channel_id=1, source_target_pairs={{0,17},{1,18},{2,19},{3,20},{4,21},{5,22},{6,23},{7,24},{8,25},{9,... | collective-permute-start | bytes 516104 | tf_op jit(solution)/shard_map/ppermute | solution.py:241
  9.9 37.0 %collective-permute-start = (f32[21,4,32,128]{3,2,1,0:T(8,128)S(1)}, f32[21,4,32,128]{3,2,1,0:T(8,128)}, u32[]{:S(2)}, u32[]{:S(2)}) collective-permute-start(f32[21,4,32,128]{3,2,1,0:T(8,128)S(1)} %get-tuple-element.14), channel_id=1, source_target_pairs={{0,16},{16,32},{32,48},{48,64},{64,80},{80,96},{96,112},{112,0},{1... | collective-permute-start | bytes 4128776 | tf_op jit(solution)/shard_map/ppermute | solution.py:234
  11.5 35.5 %collective-permute-start.1 = (f32[21,4,32,128]{3,2,1,0:T(8,128)S(1)}, f32[21,4,32,128]{3,2,1,0:T(8,128)}, u32[]{:S(2)}, u32[]{:S(2)}) collective-permute-start(f32[21,4,32,128]{3,2,1,0:T(8,128)S(1)} %get-tuple-element.15), channel_id=1, source_target_pairs={{0,112},{16,0},{32,16},{48,32},{64,48},{80,64},{96,80},{112,96},{1... | collective-permute-start | bytes 4128776 | tf_op jit(solution)/shard_map/ppermute | solution.py:234
  12.9 21.9 %collective-permute-start.6 = (f32[21,4,4,128]{3,2,1,0:T(4,128)}, f32[21,4,4,128]{3,2,1,0:T(4,128)}, u32[]{:S(2)}, u32[]{:S(2)}) collective-permute-start(f32[21,4,4,128]{3,2,1,0:T(4,128)} %get-tuple-element.20), channel_id=1, source_target_pairs={{0,31},{1,16},{2,17},{3,18},{4,19},{5,20},{6,21},{7,22},{8,23},{9,... | collective-permute-start | bytes 516104 | tf_op jit(solution)/shard_map/ppermute | solution.py:241
  16.6 20.2 %collective-permute-start.5 = (f32[21,4,4,128]{3,2,1,0:T(4,128)}, f32[21,4,4,128]{3,2,1,0:T(4,128)}, u32[]{:S(2)}, u32[]{:S(2)}) collective-permute-start(f32[21,4,4,128]{3,2,1,0:T(4,128)} %get-tuple-element.19), channel_id=1, source_target_pairs={{0,113},{1,114},{2,115},{3,116},{4,117},{5,118},{6,119},{7,120},{8... | collective-permute-start | bytes 516104 | tf_op jit(solution)/shard_map/ppermute | solution.py:241
  20.2 4.2 %copy-start.2 = (f32[21,4,4,128]{3,2,1,0:T(4,128)}, f32[21,4,4,128]{3,2,1,0:T(4,128)S(1)}, u32[]{:S(2)}) copy-start(f32[21,4,4,128]{3,2,1,0:T(4,128)S(1)} %collective-permute-done.4.refs_6_) | copy-start | bytes 516100
  20.2 21.4 %collective-permute-start.7 = (f32[21,4,4,128]{3,2,1,0:T(4,128)}, f32[21,4,4,128]{3,2,1,0:T(4,128)}, u32[]{:S(2)}, u32[]{:S(2)}) collective-permute-start(f32[21,4,4,128]{3,2,1,0:T(4,128)} %get-tuple-element.21), channel_id=1, source_target_pairs={{0,127},{1,112},{2,113},{3,114},{4,115},{5,116},{6,117},{7,118},{8... | collective-permute-start | bytes 516104 | tf_op jit(solution)/shard_map/ppermute | solution.py:241
  34.8 10.7 %collective-permute-start.2 = (f32[21,8,4,128]{3,2,1,0:T(4,128)S(1)}, f32[21,8,4,128]{3,2,1,0:T(4,128)}, u32[]{:S(2)}, u32[]{:S(2)}) collective-permute-start(f32[21,8,4,128]{3,2,1,0:T(4,128)S(1)} %get-tuple-element.16), channel_id=1, source_target_pairs={{0,1},{1,2},{2,3},{3,4},{4,5},{5,6},{6,7},{7,8},{8,9},{9,10},{10,1... | collective-permute-start | bytes 1032200 | tf_op jit(solution)/shard_map/ppermute | solution.py:236
  36.8 9.4 %collective-permute-start.3 = (f32[21,8,4,128]{3,2,1,0:T(4,128)S(1)}, f32[21,8,4,128]{3,2,1,0:T(4,128)}, u32[]{:S(2)}, u32[]{:S(2)}) collective-permute-start(f32[21,8,4,128]{3,2,1,0:T(4,128)S(1)} %get-tuple-element.17), channel_id=1, source_target_pairs={{0,15},{1,0},{2,1},{3,2},{4,3},{5,4},{6,5},{7,6},{8,7},{9,8},{10,9... | collective-permute-start | bytes 1032200 | tf_op jit(solution)/shard_map/ppermute | solution.py:236
  64.7 9.9 %copy-start.1 = (f32[4,4,256]{2,1,0:T(4,128)S(1)}, f32[4,4,256]{2,1,0:T(4,128)}, u32[]{:S(2)}) copy-start(f32[4,4,256]{2,1,0:T(4,128)} %param.5) | copy-start | bytes 49156
  65.8 15.6 %all-to-all-start = ((f32[16,1,1536]{2,1,0:T(1,128)}), f32[16,1,1536]{2,1,0:T(1,128)S(1)}, u32[]{:S(2)}, u32[]{:S(2)}) async-start(f32[16,1,1536]{2,1,0:T(1,128)} %reshape.119), calls=%async_computation | async-start | bytes 196608 | tf_op jit(solution)/shard_map/all_to_all | solution.py:335
  84.0 4.7 %collective-permute-start.8 = (f32[3,2,8,256]{3,2,1,0:T(8,128)S(1)}, f32[3,2,8,256]{3,2,1,0:T(8,128)S(1)}, u32[]{:S(2)}, u32[]{:S(2)}) collective-permute-start(f32[3,2,8,256]{3,2,1,0:T(8,128)S(1)} %get-tuple-element.37), channel_id=1, source_target_pairs={{0,16},{16,32},{32,48},{48,64},{64,80},{80,96},{96,112},{112,0},{1... | collective-permute-start | bytes 147464 | tf_op jit(solution)/shard_map/ppermute | solution.py:234
  84.1 4.7 %collective-permute-start.9 = (f32[3,2,8,256]{3,2,1,0:T(8,128)S(1)}, f32[3,2,8,256]{3,2,1,0:T(8,128)S(1)}, u32[]{:S(2)}, u32[]{:S(2)}) collective-permute-start(f32[3,2,8,256]{3,2,1,0:T(8,128)S(1)} %get-tuple-element.38), channel_id=1, source_target_pairs={{0,112},{16,0},{32,16},{48,32},{64,48},{80,64},{96,80},{112,96},{1... | collective-permute-start | bytes 147464 | tf_op jit(solution)/shard_map/ppermute | solution.py:234

commit v6 on v5

--- a/solution.py
+++ b/solution.py
@@ -295,8 +295,10 @@
     )(g0, mask, *tplanes)
     post0, msgs = outs[0], outs[1:]
     pieces, tracer_pieces = [], []
-    for (dv, db), msg, shape in zip(ORDER, msgs, tshapes):
-        got = send(msg, dv, db)
+    faces = [send(msg, dv, db) for (dv, db), msg in zip(ORDER[:4], msgs[:4])]
+    corner_msgs = lax.optimization_barrier((tuple(msgs[4:]), faces[0], faces[1]))[0]
+    corners = [send(msg, dv, db) for (dv, db), msg in zip(ORDER[4:], corner_msgs)]
+    for got, shape in zip(faces + corners, tshapes):
         pieces.append(got)
         size = int(np.prod(shape))
         tracer_pieces.append(got[NPOP + 1].reshape(-1)[:size].reshape(shape))

time: 91.8 us -> 90.7 us (0.988)
  waiting for transfers between devices: 24.7 us -> 18.8 us
  starting transfers between devices: 28.3 us -> 31.1 us
  local copies, waits for them, and re-layouts: 14.1 us -> 16.8 us
    ppermute x4, waiting for transfers between devices: 13.8 us -> 1.04 us  [send(): return lax.ppermute(x, ('vessel', 'blk'), pairs)]
    ppermute x4, waiting for transfers between devices: 1.77 us -> 5.86 us  [send(): return lax.ppermute(x, 'vessel', [(i, (i + dv) % nv) for i in range(nv)])]
    ppermute x2, waiting for transfers between devices: 3.16 us -> 6.88 us  [send(): return lax.ppermute(x, 'blk', [(i, (i + db) % nb) for i in range(nb)])]
    ppermute x4, starting transfers between devices: 9.2 us -> 12.8 us  [send(): return lax.ppermute(x, ('vessel', 'blk'), pairs)]
    unnamed x26 -> x38, local copies, waits for them, and re-layouts: 5.12 us -> 7.87 us
    ppermute x4, starting transfers between devices: 5.92 us -> 4 us  [send(): return lax.ppermute(x, 'vessel', [(i, (i + dv) % nv) for i in range(nv)])]
    ppermute x2, starting transfers between devices: 5.4 us -> 6.57 us  [send(): return lax.ppermute(x, 'blk', [(i, (i + db) % nb) for i in range(nb)])]
    all_to_all x1, waiting for transfers between devices: 5.97 us -> 4.99 us  [local(): lax.all_to_all(windows, 'blk', split_axis=2, concat_axis=4, tiled=True)]
  transfers between devices with their start and end apart: 11 -> 11, of which waited for: 5 -> 7; matrix products, arithmetic and copies ran while one was open for 6% -> 6% of each run, Pallas kernels for 0% -> 0%
where the time goes in v6:
time: 90.7 us; the launch traced here: 89.9 us
  starting transfers between devices  31.1 us (34%)
  Pallas kernels  19.6 us (22%)
  waiting for transfers between devices  18.8 us (21%)
  local copies, waits for them, and re-layouts  16.8 us (19%)
  other arithmetic  2.65 us (3%)
  between operations  0.98 us (1%)
    pallas_call x1, Pallas kernels, lb_call(): pl.pallas_call(functools.partial(lb_kernel, halo, nx, ny), out_shape=out_...  14.8 us
    ppermute x4, starting transfers between devices, send(): return lax.ppermute(x, ('vessel', 'blk'), pairs)  12.8 us
    unnamed x38, local copies, waits for them, and re-layouts  7.87 us
    all_to_all x1, starting transfers between devices, local(): lax.all_to_all(windows, 'blk', split_axis=2, concat_axis=4, tiled=True)  7.67 us
    ppermute x2, waiting for transfers between devices, send(): return lax.ppermute(x, 'blk', [(i, (i + db) % nb) for i in range(nb)])  6.88 us
    ppermute x2, starting transfers between devices, send(): return lax.ppermute(x, 'blk', [(i, (i + db) % nb) for i in range(nb)])  6.57 us
    ppermute x4, waiting for transfers between devices, send(): return lax.ppermute(x, 'vessel', [(i, (i + dv) % nv) for i in range(nv)])  5.86 us
    slice x12, local copies, waits for them, and re-layouts, lattice_halos(): tracer_pieces.append(got[NPOP + 1].reshape(-1)[:size].reshape(shape))  5.2 us
  transfers between devices with their start and end apart: 11, of which 7 were waited for; matrix products, arithmetic and copies ran while one was open for 6% of the time, Pallas kernels for 0%

profile of v6, /device:TPU:0, one launch (start us, length us, event | category | flops | bytes accessed | tf_op | source)
XLA Modules:
  0.0 89.9 jit_solution(4182584745292301154)
XLA Ops:
  0.6 0.8 slice_bitcast_fusion.5
  1.4 0.7 slice_bitcast_fusion.3
  2.2 0.8 slice_bitcast_fusion.7
  3.2 0.9 copy-done
  4.0 4.8 %shard_map.50 = (f32[19,8,32,128]{3,2,1,0:T(8,128)}, f32[21,4,32,128]{3,2,1,0:T(8,128)S(1)}, f32[21,4,32,128]{3,2,1,0:T(8,128)S(1)}, f32[21,8,4,128]{3,2,1,0:T(4...) custom-call(f32[19,8,32,128]{3,2,1,0:T(8,128)} %refs_0_.1, ...), custom_call_target="tpu_custom_call" | custom-call | flops 6553600 | bytes 7471104 | tf_op jit(solution)/shard_map/pallas_call | solution.py:288
  8.8 0.7 copy-done.1
  9.5 0.7 copy-done.2
  10.2 3.0 %collective-permute-start.1 = (f32[21,4,32,128]{3,2,1,0:T(8,128)S(1)}, f32[21,4,32,128]{3,2,1,0:T(8,128)}, u32[]{:S(2)}, u32[]{:S(2)}) collective-permute-start(f32[21,4,32,128]{3,2,1,0:T(8,128)S(1)} %get-tuple-element.19), channel_id=1, source_target_pairs={{0,112},{16,0},{32,16},{48,32},{64,48},{80,64},{96,80},{112,96},{1... | collective-permute-start | bytes 4128776 | tf_op jit(solution)/shard_map/ppermute | solution.py:234
  13.1 1.7 %collective-permute-start.2 = (f32[21,8,4,128]{3,2,1,0:T(4,128)S(1)}, f32[21,8,4,128]{3,2,1,0:T(4,128)S(1)}, u32[]{:S(2)}, u32[]{:S(2)}) collective-permute-start(f32[21,8,4,128]{3,2,1,0:T(4,128)S(1)} %get-tuple-element.20), channel_id=1, source_target_pairs={{0,1},{1,2},{2,3},{3,4},{4,5},{5,6},{6,7},{7,8},{8,9},{9,10},{10,1... | collective-permute-start | bytes 1032200 | tf_op jit(solution)/shard_map/ppermute | solution.py:236
  14.8 4.9 %collective-permute-start.3 = (f32[21,8,4,128]{3,2,1,0:T(4,128)S(1)}, f32[21,8,4,128]{3,2,1,0:T(4,128)}, u32[]{:S(2)}, u32[]{:S(2)}) collective-permute-start(f32[21,8,4,128]{3,2,1,0:T(4,128)S(1)} %get-tuple-element.21), channel_id=1, source_target_pairs={{0,15},{1,0},{2,1},{3,2},{4,3},{5,4},{6,5},{7,6},{8,7},{9,8},{10,9... | collective-permute-start | bytes 1032200 | tf_op jit(solution)/shard_map/ppermute | solution.py:236
  19.7 6.9 %collective-permute-done.2.refs_4_ = f32[21,8,4,128]{3,2,1,0:T(4,128)S(1)} collective-permute-done((f32[21,8,4,128]{3,2,1,0:T(4,128)S(1)}, f32[21,8,4,128]{3,2,1,0:T(4,128)S(1)}, u32[]{:S(2)}, u32[]{:S(2)}) %collective-permute-start.2) | collective-permute-done | bytes 344096 | tf_op jit(solution)/shard_map/ppermute | solution.py:236
  26.6 0.7 copy-done.3
  27.4 0.7 slice.318
  28.1 1.2 %collective-permute-done.refs_2_ = f32[21,4,32,128]{3,2,1,0:T(8,128)} collective-permute-done((f32[21,4,32,128]{3,2,1,0:T(8,128)S(1)}, f32[21,4,32,128]{3,2,1,0:T(8,128)}, u32[]{:S(2)}, u32[]{:S(2)}) %collective-permute-start) | collective-permute-done | bytes 1376288 | tf_op jit(solution)/shard_map/ppermute | solution.py:234
  29.2 1.7 %collective-permute-start.4 = (f32[21,4,4,128]{3,2,1,0:T(4,128)}, f32[21,4,4,128]{3,2,1,0:T(4,128)S(1)}, u32[]{:S(2)}, u32[]{:S(2)}) collective-permute-start(f32[21,4,4,128]{3,2,1,0:T(4,128)} %copy-done.2), channel_id=1, source_target_pairs={{0,17},{1,18},{2,19},{3,20},{4,21},{5,22},{6,23},{7,24},{8,25},{9,... | collective-permute-start | bytes 516104 | tf_op jit(solution)/shard_map/ppermute | solution.py:241
  30.9 3.4 %collective-permute-start.5 = (f32[21,4,4,128]{3,2,1,0:T(4,128)}, f32[21,4,4,128]{3,2,1,0:T(4,128)S(1)}, u32[]{:S(2)}, u32[]{:S(2)}) collective-permute-start(f32[21,4,4,128]{3,2,1,0:T(4,128)} %copy-done.1), channel_id=1, source_target_pairs={{0,113},{1,114},{2,115},{3,116},{4,117},{5,118},{6,119},{7,120},{8... | collective-permute-start | bytes 516104 | tf_op jit(solution)/shard_map/ppermute | solution.py:241
  34.3 1.7 %collective-permute-start.6 = (f32[21,4,4,128]{3,2,1,0:T(4,128)S(1)}, f32[21,4,4,128]{3,2,1,0:T(4,128)S(1)}, u32[]{:S(2)}, u32[]{:S(2)}) collective-permute-start(f32[21,4,4,128]{3,2,1,0:T(4,128)S(1)} %get-tuple-element.28), channel_id=1, source_target_pairs={{0,31},{1,16},{2,17},{3,18},{4,19},{5,20},{6,21},{7,22},{8,23},{9,... | collective-permute-start | bytes 516104 | tf_op jit(solution)/shard_map/ppermute | solution.py:241
  36.0 6.1 %collective-permute-start.7 = (f32[21,4,4,128]{3,2,1,0:T(4,128)S(1)}, f32[21,4,4,128]{3,2,1,0:T(4,128)S(1)}, u32[]{:S(2)}, u32[]{:S(2)}) collective-permute-start(f32[21,4,4,128]{3,2,1,0:T(4,128)S(1)} %get-tuple-element.29), channel_id=1, source_target_pairs={{0,127},{1,112},{2,113},{3,114},{4,115},{5,116},{6,117},{7,118},{8... | collective-permute-start | bytes 516104 | tf_op jit(solution)/shard_map/ppermute | solution.py:241
  42.1 0.8 slice.313
  43.0 0.8 slice.315
  43.9 0.7 collective-permute-done.5.refs_7_
  44.6 0.3 collective-permute-done.7.refs_9_
  45.0 0.3 copy-done.5
  45.4 0.3 copy-done.6
  45.7 14.8 %shard_map.51 = (f32[19,8,32,128]{3,2,1,0:T(8,128)}, f32[3,4,64,16]{3,2,1,0:T(8,128)}) custom-call(f32[19,8,32,128]{3,2,1,0:T(8,128)} %get-tuple-element.17.refs_0_, s32[8,32,128]{2,1,0:T(8,128)} %refs_1_.3, f32[21,4,32,128]{3,2,1,0:T(8,128)} %collective-permute-done.refs_2_, f32[21,4,32,128]{3,2,1,0:T(8,128)} %collective-permute-done.1.refs_3_, ...), custom_call_target="tpu_custom_call" | custom-call | flops 78643200 | bytes 9961472 | tf_op jit(solution)/shard_map/pallas_call | solution.py:219
  60.5 0.8 slice.264
  61.3 0.8 slice.266
  62.1 1.3 %pad_maximum_fusion.2 = (f32[3,4,64,16]{3,2,1,0:T(8,128)S(1)}, f32[3,4,64,16]{3,2,1,0:T(8,128)S(1)}) fusion(f32[3,4,64,16]{3,2,1,0:T(8,128)} %get-tuple-element.31, f32[3,4,2,16]{3,2,1,0:T(2,128)S(1)} %slice.264, f32[3,4,4,16]{3,2,1,0:T(4,128)S(1)} %slice.266), kind=kLoop, calls=%fused_computation.2 | loop fusion | flops 24576 | bytes 152064 | tf_op jit(solution)/shard_map/concatenate | solution.py:333
  63.4 0.2 copy_bitcast_fusion
  63.6 0.9 %reshape.119 = f32[16,1,1536]{2,1,0:T(1,128)} reshape(f32[16,3,4,8,16]{4,3,2,1,0:T(8,128)S(1)} %copy_bitcast_fusion) | data formatting | bytes 196608
  64.5 7.7 %all-to-all-start = ((f32[16,1,1536]{2,1,0:T(1,128)}), f32[16,1,1536]{2,1,0:T(1,128)S(1)}, u32[]{:S(2)}, u32[]{:S(2)}) async-start(f32[16,1,1536]{2,1,0:T(1,128)} %reshape.119), calls=%async_computation | async-start | bytes 196608 | tf_op jit(solution)/shard_map/all_to_all | solution.py:337
  72.2 0.7 slice.310
  72.9 0.7 slice.317
  73.6 0.7 slice.312
  74.3 0.7 slice.319
  75.0 5.0 %all-to-all-done = f32[16,1,1536]{2,1,0:T(1,128)S(1)} async-done(((f32[16,1,1536]{2,1,0:T(1,128)}), f32[16,1,1536]{2,1,0:T(1,128)S(1)}, u32[]{:S(2)}, u32[]{:S(2)}) %all-to-all-start) | async-done | bytes 98336 | tf_op jit(solution)/shard_map/all_to_all | solution.py:337
  80.0 0.5 broadcast.20
  80.5 0.9 reduce
  81.4 0.3 reshape.120
  81.7 0.5 copy.39
  82.2 0.3 squeeze.12
  82.6 1.0 %collective-permute-start.9 = (f32[3,2,8,256]{3,2,1,0:T(8,128)S(1)}, f32[3,2,8,256]{3,2,1,0:T(8,128)S(1)}, u32[]{:S(2)}, u32[]{:S(2)}) collective-permute-start(f32[3,2,8,256]{3,2,1,0:T(8,128)S(1)} %get-tuple-element.46), channel_id=1, source_target_pairs={{0,112},{16,0},{32,16},{48,32},{64,48},{80,64},{96,80},{112,96},{1... | collective-permute-start | bytes 147464 | tf_op jit(solution)/shard_map/ppermute | solution.py:234
  83.6 1.7 %collective-permute-done.9 = f32[3,2,8,256]{3,2,1,0:T(8,128)S(1)} collective-permute-done((f32[3,2,8,256]{3,2,1,0:T(8,128)S(1)}, f32[3,2,8,256]{3,2,1,0:T(8,128)S(1)}, u32[]{:S(2)}, u32[]{:S(2)}) %collective-permute-start.9) | collective-permute-done | bytes 49184 | tf_op jit(solution)/shard_map/ppermute | solution.py:234
  85.4 3.0 %collective-permute-done.8 = f32[3,2,8,256]{3,2,1,0:T(8,128)S(1)} collective-permute-done((f32[3,2,8,256]{3,2,1,0:T(8,128)S(1)}, f32[3,2,8,256]{3,2,1,0:T(8,128)S(1)}, u32[]{:S(2)}, u32[]{:S(2)}) %collective-permute-start.8) | collective-permute-done | bytes 49184 | tf_op jit(solution)/shard_map/ppermute | solution.py:234
  88.4 0.1 fusion.23
  88.7 0.1 slice_multiply_fusion.1
  89.2 0.1 fusion.13
  89.3 0.6 copy.40
  (68 shorter events, 1.1 us)
Async XLA Ops:
  3.1 0.9 %copy-start = (s32[8,32,128]{2,1,0:T(8,128)S(1)}, s32[8,32,128]{2,1,0:T(8,128)}, u32[]{:S(2)}) copy-start(s32[8,32,128]{2,1,0:T(8,128)} %refs_1_.3) | copy-start | bytes 393220
  4.0 38.9 %copy-start.4 = (f32[4,4,256]{2,1,0:T(4,128)S(1)}, f32[4,4,256]{2,1,0:T(4,128)}, u32[]{:S(2)}) copy-start(f32[4,4,256]{2,1,0:T(4,128)} %param.5) | copy-start | bytes 49156
  8.8 0.7 copy-start.1
  9.5 0.7 copy-start.2
  10.2 19.1 %collective-permute-start = (f32[21,4,32,128]{3,2,1,0:T(8,128)S(1)}, f32[21,4,32,128]{3,2,1,0:T(8,128)}, u32[]{:S(2)}, u32[]{:S(2)}) collective-permute-start(f32[21,4,32,128]{3,2,1,0:T(8,128)S(1)} %get-tuple-element.18), channel_id=1, source_target_pairs={{0,16},{16,32},{32,48},{48,64},{64,80},{80,96},{96,112},{112,0},{1... | collective-permute-start | bytes 4128776 | tf_op jit(solution)/shard_map/ppermute | solution.py:234
  10.2 19.1 %collective-permute-start.1 = (f32[21,4,32,128]{3,2,1,0:T(8,128)S(1)}, f32[21,4,32,128]{3,2,1,0:T(8,128)}, u32[]{:S(2)}, u32[]{:S(2)}) collective-permute-start(f32[21,4,32,128]{3,2,1,0:T(8,128)S(1)} %get-tuple-element.19), channel_id=1, source_target_pairs={{0,112},{16,0},{32,16},{48,32},{64,48},{80,64},{96,80},{112,96},{1... | collective-permute-start | bytes 4128776 | tf_op jit(solution)/shard_map/ppermute | solution.py:234
  13.1 13.4 %collective-permute-start.2 = (f32[21,8,4,128]{3,2,1,0:T(4,128)S(1)}, f32[21,8,4,128]{3,2,1,0:T(4,128)S(1)}, u32[]{:S(2)}, u32[]{:S(2)}) collective-permute-start(f32[21,8,4,128]{3,2,1,0:T(4,128)S(1)} %get-tuple-element.20), channel_id=1, source_target_pairs={{0,1},{1,2},{2,3},{3,4},{4,5},{5,6},{6,7},{7,8},{8,9},{9,10},{10,1... | collective-permute-start | bytes 1032200 | tf_op jit(solution)/shard_map/ppermute | solution.py:236
  14.8 12.6 %collective-permute-start.3 = (f32[21,8,4,128]{3,2,1,0:T(4,128)S(1)}, f32[21,8,4,128]{3,2,1,0:T(4,128)}, u32[]{:S(2)}, u32[]{:S(2)}) collective-permute-start(f32[21,8,4,128]{3,2,1,0:T(4,128)S(1)} %get-tuple-element.21), channel_id=1, source_target_pairs={{0,15},{1,0},{2,1},{3,2},{4,3},{5,4},{6,5},{7,6},{8,7},{9,8},{10,9... | collective-permute-start | bytes 1032200 | tf_op jit(solution)/shard_map/ppermute | solution.py:236
  26.6 0.8 copy-start.3
  29.2 14.7 %collective-permute-start.4 = (f32[21,4,4,128]{3,2,1,0:T(4,128)}, f32[21,4,4,128]{3,2,1,0:T(4,128)S(1)}, u32[]{:S(2)}, u32[]{:S(2)}) collective-permute-start(f32[21,4,4,128]{3,2,1,0:T(4,128)} %copy-done.2), channel_id=1, source_target_pairs={{0,17},{1,18},{2,19},{3,20},{4,21},{5,22},{6,23},{7,24},{8,25},{9,... | collective-permute-start | bytes 516104 | tf_op jit(solution)/shard_map/ppermute | solution.py:241
  30.9 13.7 %collective-permute-start.5 = (f32[21,4,4,128]{3,2,1,0:T(4,128)}, f32[21,4,4,128]{3,2,1,0:T(4,128)S(1)}, u32[]{:S(2)}, u32[]{:S(2)}) collective-permute-start(f32[21,4,4,128]{3,2,1,0:T(4,128)} %copy-done.1), channel_id=1, source_target_pairs={{0,113},{1,114},{2,115},{3,116},{4,117},{5,118},{6,119},{7,120},{8... | collective-permute-start | bytes 516104 | tf_op jit(solution)/shard_map/ppermute | solution.py:241
  34.3 10.3 %collective-permute-start.6 = (f32[21,4,4,128]{3,2,1,0:T(4,128)S(1)}, f32[21,4,4,128]{3,2,1,0:T(4,128)S(1)}, u32[]{:S(2)}, u32[]{:S(2)}) collective-permute-start(f32[21,4,4,128]{3,2,1,0:T(4,128)S(1)} %get-tuple-element.28), channel_id=1, source_target_pairs={{0,31},{1,16},{2,17},{3,18},{4,19},{5,20},{6,21},{7,22},{8,23},{9,... | collective-permute-start | bytes 516104 | tf_op jit(solution)/shard_map/ppermute | solution.py:241
  36.0 9.0 %collective-permute-start.7 = (f32[21,4,4,128]{3,2,1,0:T(4,128)S(1)}, f32[21,4,4,128]{3,2,1,0:T(4,128)S(1)}, u32[]{:S(2)}, u32[]{:S(2)}) collective-permute-start(f32[21,4,4,128]{3,2,1,0:T(4,128)S(1)} %get-tuple-element.29), channel_id=1, source_target_pairs={{0,127},{1,112},{2,113},{3,114},{4,115},{5,116},{6,117},{7,118},{8... | collective-permute-start | bytes 516104 | tf_op jit(solution)/shard_map/ppermute | solution.py:241
  43.9 1.1 %copy-start.7 = (f32[21,4,4,128]{3,2,1,0:T(4,128)}, f32[21,4,4,128]{3,2,1,0:T(4,128)S(1)}, u32[]{:S(2)}) copy-start(f32[21,4,4,128]{3,2,1,0:T(4,128)S(1)} %collective-permute-done.4.refs_6_) | copy-start | bytes 516100
  44.6 0.7 copy-start.5
  44.6 0.7 copy-start.8
  45.0 0.7 copy-start.6
  64.5 15.5 %all-to-all-start = ((f32[16,1,1536]{2,1,0:T(1,128)}), f32[16,1,1536]{2,1,0:T(1,128)S(1)}, u32[]{:S(2)}, u32[]{:S(2)}) async-start(f32[16,1,1536]{2,1,0:T(1,128)} %reshape.119), calls=%async_computation | async-start | bytes 196608 | tf_op jit(solution)/shard_map/all_to_all | solution.py:337
  82.6 2.8 %collective-permute-start.9 = (f32[3,2,8,256]{3,2,1,0:T(8,128)S(1)}, f32[3,2,8,256]{3,2,1,0:T(8,128)S(1)}, u32[]{:S(2)}, u32[]{:S(2)}) collective-permute-start(f32[3,2,8,256]{3,2,1,0:T(8,128)S(1)} %get-tuple-element.46), channel_id=1, source_target_pairs={{0,112},{16,0},{32,16},{48,32},{64,48},{80,64},{96,80},{112,96},{1... | collective-permute-start | bytes 147464 | tf_op jit(solution)/shard_map/ppermute | solution.py:234
  83.6 4.7 %collective-permute-start.8 = (f32[3,2,8,256]{3,2,1,0:T(8,128)S(1)}, f32[3,2,8,256]{3,2,1,0:T(8,128)S(1)}, u32[]{:S(2)}, u32[]{:S(2)}) collective-permute-start(f32[3,2,8,256]{3,2,1,0:T(8,128)S(1)} %get-tuple-element.45), channel_id=1, source_target_pairs={{0,16},{16,32},{32,48},{48,64},{64,80},{80,96},{96,112},{112,0},{1... | collective-permute-start | bytes 147464 | tf_op jit(solution)/shard_map/ppermute | solution.py:234

commit v7 on v3

--- a/solution.py
+++ b/solution.py
@@ -113,7 +113,11 @@
 
 def lb_kernel(halo, nx, ny, *refs):
     g0, mask_ref, xlo, xhi, ylo, yhi, c_mm, c_mp, c_pm, c_pp = refs[:10]
-    out_ref, coarse_ref, abuf, bbuf, flow_s = refs[10:]
+    out_ref, coarse_ref = refs[10:12]
+    tplanes = refs[12:20]
+    abuf, bbuf, flow_s = refs[20:]
+    for t_ref, m_ref in zip(tplanes, (xlo, xhi, ylo, yhi, c_mm, c_mp, c_pm, c_pp)):
+        t_ref[...] = m_ref[NPOP + 1]
     h = halo
     top = YOFF
     abuf[0:NPOP, h : h + nx, top : top + ny, :] = g0[...]
@@ -214,7 +218,7 @@
     out_shape = (
         jax.ShapeDtypeStruct(g0.shape, f32),
         jax.ShapeDtypeStruct((3, nx // 2, nz // 2, ny // 2), f32),
-    )
+    ) + tuple(jax.ShapeDtypeStruct(m.shape[1:], f32) for m in halos)
     scratch = [
         pltpu.VMEM((NPOP + 1, nx + 2 * halo, rows, nz), f32),
         pltpu.VMEM((NPOP, nx + 2 * halo, rows, nz), f32),
@@ -226,7 +230,7 @@
         functools.partial(lb_kernel, halo, nx, ny),
         out_shape=out_shape,
         in_specs=[vmem] * (2 + len(halos)),
-        out_specs=(vmem, vmem),
+        out_specs=tuple(vmem for _ in out_shape),
         scratch_shapes=scratch,
         cost_estimate=cost,
         compiler_params=pltpu.CompilerParams(vmem_limit_bytes=60 * 1024 * 1024),
@@ -256,7 +260,7 @@
     trc_x = {1: slice(nxc - w, nxc), -1: slice(0, w), 0: slice(0, nxc)}
     trc_z = {1: slice(nzc - w, nzc), -1: slice(0, w), 0: slice(0, nzc)}
     order = ((1, 0), (-1, 0), (0, 1), (0, -1), (1, 1), (-1, 1), (1, -1), (-1, -1))
-    pieces, tracer_pieces = [], []
+    pieces, shapes = [], []
     for dv, db in order:
         xs, ys = lat[dv], lat_y[db]
         lb = jnp.concatenate([g0[:, xs, ys], maskf[:, xs, ys]], axis=0)
@@ -264,10 +268,9 @@
         plane = lb.shape[1] * lb.shape[2] * nz
         flat = jnp.pad(tp.reshape(-1), (0, plane - tp.size))
         msg = jnp.concatenate([lb, flat.reshape(1, lb.shape[1], lb.shape[2], nz)], axis=0)
-        got = send(msg, dv, db)
-        pieces.append(got)
-        tracer_pieces.append(got[NPOP + 1].reshape(-1)[: tp.size].reshape(tp.shape))
-    return pieces, tracer_pieces
+        pieces.append(send(msg, dv, db))
+        shapes.append(tp.shape)
+    return pieces, shapes
 
 
 def tracer_update(c, fx, fy, fz):
@@ -290,8 +293,9 @@
 
 def local(populations, voxel_mask, tracer):
     w = TRACER_STEPS
-    halos, tp = lattice_halos(populations, voxel_mask, tracer, STEPS, w)
-    state, coarse = lb_call(populations, voxel_mask, halos, STEPS)
+    halos, shapes = lattice_halos(populations, voxel_mask, tracer, STEPS, w)
+    state, coarse, *planes = lb_call(populations, voxel_mask, halos, STEPS)
+    tp = [p.reshape(-1)[: int(np.prod(s))].reshape(s) for p, s in zip(planes, shapes)]
     nzt = coarse.shape[2]
     nb = lax.axis_size("blk")
     zb = nzt // nb

time: 84.3 us -> 90.8 us (1.077)
  waiting for transfers between devices: 16.1 us -> 26.3 us
  starting transfers between devices: 30.3 us -> 26.6 us
  other arithmetic: 6.24 us -> 4.21 us
  local copies, waits for them, and re-layouts: 11 us -> 13 us
    ppermute x4, waiting for transfers between devices: 7.47 us -> 17.1 us  [send(): return lax.ppermute(x, ('vessel', 'blk'), pairs)]
    all_to_all x1, starting transfers between devices: 6.12 us -> 9.34 us  [local(): lax.all_to_all(windows, 'blk', split_axis=2, concat_axis=4, tiled=True)]
    ppermute x4, starting transfers between devices: 10.7 us -> 7.98 us  [send(): return lax.ppermute(x, ('vessel', 'blk'), pairs)]
    concatenate x8, other arithmetic: 2.71 us -> 0.53 us  [lattice_halos(): jnp.concatenate([lb, flat.reshape(1, lb.shape[1], lb.shape[2], nz)], axis=0)]
    ppermute x4, starting transfers between devices: 8.03 us -> 5.91 us  [send(): return lax.ppermute(x, 'vessel', [(i, (i + dv) % nv) for i in range(nv)])]
    ppermute x2, starting transfers between devices: 5.45 us -> 3.37 us  [send(): return lax.ppermute(x, 'blk', [(i, (i + db) % nb) for i in range(nb)])]
    unnamed x36 -> x46, local copies, waits for them, and re-layouts: 3.45 us -> 4.53 us
    slice x12 -> x10, local copies, waits for them, and re-layouts: 1.8 us -> 2.85 us  [local(): p.reshape(-1)[:int(np.prod(s))].reshape(s)]
  transfers between devices with their start and end apart: 11 -> 11, of which waited for: 3 -> 6; matrix products, arithmetic and copies ran while one was open for 5% -> 1% of each run, Pallas kernels for 0% -> 0%
where the time goes in v7:
time: 90.8 us; the launch traced here: 89.6 us
  starting transfers between devices  26.6 us (29%)
  waiting for transfers between devices  26.3 us (29%)
  Pallas kernels  18.3 us (20%)
  local copies, waits for them, and re-layouts  13 us (14%)
  other arithmetic  4.21 us (5%)
  between operations  1.16 us (1%)
    pallas_call x1, Pallas kernels, lb_call(): pl.pallas_call(functools.partial(lb_kernel, halo, nx, ny), out_shape=out_...  18.3 us
    ppermute x4, waiting for transfers between devices, send(): return lax.ppermute(x, ('vessel', 'blk'), pairs)  17.1 us
    all_to_all x1, starting transfers between devices, local(): lax.all_to_all(windows, 'blk', split_axis=2, concat_axis=4, tiled=True)  9.34 us
    ppermute x4, starting transfers between devices, send(): return lax.ppermute(x, ('vessel', 'blk'), pairs)  7.98 us
    all_to_all x1, waiting for transfers between devices, local(): lax.all_to_all(windows, 'blk', split_axis=2, concat_axis=4, tiled=True)  7.52 us
    ppermute x4, starting transfers between devices, send(): return lax.ppermute(x, 'vessel', [(i, (i + dv) % nv) for i in range(nv)])  5.91 us
    unnamed x46, local copies, waits for them, and re-layouts  4.53 us
    ppermute x2, starting transfers between devices, send(): return lax.ppermute(x, 'blk', [(i, (i + db) % nb) for i in range(nb)])  3.37 us
  transfers between devices with their start and end apart: 11, of which 6 were waited for; matrix products, arithmetic and copies ran while one was open for 1% of the time, Pallas kernels for 0%

profile of v7, /device:TPU:0, one launch (start us, length us, event | category | flops | bytes accessed | tf_op | source)
XLA Modules:
  0.0 89.6 jit_solution(12495756638251456761)
XLA Ops:
  0.6 1.1 %convert_bitcast_fusion = f32[1,8,32,128]{3,2,1,0:T(8,128)S(1)} fusion(s32[8,32,128]{2,1,0:T(8,128)} %refs_1_.1), kind=kLoop, calls=%fused_computation.12 | loop fusion | flops 32768 | bytes 262144 | tf_op jit(solution)/shard_map/broadcast_in_dim | solution.py:257
  1.7 1.4 %fusion.22 = (f32[19,4,4,128]{3,2,1,0:T(4,128)S(1)}, f32[19,4,4,128]{3,2,1,0:T(4,128)S(1)}, f32[19,4,4,128]{3,2,1,0:T(4,128)S(1)}, f32[19,4,4,128]{3,2,1,0:T(4,128)S(1)}) fusion(f32[19,8,32,128]{3,2,1,0:T(8,128)} %refs_0_.1), kind=kLoop, calls=%fused_computation.72 | loop fusion | bytes 1245184 | tf_op jit(solution)/shard_map/slice | solution.py:266
  3.1 0.8 slice_bitcast_fusion.7
  4.0 1.2 %collective-permute-start.4 = (f32[21,4,4,128]{3,2,1,0:T(4,128)S(1)}, f32[21,4,4,128]{3,2,1,0:T(4,128)S(1)}, u32[]{:S(2)}, u32[]{:S(2)}) collective-permute-start(f32[21,4,4,128]{3,2,1,0:T(4,128)S(1)} %pad_maximum_fusion.7), channel_id=1, source_target_pairs={{0,17},{1,18},{2,19},{3,20},{4,21},{5,22},{6,23},{7,24},{8,25},{9,... | collective-permute-start | bytes 516104 | tf_op jit(solution)/shard_map/ppermute | solution.py:251
  5.2 4.0 %collective-permute-start.5 = (f32[21,4,4,128]{3,2,1,0:T(4,128)S(1)}, f32[21,4,4,128]{3,2,1,0:T(4,128)S(1)}, u32[]{:S(2)}, u32[]{:S(2)}) collective-permute-start(f32[21,4,4,128]{3,2,1,0:T(4,128)S(1)} %pad_maximum_fusion.8), channel_id=1, source_target_pairs={{0,113},{1,114},{2,115},{3,116},{4,117},{5,118},{6,119},{7,120},{8... | collective-permute-start | bytes 516104 | tf_op jit(solution)/shard_map/ppermute | solution.py:251
  9.3 0.2 fusion.24
  9.5 0.5 copy-done.4
  10.0 0.1 pad_maximum_fusion
  10.2 0.1 pad_maximum_fusion.1
  10.3 2.9 %collective-permute-start.1 = (f32[21,4,32,128]{3,2,1,0:T(8,128)S(1)}, f32[21,4,32,128]{3,2,1,0:T(8,128)}, u32[]{:S(2)}, u32[]{:S(2)}) collective-permute-start(f32[21,4,32,128]{3,2,1,0:T(8,128)S(1)} %pad_maximum_fusion.1), channel_id=1, source_target_pairs={{0,112},{16,0},{32,16},{48,32},{64,48},{80,64},{96,80},{112,96},{1... | collective-permute-start | bytes 4128776 | tf_op jit(solution)/shard_map/ppermute | solution.py:244
  13.3 1.0 %collective-permute-start.6 = (f32[21,4,4,128]{3,2,1,0:T(4,128)S(1)}, f32[21,4,4,128]{3,2,1,0:T(4,128)S(1)}, u32[]{:S(2)}, u32[]{:S(2)}) collective-permute-start(f32[21,4,4,128]{3,2,1,0:T(4,128)S(1)} %pad_maximum_fusion.9), channel_id=1, source_target_pairs={{0,31},{1,16},{2,17},{3,18},{4,19},{5,20},{6,21},{7,22},{8,23},{9,... | collective-permute-start | bytes 516104 | tf_op jit(solution)/shard_map/ppermute | solution.py:251
  14.4 0.2 fusion.23
  14.5 0.1 pad_maximum_fusion.5
  14.6 0.1 pad_maximum_fusion.6
  14.7 1.7 %collective-permute-done.4.refs_6_ = f32[21,4,4,128]{3,2,1,0:T(4,128)S(1)} collective-permute-done((f32[21,4,4,128]{3,2,1,0:T(4,128)S(1)}, f32[21,4,4,128]{3,2,1,0:T(4,128)S(1)}, u32[]{:S(2)}, u32[]{:S(2)}) %collective-permute-start.4) | collective-permute-done | bytes 172064 | tf_op jit(solution)/shard_map/ppermute | solution.py:251
  16.5 2.0 %collective-permute-done.5.refs_7_ = f32[21,4,4,128]{3,2,1,0:T(4,128)S(1)} collective-permute-done((f32[21,4,4,128]{3,2,1,0:T(4,128)S(1)}, f32[21,4,4,128]{3,2,1,0:T(4,128)S(1)}, u32[]{:S(2)}, u32[]{:S(2)}) %collective-permute-start.5) | collective-permute-done | bytes 172064 | tf_op jit(solution)/shard_map/ppermute | solution.py:251
  18.5 3.4 %collective-permute-start.3 = (f32[21,8,4,128]{3,2,1,0:T(4,128)S(1)}, f32[21,8,4,128]{3,2,1,0:T(4,128)S(1)}, u32[]{:S(2)}, u32[]{:S(2)}) collective-permute-start(f32[21,8,4,128]{3,2,1,0:T(4,128)S(1)} %pad_maximum_fusion.6), channel_id=1, source_target_pairs={{0,15},{1,0},{2,1},{3,2},{4,3},{5,4},{6,5},{7,6},{8,7},{9,8},{10,9... | collective-permute-start | bytes 1032200 | tf_op jit(solution)/shard_map/ppermute | solution.py:246
  21.9 9.8 %collective-permute-done.6.refs_8_ = f32[21,4,4,128]{3,2,1,0:T(4,128)S(1)} collective-permute-done((f32[21,4,4,128]{3,2,1,0:T(4,128)S(1)}, f32[21,4,4,128]{3,2,1,0:T(4,128)S(1)}, u32[]{:S(2)}, u32[]{:S(2)}) %collective-permute-start.6) | collective-permute-done | bytes 172064 | tf_op jit(solution)/shard_map/ppermute | solution.py:251
  31.7 1.8 %collective-permute-start.7 = (f32[21,4,4,128]{3,2,1,0:T(4,128)S(1)}, f32[21,4,4,128]{3,2,1,0:T(4,128)S(1)}, u32[]{:S(2)}, u32[]{:S(2)}) collective-permute-start(f32[21,4,4,128]{3,2,1,0:T(4,128)S(1)} %pad_maximum_fusion.10), channel_id=1, source_target_pairs={{0,127},{1,112},{2,113},{3,114},{4,115},{5,116},{6,117},{7,118},{8... | collective-permute-start | bytes 516104 | tf_op jit(solution)/shard_map/ppermute | solution.py:251
  33.4 3.6 %collective-permute-done.7.refs_9_ = f32[21,4,4,128]{3,2,1,0:T(4,128)S(1)} collective-permute-done((f32[21,4,4,128]{3,2,1,0:T(4,128)S(1)}, f32[21,4,4,128]{3,2,1,0:T(4,128)S(1)}, u32[]{:S(2)}, u32[]{:S(2)}) %collective-permute-start.7) | collective-permute-done | bytes 172064 | tf_op jit(solution)/shard_map/ppermute | solution.py:251
  37.1 0.6 copy-done.8
  37.7 0.1 copy-done.2
  37.8 0.1 copy-done.3
  37.9 0.4 copy-done.1
  38.4 18.3 %shard_map.50 = (f32[19,8,32,128]{3,2,1,0:T(8,128)}, f32[3,4,64,16]{3,2,1,0:T(8,128)}, f32[4,32,128]{2,1,0:T(8,128)}, f32[4,32,128]{2,1,0:T(8,128)}, f32[8,4,128...) custom-call(f32[19,8,32,128]{3,2,1,0:T(8,128)} %refs_0_.1, ...), custom_call_target="tpu_custom_call" | custom-call | flops 78643200 | bytes 9961472 | tf_op jit(solution)/shard_map/pallas_call | solution.py:229
  56.6 0.8 slice.310
  57.4 0.8 slice.308
  58.2 0.7 slice.304
  58.9 0.7 slice.305
  59.7 0.7 slice.297
  60.4 0.7 slice.298
  61.1 1.2 %pad_maximum_fusion.4 = (f32[3,4,64,16]{3,2,1,0:T(8,128)S(1)}, f32[3,4,64,16]{3,2,1,0:T(8,128)S(1)}) fusion(f32[3,4,64,16]{3,2,1,0:T(8,128)} %get-tuple-element.21, f32[3,4,2,16]{3,2,1,0:T(2,128)S(1)} %slice.308, f32[3,4,4,16]{3,2,1,0:T(4,128)S(1)} %slice.310), kind=kLoop, calls=%fused_computation.4 | loop fusion | flops 24576 | bytes 152064 | tf_op jit(solution)/shard_map/concatenate | solution.py:302
  62.4 0.2 copy_bitcast_fusion
  62.6 0.9 %reshape.127 = f32[16,1,1536]{2,1,0:T(1,128)} reshape(f32[16,3,4,8,16]{4,3,2,1,0:T(8,128)S(1)} %copy_bitcast_fusion) | data formatting | bytes 196608
  63.5 9.3 %all-to-all-start = ((f32[16,1,1536]{2,1,0:T(1,128)}), f32[16,1,1536]{2,1,0:T(1,128)S(1)}, u32[]{:S(2)}, u32[]{:S(2)}) async-start(f32[16,1,1536]{2,1,0:T(1,128)} %reshape.127), calls=%async_computation | async-start | bytes 196608 | tf_op jit(solution)/shard_map/all_to_all | solution.py:306
  73.1 7.5 %all-to-all-done = f32[16,1,1536]{2,1,0:T(1,128)S(1)} async-done(((f32[16,1,1536]{2,1,0:T(1,128)}), f32[16,1,1536]{2,1,0:T(1,128)S(1)}, u32[]{:S(2)}, u32[]{:S(2)}) %all-to-all-start) | async-done | bytes 98336 | tf_op jit(solution)/shard_map/all_to_all | solution.py:306
  80.7 0.5 broadcast.20
  81.2 0.9 reduce
  82.1 0.3 reshape.128
  82.4 0.5 copy.39
  82.9 0.3 squeeze.12
  83.2 2.9 %collective-permute-start.9 = (f32[3,2,8,256]{3,2,1,0:T(8,128)S(1)}, f32[3,2,8,256]{3,2,1,0:T(8,128)S(1)}, u32[]{:S(2)}, u32[]{:S(2)}) collective-permute-start(f32[3,2,8,256]{3,2,1,0:T(8,128)S(1)} %get-tuple-element.52), channel_id=1, source_target_pairs={{0,112},{16,0},{32,16},{48,32},{64,48},{80,64},{96,80},{112,96},{1... | collective-permute-start | bytes 147464 | tf_op jit(solution)/shard_map/ppermute | solution.py:244
  86.2 1.8 %collective-permute-done.8 = f32[3,2,8,256]{3,2,1,0:T(8,128)S(1)} collective-permute-done((f32[3,2,8,256]{3,2,1,0:T(8,128)S(1)}, f32[3,2,8,256]{3,2,1,0:T(8,128)S(1)}, u32[]{:S(2)}, u32[]{:S(2)}) %collective-permute-start.8) | collective-permute-done | bytes 49184 | tf_op jit(solution)/shard_map/ppermute | solution.py:244
  88.2 0.1 fusion.29
  88.4 0.1 slice_multiply_fusion.1
  88.7 0.1 fusion.32
  88.8 0.1 fusion.13
  88.9 0.6 copy.40
  (88 shorter events, 1.3 us)
Async XLA Ops:
  0.6 8.6 %copy-start = (f32[19,8,32,128]{3,2,1,0:T(8,128)S(1)}, f32[19,8,32,128]{3,2,1,0:T(8,128)}, u32[]{:S(2)}) copy-start(f32[19,8,32,128]{3,2,1,0:T(8,128)} %refs_0_.1) | copy-start | bytes 7471108
  4.0 12.5 %collective-permute-start.4 = (f32[21,4,4,128]{3,2,1,0:T(4,128)S(1)}, f32[21,4,4,128]{3,2,1,0:T(4,128)S(1)}, u32[]{:S(2)}, u32[]{:S(2)}) collective-permute-start(f32[21,4,4,128]{3,2,1,0:T(4,128)S(1)} %pad_maximum_fusion.7), channel_id=1, source_target_pairs={{0,17},{1,18},{2,19},{3,20},{4,21},{5,22},{6,23},{7,24},{8,25},{9,... | collective-permute-start | bytes 516104 | tf_op jit(solution)/shard_map/ppermute | solution.py:251
  5.2 13.2 %collective-permute-start.5 = (f32[21,4,4,128]{3,2,1,0:T(4,128)S(1)}, f32[21,4,4,128]{3,2,1,0:T(4,128)S(1)}, u32[]{:S(2)}, u32[]{:S(2)}) collective-permute-start(f32[21,4,4,128]{3,2,1,0:T(4,128)S(1)} %pad_maximum_fusion.8), channel_id=1, source_target_pairs={{0,113},{1,114},{2,115},{3,116},{4,117},{5,118},{6,119},{7,120},{8... | collective-permute-start | bytes 516104 | tf_op jit(solution)/shard_map/ppermute | solution.py:251
  9.3 0.7 copy-start.4
  10.1 26.9 %collective-permute-start = (f32[21,4,32,128]{3,2,1,0:T(8,128)S(1)}, f32[21,4,32,128]{3,2,1,0:T(8,128)S(1)}, u32[]{:S(2)}, u32[]{:S(2)}) collective-permute-start(f32[21,4,32,128]{3,2,1,0:T(8,128)S(1)} %pad_maximum_fusion), channel_id=1, source_target_pairs={{0,16},{16,32},{32,48},{48,64},{64,80},{80,96},{96,112},{112,0},{1... | collective-permute-start | bytes 4128776 | tf_op jit(solution)/shard_map/ppermute | solution.py:244
  10.3 26.7 %collective-permute-start.1 = (f32[21,4,32,128]{3,2,1,0:T(8,128)S(1)}, f32[21,4,32,128]{3,2,1,0:T(8,128)}, u32[]{:S(2)}, u32[]{:S(2)}) collective-permute-start(f32[21,4,32,128]{3,2,1,0:T(8,128)S(1)} %pad_maximum_fusion.1), channel_id=1, source_target_pairs={{0,112},{16,0},{32,16},{48,32},{64,48},{80,64},{96,80},{112,96},{1... | collective-permute-start | bytes 4128776 | tf_op jit(solution)/shard_map/ppermute | solution.py:244
  13.3 18.4 %collective-permute-start.6 = (f32[21,4,4,128]{3,2,1,0:T(4,128)S(1)}, f32[21,4,4,128]{3,2,1,0:T(4,128)S(1)}, u32[]{:S(2)}, u32[]{:S(2)}) collective-permute-start(f32[21,4,4,128]{3,2,1,0:T(4,128)S(1)} %pad_maximum_fusion.9), channel_id=1, source_target_pairs={{0,31},{1,16},{2,17},{3,18},{4,19},{5,20},{6,21},{7,22},{8,23},{9,... | collective-permute-start | bytes 516104 | tf_op jit(solution)/shard_map/ppermute | solution.py:251
  16.5 20.6 %copy-start.5 = (f32[21,4,4,128]{3,2,1,0:T(4,128)}, f32[21,4,4,128]{3,2,1,0:T(4,128)S(1)}, u32[]{:S(2)}) copy-start(f32[21,4,4,128]{3,2,1,0:T(4,128)S(1)} %collective-permute-done.4.refs_6_) | copy-start | bytes 516100
  16.5 20.5 %collective-permute-start.2 = (f32[21,8,4,128]{3,2,1,0:T(4,128)S(1)}, f32[21,8,4,128]{3,2,1,0:T(4,128)S(1)}, u32[]{:S(2)}, u32[]{:S(2)}) collective-permute-start(f32[21,8,4,128]{3,2,1,0:T(4,128)S(1)} %pad_maximum_fusion.5), channel_id=1, source_target_pairs={{0,1},{1,2},{2,3},{3,4},{4,5},{5,6},{6,7},{7,8},{8,9},{9,10},{10,1... | collective-permute-start | bytes 1032200 | tf_op jit(solution)/shard_map/ppermute | solution.py:246
  18.5 18.6 %copy-start.6 = (f32[21,4,4,128]{3,2,1,0:T(4,128)}, f32[21,4,4,128]{3,2,1,0:T(4,128)S(1)}, u32[]{:S(2)}) copy-start(f32[21,4,4,128]{3,2,1,0:T(4,128)S(1)} %collective-permute-done.5.refs_7_) | copy-start | bytes 516100
  18.5 18.5 %collective-permute-start.3 = (f32[21,8,4,128]{3,2,1,0:T(4,128)S(1)}, f32[21,8,4,128]{3,2,1,0:T(4,128)S(1)}, u32[]{:S(2)}, u32[]{:S(2)}) collective-permute-start(f32[21,8,4,128]{3,2,1,0:T(4,128)S(1)} %pad_maximum_fusion.6), channel_id=1, source_target_pairs={{0,15},{1,0},{2,1},{3,2},{4,3},{5,4},{6,5},{7,6},{8,7},{9,8},{10,9... | collective-permute-start | bytes 1032200 | tf_op jit(solution)/shard_map/ppermute | solution.py:246
  31.7 5.4 %copy-start.7 = (f32[21,4,4,128]{3,2,1,0:T(4,128)}, f32[21,4,4,128]{3,2,1,0:T(4,128)S(1)}, u32[]{:S(2)}) copy-start(f32[21,4,4,128]{3,2,1,0:T(4,128)S(1)} %collective-permute-done.6.refs_8_) | copy-start | bytes 516100
  31.7 5.3 %collective-permute-start.7 = (f32[21,4,4,128]{3,2,1,0:T(4,128)S(1)}, f32[21,4,4,128]{3,2,1,0:T(4,128)S(1)}, u32[]{:S(2)}, u32[]{:S(2)}) collective-permute-start(f32[21,4,4,128]{3,2,1,0:T(4,128)S(1)} %pad_maximum_fusion.10), channel_id=1, source_target_pairs={{0,127},{1,112},{2,113},{3,114},{4,115},{5,116},{6,117},{7,118},{8... | collective-permute-start | bytes 516104 | tf_op jit(solution)/shard_map/ppermute | solution.py:251
  37.0 0.7 copy-start.8
  37.0 0.8 copy-start.2
  37.0 0.9 %copy-start.3 = (f32[21,8,4,128]{3,2,1,0:T(4,128)}, f32[21,8,4,128]{3,2,1,0:T(4,128)S(1)}, u32[]{:S(2)}) copy-start(f32[21,8,4,128]{3,2,1,0:T(4,128)S(1)} %collective-permute-done.3.refs_5_) | copy-start | bytes 1032196
  37.0 1.3 %copy-start.1 = (f32[21,4,32,128]{3,2,1,0:T(8,128)}, f32[21,4,32,128]{3,2,1,0:T(8,128)S(1)}, u32[]{:S(2)}) copy-start(f32[21,4,32,128]{3,2,1,0:T(8,128)S(1)} %collective-permute-done.refs_2_) | copy-start | bytes 4128772
  62.3 10.5 %copy-start.10 = (f32[4,32,128]{2,1,0:T(8,128)S(1)}, f32[4,32,128]{2,1,0:T(8,128)}, u32[]{:S(2)}) copy-start(f32[4,32,128]{2,1,0:T(8,128)} %get-tuple-element.16) | copy-start | bytes 196612
  62.3 10.6 %copy-start.9 = (f32[4,32,128]{2,1,0:T(8,128)S(1)}, f32[4,32,128]{2,1,0:T(8,128)}, u32[]{:S(2)}) copy-start(f32[4,32,128]{2,1,0:T(8,128)} %get-tuple-element.17) | copy-start | bytes 196612
  62.3 10.7 %copy-start.12 = (f32[4,4,128]{2,1,0:T(4,128)S(1)}, f32[4,4,128]{2,1,0:T(4,128)}, u32[]{:S(2)}) copy-start(f32[4,4,128]{2,1,0:T(4,128)} %get-tuple-element.15) | copy-start | bytes 24580
  62.3 10.8 %copy-start.11 = (f32[4,4,128]{2,1,0:T(4,128)S(1)}, f32[4,4,128]{2,1,0:T(4,128)}, u32[]{:S(2)}) copy-start(f32[4,4,128]{2,1,0:T(4,128)} %get-tuple-element.20) | copy-start | bytes 24580
  63.5 17.2 %all-to-all-start = ((f32[16,1,1536]{2,1,0:T(1,128)}), f32[16,1,1536]{2,1,0:T(1,128)S(1)}, u32[]{:S(2)}, u32[]{:S(2)}) async-start(f32[16,1,1536]{2,1,0:T(1,128)} %reshape.127), calls=%async_computation | async-start | bytes 196608 | tf_op jit(solution)/shard_map/all_to_all | solution.py:306
  83.2 4.7 %collective-permute-start.8 = (f32[3,2,8,256]{3,2,1,0:T(8,128)S(1)}, f32[3,2,8,256]{3,2,1,0:T(8,128)S(1)}, u32[]{:S(2)}, u32[]{:S(2)}) collective-permute-start(f32[3,2,8,256]{3,2,1,0:T(8,128)S(1)} %get-tuple-element.51), channel_id=1, source_target_pairs={{0,16},{16,32},{32,48},{48,64},{64,80},{80,96},{96,112},{112,0},{1... | collective-permute-start | bytes 147464 | tf_op jit(solution)/shard_map/ppermute | solution.py:244
  83.2 4.7 %collective-permute-start.9 = (f32[3,2,8,256]{3,2,1,0:T(8,128)S(1)}, f32[3,2,8,256]{3,2,1,0:T(8,128)S(1)}, u32[]{:S(2)}, u32[]{:S(2)}) collective-permute-start(f32[3,2,8,256]{3,2,1,0:T(8,128)S(1)} %get-tuple-element.52), channel_id=1, source_target_pairs={{0,112},{16,0},{32,16},{48,32},{64,48},{80,64},{96,80},{112,96},{1... | collective-permute-start | bytes 147464 | tf_op jit(solution)/shard_map/ppermute | solution.py:244

commit v8 on v3

--- a/solution.py
+++ b/solution.py
@@ -250,7 +250,6 @@
 def lattice_halos(g0, mask, conc, h, w):
     _, nx, ny, nz = g0.shape
     nzc, nxc, nyc = conc.shape
-    maskf = mask.astype(jnp.float32)[None]
     lat = {1: slice(nx - h, nx), -1: slice(0, h), 0: slice(0, nx)}
     lat_y = {1: slice(ny - h, ny), -1: slice(0, h), 0: slice(0, ny)}
     trc_x = {1: slice(nxc - w, nxc), -1: slice(0, w), 0: slice(0, nxc)}
@@ -259,7 +258,7 @@
     pieces, tracer_pieces = [], []
     for dv, db in order:
         xs, ys = lat[dv], lat_y[db]
-        lb = jnp.concatenate([g0[:, xs, ys], maskf[:, xs, ys]], axis=0)
+        lb = jnp.concatenate([g0[:, xs, ys], mask[None, xs, ys].astype(jnp.float32)], axis=0)
         tp = conc[trc_z[db], trc_x[dv]]
         plane = lb.shape[1] * lb.shape[2] * nz
         flat = jnp.pad(tp.reshape(-1), (0, plane - tp.size))

time: 84.3 us -> 84.1 us (level)
    broadcast_in_dim x1 -> x0, other arithmetic: 0.92 us -> none  [lattice_halos(): maskf = mask.astype(jnp.float32)[None]]
    slice x6 -> x3, local copies, waits for them, and re-layouts: 1.97 us -> 1.8 us  [lattice_halos(): g0[:, xs, ys]]
    unnamed x36 -> x38, local copies, waits for them, and re-layouts: 3.45 us -> 3.57 us
where the time goes in v8:
time: 84.1 us; the launch traced here: 82.9 us
  starting transfers between devices  30.3 us (36%)
  Pallas kernels  18.3 us (22%)
  waiting for transfers between devices  16.1 us (19%)
  local copies, waits for them, and re-layouts  10.9 us (13%)
  other arithmetic  6.12 us (7%)
  between operations  1.18 us (1%)
    pallas_call x1, Pallas kernels, lb_call(): pl.pallas_call(functools.partial(lb_kernel, halo, nx, ny), out_shape=out_...  18.3 us
    ppermute x4, starting transfers between devices, send(): return lax.ppermute(x, ('vessel', 'blk'), pairs)  10.7 us
    ppermute x4, starting transfers between devices, send(): return lax.ppermute(x, 'vessel', [(i, (i + dv) % nv) for i in range(nv)])  8.03 us
    ppermute x4, waiting for transfers between devices, send(): return lax.ppermute(x, ('vessel', 'blk'), pairs)  7.47 us
    all_to_all x1, waiting for transfers between devices, local(): lax.all_to_all(windows, 'blk', split_axis=2, concat_axis=4, tiled=True)  6.89 us
    all_to_all x1, starting transfers between devices, local(): lax.all_to_all(windows, 'blk', split_axis=2, concat_axis=4, tiled=True)  6.13 us
    ppermute x2, starting transfers between devices, send(): return lax.ppermute(x, 'blk', [(i, (i + db) % nb) for i in range(nb)])  5.45 us
    unnamed x38, local copies, waits for them, and re-layouts  3.57 us
  transfers between devices with their start and end apart: 11, of which 3 were waited for; matrix products, arithmetic and copies ran while one was open for 5% of the time, Pallas kernels for 0%

profile of v8, /device:TPU:0, one launch (start us, length us, event | category | flops | bytes accessed | tf_op | source)
XLA Modules:
  0.0 82.9 jit_solution(4462895004312075630)
XLA Ops:
  0.7 0.9 %slice_bitcast_fusion.7 = (f32[2,2,2,128]{3,2,1,0:T(2,128)S(1)}, f32[2,2,2,128]{3,2,1,0:T(2,128)S(1)}, f32[2,2,2,128]{3,2,1,0:T(2,128)S(1)}, f32[2,2,2,128]{3,2,1,0:T(2,128)S(1)}) fusion(f32[4,4,256]{2,1,0:T(4,128)} %param.5), kind=kLoop, calls=%fused_computation.73 | loop fusion | bytes 32768
  1.6 0.8 convert_bitcast_fusion.4
  2.4 1.4 %fusion.22 = (f32[19,4,4,128]{3,2,1,0:T(4,128)S(1)}, f32[19,4,4,128]{3,2,1,0:T(4,128)S(1)}, f32[19,4,4,128]{3,2,1,0:T(4,128)S(1)}, f32[19,4,4,128]{3,2,1,0:T(4,128)S(1)}) fusion(f32[19,8,32,128]{3,2,1,0:T(8,128)} %refs_0_.1), kind=kLoop, calls=%fused_computation.79 | loop fusion | bytes 1245184 | tf_op jit(solution)/shard_map/slice | solution.py:261
  3.8 1.2 %collective-permute-start.4 = (f32[21,4,4,128]{3,2,1,0:T(4,128)S(1)}, f32[21,4,4,128]{3,2,1,0:T(4,128)S(1)}, u32[]{:S(2)}, u32[]{:S(2)}) collective-permute-start(f32[21,4,4,128]{3,2,1,0:T(4,128)S(1)} %pad_maximum_fusion.7), channel_id=1, source_target_pairs={{0,17},{1,18},{2,19},{3,20},{4,21},{5,22},{6,23},{7,24},{8,25},{9,... | collective-permute-start | bytes 516104 | tf_op jit(solution)/shard_map/ppermute | solution.py:247
  5.1 4.0 %collective-permute-start.5 = (f32[21,4,4,128]{3,2,1,0:T(4,128)S(1)}, f32[21,4,4,128]{3,2,1,0:T(4,128)S(1)}, u32[]{:S(2)}, u32[]{:S(2)}) collective-permute-start(f32[21,4,4,128]{3,2,1,0:T(4,128)S(1)} %pad_maximum_fusion.8), channel_id=1, source_target_pairs={{0,113},{1,114},{2,115},{3,116},{4,117},{5,118},{6,119},{7,120},{8... | collective-permute-start | bytes 516104 | tf_op jit(solution)/shard_map/ppermute | solution.py:247
  9.2 1.2 %collective-permute-start.6 = (f32[21,4,4,128]{3,2,1,0:T(4,128)S(1)}, f32[21,4,4,128]{3,2,1,0:T(4,128)S(1)}, u32[]{:S(2)}, u32[]{:S(2)}) collective-permute-start(f32[21,4,4,128]{3,2,1,0:T(4,128)S(1)} %pad_maximum_fusion.9), channel_id=1, source_target_pairs={{0,31},{1,16},{2,17},{3,18},{4,19},{5,20},{6,21},{7,22},{8,23},{9,... | collective-permute-start | bytes 516104 | tf_op jit(solution)/shard_map/ppermute | solution.py:247
  10.4 0.2 fusion.24
  10.6 1.2 %pad_maximum_fusion = f32[21,4,32,128]{3,2,1,0:T(8,128)} fusion(f32[1,4,32,128]{3,2,1,0:T(8,128)S(1)} %bitcast.81, f32[1,4,32,128]{3,2,1,0:T(8,128)S(1)} %get-tuple-element.34, f32[19,4,32,128]{3,2,1,0:T(8,128)S(1)} %get-tuple-element.19), kind=kLoop, calls=%fused_computation | loop fusion | flops 688128 | bytes 2752512 | tf_op jit(solution)/shard_map/concatenate | solution.py:265
  11.8 2.5 %collective-permute-start = (f32[21,4,32,128]{3,2,1,0:T(8,128)}, f32[21,4,32,128]{3,2,1,0:T(8,128)}, u32[]{:S(2)}, u32[]{:S(2)}) collective-permute-start(f32[21,4,32,128]{3,2,1,0:T(8,128)} %pad_maximum_fusion), channel_id=1, source_target_pairs={{0,16},{16,32},{32,48},{48,64},{64,80},{80,96},{96,112},{112,0},{1... | collective-permute-start | bytes 4128776 | tf_op jit(solution)/shard_map/ppermute | solution.py:240
  14.3 1.2 %pad_maximum_fusion.1 = f32[21,4,32,128]{3,2,1,0:T(8,128)} fusion(f32[1,4,32,128]{3,2,1,0:T(8,128)S(1)} %bitcast.80, f32[1,4,32,128]{3,2,1,0:T(8,128)S(1)} %get-tuple-element.33, f32[19,4,32,128]{3,2,1,0:T(8,128)S(1)} %get-tuple-element.18), kind=kLoop, calls=%fused_computation.1 | loop fusion | flops 688128 | bytes 2752512 | tf_op jit(solution)/shard_map/concatenate | solution.py:265
  15.5 2.6 %collective-permute-start.1 = (f32[21,4,32,128]{3,2,1,0:T(8,128)}, f32[21,4,32,128]{3,2,1,0:T(8,128)}, u32[]{:S(2)}, u32[]{:S(2)}) collective-permute-start(f32[21,4,32,128]{3,2,1,0:T(8,128)} %pad_maximum_fusion.1), channel_id=1, source_target_pairs={{0,112},{16,0},{32,16},{48,32},{64,48},{80,64},{96,80},{112,96},{1... | collective-permute-start | bytes 4128776 | tf_op jit(solution)/shard_map/ppermute | solution.py:240
  18.1 0.2 fusion.23
  18.4 4.3 %collective-permute-start.7 = (f32[21,4,4,128]{3,2,1,0:T(4,128)S(1)}, f32[21,4,4,128]{3,2,1,0:T(4,128)S(1)}, u32[]{:S(2)}, u32[]{:S(2)}) collective-permute-start(f32[21,4,4,128]{3,2,1,0:T(4,128)S(1)} %pad_maximum_fusion.10), channel_id=1, source_target_pairs={{0,127},{1,112},{2,113},{3,114},{4,115},{5,116},{6,117},{7,118},{8... | collective-permute-start | bytes 516104 | tf_op jit(solution)/shard_map/ppermute | solution.py:247
  22.7 0.1 pad_maximum_fusion.6
  22.9 0.1 pad_maximum_fusion.5
  23.0 0.1 collective-permute-start.2
  23.1 5.4 %collective-permute-start.3 = (f32[21,8,4,128]{3,2,1,0:T(4,128)S(1)}, f32[21,8,4,128]{3,2,1,0:T(4,128)S(1)}, u32[]{:S(2)}, u32[]{:S(2)}) collective-permute-start(f32[21,8,4,128]{3,2,1,0:T(4,128)S(1)} %pad_maximum_fusion.6), channel_id=1, source_target_pairs={{0,15},{1,0},{2,1},{3,2},{4,3},{5,4},{6,5},{7,6},{8,7},{9,8},{10,9... | collective-permute-start | bytes 1032200 | tf_op jit(solution)/shard_map/ppermute | solution.py:242
  28.5 7.5 %collective-permute-done.7.refs_9_ = f32[21,4,4,128]{3,2,1,0:T(4,128)S(1)} collective-permute-done((f32[21,4,4,128]{3,2,1,0:T(4,128)S(1)}, f32[21,4,4,128]{3,2,1,0:T(4,128)S(1)}, u32[]{:S(2)}, u32[]{:S(2)}) %collective-permute-start.7) | collective-permute-done | bytes 172064 | tf_op jit(solution)/shard_map/ppermute | solution.py:247
  36.2 0.5 copy-done.8
  36.7 0.1 copy-done.2
  36.8 0.1 copy-done.3
  36.9 18.3 %shard_map.50 = (f32[19,8,32,128]{3,2,1,0:T(8,128)}, f32[3,4,64,16]{3,2,1,0:T(8,128)}) custom-call(f32[19,8,32,128]{3,2,1,0:T(8,128)} %refs_0_.1, s32[8,32,128]{2,1,0:T(8,128)} %refs_1_.1, f32[21,4,32,128]{3,2,1,0:T(8,128)} %collective-permute-done.refs_2_, f32[21,4,32,128]{3,2,1,0:T(8,128)} %collective-permute-done.1.refs_3_, f32[21,8,4,128]{3,2,1,0:T(4,128)} %copy-done.2, ...), custom_call_target="tpu_custom_call" | custom-call | flops 78643200 | bytes 9961472 | tf_op jit(solution)/shard_map/pallas_call | solution.py:225
  55.2 0.8 slice.328
  56.0 0.8 slice.330
  56.8 0.8 %slice.377 = f32[1,4,32,128]{3,2,1,0:T(8,128)S(1)} slice(f32[21,4,32,128]{3,2,1,0:T(8,128)} %collective-permute-done.refs_2_), slice={[20:21], [0:4], [0:32], [0:128]} | slice | bytes 131072 | tf_op jit(solution)/shard_map/slice | solution.py:268
  57.7 1.2 %pad_maximum_fusion.4 = (f32[3,4,64,16]{3,2,1,0:T(8,128)S(1)}, f32[3,4,64,16]{3,2,1,0:T(8,128)S(1)}) fusion(f32[3,4,64,16]{3,2,1,0:T(8,128)} %get-tuple-element.5, f32[3,4,2,16]{3,2,1,0:T(2,128)S(1)} %slice.328, f32[3,4,4,16]{3,2,1,0:T(4,128)S(1)} %slice.330), kind=kLoop, calls=%fused_computation.4 | loop fusion | flops 24576 | bytes 152064 | tf_op jit(solution)/shard_map/concatenate | solution.py:297
  58.9 0.2 copy_bitcast_fusion
  59.1 1.0 %reshape.127 = f32[16,1,1536]{2,1,0:T(1,128)} reshape(f32[16,3,4,8,16]{4,3,2,1,0:T(8,128)S(1)} %copy_bitcast_fusion) | data formatting | bytes 196608
  60.1 6.1 %all-to-all-start = ((f32[16,1,1536]{2,1,0:T(1,128)}), f32[16,1,1536]{2,1,0:T(1,128)S(1)}, u32[]{:S(2)}, u32[]{:S(2)}) async-start(f32[16,1,1536]{2,1,0:T(1,128)} %reshape.127), calls=%async_computation | async-start | bytes 196608 | tf_op jit(solution)/shard_map/all_to_all | solution.py:301
  66.2 0.8 %slice.379 = f32[1,4,32,128]{3,2,1,0:T(8,128)S(1)} slice(f32[21,4,32,128]{3,2,1,0:T(8,128)} %collective-permute-done.1.refs_3_), slice={[20:21], [0:4], [0:32], [0:128]} | slice | bytes 131072 | tf_op jit(solution)/shard_map/slice | solution.py:268
  67.2 6.9 %all-to-all-done = f32[16,1,1536]{2,1,0:T(1,128)S(1)} async-done(((f32[16,1,1536]{2,1,0:T(1,128)}), f32[16,1,1536]{2,1,0:T(1,128)S(1)}, u32[]{:S(2)}, u32[]{:S(2)}) %all-to-all-start) | async-done | bytes 98336 | tf_op jit(solution)/shard_map/all_to_all | solution.py:301
  74.0 0.5 broadcast.20
  74.6 0.9 %reduce = f32[16,1536]{1,0:T(8,128)S(1)} reduce(f32[16,1,1536]{2,1,0:T(1,128)S(1)} %all-to-all-done, f32[]{:T(128)} %broadcast.20), dimensions={1}, to_apply=%all_to_all.11.reduce_sub_computation | reduce | bytes 196612 | tf_op jit(solution)/shard_map/all_to_all | solution.py:301
  75.4 0.3 reshape.128
  75.8 0.5 copy.39
  76.2 0.3 squeeze.12
  76.6 2.9 %collective-permute-start.9 = (f32[3,2,8,256]{3,2,1,0:T(8,128)S(1)}, f32[3,2,8,256]{3,2,1,0:T(8,128)S(1)}, u32[]{:S(2)}, u32[]{:S(2)}) collective-permute-start(f32[3,2,8,256]{3,2,1,0:T(8,128)S(1)} %get-tuple-element.36), channel_id=1, source_target_pairs={{0,112},{16,0},{32,16},{48,32},{64,48},{80,64},{96,80},{112,96},{1... | collective-permute-start | bytes 147464 | tf_op jit(solution)/shard_map/ppermute | solution.py:240
  79.6 1.8 %collective-permute-done.8 = f32[3,2,8,256]{3,2,1,0:T(8,128)S(1)} collective-permute-done((f32[3,2,8,256]{3,2,1,0:T(8,128)S(1)}, f32[3,2,8,256]{3,2,1,0:T(8,128)S(1)}, u32[]{:S(2)}, u32[]{:S(2)}) %collective-permute-start.8) | collective-permute-done | bytes 49184 | tf_op jit(solution)/shard_map/ppermute | solution.py:240
  81.4 0.1 fusion.31
  81.5 0.1 fusion.30
  81.6 0.1 fusion.27
  81.7 0.1 fusion.26
  81.7 0.1 slice_multiply_fusion.1
  82.0 0.1 fusion.33
  82.0 0.1 fusion.28
  82.1 0.1 fusion.29
  82.2 0.1 fusion.13
  82.3 0.6 copy.40
  (81 shorter events, 0.8 us)
Async XLA Ops:
  0.6 9.7 %copy-start.4 = (f32[4,4,256]{2,1,0:T(4,128)S(1)}, f32[4,4,256]{2,1,0:T(4,128)}, u32[]{:S(2)}) copy-start(f32[4,4,256]{2,1,0:T(4,128)} %param.5) | copy-start | bytes 49156
  0.6 9.7 %copy-start.1 = (s32[8,32,128]{2,1,0:T(8,128)S(1)}, s32[8,32,128]{2,1,0:T(8,128)}, u32[]{:S(2)}) copy-start(s32[8,32,128]{2,1,0:T(8,128)} %refs_1_.1) | copy-start | bytes 393220
  0.7 9.7 %copy-start = (f32[19,8,32,128]{3,2,1,0:T(8,128)S(1)}, f32[19,8,32,128]{3,2,1,0:T(8,128)}, u32[]{:S(2)}) copy-start(f32[19,8,32,128]{3,2,1,0:T(8,128)} %refs_0_.1) | copy-start | bytes 7471108
  3.8 14.5 %collective-permute-start.4 = (f32[21,4,4,128]{3,2,1,0:T(4,128)S(1)}, f32[21,4,4,128]{3,2,1,0:T(4,128)S(1)}, u32[]{:S(2)}, u32[]{:S(2)}) collective-permute-start(f32[21,4,4,128]{3,2,1,0:T(4,128)S(1)} %pad_maximum_fusion.7), channel_id=1, source_target_pairs={{0,17},{1,18},{2,19},{3,20},{4,21},{5,22},{6,23},{7,24},{8,25},{9,... | collective-permute-start | bytes 516104 | tf_op jit(solution)/shard_map/ppermute | solution.py:247
  5.1 17.9 %collective-permute-start.5 = (f32[21,4,4,128]{3,2,1,0:T(4,128)S(1)}, f32[21,4,4,128]{3,2,1,0:T(4,128)S(1)}, u32[]{:S(2)}, u32[]{:S(2)}) collective-permute-start(f32[21,4,4,128]{3,2,1,0:T(4,128)S(1)} %pad_maximum_fusion.8), channel_id=1, source_target_pairs={{0,113},{1,114},{2,115},{3,116},{4,117},{5,118},{6,119},{7,120},{8... | collective-permute-start | bytes 516104 | tf_op jit(solution)/shard_map/ppermute | solution.py:247
  9.2 14.0 %collective-permute-start.6 = (f32[21,4,4,128]{3,2,1,0:T(4,128)S(1)}, f32[21,4,4,128]{3,2,1,0:T(4,128)S(1)}, u32[]{:S(2)}, u32[]{:S(2)}) collective-permute-start(f32[21,4,4,128]{3,2,1,0:T(4,128)S(1)} %pad_maximum_fusion.9), channel_id=1, source_target_pairs={{0,31},{1,16},{2,17},{3,18},{4,19},{5,20},{6,21},{7,22},{8,23},{9,... | collective-permute-start | bytes 516104 | tf_op jit(solution)/shard_map/ppermute | solution.py:247
  11.8 24.3 %collective-permute-start = (f32[21,4,32,128]{3,2,1,0:T(8,128)}, f32[21,4,32,128]{3,2,1,0:T(8,128)}, u32[]{:S(2)}, u32[]{:S(2)}) collective-permute-start(f32[21,4,32,128]{3,2,1,0:T(8,128)} %pad_maximum_fusion), channel_id=1, source_target_pairs={{0,16},{16,32},{32,48},{48,64},{64,80},{80,96},{96,112},{112,0},{1... | collective-permute-start | bytes 4128776 | tf_op jit(solution)/shard_map/ppermute | solution.py:240
  15.5 20.6 %collective-permute-start.1 = (f32[21,4,32,128]{3,2,1,0:T(8,128)}, f32[21,4,32,128]{3,2,1,0:T(8,128)}, u32[]{:S(2)}, u32[]{:S(2)}) collective-permute-start(f32[21,4,32,128]{3,2,1,0:T(8,128)} %pad_maximum_fusion.1), channel_id=1, source_target_pairs={{0,112},{16,0},{32,16},{48,32},{64,48},{80,64},{96,80},{112,96},{1... | collective-permute-start | bytes 4128776 | tf_op jit(solution)/shard_map/ppermute | solution.py:240
  18.4 17.8 %copy-start.5 = (f32[21,4,4,128]{3,2,1,0:T(4,128)}, f32[21,4,4,128]{3,2,1,0:T(4,128)S(1)}, u32[]{:S(2)}) copy-start(f32[21,4,4,128]{3,2,1,0:T(4,128)S(1)} %collective-permute-done.4.refs_6_) | copy-start | bytes 516100
  18.4 17.6 %collective-permute-start.7 = (f32[21,4,4,128]{3,2,1,0:T(4,128)S(1)}, f32[21,4,4,128]{3,2,1,0:T(4,128)S(1)}, u32[]{:S(2)}, u32[]{:S(2)}) collective-permute-start(f32[21,4,4,128]{3,2,1,0:T(4,128)S(1)} %pad_maximum_fusion.10), channel_id=1, source_target_pairs={{0,127},{1,112},{2,113},{3,114},{4,115},{5,116},{6,117},{7,118},{8... | collective-permute-start | bytes 516104 | tf_op jit(solution)/shard_map/ppermute | solution.py:247
  23.0 13.2 %copy-start.6 = (f32[21,4,4,128]{3,2,1,0:T(4,128)}, f32[21,4,4,128]{3,2,1,0:T(4,128)S(1)}, u32[]{:S(2)}) copy-start(f32[21,4,4,128]{3,2,1,0:T(4,128)S(1)} %collective-permute-done.5.refs_7_) | copy-start | bytes 516100
  23.0 13.0 %collective-permute-start.2 = (f32[21,8,4,128]{3,2,1,0:T(4,128)S(1)}, f32[21,8,4,128]{3,2,1,0:T(4,128)S(1)}, u32[]{:S(2)}, u32[]{:S(2)}) collective-permute-start(f32[21,8,4,128]{3,2,1,0:T(4,128)S(1)} %pad_maximum_fusion.5), channel_id=1, source_target_pairs={{0,1},{1,2},{2,3},{3,4},{4,5},{5,6},{6,7},{7,8},{8,9},{9,10},{10,1... | collective-permute-start | bytes 1032200 | tf_op jit(solution)/shard_map/ppermute | solution.py:242
  23.1 13.1 %copy-start.7 = (f32[21,4,4,128]{3,2,1,0:T(4,128)}, f32[21,4,4,128]{3,2,1,0:T(4,128)S(1)}, u32[]{:S(2)}) copy-start(f32[21,4,4,128]{3,2,1,0:T(4,128)S(1)} %collective-permute-done.6.refs_8_) | copy-start | bytes 516100
  23.1 12.9 %collective-permute-start.3 = (f32[21,8,4,128]{3,2,1,0:T(4,128)S(1)}, f32[21,8,4,128]{3,2,1,0:T(4,128)S(1)}, u32[]{:S(2)}, u32[]{:S(2)}) collective-permute-start(f32[21,8,4,128]{3,2,1,0:T(4,128)S(1)} %pad_maximum_fusion.6), channel_id=1, source_target_pairs={{0,15},{1,0},{2,1},{3,2},{4,3},{5,4},{6,5},{7,6},{8,7},{9,8},{10,9... | collective-permute-start | bytes 1032200 | tf_op jit(solution)/shard_map/ppermute | solution.py:242
  36.0 0.7 copy-start.8
  36.0 0.8 copy-start.2
  36.1 0.8 %copy-start.3 = (f32[21,8,4,128]{3,2,1,0:T(4,128)}, f32[21,8,4,128]{3,2,1,0:T(4,128)S(1)}, u32[]{:S(2)}) copy-start(f32[21,8,4,128]{3,2,1,0:T(4,128)S(1)} %collective-permute-done.3.refs_5_) | copy-start | bytes 1032196
  60.1 14.0 %all-to-all-start = ((f32[16,1,1536]{2,1,0:T(1,128)}), f32[16,1,1536]{2,1,0:T(1,128)S(1)}, u32[]{:S(2)}, u32[]{:S(2)}) async-start(f32[16,1,1536]{2,1,0:T(1,128)} %reshape.127), calls=%async_computation | async-start | bytes 196608 | tf_op jit(solution)/shard_map/all_to_all | solution.py:301
  76.6 4.7 %collective-permute-start.8 = (f32[3,2,8,256]{3,2,1,0:T(8,128)S(1)}, f32[3,2,8,256]{3,2,1,0:T(8,128)S(1)}, u32[]{:S(2)}, u32[]{:S(2)}) collective-permute-start(f32[3,2,8,256]{3,2,1,0:T(8,128)S(1)} %get-tuple-element.35), channel_id=1, source_target_pairs={{0,16},{16,32},{32,48},{48,64},{64,80},{80,96},{96,112},{112,0},{1... | collective-permute-start | bytes 147464 | tf_op jit(solution)/shard_map/ppermute | solution.py:240
  76.6 4.7 %collective-permute-start.9 = (f32[3,2,8,256]{3,2,1,0:T(8,128)S(1)}, f32[3,2,8,256]{3,2,1,0:T(8,128)S(1)}, u32[]{:S(2)}, u32[]{:S(2)}) collective-permute-start(f32[3,2,8,256]{3,2,1,0:T(8,128)S(1)} %get-tuple-element.36), channel_id=1, source_target_pairs={{0,112},{16,0},{32,16},{48,32},{64,48},{80,64},{96,80},{112,96},{1... | collective-permute-start | bytes 147464 | tf_op jit(solution)/shard_map/ppermute | solution.py:240

commit v9 on v4

--- a/solution.py
+++ b/solution.py
@@ -184,7 +184,6 @@
 
     lax.fori_loop(0, nx, last_body, 0)
 
-    nwin, win = coarse_ref.shape[0], coarse_ref.shape[3]
     pw = pw_ref[...]
     py = py_ref[...]
     for d in range(3):
@@ -198,9 +197,7 @@
                 preferred_element_type=jnp.float32,
             )
             zc = jnp.dot(zy, py, precision=lax.Precision.HIGHEST, preferred_element_type=jnp.float32)
-            zc = zc * jnp.float32(0.125)
-            for j in range(nwin):
-                coarse_ref[j, d, xp] = zc[j * win : (j + 1) * win]
+            coarse_ref[d, xp] = zc * jnp.float32(0.125)
 
 
 def lb_call(g0, mask, halos, halo, nwin, w):
@@ -217,7 +214,7 @@
     rows = -(-rows // ROWS) * ROWS
     out_shape = (
         jax.ShapeDtypeStruct(g0.shape, f32),
-        jax.ShapeDtypeStruct((nwin, 3, nx // 2, win, ny // 2), f32),
+        jax.ShapeDtypeStruct((3, nx // 2, nwin * win, ny // 2), f32),
     )
     scratch = [
         pltpu.VMEM((NPOP + 1, nx + 2 * halo, rows, nz), f32),
@@ -296,11 +293,13 @@
     w = TRACER_STEPS
     halos, tp = lattice_halos(populations, voxel_mask, tracer, STEPS, w)
     nb = lax.axis_size("blk")
-    state, windows = lb_call(populations, voxel_mask, halos, STEPS, nb, w)
-    moved = lax.all_to_all(windows, "blk", split_axis=0, concat_axis=0, tiled=True)
-    _, _, nxb, nzw, nys = moved.shape
-    flow = jnp.transpose(moved, (1, 3, 2, 0, 4)).reshape(3, nzw, nxb, nb * nys)
-    flow = jnp.concatenate([send(flow[:, :, nxb - w :], 1, 0), flow, send(flow[:, :, :w], -1, 0)], axis=2)
+    state, coarse = lb_call(populations, voxel_mask, halos, STEPS, nb, w)
+    windows = coarse.reshape(3, coarse.shape[1], nb, coarse.shape[2] // nb, coarse.shape[3])
+    moved = lax.all_to_all(windows, "blk", split_axis=2, concat_axis=4, tiled=True)
+    flow = moved[:, :, 0]
+    nxb = flow.shape[1]
+    flow = jnp.concatenate([send(flow[:, nxb - w :], 1, 0), flow, send(flow[:, :w], -1, 0)], axis=1)
+    flow = jnp.transpose(flow, (0, 2, 1, 3))
     xlo, xhi, zlo, zhi, c_mm, c_mp, c_pm, c_pp = tp
     conc = jnp.concatenate(
         [

time: 84.6 us -> 87.7 us (1.037)
  local copies, waits for them, and re-layouts: 13.6 us -> 15.4 us
  other arithmetic: 5.88 us -> 7.24 us
  starting transfers between devices: 27.9 us -> 29 us
  waiting for transfers between devices: 15.9 us -> 14.8 us
    unnamed x36 -> x43, local copies, waits for them, and re-layouts: 4.94 us -> 6.91 us
    ppermute x4, waiting for transfers between devices: 4.74 us -> 3.42 us  [send(): return lax.ppermute(x, 'vessel', [(i, (i + dv) % nv) for i in range(nv)])]
    concatenate x8, other arithmetic: 3.79 us -> 5.11 us  [lattice_halos(): jnp.concatenate([lb, flat.reshape(1, lb.shape[1], lb.shape[2], nz)], axis=0)]
    all_to_all x1, starting transfers between devices: 4.24 us -> 5.43 us  [local(): lax.all_to_all(windows, 'blk', split_axis=2, concat_axis=4, tiled=True)]
    slice x12 -> x13, local copies, waits for them, and re-layouts: 4.47 us -> 4.31 us  [lattice_halos(): tracer_pieces.append(got[NPOP + 1].reshape(-1)[:tp.size].reshape(tp.shape))]
  transfers between devices with their start and end apart: 11 -> 11, of which waited for: 4 -> 5; matrix products, arithmetic and copies ran while one was open for 11% -> 12% of each run, Pallas kernels for 0% -> 0%
where the time goes in v9:
time: 87.7 us; the launch traced here: 86.6 us
  starting transfers between devices  29 us (33%)
  Pallas kernels  19.1 us (22%)
  local copies, waits for them, and re-layouts  15.4 us (18%)
  waiting for transfers between devices  14.8 us (17%)
  other arithmetic  7.24 us (8%)
  between operations  1.04 us (1%)
    pallas_call x1, Pallas kernels, lb_call(): pl.pallas_call(functools.partial(lb_kernel, halo, nx, ny), out_shape=out_...  19.1 us
    ppermute x4, starting transfers between devices, send(): return lax.ppermute(x, ('vessel', 'blk'), pairs)  12.2 us
    all_to_all x1, waiting for transfers between devices, local(): lax.all_to_all(windows, 'blk', split_axis=2, concat_axis=4, tiled=True)  7.71 us
    unnamed x43, local copies, waits for them, and re-layouts  6.91 us
    ppermute x4, starting transfers between devices, send(): return lax.ppermute(x, 'vessel', [(i, (i + dv) % nv) for i in range(nv)])  5.93 us
    ppermute x2, starting transfers between devices, send(): return lax.ppermute(x, 'blk', [(i, (i + db) % nb) for i in range(nb)])  5.47 us
    all_to_all x1, starting transfers between devices, local(): lax.all_to_all(windows, 'blk', split_axis=2, concat_axis=4, tiled=True)  5.43 us
    concatenate x8, other arithmetic, lattice_halos(): jnp.concatenate([lb, flat.reshape(1, lb.shape[1], lb.shape[2], nz)], axis=0)  5.11 us
  transfers between devices with their start and end apart: 11, of which 5 were waited for; matrix products, arithmetic and copies ran while one was open for 12% of the time, Pallas kernels for 0%

profile of v9, /device:TPU:0, one launch (start us, length us, event | category | flops | bytes accessed | tf_op | source)
XLA Modules:
  0.0 86.6 jit_solution(10968229571388927298)
XLA Ops:
  0.6 0.8 slice_bitcast_fusion.7
  1.4 0.9 %convert_bitcast_fusion = f32[1,8,32,128]{3,2,1,0:T(8,128)S(1)} fusion(s32[8,32,128]{2,1,0:T(8,128)} %refs_1_.1), kind=kLoop, calls=%fused_computation.9 | loop fusion | flops 32768 | bytes 262144 | tf_op jit(solution)/shard_map/broadcast_in_dim | solution.py:254
  2.4 1.6 %fusion.22 = (f32[19,4,4,128]{3,2,1,0:T(4,128)S(1)}, f32[19,4,4,128]{3,2,1,0:T(4,128)S(1)}, f32[19,4,4,128]{3,2,1,0:T(4,128)S(1)}, f32[19,4,4,128]{3,2,1,0:T(4,128)S(1)}) fusion(f32[19,8,32,128]{3,2,1,0:T(8,128)} %refs_0_.1), kind=kLoop, calls=%fused_computation.69 | loop fusion | bytes 1245184 | tf_op jit(solution)/shard_map/slice | solution.py:263
  4.0 1.2 %collective-permute-start.4 = (f32[21,4,4,128]{3,2,1,0:T(4,128)S(1)}, f32[21,4,4,128]{3,2,1,0:T(4,128)S(1)}, u32[]{:S(2)}, u32[]{:S(2)}) collective-permute-start(f32[21,4,4,128]{3,2,1,0:T(4,128)S(1)} %pad_maximum_fusion.4), channel_id=1, source_target_pairs={{0,17},{1,18},{2,19},{3,20},{4,21},{5,22},{6,23},{7,24},{8,25},{9,... | collective-permute-start | bytes 516104 | tf_op jit(solution)/shard_map/ppermute | solution.py:248
  5.2 0.7 pad_maximum_fusion.5
  5.9 4.0 %collective-permute-start.5 = (f32[21,4,4,128]{3,2,1,0:T(4,128)}, f32[21,4,4,128]{3,2,1,0:T(4,128)}, u32[]{:S(2)}, u32[]{:S(2)}) collective-permute-start(f32[21,4,4,128]{3,2,1,0:T(4,128)} %pad_maximum_fusion.5), channel_id=1, source_target_pairs={{0,113},{1,114},{2,115},{3,116},{4,117},{5,118},{6,119},{7,120},{8... | collective-permute-start | bytes 516104 | tf_op jit(solution)/shard_map/ppermute | solution.py:248
  9.9 0.7 pad_maximum_fusion.6
  10.6 1.1 %collective-permute-start.6 = (f32[21,4,4,128]{3,2,1,0:T(4,128)}, f32[21,4,4,128]{3,2,1,0:T(4,128)}, u32[]{:S(2)}, u32[]{:S(2)}) collective-permute-start(f32[21,4,4,128]{3,2,1,0:T(4,128)} %pad_maximum_fusion.6), channel_id=1, source_target_pairs={{0,31},{1,16},{2,17},{3,18},{4,19},{5,20},{6,21},{7,22},{8,23},{9,... | collective-permute-start | bytes 516104 | tf_op jit(solution)/shard_map/ppermute | solution.py:248
  11.7 0.7 pad_maximum_fusion.7
  12.4 5.9 %collective-permute-start.7 = (f32[21,4,4,128]{3,2,1,0:T(4,128)}, f32[21,4,4,128]{3,2,1,0:T(4,128)}, u32[]{:S(2)}, u32[]{:S(2)}) collective-permute-start(f32[21,4,4,128]{3,2,1,0:T(4,128)} %pad_maximum_fusion.7), channel_id=1, source_target_pairs={{0,127},{1,112},{2,113},{3,114},{4,115},{5,116},{6,117},{7,118},{8... | collective-permute-start | bytes 516104 | tf_op jit(solution)/shard_map/ppermute | solution.py:248
  18.4 0.2 fusion.24
  18.6 1.2 %pad_maximum_fusion = f32[21,4,32,128]{3,2,1,0:T(8,128)} fusion(f32[1,4,32,128]{3,2,1,0:T(8,128)S(1)} %bitcast.66, f32[1,4,32,128]{3,2,1,0:T(8,128)S(1)} %get-tuple-element.30, f32[19,4,32,128]{3,2,1,0:T(8,128)S(1)} %get-tuple-element.17), kind=kLoop, calls=%fused_computation | loop fusion | flops 688128 | bytes 2752512 | tf_op jit(solution)/shard_map/concatenate | solution.py:267
  19.8 0.2 fusion.23
  20.0 0.1 pad_maximum_fusion.1
  20.2 0.8 pad_maximum_fusion.3
  21.0 3.0 %collective-permute-start.1 = (f32[21,4,32,128]{3,2,1,0:T(8,128)S(1)}, f32[21,4,32,128]{3,2,1,0:T(8,128)S(1)}, u32[]{:S(2)}, u32[]{:S(2)}) collective-permute-start(f32[21,4,32,128]{3,2,1,0:T(8,128)S(1)} %pad_maximum_fusion.1), channel_id=1, source_target_pairs={{0,112},{16,0},{32,16},{48,32},{64,48},{80,64},{96,80},{112,96},{1... | collective-permute-start | bytes 4128776 | tf_op jit(solution)/shard_map/ppermute | solution.py:241
  24.0 0.8 pad_maximum_fusion.2
  24.8 0.7 collective-permute-start.2
  25.5 0.7 slice.366
  26.2 4.8 %collective-permute-start.3 = (f32[21,8,4,128]{3,2,1,0:T(4,128)}, f32[21,8,4,128]{3,2,1,0:T(4,128)S(1)}, u32[]{:S(2)}, u32[]{:S(2)}) collective-permute-start(f32[21,8,4,128]{3,2,1,0:T(4,128)} %pad_maximum_fusion.3), channel_id=1, source_target_pairs={{0,15},{1,0},{2,1},{3,2},{4,3},{5,4},{6,5},{7,6},{8,7},{9,8},{10,9... | collective-permute-start | bytes 1032200 | tf_op jit(solution)/shard_map/ppermute | solution.py:243
  31.0 0.7 slice.371
  31.7 0.7 slice.373
  32.4 3.5 %collective-permute-done.2.refs_6_ = f32[21,8,4,128]{3,2,1,0:T(4,128)S(1)} collective-permute-done((f32[21,8,4,128]{3,2,1,0:T(4,128)}, f32[21,8,4,128]{3,2,1,0:T(4,128)S(1)}, u32[]{:S(2)}, u32[]{:S(2)}) %collective-permute-start.2) | collective-permute-done | bytes 344096 | tf_op jit(solution)/shard_map/ppermute | solution.py:243
  36.0 0.1 collective-permute-done.3.refs_7_
  36.2 0.7 copy-done.7
  36.8 0.6 copy-done.9
  37.4 1.7 %collective-permute-done.refs_4_ = f32[21,4,32,128]{3,2,1,0:T(8,128)} collective-permute-done((f32[21,4,32,128]{3,2,1,0:T(8,128)}, f32[21,4,32,128]{3,2,1,0:T(8,128)}, u32[]{:S(2)}, u32[]{:S(2)}) %collective-permute-start) | collective-permute-done | bytes 1376288 | tf_op jit(solution)/shard_map/ppermute | solution.py:241
  39.1 0.8 slice.367
  39.9 0.7 slice.305
  40.6 0.7 slice.368
  41.3 0.6 constant_dynamic-update-slice_fusion.5
  41.9 1.1 %copy-done.1 = f32[21,4,32,128]{3,2,1,0:T(8,128)} copy-done((f32[21,4,32,128]{3,2,1,0:T(8,128)}, f32[21,4,32,128]{3,2,1,0:T(8,128)S(1)}, u32[]{:S(2)}) %copy-start.1) | copy-done | bytes 1376280
  43.0 19.1 %shard_map.68 = (f32[19,8,32,128]{3,2,1,0:T(8,128)}, f32[3,4,128,16]{3,2,1,0:T(8,128)}) custom-call(f32[19,8,32,128]{3,2,1,0:T(8,128)} %refs_0_.1, s32[8,32,128]{2,1,0:T(8,128)} %refs_1_.1, f32[128,128]{1,0:T(8,128)} %constant.10.clone.refs_2_, f32[32,16]{1,0:T(8,128)} %constant.5.clone.refs_3_, f32[21,4,32,128]{3,2,1,0:T(8,128)} %collective-permute-done.refs_4_, ...), custom_call_target="tpu_custom_call" | custom-call | flops 78643200 | bytes 9961472 | tf_op jit(solution)/shard_map/pallas_call | solution.py:226
  62.1 1.3 %copy_bitcast_fusion = f32[16,3,4,8,16]{4,3,2,1,0:T(8,128)S(1)} fusion(f32[3,4,128,16]{3,2,1,0:T(8,128)} %get-tuple-element.5), kind=kLoop, calls=%fused_computation.85 | loop fusion | bytes 196608
  63.4 0.9 %reshape.115 = f32[16,1,1536]{2,1,0:T(1,128)} reshape(f32[16,3,4,8,16]{4,3,2,1,0:T(8,128)S(1)} %copy_bitcast_fusion) | data formatting | bytes 196608
  64.3 5.4 %all-to-all-start = ((f32[16,1,1536]{2,1,0:T(1,128)}), f32[16,1,1536]{2,1,0:T(1,128)S(1)}, u32[]{:S(2)}, u32[]{:S(2)}) async-start(f32[16,1,1536]{2,1,0:T(1,128)} %reshape.115), calls=%async_computation | async-start | bytes 196608 | tf_op jit(solution)/shard_map/all_to_all | solution.py:298
  69.8 7.7 %all-to-all-done = f32[16,1,1536]{2,1,0:T(1,128)S(1)} async-done(((f32[16,1,1536]{2,1,0:T(1,128)}), f32[16,1,1536]{2,1,0:T(1,128)S(1)}, u32[]{:S(2)}, u32[]{:S(2)}) %all-to-all-start) | async-done | bytes 98336 | tf_op jit(solution)/shard_map/all_to_all | solution.py:298
  77.5 0.6 broadcast.20
  78.1 0.9 %reduce = f32[16,1536]{1,0:T(8,128)S(1)} reduce(f32[16,1,1536]{2,1,0:T(1,128)S(1)} %all-to-all-done, f32[]{:T(128)} %broadcast.20), dimensions={1}, to_apply=%all_to_all.11.reduce_sub_computation | reduce | bytes 196612 | tf_op jit(solution)/shard_map/all_to_all | solution.py:298
  79.0 0.3 reshape.116
  79.4 0.5 copy.20
  79.9 0.3 squeeze.12
  80.2 2.9 %collective-permute-start.9 = (f32[3,2,8,256]{3,2,1,0:T(8,128)S(1)}, f32[3,2,8,256]{3,2,1,0:T(8,128)S(1)}, u32[]{:S(2)}, u32[]{:S(2)}) collective-permute-start(f32[3,2,8,256]{3,2,1,0:T(8,128)S(1)} %get-tuple-element.32), channel_id=1, source_target_pairs={{0,112},{16,0},{32,16},{48,32},{64,48},{80,64},{96,80},{112,96},{1... | collective-permute-start | bytes 147464 | tf_op jit(solution)/shard_map/ppermute | solution.py:241
  83.2 1.8 %collective-permute-done.8 = f32[3,2,8,256]{3,2,1,0:T(8,128)S(1)} collective-permute-done((f32[3,2,8,256]{3,2,1,0:T(8,128)S(1)}, f32[3,2,8,256]{3,2,1,0:T(8,128)S(1)}, u32[]{:S(2)}, u32[]{:S(2)}) %collective-permute-start.8) | collective-permute-done | bytes 49184 | tf_op jit(solution)/shard_map/ppermute | solution.py:241
  85.3 0.1 fusion.29
  85.4 0.1 slice_multiply_fusion.1
  85.8 0.1 fusion.13
  86.0 0.6 copy.21
  (84 shorter events, 1.1 us)
Async XLA Ops:
  2.4 16.0 %copy-start.4 = (f32[4,4,256]{2,1,0:T(4,128)S(1)}, f32[4,4,256]{2,1,0:T(4,128)}, u32[]{:S(2)}) copy-start(f32[4,4,256]{2,1,0:T(4,128)} %param.7) | copy-start | bytes 49156
  2.4 16.0 %copy-start = (f32[19,8,32,128]{3,2,1,0:T(8,128)S(1)}, f32[19,8,32,128]{3,2,1,0:T(8,128)}, u32[]{:S(2)}) copy-start(f32[19,8,32,128]{3,2,1,0:T(8,128)} %refs_0_.1) | copy-start | bytes 7471108
  4.0 17.0 %collective-permute-start.4 = (f32[21,4,4,128]{3,2,1,0:T(4,128)S(1)}, f32[21,4,4,128]{3,2,1,0:T(4,128)S(1)}, u32[]{:S(2)}, u32[]{:S(2)}) collective-permute-start(f32[21,4,4,128]{3,2,1,0:T(4,128)S(1)} %pad_maximum_fusion.4), channel_id=1, source_target_pairs={{0,17},{1,18},{2,19},{3,20},{4,21},{5,22},{6,23},{7,24},{8,25},{9,... | collective-permute-start | bytes 516104 | tf_op jit(solution)/shard_map/ppermute | solution.py:248
  5.9 18.9 %collective-permute-start.5 = (f32[21,4,4,128]{3,2,1,0:T(4,128)}, f32[21,4,4,128]{3,2,1,0:T(4,128)}, u32[]{:S(2)}, u32[]{:S(2)}) collective-permute-start(f32[21,4,4,128]{3,2,1,0:T(4,128)} %pad_maximum_fusion.5), channel_id=1, source_target_pairs={{0,113},{1,114},{2,115},{3,116},{4,117},{5,118},{6,119},{7,120},{8... | collective-permute-start | bytes 516104 | tf_op jit(solution)/shard_map/ppermute | solution.py:248
  10.6 15.6 %collective-permute-start.6 = (f32[21,4,4,128]{3,2,1,0:T(4,128)}, f32[21,4,4,128]{3,2,1,0:T(4,128)}, u32[]{:S(2)}, u32[]{:S(2)}) collective-permute-start(f32[21,4,4,128]{3,2,1,0:T(4,128)} %pad_maximum_fusion.6), channel_id=1, source_target_pairs={{0,31},{1,16},{2,17},{3,18},{4,19},{5,20},{6,21},{7,22},{8,23},{9,... | collective-permute-start | bytes 516104 | tf_op jit(solution)/shard_map/ppermute | solution.py:248
  12.4 19.3 %collective-permute-start.7 = (f32[21,4,4,128]{3,2,1,0:T(4,128)}, f32[21,4,4,128]{3,2,1,0:T(4,128)}, u32[]{:S(2)}, u32[]{:S(2)}) collective-permute-start(f32[21,4,4,128]{3,2,1,0:T(4,128)} %pad_maximum_fusion.7), channel_id=1, source_target_pairs={{0,127},{1,112},{2,113},{3,114},{4,115},{5,116},{6,117},{7,118},{8... | collective-permute-start | bytes 516104 | tf_op jit(solution)/shard_map/ppermute | solution.py:248
  19.8 19.3 %collective-permute-start = (f32[21,4,32,128]{3,2,1,0:T(8,128)}, f32[21,4,32,128]{3,2,1,0:T(8,128)}, u32[]{:S(2)}, u32[]{:S(2)}) collective-permute-start(f32[21,4,32,128]{3,2,1,0:T(8,128)} %pad_maximum_fusion), channel_id=1, source_target_pairs={{0,16},{16,32},{32,48},{48,64},{64,80},{80,96},{96,112},{112,0},{1... | collective-permute-start | bytes 4128776 | tf_op jit(solution)/shard_map/ppermute | solution.py:241
  21.0 3.8 %copy-start.5 = (f32[21,4,4,128]{3,2,1,0:T(4,128)}, f32[21,4,4,128]{3,2,1,0:T(4,128)S(1)}, u32[]{:S(2)}) copy-start(f32[21,4,4,128]{3,2,1,0:T(4,128)S(1)} %collective-permute-done.4.refs_8_) | copy-start | bytes 516100
  21.0 20.9 %collective-permute-start.1 = (f32[21,4,32,128]{3,2,1,0:T(8,128)S(1)}, f32[21,4,32,128]{3,2,1,0:T(8,128)S(1)}, u32[]{:S(2)}, u32[]{:S(2)}) collective-permute-start(f32[21,4,32,128]{3,2,1,0:T(8,128)S(1)} %pad_maximum_fusion.1), channel_id=1, source_target_pairs={{0,112},{16,0},{32,16},{48,32},{64,48},{80,64},{96,80},{112,96},{1... | collective-permute-start | bytes 4128776 | tf_op jit(solution)/shard_map/ppermute | solution.py:241
  24.8 11.1 %collective-permute-start.2 = (f32[21,8,4,128]{3,2,1,0:T(4,128)}, f32[21,8,4,128]{3,2,1,0:T(4,128)S(1)}, u32[]{:S(2)}, u32[]{:S(2)}) collective-permute-start(f32[21,8,4,128]{3,2,1,0:T(4,128)} %pad_maximum_fusion.2), channel_id=1, source_target_pairs={{0,1},{1,2},{2,3},{3,4},{4,5},{5,6},{6,7},{7,8},{8,9},{9,10},{10,1... | collective-permute-start | bytes 1032200 | tf_op jit(solution)/shard_map/ppermute | solution.py:243
  26.2 9.9 %collective-permute-start.3 = (f32[21,8,4,128]{3,2,1,0:T(4,128)}, f32[21,8,4,128]{3,2,1,0:T(4,128)S(1)}, u32[]{:S(2)}, u32[]{:S(2)}) collective-permute-start(f32[21,8,4,128]{3,2,1,0:T(4,128)} %pad_maximum_fusion.3), channel_id=1, source_target_pairs={{0,15},{1,0},{2,1},{3,2},{4,3},{5,4},{6,5},{7,6},{8,7},{9,8},{10,9... | collective-permute-start | bytes 1032200 | tf_op jit(solution)/shard_map/ppermute | solution.py:243
  36.0 5.9 %copy-start.2 = (f32[21,8,4,128]{3,2,1,0:T(4,128)}, f32[21,8,4,128]{3,2,1,0:T(4,128)S(1)}, u32[]{:S(2)}) copy-start(f32[21,8,4,128]{3,2,1,0:T(4,128)S(1)} %collective-permute-done.2.refs_6_) | copy-start | bytes 1032196
  36.1 5.8 %copy-start.3 = (f32[21,8,4,128]{3,2,1,0:T(4,128)}, f32[21,8,4,128]{3,2,1,0:T(4,128)S(1)}, u32[]{:S(2)}) copy-start(f32[21,8,4,128]{3,2,1,0:T(4,128)S(1)} %collective-permute-done.3.refs_7_) | copy-start | bytes 1032196
  36.2 0.7 copy-start.7
  36.8 0.6 copy-start.9
  41.9 1.1 %copy-start.1 = (f32[21,4,32,128]{3,2,1,0:T(8,128)}, f32[21,4,32,128]{3,2,1,0:T(8,128)S(1)}, u32[]{:S(2)}) copy-start(f32[21,4,32,128]{3,2,1,0:T(8,128)S(1)} %collective-permute-done.1.refs_5_) | copy-start | bytes 4128772
  62.1 7.7 %copy-start.6 = (f32[4,8,256]{2,0,1:T(4,128)S(1)}, f32[4,8,256]{2,0,1:T(4,128)}, u32[]{:S(2)}) copy-start(f32[4,8,256]{2,0,1:T(4,128)} %constant_dynamic-update-slice_fusion.5) | copy-start | bytes 98308
  62.1 7.7 %slice-start = ((f32[21,4,32,128]{3,2,1,0:T(8,128)}), f32[1,4,32,128]{3,2,1,0:T(8,128)S(1)}, s32[]{:S(2)}) async-start(f32[21,4,32,128]{3,2,1,0:T(8,128)} %copy-done.1), calls=%async_computation.1 | async-start | bytes 131072 | tf_op jit(solution)/shard_map/slice | solution.py:270
  64.3 13.2 %all-to-all-start = ((f32[16,1,1536]{2,1,0:T(1,128)}), f32[16,1,1536]{2,1,0:T(1,128)S(1)}, u32[]{:S(2)}, u32[]{:S(2)}) async-start(f32[16,1,1536]{2,1,0:T(1,128)} %reshape.115), calls=%async_computation | async-start | bytes 196608 | tf_op jit(solution)/shard_map/all_to_all | solution.py:298
  79.4 5.6 %copy-start.8 = (f32[2,8,256]{2,0,1:T(2,128)S(1)}, f32[2,8,256]{2,0,1:T(2,128)}, u32[]{:S(2)}) copy-start(f32[2,8,256]{2,0,1:T(2,128)} %copy-done.7) | copy-start | bytes 49156
  79.4 5.6 %copy-start.10 = (f32[2,8,256]{2,0,1:T(2,128)S(1)}, f32[2,8,256]{2,0,1:T(2,128)}, u32[]{:S(2)}) copy-start(f32[2,8,256]{2,0,1:T(2,128)} %copy-done.9) | copy-start | bytes 49156
  80.2 4.7 %collective-permute-start.8 = (f32[3,2,8,256]{3,2,1,0:T(8,128)S(1)}, f32[3,2,8,256]{3,2,1,0:T(8,128)S(1)}, u32[]{:S(2)}, u32[]{:S(2)}) collective-permute-start(f32[3,2,8,256]{3,2,1,0:T(8,128)S(1)} %get-tuple-element.31), channel_id=1, source_target_pairs={{0,16},{16,32},{32,48},{48,64},{64,80},{80,96},{96,112},{112,0},{1... | collective-permute-start | bytes 147464 | tf_op jit(solution)/shard_map/ppermute | solution.py:241
  80.2 4.7 %collective-permute-start.9 = (f32[3,2,8,256]{3,2,1,0:T(8,128)S(1)}, f32[3,2,8,256]{3,2,1,0:T(8,128)S(1)}, u32[]{:S(2)}, u32[]{:S(2)}) collective-permute-start(f32[3,2,8,256]{3,2,1,0:T(8,128)S(1)} %get-tuple-element.32), channel_id=1, source_target_pairs={{0,112},{16,0},{32,16},{48,32},{64,48},{80,64},{96,80},{112,96},{1... | collective-permute-start | bytes 147464 | tf_op jit(solution)/shard_map/ppermute | solution.py:241

commit v10 on v3

--- a/solution.py
+++ b/solution.py
@@ -157,7 +157,7 @@
                     dst[i, x, pl.ds(r, ROWS), :] = post[i]
             return carry
 
-        lax.fori_loop(s, nx + 2 * h - s, body, 0)
+        lax.fori_loop(s, nx + 2 * h - s, body, 0, unroll=2)
 
     for s in range(h):
         run_step(s)
@@ -182,7 +182,7 @@
                 flow_s[d, x, pl.ds(r, ROWS), :] = jnp.where(solid, jnp.float32(0.0), mom[d] * inv)
         return carry
 
-    lax.fori_loop(0, nx, last_body, 0)
+    lax.fori_loop(0, nx, last_body, 0, unroll=2)
 
     nz = flow_s.shape[3]
     pz = (

time: 84.3 us -> 82.5 us (0.979)
  Pallas kernels: 18.2 us -> 16.5 us
    pallas_call x1, Pallas kernels: 18.2 us -> 16.5 us  [lb_call(): pl.pallas_call(functools.partial(lb_kernel, halo, nx, ny), out_shape=out_...]
where the time goes in v10:
time: 82.5 us; the launch traced here: 81.4 us
  starting transfers between devices  30.3 us (37%)
  Pallas kernels  16.5 us (20%)
  waiting for transfers between devices  16.1 us (20%)
  local copies, waits for them, and re-layouts  11 us (13%)
  other arithmetic  6.24 us (8%)
  between operations  1.18 us (1%)
    pallas_call x1, Pallas kernels, lb_call(): pl.pallas_call(functools.partial(lb_kernel, halo, nx, ny), out_shape=out_...  16.5 us
    ppermute x4, starting transfers between devices, send(): return lax.ppermute(x, ('vessel', 'blk'), pairs)  10.7 us
    ppermute x4, starting transfers between devices, send(): return lax.ppermute(x, 'vessel', [(i, (i + dv) % nv) for i in range(nv)])  8.03 us
    ppermute x4, waiting for transfers between devices, send(): return lax.ppermute(x, ('vessel', 'blk'), pairs)  7.47 us
    all_to_all x1, waiting for transfers between devices, local(): lax.all_to_all(windows, 'blk', split_axis=2, concat_axis=4, tiled=True)  6.89 us
    all_to_all x1, starting transfers between devices, local(): lax.all_to_all(windows, 'blk', split_axis=2, concat_axis=4, tiled=True)  6.12 us
    ppermute x2, starting transfers between devices, send(): return lax.ppermute(x, 'blk', [(i, (i + db) % nb) for i in range(nb)])  5.45 us
    unnamed x36, local copies, waits for them, and re-layouts  3.45 us
  transfers between devices with their start and end apart: 11, of which 3 were waited for; matrix products, arithmetic and copies ran while one was open for 5% of the time, Pallas kernels for 0%

profile of v10, /device:TPU:0, one launch (start us, length us, event | category | flops | bytes accessed | tf_op | source)
XLA Modules:
  0.0 81.4 jit_solution(1841454756834786128)
XLA Ops:
  0.6 0.8 slice_bitcast_fusion.7
  1.5 0.9 %convert_bitcast_fusion = f32[1,8,32,128]{3,2,1,0:T(8,128)S(1)} fusion(s32[8,32,128]{2,1,0:T(8,128)} %refs_1_.1), kind=kLoop, calls=%fused_computation.12 | loop fusion | flops 32768 | bytes 262144 | tf_op jit(solution)/shard_map/broadcast_in_dim | solution.py:253
  2.4 1.6 %fusion.22 = (f32[19,4,4,128]{3,2,1,0:T(4,128)S(1)}, f32[19,4,4,128]{3,2,1,0:T(4,128)S(1)}, f32[19,4,4,128]{3,2,1,0:T(4,128)S(1)}, f32[19,4,4,128]{3,2,1,0:T(4,128)S(1)}) fusion(f32[19,8,32,128]{3,2,1,0:T(8,128)} %refs_0_.1), kind=kLoop, calls=%fused_computation.72 | loop fusion | bytes 1245184 | tf_op jit(solution)/shard_map/slice | solution.py:262
  4.0 1.2 %collective-permute-start.4 = (f32[21,4,4,128]{3,2,1,0:T(4,128)S(1)}, f32[21,4,4,128]{3,2,1,0:T(4,128)S(1)}, u32[]{:S(2)}, u32[]{:S(2)}) collective-permute-start(f32[21,4,4,128]{3,2,1,0:T(4,128)S(1)} %pad_maximum_fusion.7), channel_id=1, source_target_pairs={{0,17},{1,18},{2,19},{3,20},{4,21},{5,22},{6,23},{7,24},{8,25},{9,... | collective-permute-start | bytes 516104 | tf_op jit(solution)/shard_map/ppermute | solution.py:247
  5.3 4.0 %collective-permute-start.5 = (f32[21,4,4,128]{3,2,1,0:T(4,128)S(1)}, f32[21,4,4,128]{3,2,1,0:T(4,128)S(1)}, u32[]{:S(2)}, u32[]{:S(2)}) collective-permute-start(f32[21,4,4,128]{3,2,1,0:T(4,128)S(1)} %pad_maximum_fusion.8), channel_id=1, source_target_pairs={{0,113},{1,114},{2,115},{3,116},{4,117},{5,118},{6,119},{7,120},{8... | collective-permute-start | bytes 516104 | tf_op jit(solution)/shard_map/ppermute | solution.py:247
  9.3 1.2 %collective-permute-start.6 = (f32[21,4,4,128]{3,2,1,0:T(4,128)S(1)}, f32[21,4,4,128]{3,2,1,0:T(4,128)S(1)}, u32[]{:S(2)}, u32[]{:S(2)}) collective-permute-start(f32[21,4,4,128]{3,2,1,0:T(4,128)S(1)} %pad_maximum_fusion.9), channel_id=1, source_target_pairs={{0,31},{1,16},{2,17},{3,18},{4,19},{5,20},{6,21},{7,22},{8,23},{9,... | collective-permute-start | bytes 516104 | tf_op jit(solution)/shard_map/ppermute | solution.py:247
  10.6 0.2 fusion.24
  10.8 1.2 %pad_maximum_fusion = f32[21,4,32,128]{3,2,1,0:T(8,128)} fusion(f32[1,4,32,128]{3,2,1,0:T(8,128)S(1)} %bitcast.67, f32[1,4,32,128]{3,2,1,0:T(8,128)S(1)} %get-tuple-element.34, f32[19,4,32,128]{3,2,1,0:T(8,128)S(1)} %get-tuple-element.19), kind=kLoop, calls=%fused_computation | loop fusion | flops 688128 | bytes 2752512 | tf_op jit(solution)/shard_map/concatenate | solution.py:266
  12.0 2.5 %collective-permute-start = (f32[21,4,32,128]{3,2,1,0:T(8,128)}, f32[21,4,32,128]{3,2,1,0:T(8,128)}, u32[]{:S(2)}, u32[]{:S(2)}) collective-permute-start(f32[21,4,32,128]{3,2,1,0:T(8,128)} %pad_maximum_fusion), channel_id=1, source_target_pairs={{0,16},{16,32},{32,48},{48,64},{64,80},{80,96},{96,112},{112,0},{1... | collective-permute-start | bytes 4128776 | tf_op jit(solution)/shard_map/ppermute | solution.py:240
  14.5 1.2 %pad_maximum_fusion.1 = f32[21,4,32,128]{3,2,1,0:T(8,128)} fusion(f32[1,4,32,128]{3,2,1,0:T(8,128)S(1)} %bitcast.66, f32[1,4,32,128]{3,2,1,0:T(8,128)S(1)} %get-tuple-element.33, f32[19,4,32,128]{3,2,1,0:T(8,128)S(1)} %get-tuple-element.18), kind=kLoop, calls=%fused_computation.1 | loop fusion | flops 688128 | bytes 2752512 | tf_op jit(solution)/shard_map/concatenate | solution.py:266
  15.7 2.6 %collective-permute-start.1 = (f32[21,4,32,128]{3,2,1,0:T(8,128)}, f32[21,4,32,128]{3,2,1,0:T(8,128)}, u32[]{:S(2)}, u32[]{:S(2)}) collective-permute-start(f32[21,4,32,128]{3,2,1,0:T(8,128)} %pad_maximum_fusion.1), channel_id=1, source_target_pairs={{0,112},{16,0},{32,16},{48,32},{64,48},{80,64},{96,80},{112,96},{1... | collective-permute-start | bytes 4128776 | tf_op jit(solution)/shard_map/ppermute | solution.py:240
  18.3 0.2 fusion.23
  18.6 4.3 %collective-permute-start.7 = (f32[21,4,4,128]{3,2,1,0:T(4,128)S(1)}, f32[21,4,4,128]{3,2,1,0:T(4,128)S(1)}, u32[]{:S(2)}, u32[]{:S(2)}) collective-permute-start(f32[21,4,4,128]{3,2,1,0:T(4,128)S(1)} %pad_maximum_fusion.10), channel_id=1, source_target_pairs={{0,127},{1,112},{2,113},{3,114},{4,115},{5,116},{6,117},{7,118},{8... | collective-permute-start | bytes 516104 | tf_op jit(solution)/shard_map/ppermute | solution.py:247
  22.9 0.1 pad_maximum_fusion.6
  23.1 0.1 pad_maximum_fusion.5
  23.2 0.1 collective-permute-start.2
  23.3 5.4 %collective-permute-start.3 = (f32[21,8,4,128]{3,2,1,0:T(4,128)S(1)}, f32[21,8,4,128]{3,2,1,0:T(4,128)S(1)}, u32[]{:S(2)}, u32[]{:S(2)}) collective-permute-start(f32[21,8,4,128]{3,2,1,0:T(4,128)S(1)} %pad_maximum_fusion.6), channel_id=1, source_target_pairs={{0,15},{1,0},{2,1},{3,2},{4,3},{5,4},{6,5},{7,6},{8,7},{9,8},{10,9... | collective-permute-start | bytes 1032200 | tf_op jit(solution)/shard_map/ppermute | solution.py:242
  28.7 7.5 %collective-permute-done.7.refs_9_ = f32[21,4,4,128]{3,2,1,0:T(4,128)S(1)} collective-permute-done((f32[21,4,4,128]{3,2,1,0:T(4,128)S(1)}, f32[21,4,4,128]{3,2,1,0:T(4,128)S(1)}, u32[]{:S(2)}, u32[]{:S(2)}) %collective-permute-start.7) | collective-permute-done | bytes 172064 | tf_op jit(solution)/shard_map/ppermute | solution.py:247
  36.4 0.5 copy-done.7
  36.9 0.1 copy-done.1
  37.0 0.1 copy-done.2
  37.1 16.5 %shard_map.50 = (f32[19,8,32,128]{3,2,1,0:T(8,128)}, f32[3,4,64,16]{3,2,1,0:T(8,128)}) custom-call(f32[19,8,32,128]{3,2,1,0:T(8,128)} %refs_0_.1, s32[8,32,128]{2,1,0:T(8,128)} %refs_1_.1, f32[21,4,32,128]{3,2,1,0:T(8,128)} %collective-permute-done.refs_2_, f32[21,4,32,128]{3,2,1,0:T(8,128)} %collective-permute-done.1.refs_3_, f32[21,8,4,128]{3,2,1,0:T(4,128)} %copy-done.1, ...), custom_call_target="tpu_custom_call" | custom-call | flops 78643200 | bytes 9961472 | tf_op jit(solution)/shard_map/pallas_call | solution.py:225
  53.6 0.8 slice.328
  54.4 0.8 slice.330
  55.2 0.8 %slice.385 = f32[1,4,32,128]{3,2,1,0:T(8,128)S(1)} slice(f32[21,4,32,128]{3,2,1,0:T(8,128)} %collective-permute-done.refs_2_), slice={[20:21], [0:4], [0:32], [0:128]} | slice | bytes 131072 | tf_op jit(solution)/shard_map/slice | solution.py:269
  56.1 1.2 %pad_maximum_fusion.4 = (f32[3,4,64,16]{3,2,1,0:T(8,128)S(1)}, f32[3,4,64,16]{3,2,1,0:T(8,128)S(1)}) fusion(f32[3,4,64,16]{3,2,1,0:T(8,128)} %get-tuple-element.5, f32[3,4,2,16]{3,2,1,0:T(2,128)S(1)} %slice.328, f32[3,4,4,16]{3,2,1,0:T(4,128)S(1)} %slice.330), kind=kLoop, calls=%fused_computation.4 | loop fusion | flops 24576 | bytes 152064 | tf_op jit(solution)/shard_map/concatenate | solution.py:298
  57.4 0.2 copy_bitcast_fusion
  57.6 0.9 %reshape.119 = f32[16,1,1536]{2,1,0:T(1,128)} reshape(f32[16,3,4,8,16]{4,3,2,1,0:T(8,128)S(1)} %copy_bitcast_fusion) | data formatting | bytes 196608
  58.5 6.1 %all-to-all-start = ((f32[16,1,1536]{2,1,0:T(1,128)}), f32[16,1,1536]{2,1,0:T(1,128)S(1)}, u32[]{:S(2)}, u32[]{:S(2)}) async-start(f32[16,1,1536]{2,1,0:T(1,128)} %reshape.119), calls=%async_computation | async-start | bytes 196608 | tf_op jit(solution)/shard_map/all_to_all | solution.py:302
  64.7 0.8 %slice.387 = f32[1,4,32,128]{3,2,1,0:T(8,128)S(1)} slice(f32[21,4,32,128]{3,2,1,0:T(8,128)} %collective-permute-done.1.refs_3_), slice={[20:21], [0:4], [0:32], [0:128]} | slice | bytes 131072 | tf_op jit(solution)/shard_map/slice | solution.py:269
  65.6 6.9 %all-to-all-done = f32[16,1,1536]{2,1,0:T(1,128)S(1)} async-done(((f32[16,1,1536]{2,1,0:T(1,128)}), f32[16,1,1536]{2,1,0:T(1,128)S(1)}, u32[]{:S(2)}, u32[]{:S(2)}) %all-to-all-start) | async-done | bytes 98336 | tf_op jit(solution)/shard_map/all_to_all | solution.py:302
  72.5 0.5 broadcast.20
  73.0 0.9 %reduce = f32[16,1536]{1,0:T(8,128)S(1)} reduce(f32[16,1,1536]{2,1,0:T(1,128)S(1)} %all-to-all-done, f32[]{:T(128)} %broadcast.20), dimensions={1}, to_apply=%all_to_all.11.reduce_sub_computation | reduce | bytes 196612 | tf_op jit(solution)/shard_map/all_to_all | solution.py:302
  73.9 0.3 reshape.120
  74.2 0.5 copy.39
  74.7 0.3 squeeze.12
  75.0 2.9 %collective-permute-start.9 = (f32[3,2,8,256]{3,2,1,0:T(8,128)S(1)}, f32[3,2,8,256]{3,2,1,0:T(8,128)S(1)}, u32[]{:S(2)}, u32[]{:S(2)}) collective-permute-start(f32[3,2,8,256]{3,2,1,0:T(8,128)S(1)} %get-tuple-element.36), channel_id=1, source_target_pairs={{0,112},{16,0},{32,16},{48,32},{64,48},{80,64},{96,80},{112,96},{1... | collective-permute-start | bytes 147464 | tf_op jit(solution)/shard_map/ppermute | solution.py:240
  78.0 1.8 %collective-permute-done.8 = f32[3,2,8,256]{3,2,1,0:T(8,128)S(1)} collective-permute-done((f32[3,2,8,256]{3,2,1,0:T(8,128)S(1)}, f32[3,2,8,256]{3,2,1,0:T(8,128)S(1)}, u32[]{:S(2)}, u32[]{:S(2)}) %collective-permute-start.8) | collective-permute-done | bytes 49184 | tf_op jit(solution)/shard_map/ppermute | solution.py:240
  79.9 0.1 fusion.34
  79.9 0.1 fusion.33
  80.0 0.1 fusion.30
  80.1 0.1 fusion.29
  80.2 0.1 slice_multiply_fusion.1
  80.4 0.1 fusion.36
  80.5 0.1 fusion.31
  80.5 0.1 fusion.32
  80.6 0.1 fusion.13
  80.7 0.6 copy.40
  (80 shorter events, 0.8 us)
Async XLA Ops:
  0.6 9.9 %copy-start.3 = (f32[4,4,256]{2,1,0:T(4,128)S(1)}, f32[4,4,256]{2,1,0:T(4,128)}, u32[]{:S(2)}) copy-start(f32[4,4,256]{2,1,0:T(4,128)} %param.5) | copy-start | bytes 49156
  2.4 8.2 %copy-start = (f32[19,8,32,128]{3,2,1,0:T(8,128)S(1)}, f32[19,8,32,128]{3,2,1,0:T(8,128)}, u32[]{:S(2)}) copy-start(f32[19,8,32,128]{3,2,1,0:T(8,128)} %refs_0_.1) | copy-start | bytes 7471108
  4.0 14.5 %collective-permute-start.4 = (f32[21,4,4,128]{3,2,1,0:T(4,128)S(1)}, f32[21,4,4,128]{3,2,1,0:T(4,128)S(1)}, u32[]{:S(2)}, u32[]{:S(2)}) collective-permute-start(f32[21,4,4,128]{3,2,1,0:T(4,128)S(1)} %pad_maximum_fusion.7), channel_id=1, source_target_pairs={{0,17},{1,18},{2,19},{3,20},{4,21},{5,22},{6,23},{7,24},{8,25},{9,... | collective-permute-start | bytes 516104 | tf_op jit(solution)/shard_map/ppermute | solution.py:247
  5.3 17.9 %collective-permute-start.5 = (f32[21,4,4,128]{3,2,1,0:T(4,128)S(1)}, f32[21,4,4,128]{3,2,1,0:T(4,128)S(1)}, u32[]{:S(2)}, u32[]{:S(2)}) collective-permute-start(f32[21,4,4,128]{3,2,1,0:T(4,128)S(1)} %pad_maximum_fusion.8), channel_id=1, source_target_pairs={{0,113},{1,114},{2,115},{3,116},{4,117},{5,118},{6,119},{7,120},{8... | collective-permute-start | bytes 516104 | tf_op jit(solution)/shard_map/ppermute | solution.py:247
  9.3 14.0 %collective-permute-start.6 = (f32[21,4,4,128]{3,2,1,0:T(4,128)S(1)}, f32[21,4,4,128]{3,2,1,0:T(4,128)S(1)}, u32[]{:S(2)}, u32[]{:S(2)}) collective-permute-start(f32[21,4,4,128]{3,2,1,0:T(4,128)S(1)} %pad_maximum_fusion.9), channel_id=1, source_target_pairs={{0,31},{1,16},{2,17},{3,18},{4,19},{5,20},{6,21},{7,22},{8,23},{9,... | collective-permute-start | bytes 516104 | tf_op jit(solution)/shard_map/ppermute | solution.py:247
  12.0 24.4 %collective-permute-start = (f32[21,4,32,128]{3,2,1,0:T(8,128)}, f32[21,4,32,128]{3,2,1,0:T(8,128)}, u32[]{:S(2)}, u32[]{:S(2)}) collective-permute-start(f32[21,4,32,128]{3,2,1,0:T(8,128)} %pad_maximum_fusion), channel_id=1, source_target_pairs={{0,16},{16,32},{32,48},{48,64},{64,80},{80,96},{96,112},{112,0},{1... | collective-permute-start | bytes 4128776 | tf_op jit(solution)/shard_map/ppermute | solution.py:240
  15.7 20.6 %collective-permute-start.1 = (f32[21,4,32,128]{3,2,1,0:T(8,128)}, f32[21,4,32,128]{3,2,1,0:T(8,128)}, u32[]{:S(2)}, u32[]{:S(2)}) collective-permute-start(f32[21,4,32,128]{3,2,1,0:T(8,128)} %pad_maximum_fusion.1), channel_id=1, source_target_pairs={{0,112},{16,0},{32,16},{48,32},{64,48},{80,64},{96,80},{112,96},{1... | collective-permute-start | bytes 4128776 | tf_op jit(solution)/shard_map/ppermute | solution.py:240
  18.6 17.8 %copy-start.4 = (f32[21,4,4,128]{3,2,1,0:T(4,128)}, f32[21,4,4,128]{3,2,1,0:T(4,128)S(1)}, u32[]{:S(2)}) copy-start(f32[21,4,4,128]{3,2,1,0:T(4,128)S(1)} %collective-permute-done.4.refs_6_) | copy-start | bytes 516100
  18.6 17.6 %collective-permute-start.7 = (f32[21,4,4,128]{3,2,1,0:T(4,128)S(1)}, f32[21,4,4,128]{3,2,1,0:T(4,128)S(1)}, u32[]{:S(2)}, u32[]{:S(2)}) collective-permute-start(f32[21,4,4,128]{3,2,1,0:T(4,128)S(1)} %pad_maximum_fusion.10), channel_id=1, source_target_pairs={{0,127},{1,112},{2,113},{3,114},{4,115},{5,116},{6,117},{7,118},{8... | collective-permute-start | bytes 516104 | tf_op jit(solution)/shard_map/ppermute | solution.py:247
  23.2 13.2 %copy-start.5 = (f32[21,4,4,128]{3,2,1,0:T(4,128)}, f32[21,4,4,128]{3,2,1,0:T(4,128)S(1)}, u32[]{:S(2)}) copy-start(f32[21,4,4,128]{3,2,1,0:T(4,128)S(1)} %collective-permute-done.5.refs_7_) | copy-start | bytes 516100
  23.2 13.0 %collective-permute-start.2 = (f32[21,8,4,128]{3,2,1,0:T(4,128)S(1)}, f32[21,8,4,128]{3,2,1,0:T(4,128)S(1)}, u32[]{:S(2)}, u32[]{:S(2)}) collective-permute-start(f32[21,8,4,128]{3,2,1,0:T(4,128)S(1)} %pad_maximum_fusion.5), channel_id=1, source_target_pairs={{0,1},{1,2},{2,3},{3,4},{4,5},{5,6},{6,7},{7,8},{8,9},{9,10},{10,1... | collective-permute-start | bytes 1032200 | tf_op jit(solution)/shard_map/ppermute | solution.py:242
  23.3 13.1 %copy-start.6 = (f32[21,4,4,128]{3,2,1,0:T(4,128)}, f32[21,4,4,128]{3,2,1,0:T(4,128)S(1)}, u32[]{:S(2)}) copy-start(f32[21,4,4,128]{3,2,1,0:T(4,128)S(1)} %collective-permute-done.6.refs_8_) | copy-start | bytes 516100
  23.3 12.9 %collective-permute-start.3 = (f32[21,8,4,128]{3,2,1,0:T(4,128)S(1)}, f32[21,8,4,128]{3,2,1,0:T(4,128)S(1)}, u32[]{:S(2)}, u32[]{:S(2)}) collective-permute-start(f32[21,8,4,128]{3,2,1,0:T(4,128)S(1)} %pad_maximum_fusion.6), channel_id=1, source_target_pairs={{0,15},{1,0},{2,1},{3,2},{4,3},{5,4},{6,5},{7,6},{8,7},{9,8},{10,9... | collective-permute-start | bytes 1032200 | tf_op jit(solution)/shard_map/ppermute | solution.py:242
  36.2 0.7 copy-start.7
  36.2 0.8 copy-start.1
  36.3 0.8 %copy-start.2 = (f32[21,8,4,128]{3,2,1,0:T(4,128)}, f32[21,8,4,128]{3,2,1,0:T(4,128)S(1)}, u32[]{:S(2)}) copy-start(f32[21,8,4,128]{3,2,1,0:T(4,128)S(1)} %collective-permute-done.3.refs_5_) | copy-start | bytes 1032196
  58.5 13.9 %all-to-all-start = ((f32[16,1,1536]{2,1,0:T(1,128)}), f32[16,1,1536]{2,1,0:T(1,128)S(1)}, u32[]{:S(2)}, u32[]{:S(2)}) async-start(f32[16,1,1536]{2,1,0:T(1,128)} %reshape.119), calls=%async_computation | async-start | bytes 196608 | tf_op jit(solution)/shard_map/all_to_all | solution.py:302
  75.0 4.7 %collective-permute-start.8 = (f32[3,2,8,256]{3,2,1,0:T(8,128)S(1)}, f32[3,2,8,256]{3,2,1,0:T(8,128)S(1)}, u32[]{:S(2)}, u32[]{:S(2)}) collective-permute-start(f32[3,2,8,256]{3,2,1,0:T(8,128)S(1)} %get-tuple-element.35), channel_id=1, source_target_pairs={{0,16},{16,32},{32,48},{48,64},{64,80},{80,96},{96,112},{112,0},{1... | collective-permute-start | bytes 147464 | tf_op jit(solution)/shard_map/ppermute | solution.py:240
  75.0 4.7 %collective-permute-start.9 = (f32[3,2,8,256]{3,2,1,0:T(8,128)S(1)}, f32[3,2,8,256]{3,2,1,0:T(8,128)S(1)}, u32[]{:S(2)}, u32[]{:S(2)}) collective-permute-start(f32[3,2,8,256]{3,2,1,0:T(8,128)S(1)} %get-tuple-element.36), channel_id=1, source_target_pairs={{0,112},{16,0},{32,16},{48,32},{64,48},{80,64},{96,80},{112,96},{1... | collective-permute-start | bytes 147464 | tf_op jit(solution)/shard_map/ppermute | solution.py:240

commit v11 on v10

--- a/solution.py
+++ b/solution.py
@@ -157,7 +157,7 @@
                     dst[i, x, pl.ds(r, ROWS), :] = post[i]
             return carry
 
-        lax.fori_loop(s, nx + 2 * h - s, body, 0, unroll=2)
+        lax.fori_loop(s, nx + 2 * h - s, body, 0, unroll=4)
 
     for s in range(h):
         run_step(s)
@@ -182,7 +182,7 @@
                 flow_s[d, x, pl.ds(r, ROWS), :] = jnp.where(solid, jnp.float32(0.0), mom[d] * inv)
         return carry
 
-    lax.fori_loop(0, nx, last_body, 0, unroll=2)
+    lax.fori_loop(0, nx, last_body, 0, unroll=4)
 
     nz = flow_s.shape[3]
     pz = (

time: 82.5 us -> 82 us (level)
  no operation moved by 1% of the time
where the time goes in v11:
time: 82 us; the launch traced here: 80.9 us
  starting transfers between devices  30.3 us (37%)
  waiting for transfers between devices  16.1 us (20%)
  Pallas kernels  16 us (20%)
  local copies, waits for them, and re-layouts  11 us (13%)
  other arithmetic  6.24 us (8%)
  between operations  1.18 us (1%)
    pallas_call x1, Pallas kernels, lb_call(): pl.pallas_call(functools.partial(lb_kernel, halo, nx, ny), out_shape=out_...  16 us
    ppermute x4, starting transfers between devices, send(): return lax.ppermute(x, ('vessel', 'blk'), pairs)  10.7 us
    ppermute x4, starting transfers between devices, send(): return lax.ppermute(x, 'vessel', [(i, (i + dv) % nv) for i in range(nv)])  8.03 us
    ppermute x4, waiting for transfers between devices, send(): return lax.ppermute(x, ('vessel', 'blk'), pairs)  7.47 us
    all_to_all x1, waiting for transfers between devices, local(): lax.all_to_all(windows, 'blk', split_axis=2, concat_axis=4, tiled=True)  6.89 us
    all_to_all x1, starting transfers between devices, local(): lax.all_to_all(windows, 'blk', split_axis=2, concat_axis=4, tiled=True)  6.12 us
    ppermute x2, starting transfers between devices, send(): return lax.ppermute(x, 'blk', [(i, (i + db) % nb) for i in range(nb)])  5.45 us
    unnamed x36, local copies, waits for them, and re-layouts  3.45 us
  transfers between devices with their start and end apart: 11, of which 3 were waited for; matrix products, arithmetic and copies ran while one was open for 5% of the time, Pallas kernels for 0%

profile of v11, /device:TPU:0, one launch (start us, length us, event | category | flops | bytes accessed | tf_op | source)
XLA Modules:
  0.0 80.9 jit_solution(12443577810564154295)
XLA Ops:
  0.6 0.8 %slice_bitcast_fusion.7 = (f32[2,2,2,128]{3,2,1,0:T(2,128)S(1)}, f32[2,2,2,128]{3,2,1,0:T(2,128)S(1)}, f32[2,2,2,128]{3,2,1,0:T(2,128)S(1)}, f32[2,2,2,128]{3,2,1,0:T(2,128)S(1)}) fusion(f32[4,4,256]{2,1,0:T(4,128)} %param.5), kind=kLoop, calls=%fused_computation.66 | loop fusion | bytes 32768
  1.5 0.9 %convert_bitcast_fusion = f32[1,8,32,128]{3,2,1,0:T(8,128)S(1)} fusion(s32[8,32,128]{2,1,0:T(8,128)} %refs_1_.1), kind=kLoop, calls=%fused_computation.12 | loop fusion | flops 32768 | bytes 262144 | tf_op jit(solution)/shard_map/broadcast_in_dim | solution.py:253
  2.4 1.6 %fusion.22 = (f32[19,4,4,128]{3,2,1,0:T(4,128)S(1)}, f32[19,4,4,128]{3,2,1,0:T(4,128)S(1)}, f32[19,4,4,128]{3,2,1,0:T(4,128)S(1)}, f32[19,4,4,128]{3,2,1,0:T(4,128)S(1)}) fusion(f32[19,8,32,128]{3,2,1,0:T(8,128)} %refs_0_.1), kind=kLoop, calls=%fused_computation.72 | loop fusion | bytes 1245184 | tf_op jit(solution)/shard_map/slice | solution.py:262
  4.0 1.2 %collective-permute-start.4 = (f32[21,4,4,128]{3,2,1,0:T(4,128)S(1)}, f32[21,4,4,128]{3,2,1,0:T(4,128)S(1)}, u32[]{:S(2)}, u32[]{:S(2)}) collective-permute-start(f32[21,4,4,128]{3,2,1,0:T(4,128)S(1)} %pad_maximum_fusion.7), channel_id=1, source_target_pairs={{0,17},{1,18},{2,19},{3,20},{4,21},{5,22},{6,23},{7,24},{8,25},{9,... | collective-permute-start | bytes 516104 | tf_op jit(solution)/shard_map/ppermute | solution.py:247
  5.3 4.0 %collective-permute-start.5 = (f32[21,4,4,128]{3,2,1,0:T(4,128)S(1)}, f32[21,4,4,128]{3,2,1,0:T(4,128)S(1)}, u32[]{:S(2)}, u32[]{:S(2)}) collective-permute-start(f32[21,4,4,128]{3,2,1,0:T(4,128)S(1)} %pad_maximum_fusion.8), channel_id=1, source_target_pairs={{0,113},{1,114},{2,115},{3,116},{4,117},{5,118},{6,119},{7,120},{8... | collective-permute-start | bytes 516104 | tf_op jit(solution)/shard_map/ppermute | solution.py:247
  9.3 1.2 %collective-permute-start.6 = (f32[21,4,4,128]{3,2,1,0:T(4,128)S(1)}, f32[21,4,4,128]{3,2,1,0:T(4,128)S(1)}, u32[]{:S(2)}, u32[]{:S(2)}) collective-permute-start(f32[21,4,4,128]{3,2,1,0:T(4,128)S(1)} %pad_maximum_fusion.9), channel_id=1, source_target_pairs={{0,31},{1,16},{2,17},{3,18},{4,19},{5,20},{6,21},{7,22},{8,23},{9,... | collective-permute-start | bytes 516104 | tf_op jit(solution)/shard_map/ppermute | solution.py:247
  10.6 0.2 fusion.24
  10.8 1.2 %pad_maximum_fusion = f32[21,4,32,128]{3,2,1,0:T(8,128)} fusion(f32[1,4,32,128]{3,2,1,0:T(8,128)S(1)} %bitcast.67, f32[1,4,32,128]{3,2,1,0:T(8,128)S(1)} %get-tuple-element.34, f32[19,4,32,128]{3,2,1,0:T(8,128)S(1)} %get-tuple-element.19), kind=kLoop, calls=%fused_computation | loop fusion | flops 688128 | bytes 2752512 | tf_op jit(solution)/shard_map/concatenate | solution.py:266
  12.0 2.5 %collective-permute-start = (f32[21,4,32,128]{3,2,1,0:T(8,128)}, f32[21,4,32,128]{3,2,1,0:T(8,128)}, u32[]{:S(2)}, u32[]{:S(2)}) collective-permute-start(f32[21,4,32,128]{3,2,1,0:T(8,128)} %pad_maximum_fusion), channel_id=1, source_target_pairs={{0,16},{16,32},{32,48},{48,64},{64,80},{80,96},{96,112},{112,0},{1... | collective-permute-start | bytes 4128776 | tf_op jit(solution)/shard_map/ppermute | solution.py:240
  14.5 1.2 %pad_maximum_fusion.1 = f32[21,4,32,128]{3,2,1,0:T(8,128)} fusion(f32[1,4,32,128]{3,2,1,0:T(8,128)S(1)} %bitcast.66, f32[1,4,32,128]{3,2,1,0:T(8,128)S(1)} %get-tuple-element.33, f32[19,4,32,128]{3,2,1,0:T(8,128)S(1)} %get-tuple-element.18), kind=kLoop, calls=%fused_computation.1 | loop fusion | flops 688128 | bytes 2752512 | tf_op jit(solution)/shard_map/concatenate | solution.py:266
  15.7 2.6 %collective-permute-start.1 = (f32[21,4,32,128]{3,2,1,0:T(8,128)}, f32[21,4,32,128]{3,2,1,0:T(8,128)}, u32[]{:S(2)}, u32[]{:S(2)}) collective-permute-start(f32[21,4,32,128]{3,2,1,0:T(8,128)} %pad_maximum_fusion.1), channel_id=1, source_target_pairs={{0,112},{16,0},{32,16},{48,32},{64,48},{80,64},{96,80},{112,96},{1... | collective-permute-start | bytes 4128776 | tf_op jit(solution)/shard_map/ppermute | solution.py:240
  18.3 0.2 fusion.23
  18.6 4.3 %collective-permute-start.7 = (f32[21,4,4,128]{3,2,1,0:T(4,128)S(1)}, f32[21,4,4,128]{3,2,1,0:T(4,128)S(1)}, u32[]{:S(2)}, u32[]{:S(2)}) collective-permute-start(f32[21,4,4,128]{3,2,1,0:T(4,128)S(1)} %pad_maximum_fusion.10), channel_id=1, source_target_pairs={{0,127},{1,112},{2,113},{3,114},{4,115},{5,116},{6,117},{7,118},{8... | collective-permute-start | bytes 516104 | tf_op jit(solution)/shard_map/ppermute | solution.py:247
  22.9 0.1 pad_maximum_fusion.6
  23.1 0.1 pad_maximum_fusion.5
  23.2 0.1 collective-permute-start.2
  23.3 5.4 %collective-permute-start.3 = (f32[21,8,4,128]{3,2,1,0:T(4,128)S(1)}, f32[21,8,4,128]{3,2,1,0:T(4,128)S(1)}, u32[]{:S(2)}, u32[]{:S(2)}) collective-permute-start(f32[21,8,4,128]{3,2,1,0:T(4,128)S(1)} %pad_maximum_fusion.6), channel_id=1, source_target_pairs={{0,15},{1,0},{2,1},{3,2},{4,3},{5,4},{6,5},{7,6},{8,7},{9,8},{10,9... | collective-permute-start | bytes 1032200 | tf_op jit(solution)/shard_map/ppermute | solution.py:242
  28.7 7.5 %collective-permute-done.7.refs_9_ = f32[21,4,4,128]{3,2,1,0:T(4,128)S(1)} collective-permute-done((f32[21,4,4,128]{3,2,1,0:T(4,128)S(1)}, f32[21,4,4,128]{3,2,1,0:T(4,128)S(1)}, u32[]{:S(2)}, u32[]{:S(2)}) %collective-permute-start.7) | collective-permute-done | bytes 172064 | tf_op jit(solution)/shard_map/ppermute | solution.py:247
  36.4 0.5 copy-done.7
  36.9 0.1 copy-done.1
  37.0 0.1 copy-done.2
  37.1 16.0 %shard_map.50 = (f32[19,8,32,128]{3,2,1,0:T(8,128)}, f32[3,4,64,16]{3,2,1,0:T(8,128)}) custom-call(f32[19,8,32,128]{3,2,1,0:T(8,128)} %refs_0_.1, s32[8,32,128]{2,1,0:T(8,128)} %refs_1_.1, f32[21,4,32,128]{3,2,1,0:T(8,128)} %collective-permute-done.refs_2_, f32[21,4,32,128]{3,2,1,0:T(8,128)} %collective-permute-done.1.refs_3_, f32[21,8,4,128]{3,2,1,0:T(4,128)} %copy-done.1, ...), custom_call_target="tpu_custom_call" | custom-call | flops 78643200 | bytes 9961472 | tf_op jit(solution)/shard_map/pallas_call | solution.py:225
  53.1 0.8 slice.328
  53.9 0.8 slice.330
  54.7 0.8 %slice.385 = f32[1,4,32,128]{3,2,1,0:T(8,128)S(1)} slice(f32[21,4,32,128]{3,2,1,0:T(8,128)} %collective-permute-done.refs_2_), slice={[20:21], [0:4], [0:32], [0:128]} | slice | bytes 131072 | tf_op jit(solution)/shard_map/slice | solution.py:269
  55.7 1.2 %pad_maximum_fusion.4 = (f32[3,4,64,16]{3,2,1,0:T(8,128)S(1)}, f32[3,4,64,16]{3,2,1,0:T(8,128)S(1)}) fusion(f32[3,4,64,16]{3,2,1,0:T(8,128)} %get-tuple-element.5, f32[3,4,2,16]{3,2,1,0:T(2,128)S(1)} %slice.328, f32[3,4,4,16]{3,2,1,0:T(4,128)S(1)} %slice.330), kind=kLoop, calls=%fused_computation.4 | loop fusion | flops 24576 | bytes 152064 | tf_op jit(solution)/shard_map/concatenate | solution.py:298
  56.9 0.2 copy_bitcast_fusion
  57.1 0.9 %reshape.119 = f32[16,1,1536]{2,1,0:T(1,128)} reshape(f32[16,3,4,8,16]{4,3,2,1,0:T(8,128)S(1)} %copy_bitcast_fusion) | data formatting | bytes 196608
  58.0 6.1 %all-to-all-start = ((f32[16,1,1536]{2,1,0:T(1,128)}), f32[16,1,1536]{2,1,0:T(1,128)S(1)}, u32[]{:S(2)}, u32[]{:S(2)}) async-start(f32[16,1,1536]{2,1,0:T(1,128)} %reshape.119), calls=%async_computation | async-start | bytes 196608 | tf_op jit(solution)/shard_map/all_to_all | solution.py:302
  64.2 0.8 %slice.387 = f32[1,4,32,128]{3,2,1,0:T(8,128)S(1)} slice(f32[21,4,32,128]{3,2,1,0:T(8,128)} %collective-permute-done.1.refs_3_), slice={[20:21], [0:4], [0:32], [0:128]} | slice | bytes 131072 | tf_op jit(solution)/shard_map/slice | solution.py:269
  65.1 6.9 %all-to-all-done = f32[16,1,1536]{2,1,0:T(1,128)S(1)} async-done(((f32[16,1,1536]{2,1,0:T(1,128)}), f32[16,1,1536]{2,1,0:T(1,128)S(1)}, u32[]{:S(2)}, u32[]{:S(2)}) %all-to-all-start) | async-done | bytes 98336 | tf_op jit(solution)/shard_map/all_to_all | solution.py:302
  72.0 0.5 broadcast.20
  72.5 0.9 %reduce = f32[16,1536]{1,0:T(8,128)S(1)} reduce(f32[16,1,1536]{2,1,0:T(1,128)S(1)} %all-to-all-done, f32[]{:T(128)} %broadcast.20), dimensions={1}, to_apply=%all_to_all.11.reduce_sub_computation | reduce | bytes 196612 | tf_op jit(solution)/shard_map/all_to_all | solution.py:302
  73.4 0.3 reshape.120
  73.7 0.5 copy.39
  74.2 0.3 squeeze.12
  74.6 2.9 %collective-permute-start.9 = (f32[3,2,8,256]{3,2,1,0:T(8,128)S(1)}, f32[3,2,8,256]{3,2,1,0:T(8,128)S(1)}, u32[]{:S(2)}, u32[]{:S(2)}) collective-permute-start(f32[3,2,8,256]{3,2,1,0:T(8,128)S(1)} %get-tuple-element.36), channel_id=1, source_target_pairs={{0,112},{16,0},{32,16},{48,32},{64,48},{80,64},{96,80},{112,96},{1... | collective-permute-start | bytes 147464 | tf_op jit(solution)/shard_map/ppermute | solution.py:240
  77.5 1.8 %collective-permute-done.8 = f32[3,2,8,256]{3,2,1,0:T(8,128)S(1)} collective-permute-done((f32[3,2,8,256]{3,2,1,0:T(8,128)S(1)}, f32[3,2,8,256]{3,2,1,0:T(8,128)S(1)}, u32[]{:S(2)}, u32[]{:S(2)}) %collective-permute-start.8) | collective-permute-done | bytes 49184 | tf_op jit(solution)/shard_map/ppermute | solution.py:240
  79.4 0.1 fusion.34
  79.5 0.1 fusion.33
  79.5 0.1 fusion.30
  79.6 0.1 fusion.29
  79.7 0.1 slice_multiply_fusion.1
  79.9 0.1 fusion.36
  80.0 0.1 fusion.31
  80.1 0.1 fusion.32
  80.2 0.1 fusion.13
  80.3 0.6 copy.40
  (80 shorter events, 0.8 us)
Async XLA Ops:
  0.6 9.9 %copy-start.3 = (f32[4,4,256]{2,1,0:T(4,128)S(1)}, f32[4,4,256]{2,1,0:T(4,128)}, u32[]{:S(2)}) copy-start(f32[4,4,256]{2,1,0:T(4,128)} %param.5) | copy-start | bytes 49156
  2.4 8.2 %copy-start = (f32[19,8,32,128]{3,2,1,0:T(8,128)S(1)}, f32[19,8,32,128]{3,2,1,0:T(8,128)}, u32[]{:S(2)}) copy-start(f32[19,8,32,128]{3,2,1,0:T(8,128)} %refs_0_.1) | copy-start | bytes 7471108
  4.0 14.5 %collective-permute-start.4 = (f32[21,4,4,128]{3,2,1,0:T(4,128)S(1)}, f32[21,4,4,128]{3,2,1,0:T(4,128)S(1)}, u32[]{:S(2)}, u32[]{:S(2)}) collective-permute-start(f32[21,4,4,128]{3,2,1,0:T(4,128)S(1)} %pad_maximum_fusion.7), channel_id=1, source_target_pairs={{0,17},{1,18},{2,19},{3,20},{4,21},{5,22},{6,23},{7,24},{8,25},{9,... | collective-permute-start | bytes 516104 | tf_op jit(solution)/shard_map/ppermute | solution.py:247
  5.3 17.9 %collective-permute-start.5 = (f32[21,4,4,128]{3,2,1,0:T(4,128)S(1)}, f32[21,4,4,128]{3,2,1,0:T(4,128)S(1)}, u32[]{:S(2)}, u32[]{:S(2)}) collective-permute-start(f32[21,4,4,128]{3,2,1,0:T(4,128)S(1)} %pad_maximum_fusion.8), channel_id=1, source_target_pairs={{0,113},{1,114},{2,115},{3,116},{4,117},{5,118},{6,119},{7,120},{8... | collective-permute-start | bytes 516104 | tf_op jit(solution)/shard_map/ppermute | solution.py:247
  9.3 14.0 %collective-permute-start.6 = (f32[21,4,4,128]{3,2,1,0:T(4,128)S(1)}, f32[21,4,4,128]{3,2,1,0:T(4,128)S(1)}, u32[]{:S(2)}, u32[]{:S(2)}) collective-permute-start(f32[21,4,4,128]{3,2,1,0:T(4,128)S(1)} %pad_maximum_fusion.9), channel_id=1, source_target_pairs={{0,31},{1,16},{2,17},{3,18},{4,19},{5,20},{6,21},{7,22},{8,23},{9,... | collective-permute-start | bytes 516104 | tf_op jit(solution)/shard_map/ppermute | solution.py:247
  12.0 24.4 %collective-permute-start = (f32[21,4,32,128]{3,2,1,0:T(8,128)}, f32[21,4,32,128]{3,2,1,0:T(8,128)}, u32[]{:S(2)}, u32[]{:S(2)}) collective-permute-start(f32[21,4,32,128]{3,2,1,0:T(8,128)} %pad_maximum_fusion), channel_id=1, source_target_pairs={{0,16},{16,32},{32,48},{48,64},{64,80},{80,96},{96,112},{112,0},{1... | collective-permute-start | bytes 4128776 | tf_op jit(solution)/shard_map/ppermute | solution.py:240
  15.7 20.6 %collective-permute-start.1 = (f32[21,4,32,128]{3,2,1,0:T(8,128)}, f32[21,4,32,128]{3,2,1,0:T(8,128)}, u32[]{:S(2)}, u32[]{:S(2)}) collective-permute-start(f32[21,4,32,128]{3,2,1,0:T(8,128)} %pad_maximum_fusion.1), channel_id=1, source_target_pairs={{0,112},{16,0},{32,16},{48,32},{64,48},{80,64},{96,80},{112,96},{1... | collective-permute-start | bytes 4128776 | tf_op jit(solution)/shard_map/ppermute | solution.py:240
  18.6 17.8 %copy-start.4 = (f32[21,4,4,128]{3,2,1,0:T(4,128)}, f32[21,4,4,128]{3,2,1,0:T(4,128)S(1)}, u32[]{:S(2)}) copy-start(f32[21,4,4,128]{3,2,1,0:T(4,128)S(1)} %collective-permute-done.4.refs_6_) | copy-start | bytes 516100
  18.6 17.6 %collective-permute-start.7 = (f32[21,4,4,128]{3,2,1,0:T(4,128)S(1)}, f32[21,4,4,128]{3,2,1,0:T(4,128)S(1)}, u32[]{:S(2)}, u32[]{:S(2)}) collective-permute-start(f32[21,4,4,128]{3,2,1,0:T(4,128)S(1)} %pad_maximum_fusion.10), channel_id=1, source_target_pairs={{0,127},{1,112},{2,113},{3,114},{4,115},{5,116},{6,117},{7,118},{8... | collective-permute-start | bytes 516104 | tf_op jit(solution)/shard_map/ppermute | solution.py:247
  23.2 13.2 %copy-start.5 = (f32[21,4,4,128]{3,2,1,0:T(4,128)}, f32[21,4,4,128]{3,2,1,0:T(4,128)S(1)}, u32[]{:S(2)}) copy-start(f32[21,4,4,128]{3,2,1,0:T(4,128)S(1)} %collective-permute-done.5.refs_7_) | copy-start | bytes 516100
  23.2 13.0 %collective-permute-start.2 = (f32[21,8,4,128]{3,2,1,0:T(4,128)S(1)}, f32[21,8,4,128]{3,2,1,0:T(4,128)S(1)}, u32[]{:S(2)}, u32[]{:S(2)}) collective-permute-start(f32[21,8,4,128]{3,2,1,0:T(4,128)S(1)} %pad_maximum_fusion.5), channel_id=1, source_target_pairs={{0,1},{1,2},{2,3},{3,4},{4,5},{5,6},{6,7},{7,8},{8,9},{9,10},{10,1... | collective-permute-start | bytes 1032200 | tf_op jit(solution)/shard_map/ppermute | solution.py:242
  23.3 13.1 %copy-start.6 = (f32[21,4,4,128]{3,2,1,0:T(4,128)}, f32[21,4,4,128]{3,2,1,0:T(4,128)S(1)}, u32[]{:S(2)}) copy-start(f32[21,4,4,128]{3,2,1,0:T(4,128)S(1)} %collective-permute-done.6.refs_8_) | copy-start | bytes 516100
  23.3 12.9 %collective-permute-start.3 = (f32[21,8,4,128]{3,2,1,0:T(4,128)S(1)}, f32[21,8,4,128]{3,2,1,0:T(4,128)S(1)}, u32[]{:S(2)}, u32[]{:S(2)}) collective-permute-start(f32[21,8,4,128]{3,2,1,0:T(4,128)S(1)} %pad_maximum_fusion.6), channel_id=1, source_target_pairs={{0,15},{1,0},{2,1},{3,2},{4,3},{5,4},{6,5},{7,6},{8,7},{9,8},{10,9... | collective-permute-start | bytes 1032200 | tf_op jit(solution)/shard_map/ppermute | solution.py:242
  36.2 0.7 copy-start.7
  36.2 0.8 copy-start.1
  36.3 0.8 %copy-start.2 = (f32[21,8,4,128]{3,2,1,0:T(4,128)}, f32[21,8,4,128]{3,2,1,0:T(4,128)S(1)}, u32[]{:S(2)}) copy-start(f32[21,8,4,128]{3,2,1,0:T(4,128)S(1)} %collective-permute-done.3.refs_5_) | copy-start | bytes 1032196
  58.0 13.9 %all-to-all-start = ((f32[16,1,1536]{2,1,0:T(1,128)}), f32[16,1,1536]{2,1,0:T(1,128)S(1)}, u32[]{:S(2)}, u32[]{:S(2)}) async-start(f32[16,1,1536]{2,1,0:T(1,128)} %reshape.119), calls=%async_computation | async-start | bytes 196608 | tf_op jit(solution)/shard_map/all_to_all | solution.py:302
  74.5 4.7 %collective-permute-start.8 = (f32[3,2,8,256]{3,2,1,0:T(8,128)S(1)}, f32[3,2,8,256]{3,2,1,0:T(8,128)S(1)}, u32[]{:S(2)}, u32[]{:S(2)}) collective-permute-start(f32[3,2,8,256]{3,2,1,0:T(8,128)S(1)} %get-tuple-element.35), channel_id=1, source_target_pairs={{0,16},{16,32},{32,48},{48,64},{64,80},{80,96},{96,112},{112,0},{1... | collective-permute-start | bytes 147464 | tf_op jit(solution)/shard_map/ppermute | solution.py:240
  74.6 4.7 %collective-permute-start.9 = (f32[3,2,8,256]{3,2,1,0:T(8,128)S(1)}, f32[3,2,8,256]{3,2,1,0:T(8,128)S(1)}, u32[]{:S(2)}, u32[]{:S(2)}) collective-permute-start(f32[3,2,8,256]{3,2,1,0:T(8,128)S(1)} %get-tuple-element.36), channel_id=1, source_target_pairs={{0,112},{16,0},{32,16},{48,32},{64,48},{80,64},{96,80},{112,96},{1... | collective-permute-start | bytes 147464 | tf_op jit(solution)/shard_map/ppermute | solution.py:240

commit v12 on v11

--- a/solution.py
+++ b/solution.py
@@ -157,7 +157,7 @@
                     dst[i, x, pl.ds(r, ROWS), :] = post[i]
             return carry
 
-        lax.fori_loop(s, nx + 2 * h - s, body, 0, unroll=4)
+        lax.fori_loop(s, nx + 2 * h - s, body, 0, unroll=8)
 
     for s in range(h):
         run_step(s)
@@ -182,7 +182,7 @@
                 flow_s[d, x, pl.ds(r, ROWS), :] = jnp.where(solid, jnp.float32(0.0), mom[d] * inv)
         return carry
 
-    lax.fori_loop(0, nx, last_body, 0, unroll=4)
+    lax.fori_loop(0, nx, last_body, 0, unroll=8)
 
     nz = flow_s.shape[3]
     pz = (

time: 82 us -> 81.8 us (level)
  no operation moved by 1% of the time
where the time goes in v12:
time: 81.8 us; the launch traced here: 80.7 us
  starting transfers between devices  30.7 us (38%)
  waiting for transfers between devices  16 us (20%)
  Pallas kernels  15.6 us (19%)
  local copies, waits for them, and re-layouts  11 us (13%)
  other arithmetic  6.24 us (8%)
  between operations  1.18 us (1%)
    pallas_call x1, Pallas kernels, lb_call(): pl.pallas_call(functools.partial(lb_kernel, halo, nx, ny), out_shape=out_...  15.6 us
    ppermute x4, starting transfers between devices, send(): return lax.ppermute(x, ('vessel', 'blk'), pairs)  10.7 us
    ppermute x4, starting transfers between devices, send(): return lax.ppermute(x, 'vessel', [(i, (i + dv) % nv) for i in range(nv)])  8.03 us
    ppermute x4, waiting for transfers between devices, send(): return lax.ppermute(x, ('vessel', 'blk'), pairs)  7.28 us
    all_to_all x1, waiting for transfers between devices, local(): lax.all_to_all(windows, 'blk', split_axis=2, concat_axis=4, tiled=True)  6.89 us
    all_to_all x1, starting transfers between devices, local(): lax.all_to_all(windows, 'blk', split_axis=2, concat_axis=4, tiled=True)  6.3 us
    ppermute x2, starting transfers between devices, send(): return lax.ppermute(x, 'blk', [(i, (i + db) % nb) for i in range(nb)])  5.64 us
    unnamed x36, local copies, waits for them, and re-layouts  3.45 us
  transfers between devices with their start and end apart: 11, of which 3 were waited for; matrix products, arithmetic and copies ran while one was open for 5% of the time, Pallas kernels for 0%

profile of v12, /device:TPU:0, one launch (start us, length us, event | category | flops | bytes accessed | tf_op | source)
XLA Modules:
  0.0 80.7 jit_solution(4317565490711730584)
XLA Ops:
  0.6 0.8 %slice_bitcast_fusion.7 = (f32[2,2,2,128]{3,2,1,0:T(2,128)S(1)}, f32[2,2,2,128]{3,2,1,0:T(2,128)S(1)}, f32[2,2,2,128]{3,2,1,0:T(2,128)S(1)}, f32[2,2,2,128]{3,2,1,0:T(2,128)S(1)}) fusion(f32[4,4,256]{2,1,0:T(4,128)} %param.5), kind=kLoop, calls=%fused_computation.66 | loop fusion | bytes 32768
  1.5 0.9 %convert_bitcast_fusion = f32[1,8,32,128]{3,2,1,0:T(8,128)S(1)} fusion(s32[8,32,128]{2,1,0:T(8,128)} %refs_1_.1), kind=kLoop, calls=%fused_computation.12 | loop fusion | flops 32768 | bytes 262144 | tf_op jit(solution)/shard_map/broadcast_in_dim | solution.py:253
  2.4 1.6 %fusion.22 = (f32[19,4,4,128]{3,2,1,0:T(4,128)S(1)}, f32[19,4,4,128]{3,2,1,0:T(4,128)S(1)}, f32[19,4,4,128]{3,2,1,0:T(4,128)S(1)}, f32[19,4,4,128]{3,2,1,0:T(4,128)S(1)}) fusion(f32[19,8,32,128]{3,2,1,0:T(8,128)} %refs_0_.1), kind=kLoop, calls=%fused_computation.72 | loop fusion | bytes 1245184 | tf_op jit(solution)/shard_map/slice | solution.py:262
  4.0 1.2 %collective-permute-start.4 = (f32[21,4,4,128]{3,2,1,0:T(4,128)S(1)}, f32[21,4,4,128]{3,2,1,0:T(4,128)S(1)}, u32[]{:S(2)}, u32[]{:S(2)}) collective-permute-start(f32[21,4,4,128]{3,2,1,0:T(4,128)S(1)} %pad_maximum_fusion.7), channel_id=1, source_target_pairs={{0,17},{1,18},{2,19},{3,20},{4,21},{5,22},{6,23},{7,24},{8,25},{9,... | collective-permute-start | bytes 516104 | tf_op jit(solution)/shard_map/ppermute | solution.py:247
  5.3 4.0 %collective-permute-start.5 = (f32[21,4,4,128]{3,2,1,0:T(4,128)S(1)}, f32[21,4,4,128]{3,2,1,0:T(4,128)S(1)}, u32[]{:S(2)}, u32[]{:S(2)}) collective-permute-start(f32[21,4,4,128]{3,2,1,0:T(4,128)S(1)} %pad_maximum_fusion.8), channel_id=1, source_target_pairs={{0,113},{1,114},{2,115},{3,116},{4,117},{5,118},{6,119},{7,120},{8... | collective-permute-start | bytes 516104 | tf_op jit(solution)/shard_map/ppermute | solution.py:247
  9.3 1.2 %collective-permute-start.6 = (f32[21,4,4,128]{3,2,1,0:T(4,128)S(1)}, f32[21,4,4,128]{3,2,1,0:T(4,128)S(1)}, u32[]{:S(2)}, u32[]{:S(2)}) collective-permute-start(f32[21,4,4,128]{3,2,1,0:T(4,128)S(1)} %pad_maximum_fusion.9), channel_id=1, source_target_pairs={{0,31},{1,16},{2,17},{3,18},{4,19},{5,20},{6,21},{7,22},{8,23},{9,... | collective-permute-start | bytes 516104 | tf_op jit(solution)/shard_map/ppermute | solution.py:247
  10.6 0.2 fusion.24
  10.8 1.2 %pad_maximum_fusion = f32[21,4,32,128]{3,2,1,0:T(8,128)} fusion(f32[1,4,32,128]{3,2,1,0:T(8,128)S(1)} %bitcast.67, f32[1,4,32,128]{3,2,1,0:T(8,128)S(1)} %get-tuple-element.34, f32[19,4,32,128]{3,2,1,0:T(8,128)S(1)} %get-tuple-element.19), kind=kLoop, calls=%fused_computation | loop fusion | flops 688128 | bytes 2752512 | tf_op jit(solution)/shard_map/concatenate | solution.py:266
  12.0 2.5 %collective-permute-start = (f32[21,4,32,128]{3,2,1,0:T(8,128)}, f32[21,4,32,128]{3,2,1,0:T(8,128)}, u32[]{:S(2)}, u32[]{:S(2)}) collective-permute-start(f32[21,4,32,128]{3,2,1,0:T(8,128)} %pad_maximum_fusion), channel_id=1, source_target_pairs={{0,16},{16,32},{32,48},{48,64},{64,80},{80,96},{96,112},{112,0},{1... | collective-permute-start | bytes 4128776 | tf_op jit(solution)/shard_map/ppermute | solution.py:240
  14.5 1.2 %pad_maximum_fusion.1 = f32[21,4,32,128]{3,2,1,0:T(8,128)} fusion(f32[1,4,32,128]{3,2,1,0:T(8,128)S(1)} %bitcast.66, f32[1,4,32,128]{3,2,1,0:T(8,128)S(1)} %get-tuple-element.33, f32[19,4,32,128]{3,2,1,0:T(8,128)S(1)} %get-tuple-element.18), kind=kLoop, calls=%fused_computation.1 | loop fusion | flops 688128 | bytes 2752512 | tf_op jit(solution)/shard_map/concatenate | solution.py:266
  15.7 2.6 %collective-permute-start.1 = (f32[21,4,32,128]{3,2,1,0:T(8,128)}, f32[21,4,32,128]{3,2,1,0:T(8,128)}, u32[]{:S(2)}, u32[]{:S(2)}) collective-permute-start(f32[21,4,32,128]{3,2,1,0:T(8,128)} %pad_maximum_fusion.1), channel_id=1, source_target_pairs={{0,112},{16,0},{32,16},{48,32},{64,48},{80,64},{96,80},{112,96},{1... | collective-permute-start | bytes 4128776 | tf_op jit(solution)/shard_map/ppermute | solution.py:240
  18.3 0.2 fusion.23
  18.6 4.3 %collective-permute-start.7 = (f32[21,4,4,128]{3,2,1,0:T(4,128)S(1)}, f32[21,4,4,128]{3,2,1,0:T(4,128)S(1)}, u32[]{:S(2)}, u32[]{:S(2)}) collective-permute-start(f32[21,4,4,128]{3,2,1,0:T(4,128)S(1)} %pad_maximum_fusion.10), channel_id=1, source_target_pairs={{0,127},{1,112},{2,113},{3,114},{4,115},{5,116},{6,117},{7,118},{8... | collective-permute-start | bytes 516104 | tf_op jit(solution)/shard_map/ppermute | solution.py:247
  22.9 0.1 pad_maximum_fusion.6
  23.1 0.1 pad_maximum_fusion.5
  23.2 0.1 collective-permute-start.2
  23.3 5.6 %collective-permute-start.3 = (f32[21,8,4,128]{3,2,1,0:T(4,128)S(1)}, f32[21,8,4,128]{3,2,1,0:T(4,128)S(1)}, u32[]{:S(2)}, u32[]{:S(2)}) collective-permute-start(f32[21,8,4,128]{3,2,1,0:T(4,128)S(1)} %pad_maximum_fusion.6), channel_id=1, source_target_pairs={{0,15},{1,0},{2,1},{3,2},{4,3},{5,4},{6,5},{7,6},{8,7},{9,8},{10,9... | collective-permute-start | bytes 1032200 | tf_op jit(solution)/shard_map/ppermute | solution.py:242
  28.9 7.3 %collective-permute-done.7.refs_9_ = f32[21,4,4,128]{3,2,1,0:T(4,128)S(1)} collective-permute-done((f32[21,4,4,128]{3,2,1,0:T(4,128)S(1)}, f32[21,4,4,128]{3,2,1,0:T(4,128)S(1)}, u32[]{:S(2)}, u32[]{:S(2)}) %collective-permute-start.7) | collective-permute-done | bytes 172064 | tf_op jit(solution)/shard_map/ppermute | solution.py:247
  36.4 0.5 copy-done.7
  36.9 0.1 copy-done.1
  37.0 0.1 copy-done.2
  37.1 15.6 %shard_map.50 = (f32[19,8,32,128]{3,2,1,0:T(8,128)}, f32[3,4,64,16]{3,2,1,0:T(8,128)}) custom-call(f32[19,8,32,128]{3,2,1,0:T(8,128)} %refs_0_.1, s32[8,32,128]{2,1,0:T(8,128)} %refs_1_.1, f32[21,4,32,128]{3,2,1,0:T(8,128)} %collective-permute-done.refs_2_, f32[21,4,32,128]{3,2,1,0:T(8,128)} %collective-permute-done.1.refs_3_, f32[21,8,4,128]{3,2,1,0:T(4,128)} %copy-done.1, ...), custom_call_target="tpu_custom_call" | custom-call | flops 78643200 | bytes 9961472 | tf_op jit(solution)/shard_map/pallas_call | solution.py:225
  52.7 0.8 slice.328
  53.5 0.8 slice.330
  54.4 0.8 %slice.385 = f32[1,4,32,128]{3,2,1,0:T(8,128)S(1)} slice(f32[21,4,32,128]{3,2,1,0:T(8,128)} %collective-permute-done.refs_2_), slice={[20:21], [0:4], [0:32], [0:128]} | slice | bytes 131072 | tf_op jit(solution)/shard_map/slice | solution.py:269
  55.3 1.2 %pad_maximum_fusion.4 = (f32[3,4,64,16]{3,2,1,0:T(8,128)S(1)}, f32[3,4,64,16]{3,2,1,0:T(8,128)S(1)}) fusion(f32[3,4,64,16]{3,2,1,0:T(8,128)} %get-tuple-element.5, f32[3,4,2,16]{3,2,1,0:T(2,128)S(1)} %slice.328, f32[3,4,4,16]{3,2,1,0:T(4,128)S(1)} %slice.330), kind=kLoop, calls=%fused_computation.4 | loop fusion | flops 24576 | bytes 152064 | tf_op jit(solution)/shard_map/concatenate | solution.py:298
  56.5 0.2 copy_bitcast_fusion
  56.7 0.9 %reshape.119 = f32[16,1,1536]{2,1,0:T(1,128)} reshape(f32[16,3,4,8,16]{4,3,2,1,0:T(8,128)S(1)} %copy_bitcast_fusion) | data formatting | bytes 196608
  57.7 6.3 %all-to-all-start = ((f32[16,1,1536]{2,1,0:T(1,128)}), f32[16,1,1536]{2,1,0:T(1,128)S(1)}, u32[]{:S(2)}, u32[]{:S(2)}) async-start(f32[16,1,1536]{2,1,0:T(1,128)} %reshape.119), calls=%async_computation | async-start | bytes 196608 | tf_op jit(solution)/shard_map/all_to_all | solution.py:302
  64.0 0.8 %slice.387 = f32[1,4,32,128]{3,2,1,0:T(8,128)S(1)} slice(f32[21,4,32,128]{3,2,1,0:T(8,128)} %collective-permute-done.1.refs_3_), slice={[20:21], [0:4], [0:32], [0:128]} | slice | bytes 131072 | tf_op jit(solution)/shard_map/slice | solution.py:269
  64.9 6.9 %all-to-all-done = f32[16,1,1536]{2,1,0:T(1,128)S(1)} async-done(((f32[16,1,1536]{2,1,0:T(1,128)}), f32[16,1,1536]{2,1,0:T(1,128)S(1)}, u32[]{:S(2)}, u32[]{:S(2)}) %all-to-all-start) | async-done | bytes 98336 | tf_op jit(solution)/shard_map/all_to_all | solution.py:302
  71.8 0.5 broadcast.20
  72.3 0.9 %reduce = f32[16,1536]{1,0:T(8,128)S(1)} reduce(f32[16,1,1536]{2,1,0:T(1,128)S(1)} %all-to-all-done, f32[]{:T(128)} %broadcast.20), dimensions={1}, to_apply=%all_to_all.11.reduce_sub_computation | reduce | bytes 196612 | tf_op jit(solution)/shard_map/all_to_all | solution.py:302
  73.2 0.3 reshape.120
  73.5 0.5 copy.39
  74.0 0.3 squeeze.12
  74.3 2.9 %collective-permute-start.9 = (f32[3,2,8,256]{3,2,1,0:T(8,128)S(1)}, f32[3,2,8,256]{3,2,1,0:T(8,128)S(1)}, u32[]{:S(2)}, u32[]{:S(2)}) collective-permute-start(f32[3,2,8,256]{3,2,1,0:T(8,128)S(1)} %get-tuple-element.36), channel_id=1, source_target_pairs={{0,112},{16,0},{32,16},{48,32},{64,48},{80,64},{96,80},{112,96},{1... | collective-permute-start | bytes 147464 | tf_op jit(solution)/shard_map/ppermute | solution.py:240
  77.3 1.8 %collective-permute-done.8 = f32[3,2,8,256]{3,2,1,0:T(8,128)S(1)} collective-permute-done((f32[3,2,8,256]{3,2,1,0:T(8,128)S(1)}, f32[3,2,8,256]{3,2,1,0:T(8,128)S(1)}, u32[]{:S(2)}, u32[]{:S(2)}) %collective-permute-start.8) | collective-permute-done | bytes 49184 | tf_op jit(solution)/shard_map/ppermute | solution.py:240
  79.2 0.1 fusion.34
  79.2 0.1 fusion.33
  79.3 0.1 fusion.30
  79.4 0.1 fusion.29
  79.5 0.1 slice_multiply_fusion.1
  79.7 0.1 fusion.36
  79.8 0.1 fusion.31
  79.8 0.1 fusion.32
  79.9 0.1 fusion.13
  80.1 0.6 copy.40
  (80 shorter events, 0.8 us)
Async XLA Ops:
  0.6 9.9 %copy-start.3 = (f32[4,4,256]{2,1,0:T(4,128)S(1)}, f32[4,4,256]{2,1,0:T(4,128)}, u32[]{:S(2)}) copy-start(f32[4,4,256]{2,1,0:T(4,128)} %param.5) | copy-start | bytes 49156
  2.4 8.2 %copy-start = (f32[19,8,32,128]{3,2,1,0:T(8,128)S(1)}, f32[19,8,32,128]{3,2,1,0:T(8,128)}, u32[]{:S(2)}) copy-start(f32[19,8,32,128]{3,2,1,0:T(8,128)} %refs_0_.1) | copy-start | bytes 7471108
  4.0 14.5 %collective-permute-start.4 = (f32[21,4,4,128]{3,2,1,0:T(4,128)S(1)}, f32[21,4,4,128]{3,2,1,0:T(4,128)S(1)}, u32[]{:S(2)}, u32[]{:S(2)}) collective-permute-start(f32[21,4,4,128]{3,2,1,0:T(4,128)S(1)} %pad_maximum_fusion.7), channel_id=1, source_target_pairs={{0,17},{1,18},{2,19},{3,20},{4,21},{5,22},{6,23},{7,24},{8,25},{9,... | collective-permute-start | bytes 516104 | tf_op jit(solution)/shard_map/ppermute | solution.py:247
  5.3 17.9 %collective-permute-start.5 = (f32[21,4,4,128]{3,2,1,0:T(4,128)S(1)}, f32[21,4,4,128]{3,2,1,0:T(4,128)S(1)}, u32[]{:S(2)}, u32[]{:S(2)}) collective-permute-start(f32[21,4,4,128]{3,2,1,0:T(4,128)S(1)} %pad_maximum_fusion.8), channel_id=1, source_target_pairs={{0,113},{1,114},{2,115},{3,116},{4,117},{5,118},{6,119},{7,120},{8... | collective-permute-start | bytes 516104 | tf_op jit(solution)/shard_map/ppermute | solution.py:247
  9.3 14.0 %collective-permute-start.6 = (f32[21,4,4,128]{3,2,1,0:T(4,128)S(1)}, f32[21,4,4,128]{3,2,1,0:T(4,128)S(1)}, u32[]{:S(2)}, u32[]{:S(2)}) collective-permute-start(f32[21,4,4,128]{3,2,1,0:T(4,128)S(1)} %pad_maximum_fusion.9), channel_id=1, source_target_pairs={{0,31},{1,16},{2,17},{3,18},{4,19},{5,20},{6,21},{7,22},{8,23},{9,... | collective-permute-start | bytes 516104 | tf_op jit(solution)/shard_map/ppermute | solution.py:247
  12.0 24.4 %collective-permute-start = (f32[21,4,32,128]{3,2,1,0:T(8,128)}, f32[21,4,32,128]{3,2,1,0:T(8,128)}, u32[]{:S(2)}, u32[]{:S(2)}) collective-permute-start(f32[21,4,32,128]{3,2,1,0:T(8,128)} %pad_maximum_fusion), channel_id=1, source_target_pairs={{0,16},{16,32},{32,48},{48,64},{64,80},{80,96},{96,112},{112,0},{1... | collective-permute-start | bytes 4128776 | tf_op jit(solution)/shard_map/ppermute | solution.py:240
  15.7 20.6 %collective-permute-start.1 = (f32[21,4,32,128]{3,2,1,0:T(8,128)}, f32[21,4,32,128]{3,2,1,0:T(8,128)}, u32[]{:S(2)}, u32[]{:S(2)}) collective-permute-start(f32[21,4,32,128]{3,2,1,0:T(8,128)} %pad_maximum_fusion.1), channel_id=1, source_target_pairs={{0,112},{16,0},{32,16},{48,32},{64,48},{80,64},{96,80},{112,96},{1... | collective-permute-start | bytes 4128776 | tf_op jit(solution)/shard_map/ppermute | solution.py:240
  18.6 17.8 %copy-start.4 = (f32[21,4,4,128]{3,2,1,0:T(4,128)}, f32[21,4,4,128]{3,2,1,0:T(4,128)S(1)}, u32[]{:S(2)}) copy-start(f32[21,4,4,128]{3,2,1,0:T(4,128)S(1)} %collective-permute-done.4.refs_6_) | copy-start | bytes 516100
  18.6 17.6 %collective-permute-start.7 = (f32[21,4,4,128]{3,2,1,0:T(4,128)S(1)}, f32[21,4,4,128]{3,2,1,0:T(4,128)S(1)}, u32[]{:S(2)}, u32[]{:S(2)}) collective-permute-start(f32[21,4,4,128]{3,2,1,0:T(4,128)S(1)} %pad_maximum_fusion.10), channel_id=1, source_target_pairs={{0,127},{1,112},{2,113},{3,114},{4,115},{5,116},{6,117},{7,118},{8... | collective-permute-start | bytes 516104 | tf_op jit(solution)/shard_map/ppermute | solution.py:247
  23.2 13.2 %copy-start.5 = (f32[21,4,4,128]{3,2,1,0:T(4,128)}, f32[21,4,4,128]{3,2,1,0:T(4,128)S(1)}, u32[]{:S(2)}) copy-start(f32[21,4,4,128]{3,2,1,0:T(4,128)S(1)} %collective-permute-done.5.refs_7_) | copy-start | bytes 516100
  23.2 13.0 %collective-permute-start.2 = (f32[21,8,4,128]{3,2,1,0:T(4,128)S(1)}, f32[21,8,4,128]{3,2,1,0:T(4,128)S(1)}, u32[]{:S(2)}, u32[]{:S(2)}) collective-permute-start(f32[21,8,4,128]{3,2,1,0:T(4,128)S(1)} %pad_maximum_fusion.5), channel_id=1, source_target_pairs={{0,1},{1,2},{2,3},{3,4},{4,5},{5,6},{6,7},{7,8},{8,9},{9,10},{10,1... | collective-permute-start | bytes 1032200 | tf_op jit(solution)/shard_map/ppermute | solution.py:242
  23.3 13.1 %copy-start.6 = (f32[21,4,4,128]{3,2,1,0:T(4,128)}, f32[21,4,4,128]{3,2,1,0:T(4,128)S(1)}, u32[]{:S(2)}) copy-start(f32[21,4,4,128]{3,2,1,0:T(4,128)S(1)} %collective-permute-done.6.refs_8_) | copy-start | bytes 516100
  23.3 12.9 %collective-permute-start.3 = (f32[21,8,4,128]{3,2,1,0:T(4,128)S(1)}, f32[21,8,4,128]{3,2,1,0:T(4,128)S(1)}, u32[]{:S(2)}, u32[]{:S(2)}) collective-permute-start(f32[21,8,4,128]{3,2,1,0:T(4,128)S(1)} %pad_maximum_fusion.6), channel_id=1, source_target_pairs={{0,15},{1,0},{2,1},{3,2},{4,3},{5,4},{6,5},{7,6},{8,7},{9,8},{10,9... | collective-permute-start | bytes 1032200 | tf_op jit(solution)/shard_map/ppermute | solution.py:242
  36.2 0.7 copy-start.7
  36.2 0.8 copy-start.1
  36.3 0.8 %copy-start.2 = (f32[21,8,4,128]{3,2,1,0:T(4,128)}, f32[21,8,4,128]{3,2,1,0:T(4,128)S(1)}, u32[]{:S(2)}) copy-start(f32[21,8,4,128]{3,2,1,0:T(4,128)S(1)} %collective-permute-done.3.refs_5_) | copy-start | bytes 1032196
  57.7 14.1 %all-to-all-start = ((f32[16,1,1536]{2,1,0:T(1,128)}), f32[16,1,1536]{2,1,0:T(1,128)S(1)}, u32[]{:S(2)}, u32[]{:S(2)}) async-start(f32[16,1,1536]{2,1,0:T(1,128)} %reshape.119), calls=%async_computation | async-start | bytes 196608 | tf_op jit(solution)/shard_map/all_to_all | solution.py:302
  74.3 4.7 %collective-permute-start.8 = (f32[3,2,8,256]{3,2,1,0:T(8,128)S(1)}, f32[3,2,8,256]{3,2,1,0:T(8,128)S(1)}, u32[]{:S(2)}, u32[]{:S(2)}) collective-permute-start(f32[3,2,8,256]{3,2,1,0:T(8,128)S(1)} %get-tuple-element.35), channel_id=1, source_target_pairs={{0,16},{16,32},{32,48},{48,64},{64,80},{80,96},{96,112},{112,0},{1... | collective-permute-start | bytes 147464 | tf_op jit(solution)/shard_map/ppermute | solution.py:240
  74.3 4.7 %collective-permute-start.9 = (f32[3,2,8,256]{3,2,1,0:T(8,128)S(1)}, f32[3,2,8,256]{3,2,1,0:T(8,128)S(1)}, u32[]{:S(2)}, u32[]{:S(2)}) collective-permute-start(f32[3,2,8,256]{3,2,1,0:T(8,128)S(1)} %get-tuple-element.36), channel_id=1, source_target_pairs={{0,112},{16,0},{32,16},{48,32},{64,48},{80,64},{96,80},{112,96},{1... | collective-permute-start | bytes 147464 | tf_op jit(solution)/shard_map/ppermute | solution.py:240
